TPU v7x, 32 devices: a whole 2x2x4 slice. The times are simulated.
32 devices in a mesh: row: 2 (over core), col: 16 (over z, y, x).
Axes of the slice: x: 2, y: 2, z: 4, core: 2. Of those that a mesh axis runs over, the one named last changes fastest.
Arguments:
- features: bfloat16 [8192, 128], P(('row', 'col')), may hold values from -6 to 6
- tile_vals: bfloat16 [2, 16, 128, 128, 128], P('row', 'col'), may hold values from -0.15625 to 0.15625
- tile_rows: int32 [2, 16, 128], P('row', 'col'), may hold values from 0 to 31, as said below
- tile_cols: int32 [2, 16, 128], P('row', 'col'), may hold values from 0 to 3
- tile_count: int32 [2, 16], P('row', 'col'), may hold values from 16 to 128, as said below
- w_fwd: bfloat16 [128, 256], replicated, may hold values from -0.5 to 0.5
- w_bwd: bfloat16 [128, 256], replicated, may hold values from -0.5 to 0.5
Outputs:
- updated: bfloat16 [8192, 256], P(('row', 'col'))
Inputs may be any that keep to these rules, and one draw needn't show every extreme that they name: Within one grid cell the pairs (tile_rows, tile_cols) of all slots are distinct. `tile_count`: some grid cell has all 128 slots live.
All inputs are finite; a program needn't handle non-finite values.
Results may differ from a plain program's by a relative error of at most 0.001.
Values may be sent and summed in bfloat16 or wider, within the bound.
No kernel may reach another device: no remote copies, remote signals or barrier semaphores. Data moves between devices by JAX's collectives and lax.ppermute only.
A program may use at most 128 MiB of HBM per device.

v0:
```python
import jax
import jax.numpy as jnp
from jax import lax
from jax.sharding import PartitionSpec as P


def local(features, tile_vals, tile_rows, tile_cols, tile_count, w_fwd, w_bwd):
    row_size = lax.axis_size("row")
    col_size = lax.axis_size("col")
    values = tile_vals[0, 0]
    rowblk = tile_rows[0, 0]
    colblk = tile_cols[0, 0]
    slots = values.shape[0]
    side = values.shape[1]
    nodes_here = features.shape[0]
    live = jnp.arange(slots, dtype=jnp.int32) < tile_count[0, 0]
    masked = jnp.where(live[:, None, None], values, jnp.zeros_like(values))
    width = features.shape[1]
    group = lax.all_gather(features, "row", axis=0, tiled=True).reshape(-1, side, width)
    stripe = lax.all_gather(features, "col", axis=0, tiled=True).reshape(-1, side, width)
    fwd_terms = jnp.einsum(
        "kab,kbf->kaf", masked, group[colblk], preferred_element_type=jnp.float32
    )
    bwd_terms = jnp.einsum(
        "kba,kbf->kaf", masked, stripe[rowblk], preferred_element_type=jnp.float32
    )
    fwd_parts = jax.ops.segment_sum(fwd_terms, rowblk, num_segments=col_size * nodes_here // side)
    bwd_parts = jax.ops.segment_sum(bwd_terms, colblk, num_segments=row_size * nodes_here // side)
    along = lax.psum_scatter(fwd_parts.reshape(-1, width), "col", scatter_dimension=0, tiled=True)
    against = lax.psum_scatter(bwd_parts.reshape(-1, width), "row", scatter_dimension=0, tiled=True)
    result = jnp.dot(along, w_fwd.astype(jnp.float32), precision=lax.Precision.HIGHEST)
    result = result + jnp.dot(against, w_bwd.astype(jnp.float32), precision=lax.Precision.HIGHEST)
    return result.astype(jnp.bfloat16)


def solution(mesh):
    in_specs = (
        P(("row", "col"), None),
        P("row", "col", None, None, None),
        P("row", "col", None),
        P("row", "col", None),
        P("row", "col"),
        P(),
        P(),
    )
    out_specs = P(("row", "col"), None)
    return jax.shard_map(local, mesh=mesh, in_specs=in_specs, out_specs=out_specs, check_vma=False)
```

profile of v0, /device:TPU:0, one launch (start us, length us, event | category | flops | bytes accessed | tf_op | source)
XLA Modules:
  0.0 165.4 jit_solution(15567480636758884985)
XLA Ops:
  6.5 0.0 copy-start
  6.5 0.0 all-gather.2.cloned.1.call-start
  6.5 0.7 all-gather.2.cloned.1.call-update
  7.3 0.0 reduce-scatter.3.cloned.1.call-start
  8.0 2.2 %all_gather.6 = bf16[512,128]{1,0:T(8,128)(2,1)S(1)} all-gather(bf16[256,128]{1,0:T(8,128)(2,1)} %param.7), channel_id=1, replica_groups=mesh['row'=2,'col'=16] {'row'}, dimensions={0}, use_global_device_ids=true | all-gather | bytes 196608 | tf_op jit(solution)/shard_map/all_gather | solution.py:19
  10.2 0.7 fusion.3
  10.8 3.0 %gather_fusion = bf16[128,128,128]{2,1,0:T(8,128)(2,1)} fusion(bf16[4,128,128]{2,1,0:T(8,128)(2,1)S(1)} %bitcast.27, s32[1024]{0:T(1024)S(1)} %pad_clamp_fusion.1), kind=kCustom, calls=%fused_computation | custom fusion | bytes 8389120 | tf_op jit(solution)/shard_map/gather | solution.py:22
  13.9 0.0 copy-start.4
  13.9 8.0 %fusion.1 = f32[128,128,128]{2,1,0:T(8,128)} fusion(bf16[128,128,128]{2,1,0:T(8,128)(2,1)} %gather_fusion, bf16[1,1,128,128,128]{4,3,2,1,0:T(8,128)(2,1)} %param.8, pred[128]{0:T(512)(128)(4,1)S(1)} %iota_compare_fusion), kind=kOutput, calls=%fused_computation.6 | convolution fusion | flops 538968064 | bytes 16777344 | tf_op jit(solution)/shard_map/kab,kbf->kaf/dot_general | solution.py:21
  21.9 0.2 broadcast_in_dim.20
  22.1 0.0 copy-done.4
  22.1 17.1 %scatter_fusion = f32[32,128,128]{2,1,0:T(8,128)S(1)} fusion(f32[32,128,128]{2,1,0:T(8,128)S(1)} %broadcast_in_dim.20, s32[128]{0:T(128)S(1)} %bitcast.30, f32[128,128,128]{2,1,0:T(8,128)} %fusion.1), kind=kCustom, calls=%fused_computation.2 | custom fusion | flops 2097152 | bytes 25166336 | tf_op jit(solution)/shard_map/scatter-add | solution.py:27
  39.2 0.0 copy-start.2
  39.2 1.3 copy-done.2
  40.5 0.0 reduce-scatter.3.cloned.1.call-update
  40.5 0.0 reduce-scatter.5.cloned.1.call-start
  40.6 27.5 %all-gather.2.cloned.1.call-done = bf16[4096,128]{1,0:T(8,128)(2,1)} async-done(((bf16[256,128]{1,0:T(8,128)(2,1)}), bf16[4096,128]{1,0:T(8,128)(2,1)}) %all-gather.2.cloned.1.call-update) | async-done | bytes 1048592 | tf_op jit(solution)/shard_map/all_gather | solution.py:20
  68.1 4.3 %gather_fusion.1 = bf16[128,128,128]{2,1,0:T(8,128)(2,1)} fusion(bf16[32,128,128]{2,1,0:T(8,128)(2,1)} %bitcast.29, s32[1024]{0:T(1024)S(1)} %pad_clamp_fusion), kind=kCustom, calls=%fused_computation.1 | custom fusion | bytes 8389120 | tf_op jit(solution)/shard_map/gather | solution.py:25
  72.4 0.0 copy-start.5
  72.4 8.5 %fusion = f32[128,128,128]{2,1,0:T(8,128)} fusion(bf16[128,128,128]{2,1,0:T(8,128)(2,1)} %gather_fusion.1, bf16[1,1,128,128,128]{4,3,2,1,0:T(8,128)(2,1)} %param.8, pred[128]{0:T(512)(128)(4,1)S(1)} %iota_compare_fusion), kind=kOutput, calls=%fused_computation.5 | convolution fusion | flops 538968064 | bytes 16777344 | tf_op jit(solution)/shard_map/kba,kbf->kaf/dot_general | solution.py:24
  80.9 0.0 copy-done.5
  80.9 0.0 copy-start.3
  80.9 17.0 %scatter_fusion.1 = f32[4,128,128]{2,1,0:T(8,128)S(1)} fusion(f32[4,128,128]{2,1,0:T(8,128)S(1)} %broadcast_in_dim.23, s32[128]{0:T(128)S(1)} %bitcast.31, f32[128,128,128]{2,1,0:T(8,128)} %fusion), kind=kCustom, calls=%fused_computation.3 | custom fusion | flops 2097152 | bytes 25166336 | tf_op jit(solution)/shard_map/scatter-add | solution.py:28
  97.9 0.0 copy-start.1
  98.0 0.7 copy-done.1
  98.6 0.0 reduce-scatter.5.cloned.1.call-update
  98.7 51.0 %reduce-scatter.3.cloned.1.call-done = f32[256,128]{1,0:T(8,128)} async-done(((f32[4096,128]{1,0:T(8,128)}), f32[256,128]{1,0:T(8,128)}) %reduce-scatter.3.cloned.1.call-update) | async-done | bytes 131088 | tf_op jit(solution)/shard_map/reduce_scatter | solution.py:29
  149.7 0.0 copy-done
  149.7 1.2 fusion.7
  150.9 6.1 %reduce-scatter.5.cloned.1.call-done = f32[256,128]{1,0:T(8,128)} async-done(((f32[512,128]{1,0:T(8,128)}), f32[256,128]{1,0:T(8,128)}) %reduce-scatter.5.cloned.1.call-update) | async-done | bytes 131088 | tf_op jit(solution)/shard_map/reduce_scatter | solution.py:30
  157.0 0.0 copy-done.3
  157.0 1.8 %fusion.2 = bf16[256,256]{1,0:T(8,128)(2,1)} fusion(f32[256,256]{1,0:T(8,128)S(1)} %fusion.7, f32[256,128]{1,0:T(8,128)} %reduce-scatter.5.cloned.1.call-done, bf16[128,256]{1,0:T(8,128)(2,1)S(1)} %copy-done.3), kind=kOutput, calls=%fused_computation.8 | convolution fusion | flops 100794368 | bytes 589824 | tf_op jit(solution)/shard_map/dot_general | solution.py:32
  (5 shorter events, 0.0 us)
Async XLA Ops:
  6.5 143.2 %copy-start = (bf16[128,256]{1,0:T(8,128)(2,1)S(1)}, bf16[128,256]{1,0:T(8,128)(2,1)}, u32[]{:S(2)}) copy-start(bf16[128,256]{1,0:T(8,128)(2,1)} %param.12) | copy-start | bytes 196612
  6.5 61.6 %all-gather.2.cloned.1.call-start = ((), (), s32[]{:S(2)}) async-start(), calls=%async_computation.3 | async-start | bytes 1114112 | tf_op jit(solution)/shard_map/all_gather | solution.py:20
  7.3 142.5 %reduce-scatter.3.cloned.1.call-start = ((), (), s32[]{:S(2)}) async-start(), calls=%async_computation.2 | async-start | bytes 2228224 | tf_op jit(solution)/shard_map/reduce_scatter | solution.py:29
  13.9 8.2 %copy-start.4 = (s32[1,1,128]{2,1,0:T(1,128)S(1)}, s32[1,1,128]{2,1,0:T(1,128)}, u32[]{:S(2)}) copy-start(s32[1,1,128]{2,1,0:T(1,128)} %param.9) | copy-start | bytes 1540
  39.2 1.3 copy-start.2
  40.5 116.5 %reduce-scatter.5.cloned.1.call-start = ((), (), s32[]{:S(2)}) async-start(), calls=%async_computation.4 | async-start | bytes 393216 | tf_op jit(solution)/shard_map/reduce_scatter | solution.py:30
  72.4 8.5 %copy-start.5 = (s32[1,1,128]{2,1,0:T(1,128)S(1)}, s32[1,1,128]{2,1,0:T(1,128)}, u32[]{:S(2)}) copy-start(s32[1,1,128]{2,1,0:T(1,128)} %param.10) | copy-start | bytes 1540
  80.9 76.1 %copy-start.3 = (bf16[128,256]{1,0:T(8,128)(2,1)S(1)}, bf16[128,256]{1,0:T(8,128)(2,1)}, u32[]{:S(2)}) copy-start(bf16[128,256]{1,0:T(8,128)(2,1)} %param.13) | copy-start | bytes 196612
  97.9 0.7 copy-start.1
Sparse Core Ops, SparseCore 0:
  10.1 57.9 all-gather.1
  70.4 79.2 reduce-scatter.2
  151.9 5.0 reduce-scatter.4
where the time goes:
time: 166 us; the launch traced here: 165 us
  waiting for transfers between devices  85.4 us (51%)
  other arithmetic  34.8 us (21%)
  matrix products  19.4 us (12%)
  between operations  13.8 us (8%)
  local copies, waits for them, and re-layouts  9.55 us (6%)
  blocking collectives  2.21 us (1%)
    reduce_scatter x1, waiting for transfers between devices, local(): lax.psum_scatter(fwd_parts.reshape(-1, width), 'col', scatter_dimension=0...  51 us
    all_gather x1, waiting for transfers between devices, local(): lax.all_gather(features, 'col', axis=0, tiled=True).reshape(-1, side, width)  27.5 us
    scatter-add x1, other arithmetic, local(): jax.ops.segment_sum(fwd_terms, rowblk, num_segments=col_size * nodes_here...  17.1 us
    scatter-add x1, other arithmetic, local(): jax.ops.segment_sum(bwd_terms, colblk, num_segments=row_size * nodes_here...  17 us
    dot_general x1, matrix products, local(): jnp.einsum('kba,kbf->kaf', masked, stripe[rowblk], preferred_element_type...  8.47 us
    dot_general x1, matrix products, local(): jnp.einsum('kab,kbf->kaf', masked, group[colblk], preferred_element_type=...  8.01 us
    reduce_scatter x1, waiting for transfers between devices, local(): lax.psum_scatter(bwd_parts.reshape(-1, width), 'row', scatter_dimension=0...  6.15 us
    gather x1, local copies, waits for them, and re-layouts, local(): stripe[rowblk]  4.25 us
  transfers between devices with their start and end apart: 3, of which 3 were waited for; matrix products, arithmetic and copies ran while one was open for 36% of the time, Pallas kernels for 0%

commit v1 on v0

v1 whole, which is shorter than its diff:
```python
import jax
import jax.numpy as jnp
from jax import lax
from jax.sharding import PartitionSpec as P


def _nbits(n):
    bits = n.bit_length() - 1
    return bits if (1 << bits) == n else None


def _swap(x, axis, size, bit):
    perm = [(i, i ^ (1 << bit)) for i in range(size)]
    return lax.ppermute(x, axis, perm)


def gather_axis(x, axis):
    size = lax.axis_size(axis)
    nb = _nbits(size)
    if nb is None:
        return lax.all_gather(x, axis, axis=0, tiled=True)
    me = lax.axis_index(axis)
    have = x[None]
    order = list(range(nb - 1, -1, -1))
    for bit in order:
        got = _swap(have, axis, size, bit)
        mine = (me >> bit) & 1
        lo = jnp.where(mine == 0, have, got)
        hi = jnp.where(mine == 0, got, have)
        have = jnp.stack([lo, hi], axis=0).reshape((-1,) + have.shape[1:])
    shape = (2,) * nb + x.shape
    have = have.reshape(shape)
    processed = order[::-1]
    perm = [processed.index(b) for b in range(nb - 1, -1, -1)]
    have = jnp.transpose(have, perm + list(range(nb, nb + x.ndim)))
    return have.reshape((size * x.shape[0],) + x.shape[1:])


def scatter_sum_axis(x, axis):
    size = lax.axis_size(axis)
    nb = _nbits(size)
    if nb is None:
        return lax.psum_scatter(x, axis, scatter_dimension=0, tiled=True)
    me = lax.axis_index(axis)
    rest = x.shape[1:]
    data = x.reshape((2,) * nb + (x.shape[0] // size,) + rest)
    axes_bits = list(range(nb - 1, -1, -1))
    for bit in range(nb):
        a = axes_bits.index(bit)
        mine = (me >> bit) & 1
        keep = lax.dynamic_index_in_dim(data, mine, axis=a, keepdims=False)
        other = lax.dynamic_index_in_dim(data, 1 - mine, axis=a, keepdims=False)
        data = keep + _swap(other, axis, size, bit)
        axes_bits.pop(a)
    return data


def local(features, tile_vals, tile_rows, tile_cols, tile_count, w_fwd, w_bwd):
    row_size = lax.axis_size("row")
    col_size = lax.axis_size("col")
    values = tile_vals[0, 0]
    rowblk = tile_rows[0, 0]
    colblk = tile_cols[0, 0]
    slots = values.shape[0]
    side = values.shape[1]
    nodes_here = features.shape[0]
    nbc = nodes_here // side
    width = features.shape[1]
    nrow_blocks = col_size * nbc
    ncol_blocks = row_size * nbc
    cells = nrow_blocks * ncol_blocks

    slot_ids = jnp.arange(slots, dtype=jnp.int32)
    live = slot_ids < tile_count[0, 0]
    pos = jnp.where(live, rowblk * ncol_blocks + colblk, cells)
    inv = jnp.full((cells,), slots, jnp.int32).at[pos].set(slot_ids, mode="drop")
    present = inv < slots
    dense = values[jnp.minimum(inv, slots - 1)]
    dense = jnp.where(present[:, None, None], dense, jnp.zeros_like(dense))
    dense = dense.reshape(nrow_blocks, ncol_blocks, side, side)

    group = gather_axis(features, "row").reshape(ncol_blocks, side, width)
    stripe = gather_axis(features, "col").reshape(nrow_blocks, side, width)

    fwd_parts = jnp.einsum("bjak,jkf->baf", dense, group, preferred_element_type=jnp.float32)
    along = scatter_sum_axis(fwd_parts.reshape(-1, width), "col")
    bwd_parts = jnp.einsum("bjak,baf->jkf", dense, stripe, preferred_element_type=jnp.float32)
    against = scatter_sum_axis(bwd_parts.reshape(-1, width), "row")

    along = along.reshape(-1, width)
    against = against.reshape(-1, width)
    result = jnp.dot(along, w_fwd.astype(jnp.float32), precision=lax.Precision.HIGHEST)
    result = result + jnp.dot(against, w_bwd.astype(jnp.float32), precision=lax.Precision.HIGHEST)
    return result.astype(jnp.bfloat16)


def solution(mesh):
    in_specs = (
        P(("row", "col"), None),
        P("row", "col", None, None, None),
        P("row", "col", None),
        P("row", "col", None),
        P("row", "col"),
        P(),
        P(),
    )
    out_specs = P(("row", "col"), None)
    return jax.shard_map(local, mesh=mesh, in_specs=in_specs, out_specs=out_specs, check_vma=False)
```

time: 166 us -> 82.5 us (0.50)
  waiting for transfers between devices: 85.4 us -> 31.5 us
  other arithmetic: 34.8 us -> 11.4 us
  matrix products: 19.4 us -> 5.92 us
  between operations: 13.8 us -> 0.84 us
  starting transfers between devices: 0.08 us -> 12.8 us
  local copies, waits for them, and re-layouts: 9.55 us -> 19.5 us
  blocking collectives: 2.21 us -> 0 us
    reduce_scatter x2 -> x0, waiting for transfers between devices: 57.2 us -> none  [the longest x1 51 us: local(): lax.psum_scatter(fwd_parts.reshape(-1, width), 'col', scatter_dimension=0...]
    scatter-add x2 -> x0, other arithmetic: 34.1 us -> none  [the longest x1 17.1 us: local(): jax.ops.segment_sum(fwd_terms, rowblk, num_segments=col_size * nodes_here...]
    ppermute x0 -> x10, waiting for transfers between devices: none -> 31.5 us  [_swap(): return lax.ppermute(x, axis, perm)]
    all_gather x1 -> x0, waiting for transfers between devices: 27.5 us -> none  [local(): lax.all_gather(features, 'col', axis=0, tiled=True).reshape(-1, side, width)]
    dot_general x0 -> x3, local copies, waits for them, and re-layouts: none -> 12.9 us  [the longest x1 7.94 us: local(): jnp.einsum('bjak,baf->jkf', dense, stripe, preferred_element_type=jnp.flo...]
    ppermute x0 -> x10, starting transfers between devices: none -> 12.8 us  [_swap(): return lax.ppermute(x, axis, perm)]
    dot_general x2, matrix products: 16.5 us -> 4.76 us  [the longest x1 3.44 us: local(): jnp.einsum('bjak,jkf->baf', dense, group, preferred_element_type=jnp.floa...]
    dot_general x0 -> x1, other arithmetic: none -> 5.17 us  [local(): jnp.einsum('bjak,jkf->baf', dense, group, preferred_element_type=jnp.floa...]
  transfers between devices with their start and end apart: 3 -> 10, of which waited for: 3 -> 6; matrix products, arithmetic and copies ran while one was open for 36% -> 38% of each run, Pallas kernels for 0% -> 0%
where the time goes in v1:
time: 82.5 us; the launch traced here: 82 us
  waiting for transfers between devices  31.5 us (38%)
  local copies, waits for them, and re-layouts  19.5 us (24%)
  starting transfers between devices  12.8 us (16%)
  other arithmetic  11.4 us (14%)
  matrix products  5.92 us (7%)
  between operations  0.84 us (1%)
    ppermute x10, waiting for transfers between devices, _swap(): return lax.ppermute(x, axis, perm)  31.5 us
    ppermute x10, starting transfers between devices, _swap(): return lax.ppermute(x, axis, perm)  12.8 us
    dot_general x1, local copies, waits for them, and re-layouts, local(): jnp.einsum('bjak,baf->jkf', dense, stripe, preferred_element_type=jnp.flo...  7.94 us
    gather x1, local copies, waits for them, and re-layouts, local(): dense = values[jnp.minimum(inv, slots - 1)]  5.25 us
    dot_general x1, other arithmetic, local(): jnp.einsum('bjak,jkf->baf', dense, group, preferred_element_type=jnp.floa...  5.17 us
    dot_general x2, local copies, waits for them, and re-layouts, local(): jnp.einsum('bjak,jkf->baf', dense, group, preferred_element_type=jnp.floa...  4.92 us
    dot_general x1, matrix products, local(): jnp.einsum('bjak,jkf->baf', dense, group, preferred_element_type=jnp.floa...  3.44 us
    another operation x6, other arithmetic, gather_axis(): have = jnp.stack([lo, hi], axis=0).reshape((-1,) + have.shape[1:])  1.97 us
  transfers between devices with their start and end apart: 10, of which 6 were waited for; matrix products, arithmetic and copies ran while one was open for 38% of the time, Pallas kernels for 0%

profile of v1, /device:TPU:0, one launch (start us, length us, event | category | flops | bytes accessed | tf_op | source)
XLA Modules:
  0.0 82.0 jit_solution(5567555319106403155)
XLA Ops:
  0.0 0.5 collective-permute-start
  0.5 3.7 %collective-permute-start.5 = (bf16[1,256,128]{2,1,0:T(8,128)(2,1)}, bf16[1,256,128]{2,1,0:T(8,128)(2,1)S(1)}, u32[]{:S(2)}, u32[]{:S(2)}) collective-permute-start(bf16[1,256,128]{2,1,0:T(8,128)(2,1)} %bitcast.105), channel_id=1, source_target_pairs={{0,8},{1,9},{2,10},{3,11},{4,12},{5,13},{6,14},{7,15},{8,0},{9,1},... | collective-permute-start | bytes 196616 | tf_op jit(solution)/shard_map/ppermute | solution.py:14
  4.8 0.7 fusion.15
  5.4 1.0 %scatter_custom_fusion = s32[128]{0:T(128)S(1)} fusion(s32[128]{0:T(128)S(1)} %fusion.15, s32[128]{0:T(128)S(1)} %iota.7, s32[]{:T(128)} %constant.49.clone.1), kind=kCustom, calls=%fused_computation.49 | custom fusion | bytes 516 | tf_op jit(solution)/shard_map/scatter | solution.py:76
  6.5 0.1 broadcast_in_dim.24
  6.6 5.2 %gather_fusion = bf16[128,128,128]{2,1,0:T(8,128)(2,1)} fusion(bf16[128,128,128]{2,1,0:T(8,128)(2,1)} %bitcast.96, s32[1024]{0:T(1024)S(1)} %pad_clamp_fusion), kind=kCustom, calls=%fused_computation | custom fusion | bytes 8389120 | tf_op jit(solution)/shard_map/gather | solution.py:78
  11.8 5.2 %fusion.5 = (bf16[32,128,4,128]{3,1,2,0:T(8,128)(2,1)}, bf16[4,128,128,32]{1,2,0,3:T(8,128)(2,1)}) fusion(bf16[32,4,128,128]{3,2,1,0:T(8,128)(2,1)} %bitcast.93, pred[32,4]{1,0:T(8,128)(4,1)S(1)} %broadcast_in_dim.24), kind=kLoop, calls=%fused_computation.8 | loop fusion | flops 2097152 | bytes 12583040 | tf_op jit(solution)/shard_map/bjak,jkf->baf/dot_general | solution.py:85
  17.0 4.8 %copy.13 = bf16[32,128,4,128]{3,1,0,2:T(8,128)(2,1)} copy(bf16[32,128,4,128]{3,1,2,0:T(8,128)(2,1)} %get-tuple-element.5) | data formatting | bytes 8388608 | tf_op jit(solution)/shard_map/bjak,jkf->baf/dot_general | solution.py:85
  21.8 3.4 %fusion = f32[2,2,2,2,256,128,1]{5,4,1,0,3,2,6:T(8,128)S(1)} fusion(bf16[4,128,128,1,1,1,1]{2,1,4,3,6,5,0:T(8,128)(2,1)S(1)} %bitcast.103, bf16[2,2,2,2,256,4,128]{6,4,3,2,1,0,5:T(8,128)(2,1)} %bitcast.98), kind=kOutput, calls=%fused_computation.2 | convolution fusion | flops 536870912 | bytes 6422528 | tf_op jit(solution)/shard_map/bjak,jkf->baf/dot_general | solution.py:85
  25.3 0.1 copy.30
  25.4 0.7 maximum_bitcast_fusion.1
  26.1 1.6 %collective-permute-start.6 = (bf16[2,256,128]{2,1,0:T(8,128)(2,1)}, bf16[2,256,128]{2,1,0:T(8,128)(2,1)S(1)}, u32[]{:S(2)}, u32[]{:S(2)}) collective-permute-start(bf16[2,256,128]{2,1,0:T(8,128)(2,1)} %maximum_bitcast_fusion.1), channel_id=1, source_target_pairs={{0,4},{1,5},{2,6},{3,7},{4,0},{5,1},{6,2},{7,3},{8,12},{9,13},{10,... | collective-permute-start | bytes 393224 | tf_op jit(solution)/shard_map/ppermute | solution.py:14
  27.8 1.6 %collective-permute-start.1 = (f32[2,2,2,256,128]{4,3,0,2,1:T(8,128)S(1)}, f32[2,2,2,256,128]{4,3,0,2,1:T(8,128)}, u32[]{:S(2)}, u32[]{:S(2)}) collective-permute-start(f32[2,2,2,256,128]{4,3,0,2,1:T(8,128)S(1)} %dynamic-slice_bitcast_fusion), channel_id=1, source_target_pairs={{0,1},{1,0},{2,3},{3,2},{4,5},{5,4},{6,7},{7,6},{8,9},{9,8},{10,11... | collective-permute-start | bytes 3145736 | tf_op jit(solution)/shard_map/ppermute | solution.py:14
  29.3 2.6 %collective-permute-done.6 = bf16[2,256,128]{2,1,0:T(8,128)(2,1)S(1)} collective-permute-done((bf16[2,256,128]{2,1,0:T(8,128)(2,1)}, bf16[2,256,128]{2,1,0:T(8,128)(2,1)S(1)}, u32[]{:S(2)}, u32[]{:S(2)}) %collective-permute-start.6) | collective-permute-done | bytes 131104 | tf_op jit(solution)/shard_map/ppermute | solution.py:14
  31.9 1.6 %collective-permute-start.7 = (bf16[4,256,128]{2,1,0:T(8,128)(2,1)S(1)}, bf16[4,256,128]{2,1,0:T(8,128)(2,1)}, u32[]{:S(2)}, u32[]{:S(2)}) collective-permute-start(bf16[4,256,128]{2,1,0:T(8,128)(2,1)S(1)} %bitcast.102), channel_id=1, source_target_pairs={{0,2},{1,3},{2,0},{3,1},{4,6},{5,7},{6,4},{7,5},{8,10},{9,11},{10,... | collective-permute-start | bytes 786440 | tf_op jit(solution)/shard_map/ppermute | solution.py:14
  33.5 6.1 %collective-permute-done.7 = bf16[4,256,128]{2,1,0:T(8,128)(2,1)} collective-permute-done((bf16[4,256,128]{2,1,0:T(8,128)(2,1)S(1)}, bf16[4,256,128]{2,1,0:T(8,128)(2,1)}, u32[]{:S(2)}, u32[]{:S(2)}) %collective-permute-start.7) | collective-permute-done | bytes 262176 | tf_op jit(solution)/shard_map/ppermute | solution.py:14
  39.7 1.0 %select_bitcast_fusion.1 = (bf16[1,4,256,128]{3,2,1,0:T(8,128)(2,1)S(1)}, bf16[1,4,256,128]{3,2,1,0:T(8,128)(2,1)S(1)}) fusion(bf16[4,256,128]{2,1,0:T(8,128)(2,1)} %collective-permute-done.7, pred[]{:T(512)S(6)} %eq.22, bf16[2,2,256,128]{3,2,1,0:T(8,128)(2,1)S(1)} %pad_maximum_fusion.1), kind=kLoop, calls=%fused_computation.24 | loop fusion | flops 262144 | bytes 1048577 | tf_op jit(solution)/shard_map/stack | solution.py:30
  40.6 0.9 %pad_maximum_fusion = bf16[2,4,256,128]{3,2,1,0:T(8,128)(2,1)} fusion(bf16[1,4,256,128]{3,2,1,0:T(8,128)(2,1)S(1)} %get-tuple-element.10, bf16[1,4,256,128]{3,2,1,0:T(8,128)(2,1)S(1)} %get-tuple-element.9), kind=kLoop, calls=%fused_computation.16 | loop fusion | flops 262144 | bytes 1048576 | tf_op jit(solution)/shard_map/stack | solution.py:30
  41.5 1.5 %collective-permute-start.8 = (bf16[8,256,128]{2,1,0:T(8,128)(2,1)}, bf16[8,256,128]{2,1,0:T(8,128)(2,1)}, u32[]{:S(2)}, u32[]{:S(2)}) collective-permute-start(bf16[8,256,128]{2,1,0:T(8,128)(2,1)} %bitcast.32), channel_id=1, source_target_pairs={{0,1},{1,0},{2,3},{3,2},{4,5},{5,4},{6,7},{7,6},{8,9},{9,8},{10,11... | collective-permute-start | bytes 1572872 | tf_op jit(solution)/shard_map/ppermute | solution.py:14
  43.0 11.0 %collective-permute-done.1 = f32[2,2,2,256,128]{4,3,0,2,1:T(8,128)} collective-permute-done((f32[2,2,2,256,128]{4,3,0,2,1:T(8,128)S(1)}, f32[2,2,2,256,128]{4,3,0,2,1:T(8,128)}, u32[]{:S(2)}, u32[]{:S(2)}) %collective-permute-start.1) | collective-permute-done | bytes 1048608 | tf_op jit(solution)/shard_map/ppermute | solution.py:14
  54.0 1.3 %bitcast_add_fusion = f32[2,2,2,256,128]{4,3,0,2,1:T(8,128)S(1)} fusion(f32[2,2,2,256,128]{4,3,0,2,1:T(8,128)} %collective-permute-done.1, f32[2,2,2,2,256,128]{5,4,0,3,2,1:T(8,128)S(1)} %bitcast.95, s32[]{:T(128)S(6)} %select_n.128), kind=kLoop, calls=%fused_computation.14 | loop fusion | flops 262144 | bytes 3145732 | tf_op jit(solution)/shard_map/add | solution.py:53
  55.4 1.6 %collective-permute-start.2 = (f32[2,2,256,128]{3,2,0,1:T(8,128)S(1)}, f32[2,2,256,128]{3,2,0,1:T(8,128)S(1)}, u32[]{:S(2)}, u32[]{:S(2)}) collective-permute-start(f32[2,2,256,128]{3,2,0,1:T(8,128)S(1)} %dynamic-slice_bitcast_fusion.1), channel_id=1, source_target_pairs={{0,2},{1,3},{2,0},{3,1},{4,6},{5,7},{6,4},{7,5},{8,10},{9,11},{10,... | collective-permute-start | bytes 1572872 | tf_op jit(solution)/shard_map/ppermute | solution.py:14
  56.9 7.9 %copy.15 = bf16[4,128,128,32]{2,3,1,0:T(8,128)(2,1)} copy(bf16[4,128,128,32]{1,2,0,3:T(8,128)(2,1)} %get-tuple-element.6) | data formatting | bytes 8388608 | tf_op jit(solution)/shard_map/bjak,baf->jkf/dot_general | solution.py:87
  64.9 1.4 %broadcast_select_fusion.2 = (bf16[8,256,128]{2,1,0:T(8,128)(2,1)S(1)}, bf16[8,256,128]{2,1,0:T(8,128)(2,1)S(1)}) fusion(bf16[8,256,128]{2,1,0:T(8,128)(2,1)} %collective-permute-done.8, pred[]{:T(512)S(6)} %eq.21, bf16[2,4,256,128]{3,2,1,0:T(8,128)(2,1)} %pad_maximum_fusion), kind=kLoop, calls=%fused_computation.20 | loop fusion | flops 524288 | bytes 2097153 | tf_op jit(solution)/shard_map/jit(_where)/select_n | solution.py:28
  66.5 0.7 collective-permute-done.2
  67.3 0.5 collective-permute-start.3
  67.8 1.3 %fusion.6 = f32[2,256,128]{2,1,0:T(8,128)S(1)} fusion(bf16[32,128,128,1]{2,1,0,3:T(8,128)(2,1)S(1)} %bitcast.101, bf16[2,256,128,32]{2,3,1,0:T(8,128)(2,1)S(1)} %bitcast.97), kind=kOutput, calls=%fused_computation.10 | convolution fusion | flops 536870912 | bytes 5505024 | tf_op jit(solution)/shard_map/bjak,baf->jkf/dot_general | solution.py:87
  69.2 4.5 %collective-permute-done.3 = f32[2,256,128]{2,1,0:T(8,128)S(1)} collective-permute-done((f32[2,256,128]{2,1,0:T(8,128)S(1)}, f32[2,256,128]{2,1,0:T(8,128)S(1)}, u32[]{:S(2)}, u32[]{:S(2)}) %collective-permute-start.3) | collective-permute-done | bytes 262176 | tf_op jit(solution)/shard_map/ppermute | solution.py:14
  73.8 0.4 collective-permute-start.4
  74.2 0.3 fusion.10
  74.4 6.7 %collective-permute-done.4 = f32[256,128]{1,0:T(8,128)S(1)} collective-permute-done((f32[256,128]{1,0:T(8,128)S(1)}, f32[256,128]{1,0:T(8,128)S(1)}, u32[]{:S(2)}, u32[]{:S(2)}) %collective-permute-start.4) | collective-permute-done | bytes 131104 | tf_op jit(solution)/shard_map/ppermute | solution.py:14
  81.1 0.9 %fusion.9 = bf16[256,256]{1,0:T(8,128)(2,1)} fusion(f32[256,256]{1,0:T(8,128)S(1)} %fusion.10, bf16[128,256]{1,0:T(8,128)(2,1)S(1)} %copy-done.3, f32[256,128]{1,0:T(8,128)S(1)} %collective-permute-done.4, f32[2,256,128]{2,1,0:T(8,128)S(1)} %bitcast_add_fusion.2, s32[]{:T(128)S(6)} %select_n.134), kind=kOutput, calls=%fused_computation.12 | convolution fusion | flops 100827136 | bytes 720900 | tf_op jit(solution)/shard_map/dot_general | solution.py:92
  (30 shorter events, 0.6 us)
Async XLA Ops:
  0.0 74.2 %copy-start = (bf16[128,256]{1,0:T(8,128)(2,1)S(1)}, bf16[128,256]{1,0:T(8,128)(2,1)}, u32[]{:S(2)}) copy-start(bf16[128,256]{1,0:T(8,128)(2,1)} %param.13) | copy-start | bytes 196612
  0.0 21.8 %collective-permute-start = (bf16[1,256,128]{2,1,0:T(8,128)(2,1)}, bf16[1,256,128]{2,1,0:T(8,128)(2,1)S(1)}, u32[]{:S(2)}, u32[]{:S(2)}) collective-permute-start(bf16[1,256,128]{2,1,0:T(8,128)(2,1)} %bitcast.104), channel_id=1, source_target_pairs={{0,16},{16,0},{1,17},{17,1},{2,18},{18,2},{3,19},{19,3},{4,20},{20... | collective-permute-start | bytes 196616 | tf_op jit(solution)/shard_map/ppermute | solution.py:14
  0.5 21.3 %collective-permute-start.5 = (bf16[1,256,128]{2,1,0:T(8,128)(2,1)}, bf16[1,256,128]{2,1,0:T(8,128)(2,1)S(1)}, u32[]{:S(2)}, u32[]{:S(2)}) collective-permute-start(bf16[1,256,128]{2,1,0:T(8,128)(2,1)} %bitcast.105), channel_id=1, source_target_pairs={{0,8},{1,9},{2,10},{3,11},{4,12},{5,13},{6,14},{7,15},{8,0},{9,1},... | collective-permute-start | bytes 196616 | tf_op jit(solution)/shard_map/ppermute | solution.py:14
  17.0 4.8 %copy-start.2 = (bf16[256,128]{1,0:T(8,128)(2,1)S(1)}, bf16[256,128]{1,0:T(8,128)(2,1)}, u32[]{:S(2)}) copy-start(bf16[256,128]{1,0:T(8,128)(2,1)} %param.7) | copy-start | bytes 196612
  26.1 5.8 %collective-permute-start.6 = (bf16[2,256,128]{2,1,0:T(8,128)(2,1)}, bf16[2,256,128]{2,1,0:T(8,128)(2,1)S(1)}, u32[]{:S(2)}, u32[]{:S(2)}) collective-permute-start(bf16[2,256,128]{2,1,0:T(8,128)(2,1)} %maximum_bitcast_fusion.1), channel_id=1, source_target_pairs={{0,4},{1,5},{2,6},{3,7},{4,0},{5,1},{6,2},{7,3},{8,12},{9,13},{10,... | collective-permute-start | bytes 393224 | tf_op jit(solution)/shard_map/ppermute | solution.py:14
  27.8 26.2 %collective-permute-start.1 = (f32[2,2,2,256,128]{4,3,0,2,1:T(8,128)S(1)}, f32[2,2,2,256,128]{4,3,0,2,1:T(8,128)}, u32[]{:S(2)}, u32[]{:S(2)}) collective-permute-start(f32[2,2,2,256,128]{4,3,0,2,1:T(8,128)S(1)} %dynamic-slice_bitcast_fusion), channel_id=1, source_target_pairs={{0,1},{1,0},{2,3},{3,2},{4,5},{5,4},{6,7},{7,6},{8,9},{9,8},{10,11... | collective-permute-start | bytes 3145736 | tf_op jit(solution)/shard_map/ppermute | solution.py:14
  31.9 7.7 %collective-permute-start.7 = (bf16[4,256,128]{2,1,0:T(8,128)(2,1)S(1)}, bf16[4,256,128]{2,1,0:T(8,128)(2,1)}, u32[]{:S(2)}, u32[]{:S(2)}) collective-permute-start(bf16[4,256,128]{2,1,0:T(8,128)(2,1)S(1)} %bitcast.102), channel_id=1, source_target_pairs={{0,2},{1,3},{2,0},{3,1},{4,6},{5,7},{6,4},{7,5},{8,10},{9,11},{10,... | collective-permute-start | bytes 786440 | tf_op jit(solution)/shard_map/ppermute | solution.py:14
  41.5 23.3 %collective-permute-start.8 = (bf16[8,256,128]{2,1,0:T(8,128)(2,1)}, bf16[8,256,128]{2,1,0:T(8,128)(2,1)}, u32[]{:S(2)}, u32[]{:S(2)}) collective-permute-start(bf16[8,256,128]{2,1,0:T(8,128)(2,1)} %bitcast.32), channel_id=1, source_target_pairs={{0,1},{1,0},{2,3},{3,2},{4,5},{5,4},{6,7},{7,6},{8,9},{9,8},{10,11... | collective-permute-start | bytes 1572872 | tf_op jit(solution)/shard_map/ppermute | solution.py:14
  55.4 11.8 %collective-permute-start.2 = (f32[2,2,256,128]{3,2,0,1:T(8,128)S(1)}, f32[2,2,256,128]{3,2,0,1:T(8,128)S(1)}, u32[]{:S(2)}, u32[]{:S(2)}) collective-permute-start(f32[2,2,256,128]{3,2,0,1:T(8,128)S(1)} %dynamic-slice_bitcast_fusion.1), channel_id=1, source_target_pairs={{0,2},{1,3},{2,0},{3,1},{4,6},{5,7},{6,4},{7,5},{8,10},{9,11},{10,... | collective-permute-start | bytes 1572872 | tf_op jit(solution)/shard_map/ppermute | solution.py:14
  64.9 2.9 %copy-start.1 = (bf16[4,128,128,32]{2,3,1,0:T(8,128)(2,1)S(1)}, bf16[4,128,128,32]{2,3,1,0:T(8,128)(2,1)}, u32[]{:S(2)}) copy-start(bf16[4,128,128,32]{2,3,1,0:T(8,128)(2,1)} %copy.15) | copy-start | bytes 12582916
  67.3 6.4 %collective-permute-start.3 = (f32[2,256,128]{2,1,0:T(8,128)S(1)}, f32[2,256,128]{2,1,0:T(8,128)S(1)}, u32[]{:S(2)}, u32[]{:S(2)}) collective-permute-start(f32[2,256,128]{2,1,0:T(8,128)S(1)} %dynamic-slice_bitcast_fusion.2), channel_id=1, source_target_pairs={{0,4},{1,5},{2,6},{3,7},{4,0},{5,1},{6,2},{7,3},{8,12},{9,13},{10,... | collective-permute-start | bytes 786440 | tf_op jit(solution)/shard_map/ppermute | solution.py:14
  67.8 13.3 %copy-start.3 = (bf16[128,256]{1,0:T(8,128)(2,1)S(1)}, bf16[128,256]{1,0:T(8,128)(2,1)}, u32[]{:S(2)}) copy-start(bf16[128,256]{1,0:T(8,128)(2,1)} %param.12) | copy-start | bytes 196612
  69.1 5.0 %collective-permute-start.9 = (f32[256,128]{1,0:T(8,128)S(1)}, f32[256,128]{1,0:T(8,128)S(1)}, u32[]{:S(2)}, u32[]{:S(2)}) collective-permute-start(f32[256,128]{1,0:T(8,128)S(1)} %dynamic-slice_bitcast_fusion.3), channel_id=1, source_target_pairs={{0,16},{16,0},{1,17},{17,1},{2,18},{18,2},{3,19},{19,3},{4,20},{20... | collective-permute-start | bytes 393224 | tf_op jit(solution)/shard_map/ppermute | solution.py:14
  73.8 7.3 %collective-permute-start.4 = (f32[256,128]{1,0:T(8,128)S(1)}, f32[256,128]{1,0:T(8,128)S(1)}, u32[]{:S(2)}, u32[]{:S(2)}) collective-permute-start(f32[256,128]{1,0:T(8,128)S(1)} %dynamic-slice_bitcast_fusion.4), channel_id=1, source_target_pairs={{0,8},{1,9},{2,10},{3,11},{4,12},{5,13},{6,14},{7,15},{8,0},{9,1},... | collective-permute-start | bytes 393224 | tf_op jit(solution)/shard_map/ppermute | solution.py:14

commit v2 on v1

v2 whole, which is shorter than its diff:
```python
import jax
import jax.numpy as jnp
from jax import lax
from jax.experimental import pallas as pl
from jax.experimental.pallas import tpu as pltpu
from jax.sharding import PartitionSpec as P


def _nbits(n):
    bits = n.bit_length() - 1
    return bits if (1 << bits) == n else None


def _orders(nb):
    if nb == 4:
        return ((0, 1, 2, 3), (2, 0, 1, 3)), ((3, 0, 1, 2), (3, 2, 0, 1))
    rs = tuple(range(nb))
    return (rs, rs), (rs[::-1], rs[::-1])


def _pick(parity, pair, t):
    return jnp.where(parity == 0, pair[0][t], pair[1][t])


def _swap_col(x, row_size, col_size, bits):
    perm = []
    for r in range(row_size):
        b = bits[r % 2]
        for c in range(col_size):
            perm.append((r * col_size + c, r * col_size + (c ^ (1 << b))))
    return lax.ppermute(x, ("row", "col"), perm)


def _swap(x, axis, size, bit):
    perm = [(i, i ^ (1 << bit)) for i in range(size)]
    return lax.ppermute(x, axis, perm)


def gather_row(x):
    size = lax.axis_size("row")
    nb = _nbits(size)
    if nb is None:
        return lax.all_gather(x, "row", axis=0, tiled=True)
    me = lax.axis_index("row")
    have = x[None]
    order = list(range(nb - 1, -1, -1))
    for bit in order:
        got = _swap(have, "row", size, bit)
        mine = (me >> bit) & 1
        lo = jnp.where(mine == 0, have, got)
        hi = jnp.where(mine == 0, got, have)
        have = jnp.stack([lo, hi], axis=0).reshape((-1,) + have.shape[1:])
    have = have.reshape((2,) * nb + x.shape)
    processed = order[::-1]
    perm = [processed.index(b) for b in range(nb - 1, -1, -1)]
    have = jnp.transpose(have, perm + list(range(nb, nb + x.ndim)))
    return have.reshape((size * x.shape[0],) + x.shape[1:])


def scatter_sum_row(x):
    size = lax.axis_size("row")
    nb = _nbits(size)
    if nb is None:
        return lax.psum_scatter(x, "row", scatter_dimension=0, tiled=True)
    me = lax.axis_index("row")
    data = x.reshape((2,) * nb + (x.shape[0] // size,) + x.shape[1:])
    axes_bits = list(range(nb - 1, -1, -1))
    for bit in range(nb):
        a = axes_bits.index(bit)
        mine = (me >> bit) & 1
        keep = lax.dynamic_index_in_dim(data, mine, axis=a, keepdims=False)
        other = lax.dynamic_index_in_dim(data, 1 - mine, axis=a, keepdims=False)
        data = keep + _swap(other, "row", size, bit)
        axes_bits.pop(a)
    return data


def gather_col(x, order):
    row_size = lax.axis_size("row")
    col_size = lax.axis_size("col")
    nb = len(order[0])
    me = lax.axis_index("col")
    parity = lax.axis_index("row") % 2
    have = x[None]
    for t in range(nb):
        got = _swap_col(have, row_size, col_size, (order[0][t], order[1][t]))
        mine = (me >> _pick(parity, order, t)) & 1
        lo = jnp.where(mine == 0, have, got)
        hi = jnp.where(mine == 0, got, have)
        have = jnp.stack([lo, hi], axis=0).reshape((-1,) + have.shape[1:])
    return have


def scatter_sum_col(data, order):
    row_size = lax.axis_size("row")
    col_size = lax.axis_size("col")
    nb = len(order[0])
    me = lax.axis_index("col")
    parity = lax.axis_index("row") % 2
    for t in range(nb):
        mine = (me >> _pick(parity, order, t)) & 1
        keep = lax.dynamic_index_in_dim(data, mine, axis=0, keepdims=False)
        other = lax.dynamic_index_in_dim(data, 1 - mine, axis=0, keepdims=False)
        data = keep + _swap_col(other, row_size, col_size, (order[0][t], order[1][t]))
    return data


def _chunk(slots):
    return 16 if slots % 16 == 0 else slots


def along_call(rows, cols, cnt, values, group, nrb):
    slots, side, _ = values.shape
    width = group.shape[-1]
    k = _chunk(slots)

    def kernel(rows_ref, cols_ref, cnt_ref, vals_ref, grp_ref, out_ref):
        i = pl.program_id(0)
        n = cnt_ref[0]

        @pl.when(i == 0)
        def _():
            out_ref[...] = jnp.zeros(out_ref.shape, out_ref.dtype)

        def body(t, carry):
            s = i * k + t

            @pl.when(s < n)
            def _():
                r = rows_ref[s]
                c = cols_ref[s]
                out_ref[r] += jnp.dot(vals_ref[t], grp_ref[c], preferred_element_type=jnp.float32)

            return carry

        @pl.when(i * k < n)
        def _():
            lax.fori_loop(0, k, body, 0)

    def vals_map(i, rows_ref, cols_ref, cnt_ref):
        last = jnp.maximum(cnt_ref[0] - 1, 0) // k
        return (jnp.minimum(i, last), 0, 0)

    spec = pltpu.PrefetchScalarGridSpec(
        num_scalar_prefetch=3,
        grid=(slots // k,),
        in_specs=[
            pl.BlockSpec((k, side, side), vals_map),
            pl.BlockSpec(group.shape, lambda i, *_: (0, 0, 0)),
        ],
        out_specs=pl.BlockSpec((nrb, side, width), lambda i, *_: (0, 0, 0)),
    )
    return pl.pallas_call(
        kernel,
        grid_spec=spec,
        out_shape=jax.ShapeDtypeStruct((nrb, side, width), jnp.float32),
    )(rows, cols, cnt, values, group)


def against_call(rows, cols, cnt, values, stripe_t, ncb):
    slots, side, _ = values.shape
    width = stripe_t.shape[1]
    k = _chunk(slots)

    def kernel(rows_ref, cols_ref, cnt_ref, vals_ref, st_ref, out_ref):
        i = pl.program_id(0)
        n = cnt_ref[0]

        @pl.when(i == 0)
        def _():
            out_ref[...] = jnp.zeros(out_ref.shape, out_ref.dtype)

        def body(t, carry):
            s = i * k + t

            @pl.when(s < n)
            def _():
                r = rows_ref[s]
                c = cols_ref[s]
                out_ref[c] += jnp.dot(st_ref[r], vals_ref[t], preferred_element_type=jnp.float32)

            return carry

        @pl.when(i * k < n)
        def _():
            lax.fori_loop(0, k, body, 0)

    def vals_map(i, rows_ref, cols_ref, cnt_ref):
        last = jnp.maximum(cnt_ref[0] - 1, 0) // k
        return (jnp.minimum(i, last), 0, 0)

    spec = pltpu.PrefetchScalarGridSpec(
        num_scalar_prefetch=3,
        grid=(slots // k,),
        in_specs=[
            pl.BlockSpec((k, side, side), vals_map),
            pl.BlockSpec(stripe_t.shape, lambda i, *_: (0, 0, 0)),
        ],
        out_specs=pl.BlockSpec((ncb, width, side), lambda i, *_: (0, 0, 0)),
    )
    return pl.pallas_call(
        kernel,
        grid_spec=spec,
        out_shape=jax.ShapeDtypeStruct((ncb, width, side), jnp.float32),
    )(rows, cols, cnt, values, stripe_t)


def local(features, tile_vals, tile_rows, tile_cols, tile_count, w_fwd, w_bwd):
    row_size = lax.axis_size("row")
    col_size = lax.axis_size("col")
    values = tile_vals[0, 0]
    slots = values.shape[0]
    side = values.shape[1]
    nodes_here = features.shape[0]
    nbc = nodes_here // side
    width = features.shape[1]
    nrb = col_size * nbc
    ncb = row_size * nbc
    parity = lax.axis_index("row") % 2

    rowblk = jnp.clip(tile_rows[0, 0], 0, nrb - 1)
    colblk = jnp.clip(tile_cols[0, 0], 0, ncb - 1)
    cnt = jnp.clip(tile_count[0, 0], 0, slots).reshape(1).astype(jnp.int32)

    nb = _nbits(col_size)
    if nb is not None:
        rs_order, ag_order = _orders(nb)
        dest = rowblk // nbc
        sub = rowblk % nbc
        rs_pos = jnp.zeros_like(dest)
        ag_pos = jnp.zeros_like(dest)
        for t in range(nb):
            rs_pos = rs_pos + (((dest >> _pick(parity, rs_order, t)) & 1) << (nb - 1 - t))
            ag_pos = ag_pos + (((dest >> _pick(parity, ag_order, t)) & 1) << t)
        rows_fwd = rs_pos * nbc + sub
        rows_bwd = ag_pos * nbc + sub
    else:
        rows_fwd = rowblk
        rows_bwd = rowblk

    group = gather_row(features).reshape(ncb, side, width)
    fwd_parts = along_call(rows_fwd, colblk, cnt, values, group, nrb)

    mine_t = jnp.transpose(features.reshape(nbc, side, width), (0, 2, 1))
    if nb is not None:
        stripe_t = gather_col(mine_t, ag_order).reshape(nrb, width, side)
        along = scatter_sum_col(fwd_parts.reshape((2,) * nb + (nbc, side, width)), rs_order)
    else:
        stripe_t = lax.all_gather(mine_t, "col", axis=0, tiled=True)
        along = lax.psum_scatter(fwd_parts, "col", scatter_dimension=0, tiled=True)

    bwd_t = against_call(rows_bwd, colblk, cnt, values, stripe_t, ncb)
    against_t = scatter_sum_row(bwd_t)
    against = jnp.transpose(against_t, (0, 2, 1))

    along = along.reshape(-1, width)
    against = against.reshape(-1, width)
    result = jnp.dot(along, w_fwd.astype(jnp.float32), precision=lax.Precision.HIGHEST)
    result = result + jnp.dot(against, w_bwd.astype(jnp.float32), precision=lax.Precision.HIGHEST)
    return result.astype(jnp.bfloat16)


def solution(mesh):
    in_specs = (
        P(("row", "col"), None),
        P("row", "col", None, None, None),
        P("row", "col", None),
        P("row", "col", None),
        P("row", "col"),
        P(),
        P(),
    )
    out_specs = P(("row", "col"), None)
    return jax.shard_map(local, mesh=mesh, in_specs=in_specs, out_specs=out_specs, check_vma=False)
```

time: 82.5 us -> 91.7 us (1.11); the launches traced: 82 us -> 92.1 us
  starting transfers between devices: 12.8 us -> 40.4 us
  local copies, waits for them, and re-layouts: 19.5 us -> 3.43 us
  Pallas kernels: 0 us -> 10.8 us
  waiting for transfers between devices: 31.5 us -> 25.8 us
  matrix products: 5.92 us -> 1.16 us
  other arithmetic: 11.4 us -> 9.74 us
    ppermute x0 -> x8, starting transfers between devices: none -> 39.9 us  [_swap_col(): return lax.ppermute(x, ('row', 'col'), perm)]
    ppermute x10 -> x2, waiting for transfers between devices: 31.5 us -> 0.01 us  [_swap(): return lax.ppermute(x, axis, perm)]
    ppermute x0 -> x8, waiting for transfers between devices: none -> 25.8 us  [_swap_col(): return lax.ppermute(x, ('row', 'col'), perm)]
    dot_general x3 -> x0, local copies, waits for them, and re-layouts: 12.9 us -> none  [the longest x1 7.94 us: local(): jnp.einsum('bjak,baf->jkf', dense, stripe, preferred_element_type=jnp.flo...]
    ppermute x10 -> x2, starting transfers between devices: 12.8 us -> 0.52 us  [_swap(): return lax.ppermute(x, axis, perm)]
    pallas_call x0 -> x2, Pallas kernels: none -> 10.8 us  [the longest x1 5.6 us: along_call(): pl.pallas_call(kernel, grid_spec=spec, out_shape=jax.ShapeDtypeStruct((nr...]
    gather x1 -> x0, local copies, waits for them, and re-layouts: 5.25 us -> none  [local(): dense = values[jnp.minimum(inv, slots - 1)]]
    dot_general x1 -> x0, other arithmetic: 5.17 us -> none  [local(): jnp.einsum('bjak,jkf->baf', dense, group, preferred_element_type=jnp.floa...]
  transfers between devices with their start and end apart: 10 -> 10, of which waited for: 6 -> 6; matrix products, arithmetic and copies ran while one was open for 38% -> 14% of each run, Pallas kernels for 0% -> 12%
where the time goes in v2:
time: 91.7 us; the launch traced here: 92.1 us
  starting transfers between devices  40.4 us (44%)
  waiting for transfers between devices  25.8 us (28%)
  Pallas kernels  10.8 us (12%)
  other arithmetic  9.74 us (11%)
  local copies, waits for them, and re-layouts  3.43 us (4%)
  matrix products  1.16 us (1%)
    ppermute x8, starting transfers between devices, _swap_col(): return lax.ppermute(x, ('row', 'col'), perm)  39.9 us
    ppermute x8, waiting for transfers between devices, _swap_col(): return lax.ppermute(x, ('row', 'col'), perm)  25.8 us
    pallas_call x1, Pallas kernels, along_call(): pl.pallas_call(kernel, grid_spec=spec, out_shape=jax.ShapeDtypeStruct((nr...  5.6 us
    pallas_call x1, Pallas kernels, against_call(): pl.pallas_call(kernel, grid_spec=spec, out_shape=jax.ShapeDtypeStruct((nc...  5.16 us
    another operation x7, other arithmetic, gather_col(): have = jnp.stack([lo, hi], axis=0).reshape((-1,) + have.shape[1:])  3.13 us
  transfers between devices with their start and end apart: 10, of which 6 were waited for; matrix products, arithmetic and copies ran while one was open for 14% of the time, Pallas kernels for 12%

profile of v2, /device:TPU:0, one launch (start us, length us, event | category | flops | bytes accessed | tf_op | source)
XLA Modules:
  0.0 92.1 jit_solution(5406084990360665074)
XLA Ops:
  0.0 0.5 collective-permute-start
  0.5 3.7 %collective-permute-start.5 = (bf16[1,2,128,128]{2,3,1,0:T(8,128)(2,1)}, bf16[1,2,128,128]{2,3,1,0:T(8,128)(2,1)S(1)}, u32[]{:S(2)}, u32[]{:S(2)}) collective-permute-start(bf16[1,2,128,128]{2,3,1,0:T(8,128)(2,1)} %bitcast.103), channel_id=1, source_target_pairs={{0,8},{1,9},{2,10},{3,11},{4,12},{5,13},{6,14},{7,15},{8,0},{9,1},... | collective-permute-start | bytes 196616 | tf_op jit(solution)/shard_map/ppermute | solution.py:31
  4.1 1.2 %multiply_add_fusion.1 = (s32[128]{0:T(128)}, s32[128]{0:T(128)S(1)}) fusion(s32[]{:T(128)S(6)} %select_n.141, s32[]{:T(128)S(6)} %select_n.143, s32[]{:T(128)S(6)} %select_n.142, s32[1,1,128]{2,1,0:T(1,128)} %param.9), kind=kLoop, calls=%fused_computation.36 | loop fusion | flops 4736 | bytes 1548 | tf_op jit(solution)/shard_map/add | solution.py:235
  5.3 1.2 %clamp_bitcast_fusion.cols_ref = s32[128]{0:T(128)} fusion(s32[1,1,128]{2,1,0:T(1,128)} %param.10), kind=kLoop, calls=%fused_computation.35 | loop fusion | flops 128 | bytes 1024 | tf_op jit(solution)/shard_map/jit(clip)/min | solution.py:222
  7.2 1.2 %collective-permute-done.5 = bf16[1,2,128,128]{2,3,1,0:T(8,128)(2,1)S(1)} collective-permute-done((bf16[1,2,128,128]{2,3,1,0:T(8,128)(2,1)}, bf16[1,2,128,128]{2,3,1,0:T(8,128)(2,1)S(1)}, u32[]{:S(2)}, u32[]{:S(2)}) %collective-permute-start.5) | collective-permute-done | bytes 65568 | tf_op jit(solution)/shard_map/ppermute | solution.py:31
  8.4 0.9 select_bitcast_fusion.7
  9.3 0.7 maximum_bitcast_fusion
  9.9 1.5 %collective-permute-start.6 = (bf16[2,2,128,128]{2,3,1,0:T(8,128)(2,1)}, bf16[2,2,128,128]{2,3,1,0:T(8,128)(2,1)S(1)}, u32[]{:S(2)}, u32[]{:S(2)}) collective-permute-start(bf16[2,2,128,128]{2,3,1,0:T(8,128)(2,1)} %maximum_bitcast_fusion), channel_id=1, source_target_pairs={{0,1},{1,0},{2,3},{3,2},{4,5},{5,4},{6,7},{7,6},{8,9},{9,8},{10,11... | collective-permute-start | bytes 393224 | tf_op jit(solution)/shard_map/ppermute | solution.py:31
  11.5 0.9 select_bitcast_fusion.9
  12.3 0.7 pad_maximum_fusion.3
  13.0 5.6 %shard_map.73 = f32[32,128,128]{2,1,0:T(8,128)} custom-call(s32[128]{0:T(128)} %get-tuple-element.5.rows_ref, s32[128]{0:T(128)} %clamp_bitcast_fusion.cols_ref, s32[1]{0:T(128)} %bitcast.2.cnt_ref, bf16[128,128,128]{2,1,0:T(8,128)(2,1)} %bitcast.91, bf16[4,128,128]{2,1,0:T(8,128)(2,1)} %bitcast.100), custom_call_target="tpu_custom_call" | custom-call | tf_op jit(solution)/shard_map/pallas_call | solution.py:153
  18.6 1.3 %dynamic-slice_bitcast_fusion = f32[2,2,2,2,128,128]{5,4,3,2,1,0:T(8,128)S(1)} fusion(f32[2,2,2,2,2,128,128]{6,5,4,3,2,1,0:T(8,128)} %bitcast.93, s32[]{:T(128)S(6)} %select_n.149), kind=kLoop, calls=%fused_computation.4 | loop fusion | bytes 2097156 | tf_op jit(solution)/shard_map/jit(dynamic_index_in_dim)/squeeze | solution.py:103
  19.9 6.4 %collective-permute-start.1 = (f32[2,2,2,2,128,128]{5,4,3,2,1,0:T(8,128)S(1)}, f32[2,2,2,2,128,128]{5,4,3,2,1,0:T(8,128)}, u32[]{:S(2)}, u32[]{:S(2)}) collective-permute-start(f32[2,2,2,2,128,128]{5,4,3,2,1,0:T(8,128)S(1)} %dynamic-slice_bitcast_fusion), channel_id=1, source_target_pairs={{0,1},{1,0},{2,3},{3,2},{4,5},{5,4},{6,7},{7,6},{8,9},{9,8},{10,11... | collective-permute-start | bytes 3145736 | tf_op jit(solution)/shard_map/ppermute | solution.py:31
  26.4 0.8 copy.12
  27.2 7.0 %collective-permute-done.7 = bf16[4,2,128,128]{3,2,1,0:T(8,128)(2,1)S(1)} collective-permute-done((bf16[4,2,128,128]{3,2,1,0:T(8,128)(2,1)}, bf16[4,2,128,128]{3,2,1,0:T(8,128)(2,1)S(1)}, u32[]{:S(2)}, u32[]{:S(2)}) %collective-permute-start.7) | collective-permute-done | bytes 262176 | tf_op jit(solution)/shard_map/ppermute | solution.py:31
  34.2 1.0 %select_bitcast_fusion.3 = (bf16[1,4,2,128,128]{4,3,2,1,0:T(8,128)(2,1)S(1)}, bf16[1,4,2,128,128]{4,3,2,1,0:T(8,128)(2,1)S(1)}) fusion(bf16[4,2,128,128]{3,2,1,0:T(8,128)(2,1)} %copy.12, bf16[4,2,128,128]{3,2,1,0:T(8,128)(2,1)S(1)} %collective-permute-done.7, pred[]{:T(512)S(6)} %eq.21), kind=kLoop, calls=%fused_computation.13 | loop fusion | flops 262144 | bytes 1048577 | tf_op jit(solution)/shard_map/stack | solution.py:90
  35.4 0.5 multiply_add_fusion.rows_ref
  35.9 4.0 %collective-permute-done.1 = f32[2,2,2,2,128,128]{5,4,3,2,1,0:T(8,128)} collective-permute-done((f32[2,2,2,2,128,128]{5,4,3,2,1,0:T(8,128)S(1)}, f32[2,2,2,2,128,128]{5,4,3,2,1,0:T(8,128)}, u32[]{:S(2)}, u32[]{:S(2)}) %collective-permute-start.1) | collective-permute-done | bytes 1048608 | tf_op jit(solution)/shard_map/ppermute | solution.py:31
  39.9 1.3 %bitcast_add_fusion = f32[2,2,2,2,128,128]{5,4,3,2,1,0:T(8,128)S(1)} fusion(f32[2,2,2,2,128,128]{5,4,3,2,1,0:T(8,128)} %collective-permute-done.1, f32[2,2,2,2,2,128,128]{6,5,4,3,2,1,0:T(8,128)S(1)} %bitcast.94, s32[]{:T(128)S(6)} %select_n.148), kind=kLoop, calls=%fused_computation.3 | loop fusion | flops 262144 | bytes 3145732 | tf_op jit(solution)/shard_map/add | solution.py:104
  41.4 3.2 %collective-permute-done.8 = bf16[8,2,128,128]{3,2,1,0:T(8,128)(2,1)S(1)} collective-permute-done((bf16[8,2,128,128]{3,2,1,0:T(8,128)(2,1)S(1)}, bf16[8,2,128,128]{3,2,1,0:T(8,128)(2,1)S(1)}, u32[]{:S(2)}, u32[]{:S(2)}) %collective-permute-start.8) | collective-permute-done | bytes 524320 | tf_op jit(solution)/shard_map/ppermute | solution.py:31
  44.5 0.1 select_bitcast_fusion.1
  44.6 1.1 %pad_maximum_fusion = bf16[2,8,2,128,128]{4,3,2,1,0:T(8,128)(2,1)} fusion(bf16[1,8,2,128,128]{4,3,2,1,0:T(8,128)(2,1)S(1)} %get-tuple-element.8, bf16[1,8,2,128,128]{4,3,2,1,0:T(8,128)(2,1)S(1)} %get-tuple-element.7), kind=kLoop, calls=%fused_computation.2 | loop fusion | flops 524288 | bytes 2097152 | tf_op jit(solution)/shard_map/stack | solution.py:90
  45.7 5.2 %shard_map.74 = f32[4,128,128]{2,1,0:T(8,128)} custom-call(s32[128]{0:T(128)} %multiply_add_fusion.rows_ref, s32[128]{0:T(128)} %clamp_bitcast_fusion.cols_ref, s32[1]{0:T(128)} %bitcast.2.cnt_ref, bf16[128,128,128]{2,1,0:T(8,128)(2,1)} %bitcast.92, bf16[32,128,128]{2,1,0:T(8,128)(2,1)} %bitcast.95), custom_call_target="tpu_custom_call" | custom-call | tf_op jit(solution)/shard_map/pallas_call | solution.py:201
  50.9 1.0 %constant_dynamic-slice_fusion.1 = (f32[1,2,128,128]{3,2,1,0:T(8,128)S(1)}, f32[1,2,128,128]{3,2,1,0:T(8,128)S(1)}) fusion(f32[2,2,128,128]{3,2,1,0:T(8,128)} %bitcast.97, s32[]{:T(128)S(6)} %select_n.168, s32[]{:T(128)S(6)} %select_n.169), kind=kLoop, calls=%fused_computation.27 | loop fusion | bytes 524296 | tf_op jit(solution)/shard_map/jit(dynamic_index_in_dim)/dynamic_slice | solution.py:71
  51.9 0.1 copy.15
  52.2 1.2 %collective-permute-start.3 = (f32[2,2,128,128]{3,2,1,0:T(8,128)S(1)}, f32[2,2,128,128]{3,2,1,0:T(8,128)S(1)}, u32[]{:S(2)}, u32[]{:S(2)}) collective-permute-start(f32[2,2,128,128]{3,2,1,0:T(8,128)S(1)} %dynamic-slice_bitcast_fusion.2), channel_id=1, source_target_pairs={{0,4},{1,5},{2,6},{3,7},{4,0},{5,1},{6,2},{7,3},{8,12},{9,13},{10,... | collective-permute-start | bytes 786440 | tf_op jit(solution)/shard_map/ppermute | solution.py:31
  53.4 0.1 copy.14
  53.5 5.1 %collective-permute-done.3 = f32[2,2,128,128]{3,2,1,0:T(8,128)S(1)} collective-permute-done((f32[2,2,128,128]{3,2,1,0:T(8,128)S(1)}, f32[2,2,128,128]{3,2,1,0:T(8,128)S(1)}, u32[]{:S(2)}, u32[]{:S(2)}) %collective-permute-start.3) | collective-permute-done | bytes 262176 | tf_op jit(solution)/shard_map/ppermute | solution.py:31
  58.7 26.9 %collective-permute-start.4 = (f32[2,128,128]{2,1,0:T(8,128)S(1)}, f32[2,128,128]{2,1,0:T(8,128)S(1)}, u32[]{:S(2)}, u32[]{:S(2)}) collective-permute-start(f32[2,128,128]{2,1,0:T(8,128)S(1)} %dynamic-slice_bitcast_fusion.3), channel_id=1, source_target_pairs={{0,8},{1,9},{2,10},{3,11},{4,12},{5,13},{6,14},{7,15},{8,0},{9,1},... | collective-permute-start | bytes 393224 | tf_op jit(solution)/shard_map/ppermute | solution.py:31
  85.6 0.2 fusion.1
  85.8 5.4 %collective-permute-done.4 = f32[2,128,128]{2,1,0:T(8,128)S(1)} collective-permute-done((f32[2,128,128]{2,1,0:T(8,128)S(1)}, f32[2,128,128]{2,1,0:T(8,128)S(1)}, u32[]{:S(2)}, u32[]{:S(2)}) %collective-permute-start.4) | collective-permute-done | bytes 131104 | tf_op jit(solution)/shard_map/ppermute | solution.py:31
  91.2 0.9 fusion
  (26 shorter events, 0.6 us)
Async XLA Ops:
  0.0 85.6 %copy-start = (bf16[128,256]{1,0:T(8,128)(2,1)S(1)}, bf16[128,256]{1,0:T(8,128)(2,1)}, u32[]{:S(2)}) copy-start(bf16[128,256]{1,0:T(8,128)(2,1)} %param.13) | copy-start | bytes 196612
  0.0 11.5 %collective-permute-start = (bf16[1,256,128]{2,1,0:T(8,128)(2,1)}, bf16[1,256,128]{2,1,0:T(8,128)(2,1)S(1)}, u32[]{:S(2)}, u32[]{:S(2)}) collective-permute-start(bf16[1,256,128]{2,1,0:T(8,128)(2,1)} %bitcast.102), channel_id=1, source_target_pairs={{0,16},{16,0},{1,17},{17,1},{2,18},{18,2},{3,19},{19,3},{4,20},{20... | collective-permute-start | bytes 196616 | tf_op jit(solution)/shard_map/ppermute | solution.py:36
  0.5 8.0 %collective-permute-start.5 = (bf16[1,2,128,128]{2,3,1,0:T(8,128)(2,1)}, bf16[1,2,128,128]{2,3,1,0:T(8,128)(2,1)S(1)}, u32[]{:S(2)}, u32[]{:S(2)}) collective-permute-start(bf16[1,2,128,128]{2,3,1,0:T(8,128)(2,1)} %bitcast.103), channel_id=1, source_target_pairs={{0,8},{1,9},{2,10},{3,11},{4,12},{5,13},{6,14},{7,15},{8,0},{9,1},... | collective-permute-start | bytes 196616 | tf_op jit(solution)/shard_map/ppermute | solution.py:31
  9.9 16.4 %collective-permute-start.6 = (bf16[2,2,128,128]{2,3,1,0:T(8,128)(2,1)}, bf16[2,2,128,128]{2,3,1,0:T(8,128)(2,1)S(1)}, u32[]{:S(2)}, u32[]{:S(2)}) collective-permute-start(bf16[2,2,128,128]{2,3,1,0:T(8,128)(2,1)} %maximum_bitcast_fusion), channel_id=1, source_target_pairs={{0,1},{1,0},{2,3},{3,2},{4,5},{5,4},{6,7},{7,6},{8,9},{9,8},{10,11... | collective-permute-start | bytes 393224 | tf_op jit(solution)/shard_map/ppermute | solution.py:31
  19.9 15.4 %copy-start.3 = (s32[1,1,128]{2,1,0:T(1,128)S(1)}, s32[1,1,128]{2,1,0:T(1,128)}, u32[]{:S(2)}) copy-start(s32[1,1,128]{2,1,0:T(1,128)} %param.9) | copy-start | bytes 1540
  19.9 20.0 %copy-start.1 = (f32[32,128,128]{2,1,0:T(8,128)S(1)}, f32[32,128,128]{2,1,0:T(8,128)}, u32[]{:S(2)}) copy-start(f32[32,128,128]{2,1,0:T(8,128)} %shard_map.73) | copy-start | bytes 6291460
  19.9 20.0 %collective-permute-start.1 = (f32[2,2,2,2,128,128]{5,4,3,2,1,0:T(8,128)S(1)}, f32[2,2,2,2,128,128]{5,4,3,2,1,0:T(8,128)}, u32[]{:S(2)}, u32[]{:S(2)}) collective-permute-start(f32[2,2,2,2,128,128]{5,4,3,2,1,0:T(8,128)S(1)} %dynamic-slice_bitcast_fusion), channel_id=1, source_target_pairs={{0,1},{1,0},{2,3},{3,2},{4,5},{5,4},{6,7},{7,6},{8,9},{9,8},{10,11... | collective-permute-start | bytes 3145736 | tf_op jit(solution)/shard_map/ppermute | solution.py:31
  27.2 7.0 %collective-permute-start.7 = (bf16[4,2,128,128]{3,2,1,0:T(8,128)(2,1)}, bf16[4,2,128,128]{3,2,1,0:T(8,128)(2,1)S(1)}, u32[]{:S(2)}, u32[]{:S(2)}) collective-permute-start(bf16[4,2,128,128]{3,2,1,0:T(8,128)(2,1)} %copy.12), channel_id=1, source_target_pairs={{0,2},{1,3},{2,0},{3,1},{4,6},{5,7},{6,4},{7,5},{8,10},{9,11},{10,... | collective-permute-start | bytes 786440 | tf_op jit(solution)/shard_map/ppermute | solution.py:31
  35.3 9.2 %collective-permute-start.8 = (bf16[8,2,128,128]{3,2,1,0:T(8,128)(2,1)S(1)}, bf16[8,2,128,128]{3,2,1,0:T(8,128)(2,1)S(1)}, u32[]{:S(2)}, u32[]{:S(2)}) collective-permute-start(bf16[8,2,128,128]{3,2,1,0:T(8,128)(2,1)S(1)} %bitcast.96), channel_id=1, source_target_pairs={{0,4},{1,5},{2,6},{3,7},{4,0},{5,1},{6,2},{7,3},{8,12},{9,13},{10,... | collective-permute-start | bytes 1572872 | tf_op jit(solution)/shard_map/ppermute | solution.py:31
  41.3 10.8 %collective-permute-start.2 = (f32[2,2,2,128,128]{4,3,2,1,0:T(8,128)S(1)}, f32[2,2,2,128,128]{4,3,2,1,0:T(8,128)S(1)}, u32[]{:S(2)}, u32[]{:S(2)}) collective-permute-start(f32[2,2,2,128,128]{4,3,2,1,0:T(8,128)S(1)} %dynamic-slice_bitcast_fusion.1), channel_id=1, source_target_pairs={{0,2},{1,3},{2,0},{3,1},{4,6},{5,7},{6,4},{7,5},{8,10},{9,11},{10,... | collective-permute-start | bytes 1572872 | tf_op jit(solution)/shard_map/ppermute | solution.py:31
  52.0 39.3 %copy-start.2 = (bf16[128,256]{1,0:T(8,128)(2,1)S(1)}, bf16[128,256]{1,0:T(8,128)(2,1)}, u32[]{:S(2)}) copy-start(bf16[128,256]{1,0:T(8,128)(2,1)} %param.12) | copy-start | bytes 196612
  52.0 1.5 %collective-permute-start.9 = (f32[2,128,128]{1,2,0:T(8,128)S(1)}, f32[2,128,128]{1,2,0:T(8,128)S(1)}, u32[]{:S(2)}, u32[]{:S(2)}) collective-permute-start(f32[2,128,128]{1,2,0:T(8,128)S(1)} %bitcast.105), channel_id=1, source_target_pairs={{0,16},{16,0},{1,17},{17,1},{2,18},{18,2},{3,19},{19,3},{4,20},{20... | collective-permute-start | bytes 393224 | tf_op jit(solution)/shard_map/ppermute | solution.py:36
  52.2 6.4 %collective-permute-start.3 = (f32[2,2,128,128]{3,2,1,0:T(8,128)S(1)}, f32[2,2,128,128]{3,2,1,0:T(8,128)S(1)}, u32[]{:S(2)}, u32[]{:S(2)}) collective-permute-start(f32[2,2,128,128]{3,2,1,0:T(8,128)S(1)} %dynamic-slice_bitcast_fusion.2), channel_id=1, source_target_pairs={{0,4},{1,5},{2,6},{3,7},{4,0},{5,1},{6,2},{7,3},{8,12},{9,13},{10,... | collective-permute-start | bytes 786440 | tf_op jit(solution)/shard_map/ppermute | solution.py:31
  58.7 32.5 %collective-permute-start.4 = (f32[2,128,128]{2,1,0:T(8,128)S(1)}, f32[2,128,128]{2,1,0:T(8,128)S(1)}, u32[]{:S(2)}, u32[]{:S(2)}) collective-permute-start(f32[2,128,128]{2,1,0:T(8,128)S(1)} %dynamic-slice_bitcast_fusion.3), channel_id=1, source_target_pairs={{0,8},{1,9},{2,10},{3,11},{4,12},{5,13},{6,14},{7,15},{8,0},{9,1},... | collective-permute-start | bytes 393224 | tf_op jit(solution)/shard_map/ppermute | solution.py:31

commit v3 on v2

--- a/solution.py
+++ b/solution.py
@@ -106,7 +106,7 @@
 
 
 def _chunk(slots):
-    return 16 if slots % 16 == 0 else slots
+    return 32 if slots % 32 == 0 else slots
 
 
 def along_call(rows, cols, cnt, values, group, nrb):
@@ -122,20 +122,14 @@
         def _():
             out_ref[...] = jnp.zeros(out_ref.shape, out_ref.dtype)
 
-        def body(t, carry):
-            s = i * k + t
-
-            @pl.when(s < n)
-            def _():
+        @pl.when(i * k < n)
+        def _():
+            for t in range(k):
+                s = i * k + t
+                tile = jnp.where(s < n, vals_ref[t], jnp.zeros((side, side), vals_ref.dtype))
                 r = rows_ref[s]
                 c = cols_ref[s]
-                out_ref[r] += jnp.dot(vals_ref[t], grp_ref[c], preferred_element_type=jnp.float32)
-
-            return carry
-
-        @pl.when(i * k < n)
-        def _():
-            lax.fori_loop(0, k, body, 0)
+                out_ref[r] += jnp.dot(tile, grp_ref[c], preferred_element_type=jnp.float32)
 
     def vals_map(i, rows_ref, cols_ref, cnt_ref):
         last = jnp.maximum(cnt_ref[0] - 1, 0) // k
@@ -170,20 +164,14 @@
         def _():
             out_ref[...] = jnp.zeros(out_ref.shape, out_ref.dtype)
 
-        def body(t, carry):
-            s = i * k + t
-
-            @pl.when(s < n)
-            def _():
+        @pl.when(i * k < n)
+        def _():
+            for t in range(k):
+                s = i * k + t
+                tile = jnp.where(s < n, vals_ref[t], jnp.zeros((side, side), vals_ref.dtype))
                 r = rows_ref[s]
                 c = cols_ref[s]
-                out_ref[c] += jnp.dot(st_ref[r], vals_ref[t], preferred_element_type=jnp.float32)
-
-            return carry
-
-        @pl.when(i * k < n)
-        def _():
-            lax.fori_loop(0, k, body, 0)
+                out_ref[c] += jnp.dot(st_ref[r], tile, preferred_element_type=jnp.float32)
 
     def vals_map(i, rows_ref, cols_ref, cnt_ref):
         last = jnp.maximum(cnt_ref[0] - 1, 0) // k

time: 91.7 us -> 62.8 us (0.68)
  starting transfers between devices: 40.4 us -> 17.4 us
  Pallas kernels: 10.8 us -> 7.53 us
  waiting for transfers between devices: 25.8 us -> 23.6 us
    ppermute x8, starting transfers between devices: 39.9 us -> 15.7 us  [_swap_col(): return lax.ppermute(x, ('row', 'col'), perm)]
    ppermute x8, waiting for transfers between devices: 25.8 us -> 23.6 us  [_swap_col(): return lax.ppermute(x, ('row', 'col'), perm)]
    pallas_call x1, Pallas kernels: 5.6 us -> 3.97 us  [along_call(): pl.pallas_call(kernel, grid_spec=spec, out_shape=jax.ShapeDtypeStruct((nr...]
    pallas_call x1, Pallas kernels: 5.16 us -> 3.56 us  [against_call(): pl.pallas_call(kernel, grid_spec=spec, out_shape=jax.ShapeDtypeStruct((nc...]
    ppermute x2, starting transfers between devices: 0.52 us -> 1.7 us  [_swap(): return lax.ppermute(x, axis, perm)]
  transfers between devices with their start and end apart: 10 -> 10, of which waited for: 6 -> 6; matrix products, arithmetic and copies ran while one was open for 14% -> 21% of each run, Pallas kernels for 12% -> 12%
where the time goes in v3:
time: 62.8 us; the launch traced here: 63.7 us
  waiting for transfers between devices  23.6 us (38%)
  starting transfers between devices  17.4 us (28%)
  other arithmetic  9.73 us (15%)
  Pallas kernels  7.53 us (12%)
  local copies, waits for them, and re-layouts  3.43 us (5%)
  matrix products  1.16 us (2%)
  between operations  0.83 us (1%)
    ppermute x8, waiting for transfers between devices, _swap_col(): return lax.ppermute(x, ('row', 'col'), perm)  23.6 us
    ppermute x8, starting transfers between devices, _swap_col(): return lax.ppermute(x, ('row', 'col'), perm)  15.7 us
    pallas_call x1, Pallas kernels, along_call(): pl.pallas_call(kernel, grid_spec=spec, out_shape=jax.ShapeDtypeStruct((nr...  3.97 us
    pallas_call x1, Pallas kernels, against_call(): pl.pallas_call(kernel, grid_spec=spec, out_shape=jax.ShapeDtypeStruct((nc...  3.56 us
    another operation x7, other arithmetic, gather_col(): have = jnp.stack([lo, hi], axis=0).reshape((-1,) + have.shape[1:])  3.13 us
    ppermute x2, starting transfers between devices, _swap(): return lax.ppermute(x, axis, perm)  1.7 us
    another operation x2, other arithmetic, gather_row(): have = jnp.stack([lo, hi], axis=0).reshape((-1,) + have.shape[1:])  1.51 us
    add x4, other arithmetic, scatter_sum_col(): keep + _swap_col(other, row_size, col_size, (order[0][t], order[1][t]))  1.44 us
  transfers between devices with their start and end apart: 10, of which 6 were waited for; matrix products, arithmetic and copies ran while one was open for 21% of the time, Pallas kernels for 12%

profile of v3, /device:TPU:0, one launch (start us, length us, event | category | flops | bytes accessed | tf_op | source)
XLA Modules:
  0.0 63.7 jit_solution(9968494154906229840)
XLA Ops:
  0.0 0.5 collective-permute-start
  0.5 3.7 %collective-permute-start.5 = (bf16[1,2,128,128]{2,3,1,0:T(8,128)(2,1)}, bf16[1,2,128,128]{2,3,1,0:T(8,128)(2,1)S(1)}, u32[]{:S(2)}, u32[]{:S(2)}) collective-permute-start(bf16[1,2,128,128]{2,3,1,0:T(8,128)(2,1)} %bitcast.103), channel_id=1, source_target_pairs={{0,8},{1,9},{2,10},{3,11},{4,12},{5,13},{6,14},{7,15},{8,0},{9,1},... | collective-permute-start | bytes 196616 | tf_op jit(solution)/shard_map/ppermute | solution.py:31
  4.1 1.2 %multiply_add_fusion.1 = (s32[128]{0:T(128)}, s32[128]{0:T(128)S(1)}) fusion(s32[]{:T(128)S(6)} %select_n.141, s32[]{:T(128)S(6)} %select_n.143, s32[]{:T(128)S(6)} %select_n.142, s32[1,1,128]{2,1,0:T(1,128)} %param.9), kind=kLoop, calls=%fused_computation.36 | loop fusion | flops 4736 | bytes 1548 | tf_op jit(solution)/shard_map/add | solution.py:223
  5.3 1.2 %clamp_bitcast_fusion.cols_ref = s32[128]{0:T(128)} fusion(s32[1,1,128]{2,1,0:T(1,128)} %param.10), kind=kLoop, calls=%fused_computation.35 | loop fusion | flops 128 | bytes 1024 | tf_op jit(solution)/shard_map/jit(clip)/min | solution.py:210
  7.2 1.2 %collective-permute-done.5 = bf16[1,2,128,128]{2,3,1,0:T(8,128)(2,1)S(1)} collective-permute-done((bf16[1,2,128,128]{2,3,1,0:T(8,128)(2,1)}, bf16[1,2,128,128]{2,3,1,0:T(8,128)(2,1)S(1)}, u32[]{:S(2)}, u32[]{:S(2)}) %collective-permute-start.5) | collective-permute-done | bytes 65568 | tf_op jit(solution)/shard_map/ppermute | solution.py:31
  8.4 0.9 %select_bitcast_fusion.7 = (bf16[1,1,2,128,128]{3,4,2,1,0:T(8,128)(2,1)S(1)}, bf16[1,1,2,128,128]{3,4,2,1,0:T(8,128)(2,1)S(1)}) fusion(bf16[1,2,128,128]{2,3,1,0:T(8,128)(2,1)} %bitcast.104, bf16[1,2,128,128]{2,3,1,0:T(8,128)(2,1)S(1)} %collective-permute-done.5, pred[]{:T(512)S(6)} %eq.23), kind=kLoop, calls=%fused_computation.23 | loop fusion | flops 65536 | bytes 262145 | tf_op jit(solution)/shard_map/stack | solution.py:90
  9.3 0.7 %maximum_bitcast_fusion = bf16[2,2,128,128]{2,3,1,0:T(8,128)(2,1)} fusion(bf16[1,1,2,128,128]{3,4,2,1,0:T(8,128)(2,1)S(1)} %get-tuple-element.18, bf16[1,1,2,128,128]{3,4,2,1,0:T(8,128)(2,1)S(1)} %get-tuple-element.17), kind=kLoop, calls=%fused_computation.16 | loop fusion | flops 65536 | bytes 262144 | tf_op jit(solution)/shard_map/reshape | solution.py:90
  9.9 1.5 %collective-permute-start.6 = (bf16[2,2,128,128]{2,3,1,0:T(8,128)(2,1)}, bf16[2,2,128,128]{2,3,1,0:T(8,128)(2,1)S(1)}, u32[]{:S(2)}, u32[]{:S(2)}) collective-permute-start(bf16[2,2,128,128]{2,3,1,0:T(8,128)(2,1)} %maximum_bitcast_fusion), channel_id=1, source_target_pairs={{0,1},{1,0},{2,3},{3,2},{4,5},{5,4},{6,7},{7,6},{8,9},{9,8},{10,11... | collective-permute-start | bytes 393224 | tf_op jit(solution)/shard_map/ppermute | solution.py:31
  11.5 0.9 %select_bitcast_fusion.9 = (bf16[1,1,256,128]{3,2,1,0:T(8,128)(2,1)S(1)}, bf16[1,1,256,128]{3,2,1,0:T(8,128)(2,1)S(1)}) fusion(bf16[1,256,128]{2,1,0:T(8,128)(2,1)S(1)} %collective-permute-done, pred[]{:T(512)S(6)} %eq.19, bf16[256,128]{1,0:T(8,128)(2,1)} %param.7), kind=kLoop, calls=%fused_computation.25 | loop fusion | flops 65536 | bytes 262145 | tf_op jit(solution)/shard_map/stack | solution.py:52
  12.3 0.7 %pad_maximum_fusion.3 = bf16[2,1,256,128]{3,2,1,0:T(8,128)(2,1)} fusion(bf16[1,1,256,128]{3,2,1,0:T(8,128)(2,1)S(1)} %get-tuple-element.16, bf16[1,1,256,128]{3,2,1,0:T(8,128)(2,1)S(1)} %get-tuple-element.15), kind=kLoop, calls=%fused_computation.15 | loop fusion | flops 65536 | bytes 262144 | tf_op jit(solution)/shard_map/stack | solution.py:52
  13.0 4.0 %shard_map.73 = f32[32,128,128]{2,1,0:T(8,128)} custom-call(s32[128]{0:T(128)} %get-tuple-element.5.rows_ref, s32[128]{0:T(128)} %clamp_bitcast_fusion.cols_ref, s32[1]{0:T(128)} %bitcast.2.cnt_ref, bf16[128,128,128]{2,1,0:T(8,128)(2,1)} %bitcast.91, bf16[4,128,128]{2,1,0:T(8,128)(2,1)} %bitcast.100), custom_call_target="tpu_custom_call" | custom-call | tf_op jit(solution)/shard_map/pallas_call | solution.py:147
  17.0 1.3 %dynamic-slice_bitcast_fusion = f32[2,2,2,2,128,128]{5,4,3,2,1,0:T(8,128)S(1)} fusion(f32[2,2,2,2,2,128,128]{6,5,4,3,2,1,0:T(8,128)} %bitcast.93, s32[]{:T(128)S(6)} %select_n.149), kind=kLoop, calls=%fused_computation.4 | loop fusion | bytes 2097156 | tf_op jit(solution)/shard_map/jit(dynamic_index_in_dim)/squeeze | solution.py:103
  18.3 0.6 collective-permute-start.1
  18.9 0.8 %copy.12 = bf16[4,2,128,128]{3,2,1,0:T(8,128)(2,1)} copy(bf16[4,2,128,128]{2,3,1,0:T(8,128)(2,1)S(1)} %bitcast.98) | data formatting | bytes 524288 | tf_op jit(solution)/shard_map/reshape | solution.py:90
  19.8 1.6 %collective-permute-start.7 = (bf16[4,2,128,128]{3,2,1,0:T(8,128)(2,1)}, bf16[4,2,128,128]{3,2,1,0:T(8,128)(2,1)S(1)}, u32[]{:S(2)}, u32[]{:S(2)}) collective-permute-start(bf16[4,2,128,128]{3,2,1,0:T(8,128)(2,1)} %copy.12), channel_id=1, source_target_pairs={{0,2},{1,3},{2,0},{3,1},{4,6},{5,7},{6,4},{7,5},{8,10},{9,11},{10,... | collective-permute-start | bytes 786440 | tf_op jit(solution)/shard_map/ppermute | solution.py:31
  21.3 5.0 %collective-permute-done.7 = bf16[4,2,128,128]{3,2,1,0:T(8,128)(2,1)S(1)} collective-permute-done((bf16[4,2,128,128]{3,2,1,0:T(8,128)(2,1)}, bf16[4,2,128,128]{3,2,1,0:T(8,128)(2,1)S(1)}, u32[]{:S(2)}, u32[]{:S(2)}) %collective-permute-start.7) | collective-permute-done | bytes 262176 | tf_op jit(solution)/shard_map/ppermute | solution.py:31
  26.4 1.0 %select_bitcast_fusion.3 = (bf16[1,4,2,128,128]{4,3,2,1,0:T(8,128)(2,1)S(1)}, bf16[1,4,2,128,128]{4,3,2,1,0:T(8,128)(2,1)S(1)}) fusion(bf16[4,2,128,128]{3,2,1,0:T(8,128)(2,1)} %copy.12, bf16[4,2,128,128]{3,2,1,0:T(8,128)(2,1)S(1)} %collective-permute-done.7, pred[]{:T(512)S(6)} %eq.21), kind=kLoop, calls=%fused_computation.13 | loop fusion | flops 262144 | bytes 1048577 | tf_op jit(solution)/shard_map/stack | solution.py:90
  27.4 0.9 %collective-permute-start.8 = (bf16[8,2,128,128]{3,2,1,0:T(8,128)(2,1)S(1)}, bf16[8,2,128,128]{3,2,1,0:T(8,128)(2,1)S(1)}, u32[]{:S(2)}, u32[]{:S(2)}) collective-permute-start(bf16[8,2,128,128]{3,2,1,0:T(8,128)(2,1)S(1)} %bitcast.96), channel_id=1, source_target_pairs={{0,4},{1,5},{2,6},{3,7},{4,0},{5,1},{6,2},{7,3},{8,12},{9,13},{10,... | collective-permute-start | bytes 1572872 | tf_op jit(solution)/shard_map/ppermute | solution.py:31
  28.3 0.5 multiply_add_fusion.rows_ref
  28.8 7.3 %collective-permute-done.1 = f32[2,2,2,2,128,128]{5,4,3,2,1,0:T(8,128)} collective-permute-done((f32[2,2,2,2,128,128]{5,4,3,2,1,0:T(8,128)S(1)}, f32[2,2,2,2,128,128]{5,4,3,2,1,0:T(8,128)}, u32[]{:S(2)}, u32[]{:S(2)}) %collective-permute-start.1) | collective-permute-done | bytes 1048608 | tf_op jit(solution)/shard_map/ppermute | solution.py:31
  36.1 1.3 %bitcast_add_fusion = f32[2,2,2,2,128,128]{5,4,3,2,1,0:T(8,128)S(1)} fusion(f32[2,2,2,2,128,128]{5,4,3,2,1,0:T(8,128)} %collective-permute-done.1, f32[2,2,2,2,2,128,128]{6,5,4,3,2,1,0:T(8,128)S(1)} %bitcast.94, s32[]{:T(128)S(6)} %select_n.148), kind=kLoop, calls=%fused_computation.3 | loop fusion | flops 262144 | bytes 3145732 | tf_op jit(solution)/shard_map/add | solution.py:104
  37.5 1.1 %collective-permute-start.2 = (f32[2,2,2,128,128]{4,3,2,1,0:T(8,128)S(1)}, f32[2,2,2,128,128]{4,3,2,1,0:T(8,128)S(1)}, u32[]{:S(2)}, u32[]{:S(2)}) collective-permute-start(f32[2,2,2,128,128]{4,3,2,1,0:T(8,128)S(1)} %dynamic-slice_bitcast_fusion.1), channel_id=1, source_target_pairs={{0,2},{1,3},{2,0},{3,1},{4,6},{5,7},{6,4},{7,5},{8,10},{9,11},{10,... | collective-permute-start | bytes 1572872 | tf_op jit(solution)/shard_map/ppermute | solution.py:31
  38.6 1.1 %pad_maximum_fusion = bf16[2,8,2,128,128]{4,3,2,1,0:T(8,128)(2,1)} fusion(bf16[1,8,2,128,128]{4,3,2,1,0:T(8,128)(2,1)S(1)} %get-tuple-element.8, bf16[1,8,2,128,128]{4,3,2,1,0:T(8,128)(2,1)S(1)} %get-tuple-element.7), kind=kLoop, calls=%fused_computation.2 | loop fusion | flops 524288 | bytes 2097152 | tf_op jit(solution)/shard_map/stack | solution.py:90
  39.7 3.6 %shard_map.74 = f32[4,128,128]{2,1,0:T(8,128)} custom-call(s32[128]{0:T(128)} %multiply_add_fusion.rows_ref, s32[128]{0:T(128)} %clamp_bitcast_fusion.cols_ref, s32[1]{0:T(128)} %bitcast.2.cnt_ref, bf16[128,128,128]{2,1,0:T(8,128)(2,1)} %bitcast.92, bf16[32,128,128]{2,1,0:T(8,128)(2,1)} %bitcast.95), custom_call_target="tpu_custom_call" | custom-call | tf_op jit(solution)/shard_map/pallas_call | solution.py:189
  43.3 1.0 %constant_dynamic-slice_fusion.1 = (f32[1,2,128,128]{3,2,1,0:T(8,128)S(1)}, f32[1,2,128,128]{3,2,1,0:T(8,128)S(1)}) fusion(f32[2,2,128,128]{3,2,1,0:T(8,128)} %bitcast.97, s32[]{:T(128)S(6)} %select_n.168, s32[]{:T(128)S(6)} %select_n.169), kind=kLoop, calls=%fused_computation.27 | loop fusion | bytes 524296 | tf_op jit(solution)/shard_map/jit(dynamic_index_in_dim)/dynamic_slice | solution.py:71
  44.4 1.2 %collective-permute-start.9 = (f32[2,128,128]{1,2,0:T(8,128)S(1)}, f32[2,128,128]{1,2,0:T(8,128)S(1)}, u32[]{:S(2)}, u32[]{:S(2)}) collective-permute-start(f32[2,128,128]{1,2,0:T(8,128)S(1)} %bitcast.105), channel_id=1, source_target_pairs={{0,16},{16,0},{1,17},{17,1},{2,18},{18,2},{3,19},{19,3},{4,20},{20... | collective-permute-start | bytes 393224 | tf_op jit(solution)/shard_map/ppermute | solution.py:36
  45.6 1.1 %collective-permute-done.2 = f32[2,2,2,128,128]{4,3,2,1,0:T(8,128)S(1)} collective-permute-done((f32[2,2,2,128,128]{4,3,2,1,0:T(8,128)S(1)}, f32[2,2,2,128,128]{4,3,2,1,0:T(8,128)S(1)}, u32[]{:S(2)}, u32[]{:S(2)}) %collective-permute-start.2) | collective-permute-done | bytes 524320 | tf_op jit(solution)/shard_map/ppermute | solution.py:31
  46.8 1.3 %collective-permute-start.3 = (f32[2,2,128,128]{3,2,1,0:T(8,128)S(1)}, f32[2,2,128,128]{3,2,1,0:T(8,128)S(1)}, u32[]{:S(2)}, u32[]{:S(2)}) collective-permute-start(f32[2,2,128,128]{3,2,1,0:T(8,128)S(1)} %dynamic-slice_bitcast_fusion.2), channel_id=1, source_target_pairs={{0,4},{1,5},{2,6},{3,7},{4,0},{5,1},{6,2},{7,3},{8,12},{9,13},{10,... | collective-permute-start | bytes 786440 | tf_op jit(solution)/shard_map/ppermute | solution.py:31
  48.3 5.0 %collective-permute-done.3 = f32[2,2,128,128]{3,2,1,0:T(8,128)S(1)} collective-permute-done((f32[2,2,128,128]{3,2,1,0:T(8,128)S(1)}, f32[2,2,128,128]{3,2,1,0:T(8,128)S(1)}, u32[]{:S(2)}, u32[]{:S(2)}) %collective-permute-start.3) | collective-permute-done | bytes 262176 | tf_op jit(solution)/shard_map/ppermute | solution.py:31
  53.3 5.1 %collective-permute-start.4 = (f32[2,128,128]{2,1,0:T(8,128)S(1)}, f32[2,128,128]{2,1,0:T(8,128)S(1)}, u32[]{:S(2)}, u32[]{:S(2)}) collective-permute-start(f32[2,128,128]{2,1,0:T(8,128)S(1)} %dynamic-slice_bitcast_fusion.3), channel_id=1, source_target_pairs={{0,8},{1,9},{2,10},{3,11},{4,12},{5,13},{6,14},{7,15},{8,0},{9,1},... | collective-permute-start | bytes 393224 | tf_op jit(solution)/shard_map/ppermute | solution.py:31
  58.7 4.1 %collective-permute-done.4 = f32[2,128,128]{2,1,0:T(8,128)S(1)} collective-permute-done((f32[2,128,128]{2,1,0:T(8,128)S(1)}, f32[2,128,128]{2,1,0:T(8,128)S(1)}, u32[]{:S(2)}, u32[]{:S(2)}) %collective-permute-start.4) | collective-permute-done | bytes 131104 | tf_op jit(solution)/shard_map/ppermute | solution.py:31
  62.8 0.9 %fusion = bf16[256,256]{1,0:T(8,128)(2,1)} fusion(f32[256,256]{1,0:T(8,128)S(1)} %fusion.1, f32[256,128]{1,0:T(8,128)S(1)} %bitcast.101, bf16[128,256]{1,0:T(8,128)(2,1)S(1)} %copy-done.2), kind=kOutput, calls=%fused_computation.1 | convolution fusion | flops 100794368 | bytes 589824 | tf_op jit(solution)/shard_map/dot_general | solution.py:246
  (26 shorter events, 0.9 us)
Async XLA Ops:
  0.0 58.4 %copy-start = (bf16[128,256]{1,0:T(8,128)(2,1)S(1)}, bf16[128,256]{1,0:T(8,128)(2,1)}, u32[]{:S(2)}) copy-start(bf16[128,256]{1,0:T(8,128)(2,1)} %param.13) | copy-start | bytes 196612
  0.0 11.5 %collective-permute-start = (bf16[1,256,128]{2,1,0:T(8,128)(2,1)}, bf16[1,256,128]{2,1,0:T(8,128)(2,1)S(1)}, u32[]{:S(2)}, u32[]{:S(2)}) collective-permute-start(bf16[1,256,128]{2,1,0:T(8,128)(2,1)} %bitcast.102), channel_id=1, source_target_pairs={{0,16},{16,0},{1,17},{17,1},{2,18},{18,2},{3,19},{19,3},{4,20},{20... | collective-permute-start | bytes 196616 | tf_op jit(solution)/shard_map/ppermute | solution.py:36
  0.5 8.0 %collective-permute-start.5 = (bf16[1,2,128,128]{2,3,1,0:T(8,128)(2,1)}, bf16[1,2,128,128]{2,3,1,0:T(8,128)(2,1)S(1)}, u32[]{:S(2)}, u32[]{:S(2)}) collective-permute-start(bf16[1,2,128,128]{2,3,1,0:T(8,128)(2,1)} %bitcast.103), channel_id=1, source_target_pairs={{0,8},{1,9},{2,10},{3,11},{4,12},{5,13},{6,14},{7,15},{8,0},{9,1},... | collective-permute-start | bytes 196616 | tf_op jit(solution)/shard_map/ppermute | solution.py:31
  9.9 8.9 %collective-permute-start.6 = (bf16[2,2,128,128]{2,3,1,0:T(8,128)(2,1)}, bf16[2,2,128,128]{2,3,1,0:T(8,128)(2,1)S(1)}, u32[]{:S(2)}, u32[]{:S(2)}) collective-permute-start(bf16[2,2,128,128]{2,3,1,0:T(8,128)(2,1)} %maximum_bitcast_fusion), channel_id=1, source_target_pairs={{0,1},{1,0},{2,3},{3,2},{4,5},{5,4},{6,7},{7,6},{8,9},{9,8},{10,11... | collective-permute-start | bytes 393224 | tf_op jit(solution)/shard_map/ppermute | solution.py:31
  18.3 10.0 %copy-start.3 = (s32[1,1,128]{2,1,0:T(1,128)S(1)}, s32[1,1,128]{2,1,0:T(1,128)}, u32[]{:S(2)}) copy-start(s32[1,1,128]{2,1,0:T(1,128)} %param.9) | copy-start | bytes 1540
  18.3 17.8 %copy-start.1 = (f32[32,128,128]{2,1,0:T(8,128)S(1)}, f32[32,128,128]{2,1,0:T(8,128)}, u32[]{:S(2)}) copy-start(f32[32,128,128]{2,1,0:T(8,128)} %shard_map.73) | copy-start | bytes 6291460
  18.3 17.8 %collective-permute-start.1 = (f32[2,2,2,2,128,128]{5,4,3,2,1,0:T(8,128)S(1)}, f32[2,2,2,2,128,128]{5,4,3,2,1,0:T(8,128)}, u32[]{:S(2)}, u32[]{:S(2)}) collective-permute-start(f32[2,2,2,2,128,128]{5,4,3,2,1,0:T(8,128)S(1)} %dynamic-slice_bitcast_fusion), channel_id=1, source_target_pairs={{0,1},{1,0},{2,3},{3,2},{4,5},{5,4},{6,7},{7,6},{8,9},{9,8},{10,11... | collective-permute-start | bytes 3145736 | tf_op jit(solution)/shard_map/ppermute | solution.py:31
  19.8 6.6 %collective-permute-start.7 = (bf16[4,2,128,128]{3,2,1,0:T(8,128)(2,1)}, bf16[4,2,128,128]{3,2,1,0:T(8,128)(2,1)S(1)}, u32[]{:S(2)}, u32[]{:S(2)}) collective-permute-start(bf16[4,2,128,128]{3,2,1,0:T(8,128)(2,1)} %copy.12), channel_id=1, source_target_pairs={{0,2},{1,3},{2,0},{3,1},{4,6},{5,7},{6,4},{7,5},{8,10},{9,11},{10,... | collective-permute-start | bytes 786440 | tf_op jit(solution)/shard_map/ppermute | solution.py:31
  27.4 11.1 %collective-permute-start.8 = (bf16[8,2,128,128]{3,2,1,0:T(8,128)(2,1)S(1)}, bf16[8,2,128,128]{3,2,1,0:T(8,128)(2,1)S(1)}, u32[]{:S(2)}, u32[]{:S(2)}) collective-permute-start(bf16[8,2,128,128]{3,2,1,0:T(8,128)(2,1)S(1)} %bitcast.96), channel_id=1, source_target_pairs={{0,4},{1,5},{2,6},{3,7},{4,0},{5,1},{6,2},{7,3},{8,12},{9,13},{10,... | collective-permute-start | bytes 1572872 | tf_op jit(solution)/shard_map/ppermute | solution.py:31
  37.5 9.2 %collective-permute-start.2 = (f32[2,2,2,128,128]{4,3,2,1,0:T(8,128)S(1)}, f32[2,2,2,128,128]{4,3,2,1,0:T(8,128)S(1)}, u32[]{:S(2)}, u32[]{:S(2)}) collective-permute-start(f32[2,2,2,128,128]{4,3,2,1,0:T(8,128)S(1)} %dynamic-slice_bitcast_fusion.1), channel_id=1, source_target_pairs={{0,2},{1,3},{2,0},{3,1},{4,6},{5,7},{6,4},{7,5},{8,10},{9,11},{10,... | collective-permute-start | bytes 1572872 | tf_op jit(solution)/shard_map/ppermute | solution.py:31
  44.4 18.4 %copy-start.2 = (bf16[128,256]{1,0:T(8,128)(2,1)S(1)}, bf16[128,256]{1,0:T(8,128)(2,1)}, u32[]{:S(2)}) copy-start(bf16[128,256]{1,0:T(8,128)(2,1)} %param.12) | copy-start | bytes 196612
  44.4 3.8 %collective-permute-start.9 = (f32[2,128,128]{1,2,0:T(8,128)S(1)}, f32[2,128,128]{1,2,0:T(8,128)S(1)}, u32[]{:S(2)}, u32[]{:S(2)}) collective-permute-start(f32[2,128,128]{1,2,0:T(8,128)S(1)} %bitcast.105), channel_id=1, source_target_pairs={{0,16},{16,0},{1,17},{17,1},{2,18},{18,2},{3,19},{19,3},{4,20},{20... | collective-permute-start | bytes 393224 | tf_op jit(solution)/shard_map/ppermute | solution.py:36
  46.8 6.4 %collective-permute-start.3 = (f32[2,2,128,128]{3,2,1,0:T(8,128)S(1)}, f32[2,2,128,128]{3,2,1,0:T(8,128)S(1)}, u32[]{:S(2)}, u32[]{:S(2)}) collective-permute-start(f32[2,2,128,128]{3,2,1,0:T(8,128)S(1)} %dynamic-slice_bitcast_fusion.2), channel_id=1, source_target_pairs={{0,4},{1,5},{2,6},{3,7},{4,0},{5,1},{6,2},{7,3},{8,12},{9,13},{10,... | collective-permute-start | bytes 786440 | tf_op jit(solution)/shard_map/ppermute | solution.py:31
  53.3 9.5 %collective-permute-start.4 = (f32[2,128,128]{2,1,0:T(8,128)S(1)}, f32[2,128,128]{2,1,0:T(8,128)S(1)}, u32[]{:S(2)}, u32[]{:S(2)}) collective-permute-start(f32[2,128,128]{2,1,0:T(8,128)S(1)} %dynamic-slice_bitcast_fusion.3), channel_id=1, source_target_pairs={{0,8},{1,9},{2,10},{3,11},{4,12},{5,13},{6,14},{7,15},{8,0},{9,1},... | collective-permute-start | bytes 393224 | tf_op jit(solution)/shard_map/ppermute | solution.py:31

commit v4 on v3

v4 whole, which is shorter than its diff:
```python
import jax
import jax.numpy as jnp
from jax import lax
from jax.experimental import pallas as pl
from jax.experimental.pallas import tpu as pltpu
from jax.sharding import PartitionSpec as P


def _nbits(n):
    bits = n.bit_length() - 1
    return bits if (1 << bits) == n else None


def _orders(nb):
    if nb == 4:
        return ((0, 1, 2, 3), (2, 0, 1, 3)), ((3, 0, 1, 2), (3, 2, 0, 1))
    rs = tuple(range(nb))
    return (rs, rs), (rs[::-1], rs[::-1])


def _pick(parity, pair, t):
    return jnp.where(parity == 0, pair[0][t], pair[1][t])


def _swap_col(x, row_size, col_size, bits):
    perm = []
    for r in range(row_size):
        b = bits[r % 2]
        for c in range(col_size):
            perm.append((r * col_size + c, r * col_size + (c ^ (1 << b))))
    return lax.ppermute(x, ("row", "col"), perm)


def _swap_row(x, row_size, bit):
    perm = [(i, i ^ (1 << bit)) for i in range(row_size)]
    return lax.ppermute(x, "row", perm)


def gather_blocks(x, steps, xchg):
    have = x[None]
    for t in range(steps):
        have = jnp.concatenate([have, xchg(have, t)], axis=0)
    return have


def scatter_blocks(data, steps, xchg):
    for t in range(steps):
        data = data[1] + xchg(data[0], t)
    return data


def gather_pos(g, me, bits):
    pos = jnp.zeros_like(g)
    for t, b in enumerate(bits):
        pos = pos + ((((g ^ me) >> b) & 1) << t)
    return pos


def scatter_pos(g, me, bits):
    nb = len(bits)
    pos = jnp.zeros_like(g)
    for t, b in enumerate(bits):
        pos = pos + ((1 - (((g ^ me) >> b) & 1)) << (nb - 1 - t))
    return pos


def _chunk(slots):
    return 32 if slots % 32 == 0 else slots


def along_call(idx, cnt, values, group, nrb):
    slots, side, _ = values.shape
    width = group.shape[-1]
    k = _chunk(slots)

    def kernel(idx_ref, cnt_ref, vals_ref, grp_ref, out_ref):
        i = pl.program_id(0)
        n = cnt_ref[0]

        @pl.when(i == 0)
        def _():
            out_ref[...] = jnp.zeros(out_ref.shape, out_ref.dtype)

        @pl.when(i * k < n)
        def _():
            for t in range(k):
                s = i * k + t
                tile = jnp.where(s < n, vals_ref[t], jnp.zeros((side, side), vals_ref.dtype))
                r = idx_ref[s]
                c = idx_ref[slots + s]
                out_ref[r] += jnp.dot(tile, grp_ref[c], preferred_element_type=jnp.float32)

    def vals_map(i, idx_ref, cnt_ref):
        last = jnp.maximum(cnt_ref[0] - 1, 0) // k
        return (jnp.minimum(i, last), 0, 0)

    spec = pltpu.PrefetchScalarGridSpec(
        num_scalar_prefetch=2,
        grid=(slots // k,),
        in_specs=[
            pl.BlockSpec((k, side, side), vals_map),
            pl.BlockSpec(group.shape, lambda i, *_: (0, 0, 0)),
        ],
        out_specs=pl.BlockSpec((nrb, side, width), lambda i, *_: (0, 0, 0)),
    )
    return pl.pallas_call(
        kernel,
        grid_spec=spec,
        out_shape=jax.ShapeDtypeStruct((nrb, side, width), jnp.float32),
    )(idx, cnt, values, group)


def against_call(idx, cnt, values, stripe_t, ncb):
    slots, side, _ = values.shape
    width = stripe_t.shape[1]
    k = _chunk(slots)

    def kernel(idx_ref, cnt_ref, vals_ref, st_ref, out_ref):
        i = pl.program_id(0)
        n = cnt_ref[0]

        @pl.when(i == 0)
        def _():
            out_ref[...] = jnp.zeros(out_ref.shape, out_ref.dtype)

        @pl.when(i * k < n)
        def _():
            for t in range(k):
                s = i * k + t
                tile = jnp.where(s < n, vals_ref[t], jnp.zeros((side, side), vals_ref.dtype))
                r = idx_ref[2 * slots + s]
                c = idx_ref[3 * slots + s]
                out_ref[c] += jnp.dot(st_ref[r], tile, preferred_element_type=jnp.float32)

    def vals_map(i, idx_ref, cnt_ref):
        last = jnp.maximum(cnt_ref[0] - 1, 0) // k
        return (jnp.minimum(i, last), 0, 0)

    spec = pltpu.PrefetchScalarGridSpec(
        num_scalar_prefetch=2,
        grid=(slots // k,),
        in_specs=[
            pl.BlockSpec((k, side, side), vals_map),
            pl.BlockSpec(stripe_t.shape, lambda i, *_: (0, 0, 0)),
        ],
        out_specs=pl.BlockSpec((ncb, width, side), lambda i, *_: (0, 0, 0)),
    )
    return pl.pallas_call(
        kernel,
        grid_spec=spec,
        out_shape=jax.ShapeDtypeStruct((ncb, width, side), jnp.float32),
    )(idx, cnt, values, stripe_t)


def local(features, tile_vals, tile_rows, tile_cols, tile_count, w_fwd, w_bwd):
    row_size = lax.axis_size("row")
    col_size = lax.axis_size("col")
    values = tile_vals[0, 0]
    slots = values.shape[0]
    side = values.shape[1]
    nodes_here = features.shape[0]
    nbc = nodes_here // side
    width = features.shape[1]
    nrb = col_size * nbc
    ncb = row_size * nbc
    me_r = lax.axis_index("row")
    me_c = lax.axis_index("col")
    parity = me_r % 2

    rowblk = jnp.clip(tile_rows[0, 0], 0, nrb - 1)
    colblk = jnp.clip(tile_cols[0, 0], 0, ncb - 1)
    cnt = jnp.clip(tile_count[0, 0], 0, slots).reshape(1).astype(jnp.int32)

    nb_c = _nbits(col_size)
    nb_r = _nbits(row_size)
    assert nb_c is not None and nb_r is not None
    rs_order, ag_order = _orders(nb_c)
    row_bits = tuple(range(nb_r))

    dest = rowblk // nbc
    sub = rowblk % nbc
    src = colblk // nbc
    csub = colblk % nbc
    rs_bits = [_pick(parity, rs_order, t) for t in range(nb_c)]
    ag_bits = [_pick(parity, ag_order, t) for t in range(nb_c)]
    rows_fwd = scatter_pos(dest, me_c, rs_bits) * nbc + sub
    rows_bwd = gather_pos(dest, me_c, ag_bits) * nbc + sub
    cols_fwd = gather_pos(src, me_r, row_bits) * nbc + csub
    cols_bwd = scatter_pos(src, me_r, row_bits) * nbc + csub
    idx = jnp.stack([rows_fwd, cols_fwd, rows_bwd, cols_bwd]).reshape(-1)

    def col_x(order):
        return lambda x, t: _swap_col(x, row_size, col_size, (order[0][t], order[1][t]))

    def row_x(x, t):
        return _swap_row(x, row_size, row_bits[t])

    group = gather_blocks(features, nb_r, row_x).reshape(ncb, side, width)
    fwd_parts = along_call(idx, cnt, values, group, nrb)

    mine_t = jnp.transpose(features.reshape(nbc, side, width), (0, 2, 1))
    stripe_t = gather_blocks(mine_t, nb_c, col_x(ag_order)).reshape(nrb, width, side)
    along = scatter_blocks(fwd_parts.reshape((2,) * nb_c + (nbc, side, width)), nb_c, col_x(rs_order))

    bwd_t = against_call(idx, cnt, values, stripe_t, ncb)
    against_t = scatter_blocks(bwd_t.reshape((2,) * nb_r + (nbc, width, side)), nb_r, row_x)
    against = jnp.transpose(against_t, (0, 2, 1))

    along = along.reshape(-1, width)
    against = against.reshape(-1, width)
    result = jnp.dot(along, w_fwd.astype(jnp.float32), precision=lax.Precision.HIGHEST)
    result = result + jnp.dot(against, w_bwd.astype(jnp.float32), precision=lax.Precision.HIGHEST)
    return result.astype(jnp.bfloat16)


def solution(mesh):
    in_specs = (
        P(("row", "col"), None),
        P("row", "col", None, None, None),
        P("row", "col", None),
        P("row", "col", None),
        P("row", "col"),
        P(),
        P(),
    )
    out_specs = P(("row", "col"), None)
    return jax.shard_map(local, mesh=mesh, in_specs=in_specs, out_specs=out_specs, check_vma=False)
```

time: 62.8 us -> 74.7 us (1.19); the launches traced: 63.7 us -> 74.4 us
  starting transfers between devices: 17.4 us -> 24.7 us
  waiting for transfers between devices: 23.6 us -> 30.7 us
  other arithmetic: 9.73 us -> 4.46 us
  Pallas kernels: 7.53 us -> 8.44 us
    ppermute x8, waiting for transfers between devices: 23.6 us -> 30.7 us  [_swap_col(): return lax.ppermute(x, ('row', 'col'), perm)]
    ppermute x2, starting transfers between devices: 1.7 us -> 7.76 us  [_swap_row(): return lax.ppermute(x, 'row', perm)]
    another operation x9 -> x0, other arithmetic: 4.64 us -> none  [the longest x7 3.13 us: gather_col(): have = jnp.stack([lo, hi], axis=0).reshape((-1,) + have.shape[1:])]
    slice x0 -> x2, local copies, waits for them, and re-layouts: none -> 2.69 us  [scatter_blocks(): data = data[1] + xchg(data[0], t)]
    concatenate x0 -> x4, other arithmetic: none -> 1.6 us  [gather_blocks(): have = jnp.concatenate([have, xchg(have, t)], axis=0)]
    squeeze x4 -> x3, local copies, waits for them, and re-layouts: 1.38 us -> 0.07 us  [scatter_blocks(): data = data[1] + xchg(data[0], t)]
    ppermute x8, starting transfers between devices: 15.7 us -> 17 us  [_swap_col(): return lax.ppermute(x, ('row', 'col'), perm)]
    min x1 -> x0, other arithmetic: 1.25 us -> none  [local(): colblk = jnp.clip(tile_cols[0, 0], 0, ncb - 1)]
  transfers between devices with their start and end apart: 10 -> 10, of which waited for: 6 -> 6; matrix products, arithmetic and copies ran while one was open for 21% -> 6% of each run, Pallas kernels for 12% -> 5%
where the time goes in v4:
time: 74.7 us; the launch traced here: 74.4 us
  waiting for transfers between devices  30.7 us (41%)
  starting transfers between devices  24.7 us (33%)
  Pallas kernels  8.44 us (11%)
  other arithmetic  4.46 us (6%)
  local copies, waits for them, and re-layouts  4.11 us (6%)
  matrix products  1.16 us (2%)
  between operations  0.81 us (1%)
    ppermute x8, waiting for transfers between devices, _swap_col(): return lax.ppermute(x, ('row', 'col'), perm)  30.7 us
    ppermute x8, starting transfers between devices, _swap_col(): return lax.ppermute(x, ('row', 'col'), perm)  17 us
    ppermute x2, starting transfers between devices, _swap_row(): return lax.ppermute(x, 'row', perm)  7.76 us
    pallas_call x1, Pallas kernels, along_call(): pl.pallas_call(kernel, grid_spec=spec, out_shape=jax.ShapeDtypeStruct((nr...  4.44 us
    pallas_call x1, Pallas kernels, against_call(): pl.pallas_call(kernel, grid_spec=spec, out_shape=jax.ShapeDtypeStruct((nc...  4 us
    slice x2, local copies, waits for them, and re-layouts, scatter_blocks(): data = data[1] + xchg(data[0], t)  2.69 us
    concatenate x4, other arithmetic, gather_blocks(): have = jnp.concatenate([have, xchg(have, t)], axis=0)  1.6 us
  transfers between devices with their start and end apart: 10, of which 6 were waited for; matrix products, arithmetic and copies ran while one was open for 6% of the time, Pallas kernels for 5%

profile of v4, /device:TPU:0, one launch (start us, length us, event | category | flops | bytes accessed | tf_op | source)
XLA Modules:
  0.0 74.4 jit_solution(1382315287070464813)
XLA Ops:
  0.0 0.5 collective-permute-start
  0.5 0.7 multiply_add_fusion.2
  1.8 0.7 multiply_add_fusion.3
  2.5 0.7 multiply_add_fusion
  3.1 0.6 add_bitcast_fusion.idx_ref
  3.7 1.5 %pad_maximum_fusion.2 = bf16[2,256,128]{2,1,0:T(8,128)(2,1)} fusion(bf16[1,256,128]{2,1,0:T(8,128)(2,1)S(1)} %collective-permute-done, bf16[1,256,128]{2,1,0:T(8,128)(2,1)} %bitcast.88), kind=kLoop, calls=%fused_computation.15 | loop fusion | flops 65536 | bytes 262144 | tf_op jit(solution)/shard_map/concatenate | solution.py:42
  5.2 4.4 %shard_map.73 = f32[32,128,128]{2,1,0:T(8,128)} custom-call(s32[512]{0:T(512)} %add_bitcast_fusion.idx_ref, s32[1]{0:T(128)} %bitcast.3.cnt_ref, bf16[128,128,128]{2,1,0:T(8,128)(2,1)} %bitcast.75, bf16[4,128,128]{2,1,0:T(8,128)(2,1)} %bitcast.85), custom_call_target="tpu_custom_call" | custom-call | tf_op jit(solution)/shard_map/pallas_call | solution.py:106
  9.7 1.7 %fusion.7 = (f32[16,128,128]{2,1,0:T(8,128)S(1)}, f32[16,128,128]{2,1,0:T(8,128)S(1)}) fusion(f32[32,128,128]{2,1,0:T(8,128)} %shard_map.73), kind=kLoop, calls=%fused_computation.46 | loop fusion | bytes 4194304 | tf_op jit(solution)/shard_map/slice | solution.py:48
  11.4 2.1 %collective-permute-start.1 = (f32[2,2,2,2,128,128]{5,4,3,2,1,0:T(8,128)S(1)}, f32[2,2,2,2,128,128]{5,4,3,2,1,0:T(8,128)S(1)}, u32[]{:S(2)}, u32[]{:S(2)}) collective-permute-start(f32[2,2,2,2,128,128]{5,4,3,2,1,0:T(8,128)S(1)} %bitcast.83), channel_id=1, source_target_pairs={{0,1},{1,0},{2,3},{3,2},{4,5},{5,4},{6,7},{7,6},{8,9},{9,8},{10,11... | collective-permute-start | bytes 3145736 | tf_op jit(solution)/shard_map/ppermute | solution.py:31
  13.5 0.1 copy.9
  13.6 2.7 %collective-permute-start.5 = (bf16[1,2,128,128]{3,2,1,0:T(8,128)(2,1)S(1)}, bf16[1,2,128,128]{3,2,1,0:T(8,128)(2,1)S(1)}, u32[]{:S(2)}, u32[]{:S(2)}) collective-permute-start(bf16[1,2,128,128]{3,2,1,0:T(8,128)(2,1)S(1)} %bitcast.78), channel_id=1, source_target_pairs={{0,8},{1,9},{2,10},{3,11},{4,12},{5,13},{6,14},{7,15},{8,0},{9,1},... | collective-permute-start | bytes 196616 | tf_op jit(solution)/shard_map/ppermute | solution.py:31
  16.3 2.7 %collective-permute-done.5 = bf16[1,2,128,128]{3,2,1,0:T(8,128)(2,1)S(1)} collective-permute-done((bf16[1,2,128,128]{3,2,1,0:T(8,128)(2,1)S(1)}, bf16[1,2,128,128]{3,2,1,0:T(8,128)(2,1)S(1)}, u32[]{:S(2)}, u32[]{:S(2)}) %collective-permute-start.5) | collective-permute-done | bytes 65568 | tf_op jit(solution)/shard_map/ppermute | solution.py:31
  19.0 0.4 collective-permute-start.6
  19.4 8.3 %collective-permute-done.6 = bf16[2,2,128,128]{3,2,1,0:T(8,128)(2,1)S(1)} collective-permute-done((bf16[2,2,128,128]{3,2,1,0:T(8,128)(2,1)S(1)}, bf16[2,2,128,128]{3,2,1,0:T(8,128)(2,1)S(1)}, u32[]{:S(2)}, u32[]{:S(2)}) %collective-permute-start.6) | collective-permute-done | bytes 131104 | tf_op jit(solution)/shard_map/ppermute | solution.py:31
  27.7 2.6 %collective-permute-start.7 = (bf16[4,2,128,128]{3,2,1,0:T(8,128)(2,1)S(1)}, bf16[4,2,128,128]{3,2,1,0:T(8,128)(2,1)S(1)}, u32[]{:S(2)}, u32[]{:S(2)}) collective-permute-start(bf16[4,2,128,128]{3,2,1,0:T(8,128)(2,1)S(1)} %pad_maximum_fusion.1), channel_id=1, source_target_pairs={{0,2},{1,3},{2,0},{3,1},{4,6},{5,7},{6,4},{7,5},{8,10},{9,11},{10,... | collective-permute-start | bytes 786440 | tf_op jit(solution)/shard_map/ppermute | solution.py:31
  30.3 4.4 %collective-permute-done.7 = bf16[4,2,128,128]{3,2,1,0:T(8,128)(2,1)S(1)} collective-permute-done((bf16[4,2,128,128]{3,2,1,0:T(8,128)(2,1)S(1)}, bf16[4,2,128,128]{3,2,1,0:T(8,128)(2,1)S(1)}, u32[]{:S(2)}, u32[]{:S(2)}) %collective-permute-start.7) | collective-permute-done | bytes 262176 | tf_op jit(solution)/shard_map/ppermute | solution.py:31
  34.7 2.1 %collective-permute-start.8 = (bf16[8,2,128,128]{3,2,1,0:T(8,128)(2,1)S(1)}, bf16[8,2,128,128]{3,2,1,0:T(8,128)(2,1)S(1)}, u32[]{:S(2)}, u32[]{:S(2)}) collective-permute-start(bf16[8,2,128,128]{3,2,1,0:T(8,128)(2,1)S(1)} %pad_maximum_fusion), channel_id=1, source_target_pairs={{0,4},{1,5},{2,6},{3,7},{4,0},{5,1},{6,2},{7,3},{8,12},{9,13},{10,... | collective-permute-start | bytes 1572872 | tf_op jit(solution)/shard_map/ppermute | solution.py:31
  36.9 0.1 add.191
  37.0 1.1 %collective-permute-start.2 = (f32[2,2,2,128,128]{4,3,2,1,0:T(8,128)S(1)}, f32[2,2,2,128,128]{4,3,2,1,0:T(8,128)S(1)}, u32[]{:S(2)}, u32[]{:S(2)}) collective-permute-start(f32[2,2,2,128,128]{4,3,2,1,0:T(8,128)S(1)} %slice_bitcast_fusion), channel_id=1, source_target_pairs={{0,2},{1,3},{2,0},{3,1},{4,6},{5,7},{6,4},{7,5},{8,10},{9,11},{10,... | collective-permute-start | bytes 1572872 | tf_op jit(solution)/shard_map/ppermute | solution.py:31
  38.2 5.8 %collective-permute-done.8 = bf16[8,2,128,128]{3,2,1,0:T(8,128)(2,1)S(1)} collective-permute-done((bf16[8,2,128,128]{3,2,1,0:T(8,128)(2,1)S(1)}, bf16[8,2,128,128]{3,2,1,0:T(8,128)(2,1)S(1)}, u32[]{:S(2)}, u32[]{:S(2)}) %collective-permute-start.8) | collective-permute-done | bytes 524320 | tf_op jit(solution)/shard_map/ppermute | solution.py:31
  44.0 0.1 constant_dynamic-update-slice_fusion
  44.1 1.0 %copy-done.1 = bf16[16,2,128,128]{3,2,1,0:T(8,128)(2,1)} copy-done((bf16[16,2,128,128]{3,2,1,0:T(8,128)(2,1)}, bf16[16,2,128,128]{3,2,1,0:T(8,128)(2,1)S(1)}, u32[]{:S(2)}) %copy-start.1) | copy-done | bytes 1048600
  45.1 4.0 %shard_map.74 = f32[4,128,128]{2,1,0:T(8,128)} custom-call(s32[512]{0:T(512)} %add_bitcast_fusion.idx_ref, s32[1]{0:T(128)} %bitcast.3.cnt_ref, bf16[128,128,128]{2,1,0:T(8,128)(2,1)} %bitcast.76, bf16[32,128,128]{2,1,0:T(8,128)(2,1)} %bitcast.82), custom_call_target="tpu_custom_call" | custom-call | tf_op jit(solution)/shard_map/pallas_call | solution.py:148
  49.1 1.0 %slice.53 = f32[2,128,128]{2,1,0:T(8,128)S(1)} slice(f32[4,128,128]{2,1,0:T(8,128)} %shard_map.74), slice={[0:2], [0:128], [0:128]} | slice | bytes 262144 | tf_op jit(solution)/shard_map/slice | solution.py:48
  50.1 7.3 %collective-permute-start.9 = (f32[2,128,128]{2,1,0:T(8,128)S(1)}, f32[2,128,128]{2,1,0:T(8,128)S(1)}, u32[]{:S(2)}, u32[]{:S(2)}) collective-permute-start(f32[2,128,128]{2,1,0:T(8,128)S(1)} %slice.53), channel_id=1, source_target_pairs={{0,16},{16,0},{1,17},{17,1},{2,18},{18,2},{3,19},{19,3},{4,20},{20... | collective-permute-start | bytes 393224 | tf_op jit(solution)/shard_map/ppermute | solution.py:36
  57.5 2.3 %collective-permute-start.3 = (f32[2,2,128,128]{3,2,1,0:T(8,128)S(1)}, f32[2,2,128,128]{3,2,1,0:T(8,128)S(1)}, u32[]{:S(2)}, u32[]{:S(2)}) collective-permute-start(f32[2,2,128,128]{3,2,1,0:T(8,128)S(1)} %slice_bitcast_fusion.2), channel_id=1, source_target_pairs={{0,4},{1,5},{2,6},{3,7},{4,0},{5,1},{6,2},{7,3},{8,12},{9,13},{10,... | collective-permute-start | bytes 786440 | tf_op jit(solution)/shard_map/ppermute | solution.py:31
  59.8 0.1 copy.10
  59.9 4.2 %collective-permute-done.3 = f32[2,2,128,128]{3,2,1,0:T(8,128)S(1)} collective-permute-done((f32[2,2,128,128]{3,2,1,0:T(8,128)S(1)}, f32[2,2,128,128]{3,2,1,0:T(8,128)S(1)}, u32[]{:S(2)}, u32[]{:S(2)}) %collective-permute-start.3) | collective-permute-done | bytes 262176 | tf_op jit(solution)/shard_map/ppermute | solution.py:31
  64.1 3.6 %collective-permute-start.4 = (f32[2,128,128]{2,1,0:T(8,128)S(1)}, f32[2,128,128]{2,1,0:T(8,128)S(1)}, u32[]{:S(2)}, u32[]{:S(2)}) collective-permute-start(f32[2,128,128]{2,1,0:T(8,128)S(1)} %slice_bitcast_fusion.4), channel_id=1, source_target_pairs={{0,8},{1,9},{2,10},{3,11},{4,12},{5,13},{6,14},{7,15},{8,0},{9,1},... | collective-permute-start | bytes 393224 | tf_op jit(solution)/shard_map/ppermute | solution.py:31
  67.8 0.2 fusion.8
  68.0 5.4 %collective-permute-done.4 = f32[2,128,128]{2,1,0:T(8,128)S(1)} collective-permute-done((f32[2,128,128]{2,1,0:T(8,128)S(1)}, f32[2,128,128]{2,1,0:T(8,128)S(1)}, u32[]{:S(2)}, u32[]{:S(2)}) %collective-permute-start.4) | collective-permute-done | bytes 131104 | tf_op jit(solution)/shard_map/ppermute | solution.py:31
  73.5 0.9 %fusion = bf16[256,256]{1,0:T(8,128)(2,1)} fusion(f32[256,256]{1,0:T(8,128)S(1)} %fusion.8, f32[256,128]{1,0:T(8,128)S(1)} %bitcast.86, bf16[128,256]{1,0:T(8,128)(2,1)S(1)} %copy-done.4), kind=kOutput, calls=%fused_computation.1 | convolution fusion | flops 100794368 | bytes 589824 | tf_op jit(solution)/shard_map/dot_general | solution.py:211
  (27 shorter events, 0.4 us)
Async XLA Ops:
  0.0 67.8 %copy-start = (bf16[128,256]{1,0:T(8,128)(2,1)S(1)}, bf16[128,256]{1,0:T(8,128)(2,1)}, u32[]{:S(2)}) copy-start(bf16[128,256]{1,0:T(8,128)(2,1)} %param.13) | copy-start | bytes 196612
  0.0 3.7 %collective-permute-start = (bf16[1,256,128]{2,1,0:T(8,128)(2,1)}, bf16[1,256,128]{2,1,0:T(8,128)(2,1)S(1)}, u32[]{:S(2)}, u32[]{:S(2)}) collective-permute-start(bf16[1,256,128]{2,1,0:T(8,128)(2,1)} %bitcast.87), channel_id=1, source_target_pairs={{0,16},{16,0},{1,17},{17,1},{2,18},{18,2},{3,19},{19,3},{4,20},{20... | collective-permute-start | bytes 196616 | tf_op jit(solution)/shard_map/ppermute | solution.py:36
  9.7 3.8 %copy-start.3 = (bf16[256,128]{1,0:T(8,128)(2,1)S(1)}, bf16[256,128]{1,0:T(8,128)(2,1)}, u32[]{:S(2)}) copy-start(bf16[256,128]{1,0:T(8,128)(2,1)} %param.7) | copy-start | bytes 196612
  11.4 25.5 %collective-permute-start.1 = (f32[2,2,2,2,128,128]{5,4,3,2,1,0:T(8,128)S(1)}, f32[2,2,2,2,128,128]{5,4,3,2,1,0:T(8,128)S(1)}, u32[]{:S(2)}, u32[]{:S(2)}) collective-permute-start(f32[2,2,2,2,128,128]{5,4,3,2,1,0:T(8,128)S(1)} %bitcast.83), channel_id=1, source_target_pairs={{0,1},{1,0},{2,3},{3,2},{4,5},{5,4},{6,7},{7,6},{8,9},{9,8},{10,11... | collective-permute-start | bytes 3145736 | tf_op jit(solution)/shard_map/ppermute | solution.py:31
  13.6 5.3 %collective-permute-start.5 = (bf16[1,2,128,128]{3,2,1,0:T(8,128)(2,1)S(1)}, bf16[1,2,128,128]{3,2,1,0:T(8,128)(2,1)S(1)}, u32[]{:S(2)}, u32[]{:S(2)}) collective-permute-start(bf16[1,2,128,128]{3,2,1,0:T(8,128)(2,1)S(1)} %bitcast.78), channel_id=1, source_target_pairs={{0,8},{1,9},{2,10},{3,11},{4,12},{5,13},{6,14},{7,15},{8,0},{9,1},... | collective-permute-start | bytes 196616 | tf_op jit(solution)/shard_map/ppermute | solution.py:31
  19.0 8.7 %collective-permute-start.6 = (bf16[2,2,128,128]{3,2,1,0:T(8,128)(2,1)S(1)}, bf16[2,2,128,128]{3,2,1,0:T(8,128)(2,1)S(1)}, u32[]{:S(2)}, u32[]{:S(2)}) collective-permute-start(bf16[2,2,128,128]{3,2,1,0:T(8,128)(2,1)S(1)} %pad_maximum_fusion.3), channel_id=1, source_target_pairs={{0,1},{1,0},{2,3},{3,2},{4,5},{5,4},{6,7},{7,6},{8,9},{9,8},{10,11... | collective-permute-start | bytes 393224 | tf_op jit(solution)/shard_map/ppermute | solution.py:31
  27.7 6.9 %collective-permute-start.7 = (bf16[4,2,128,128]{3,2,1,0:T(8,128)(2,1)S(1)}, bf16[4,2,128,128]{3,2,1,0:T(8,128)(2,1)S(1)}, u32[]{:S(2)}, u32[]{:S(2)}) collective-permute-start(bf16[4,2,128,128]{3,2,1,0:T(8,128)(2,1)S(1)} %pad_maximum_fusion.1), channel_id=1, source_target_pairs={{0,2},{1,3},{2,0},{3,1},{4,6},{5,7},{6,4},{7,5},{8,10},{9,11},{10,... | collective-permute-start | bytes 786440 | tf_op jit(solution)/shard_map/ppermute | solution.py:31
  34.7 9.3 %collective-permute-start.8 = (bf16[8,2,128,128]{3,2,1,0:T(8,128)(2,1)S(1)}, bf16[8,2,128,128]{3,2,1,0:T(8,128)(2,1)S(1)}, u32[]{:S(2)}, u32[]{:S(2)}) collective-permute-start(bf16[8,2,128,128]{3,2,1,0:T(8,128)(2,1)S(1)} %pad_maximum_fusion), channel_id=1, source_target_pairs={{0,4},{1,5},{2,6},{3,7},{4,0},{5,1},{6,2},{7,3},{8,12},{9,13},{10,... | collective-permute-start | bytes 1572872 | tf_op jit(solution)/shard_map/ppermute | solution.py:31
  37.0 20.4 %collective-permute-start.2 = (f32[2,2,2,128,128]{4,3,2,1,0:T(8,128)S(1)}, f32[2,2,2,128,128]{4,3,2,1,0:T(8,128)S(1)}, u32[]{:S(2)}, u32[]{:S(2)}) collective-permute-start(f32[2,2,2,128,128]{4,3,2,1,0:T(8,128)S(1)} %slice_bitcast_fusion), channel_id=1, source_target_pairs={{0,2},{1,3},{2,0},{3,1},{4,6},{5,7},{6,4},{7,5},{8,10},{9,11},{10,... | collective-permute-start | bytes 1572872 | tf_op jit(solution)/shard_map/ppermute | solution.py:31
  44.1 1.0 %copy-start.1 = (bf16[16,2,128,128]{3,2,1,0:T(8,128)(2,1)}, bf16[16,2,128,128]{3,2,1,0:T(8,128)(2,1)S(1)}, u32[]{:S(2)}) copy-start(bf16[16,2,128,128]{3,2,1,0:T(8,128)(2,1)S(1)} %constant_dynamic-update-slice_fusion) | copy-start | bytes 3145732
  49.1 10.7 %copy-start.2 = (f32[4,128,128]{2,1,0:T(8,128)S(1)}, f32[4,128,128]{2,1,0:T(8,128)}, u32[]{:S(2)}) copy-start(f32[4,128,128]{2,1,0:T(8,128)} %shard_map.74) | copy-start | bytes 786436
  50.1 23.4 %copy-start.4 = (bf16[128,256]{1,0:T(8,128)(2,1)S(1)}, bf16[128,256]{1,0:T(8,128)(2,1)}, u32[]{:S(2)}) copy-start(bf16[128,256]{1,0:T(8,128)(2,1)} %param.12) | copy-start | bytes 196612
  50.1 9.7 %collective-permute-start.9 = (f32[2,128,128]{2,1,0:T(8,128)S(1)}, f32[2,128,128]{2,1,0:T(8,128)S(1)}, u32[]{:S(2)}, u32[]{:S(2)}) collective-permute-start(f32[2,128,128]{2,1,0:T(8,128)S(1)} %slice.53), channel_id=1, source_target_pairs={{0,16},{16,0},{1,17},{17,1},{2,18},{18,2},{3,19},{19,3},{4,20},{20... | collective-permute-start | bytes 393224 | tf_op jit(solution)/shard_map/ppermute | solution.py:36
  57.5 6.6 %collective-permute-start.3 = (f32[2,2,128,128]{3,2,1,0:T(8,128)S(1)}, f32[2,2,128,128]{3,2,1,0:T(8,128)S(1)}, u32[]{:S(2)}, u32[]{:S(2)}) collective-permute-start(f32[2,2,128,128]{3,2,1,0:T(8,128)S(1)} %slice_bitcast_fusion.2), channel_id=1, source_target_pairs={{0,4},{1,5},{2,6},{3,7},{4,0},{5,1},{6,2},{7,3},{8,12},{9,13},{10,... | collective-permute-start | bytes 786440 | tf_op jit(solution)/shard_map/ppermute | solution.py:31
  64.1 9.3 %collective-permute-start.4 = (f32[2,128,128]{2,1,0:T(8,128)S(1)}, f32[2,128,128]{2,1,0:T(8,128)S(1)}, u32[]{:S(2)}, u32[]{:S(2)}) collective-permute-start(f32[2,128,128]{2,1,0:T(8,128)S(1)} %slice_bitcast_fusion.4), channel_id=1, source_target_pairs={{0,8},{1,9},{2,10},{3,11},{4,12},{5,13},{6,14},{7,15},{8,0},{9,1},... | collective-permute-start | bytes 393224 | tf_op jit(solution)/shard_map/ppermute | solution.py:31

commit v5 on v4

--- a/solution.py
+++ b/solution.py
@@ -38,9 +38,11 @@
 
 def gather_blocks(x, steps, xchg):
     have = x[None]
+    firsts = []
     for t in range(steps):
         have = jnp.concatenate([have, xchg(have, t)], axis=0)
-    return have
+        firsts.append(have)
+    return have, firsts
 
 
 def scatter_blocks(data, steps, xchg):
@@ -68,12 +70,12 @@
     return 32 if slots % 32 == 0 else slots
 
 
-def along_call(idx, cnt, values, group, nrb):
+def along_call(idx, cnt, values, group, nrb, dep):
     slots, side, _ = values.shape
     width = group.shape[-1]
     k = _chunk(slots)
 
-    def kernel(idx_ref, cnt_ref, vals_ref, grp_ref, out_ref):
+    def kernel(idx_ref, cnt_ref, vals_ref, grp_ref, dep_ref, out_ref):
         i = pl.program_id(0)
         n = cnt_ref[0]
 
@@ -100,6 +102,7 @@
         in_specs=[
             pl.BlockSpec((k, side, side), vals_map),
             pl.BlockSpec(group.shape, lambda i, *_: (0, 0, 0)),
+            pl.BlockSpec(memory_space=pl.ANY),
         ],
         out_specs=pl.BlockSpec((nrb, side, width), lambda i, *_: (0, 0, 0)),
     )
@@ -107,7 +110,7 @@
         kernel,
         grid_spec=spec,
         out_shape=jax.ShapeDtypeStruct((nrb, side, width), jnp.float32),
-    )(idx, cnt, values, group)
+    )(idx, cnt, values, group, dep)
 
 
 def against_call(idx, cnt, values, stripe_t, ncb):
@@ -195,11 +198,11 @@
     def row_x(x, t):
         return _swap_row(x, row_size, row_bits[t])
 
-    group = gather_blocks(features, nb_r, row_x).reshape(ncb, side, width)
-    fwd_parts = along_call(idx, cnt, values, group, nrb)
-
+    group = gather_blocks(features, nb_r, row_x)[0].reshape(ncb, side, width)
     mine_t = jnp.transpose(features.reshape(nbc, side, width), (0, 2, 1))
-    stripe_t = gather_blocks(mine_t, nb_c, col_x(ag_order)).reshape(nrb, width, side)
+    stripe_t, stages = gather_blocks(mine_t, nb_c, col_x(ag_order))
+    stripe_t = stripe_t.reshape(nrb, width, side)
+    fwd_parts = along_call(idx, cnt, values, group, nrb, stages[0])
     along = scatter_blocks(fwd_parts.reshape((2,) * nb_c + (nbc, side, width)), nb_c, col_x(rs_order))
 
     bwd_t = against_call(idx, cnt, values, stripe_t, ncb)

time: 74.7 us -> 74.4 us (level); the launches traced: 74.4 us -> 73 us
  starting transfers between devices: 24.7 us -> 14.5 us
  waiting for transfers between devices: 30.7 us -> 38.1 us
  local copies, waits for them, and re-layouts: 4.11 us -> 4.97 us
    ppermute x8, waiting for transfers between devices: 30.7 us -> 37.2 us  [_swap_col(): return lax.ppermute(x, ('row', 'col'), perm)]
    ppermute x8, starting transfers between devices: 17 us -> 11.4 us  [_swap_col(): return lax.ppermute(x, ('row', 'col'), perm)]
    ppermute x2, starting transfers between devices: 7.76 us -> 3.09 us  [_swap_row(): return lax.ppermute(x, 'row', perm)]
    reshape x1, local copies, waits for them, and re-layouts: 0.12 us -> 0.98 us  [local(): mine_t = jnp.transpose(features.reshape(nbc, side, width), (0, 2, 1))]
    ppermute x2, waiting for transfers between devices: 0.01 us -> 0.82 us  [_swap_row(): return lax.ppermute(x, 'row', perm)]
  transfers between devices with their start and end apart: 10 -> 10, of which waited for: 6 -> 6; matrix products, arithmetic and copies ran while one was open for 6% -> 8% of each run, Pallas kernels for 5% -> 5%
where the time goes in v5:
time: 74.4 us; the launch traced here: 73 us
  waiting for transfers between devices  38.1 us (51%)
  starting transfers between devices  14.5 us (19%)
  Pallas kernels  8.44 us (11%)
  other arithmetic  5.11 us (7%)
  local copies, waits for them, and re-layouts  4.97 us (7%)
  matrix products  1.16 us (2%)
  between operations  0.83 us (1%)
    ppermute x8, waiting for transfers between devices, _swap_col(): return lax.ppermute(x, ('row', 'col'), perm)  37.2 us
    ppermute x8, starting transfers between devices, _swap_col(): return lax.ppermute(x, ('row', 'col'), perm)  11.4 us
    pallas_call x1, Pallas kernels, along_call(): pl.pallas_call(kernel, grid_spec=spec, out_shape=jax.ShapeDtypeStruct((nr...  4.44 us
    pallas_call x1, Pallas kernels, against_call(): pl.pallas_call(kernel, grid_spec=spec, out_shape=jax.ShapeDtypeStruct((nc...  4 us
    ppermute x2, starting transfers between devices, _swap_row(): return lax.ppermute(x, 'row', perm)  3.09 us
    slice x2, local copies, waits for them, and re-layouts, scatter_blocks(): data = data[1] + xchg(data[0], t)  2.7 us
    concatenate x4, other arithmetic, gather_blocks(): have = jnp.concatenate([have, xchg(have, t)], axis=0)  2.26 us
  transfers between devices with their start and end apart: 10, of which 6 were waited for; matrix products, arithmetic and copies ran while one was open for 8% of the time, Pallas kernels for 5%

profile of v5, /device:TPU:0, one launch (start us, length us, event | category | flops | bytes accessed | tf_op | source)
XLA Modules:
  0.0 73.0 jit_solution(9556619308408886505)
XLA Ops:
  0.0 1.0 %copy.8 = bf16[2,128,128]{1,2,0:T(8,128)(2,1)S(1)} copy(bf16[2,128,128]{2,1,0:T(8,128)(2,1)} %bitcast.87) | data formatting | bytes 131072 | tf_op jit(solution)/shard_map/reshape | solution.py:202
  1.0 4.1 %collective-permute-start.1 = (bf16[1,2,128,128]{3,2,1,0:T(8,128)(2,1)S(1)}, bf16[1,2,128,128]{3,2,1,0:T(8,128)(2,1)S(1)}, u32[]{:S(2)}, u32[]{:S(2)}) collective-permute-start(bf16[1,2,128,128]{3,2,1,0:T(8,128)(2,1)S(1)} %bitcast.78), channel_id=1, source_target_pairs={{0,8},{1,9},{2,10},{3,11},{4,12},{5,13},{6,14},{7,15},{8,0},{9,1},... | collective-permute-start | bytes 196616 | tf_op jit(solution)/shard_map/ppermute | solution.py:31
  5.7 0.7 multiply_add_fusion.2
  6.4 0.7 multiply_add_fusion.3
  7.1 0.7 multiply_add_fusion
  7.8 0.6 add_bitcast_fusion.idx_ref
  8.3 1.5 %pad_maximum_fusion.2 = bf16[2,256,128]{2,1,0:T(8,128)(2,1)} fusion(bf16[1,256,128]{2,1,0:T(8,128)(2,1)S(1)} %collective-permute-done, bf16[1,256,128]{2,1,0:T(8,128)(2,1)} %bitcast.89), kind=kLoop, calls=%fused_computation.15 | loop fusion | flops 65536 | bytes 262144 | tf_op jit(solution)/shard_map/concatenate | solution.py:43
  9.8 0.7 pad_maximum_fusion.3.dep_ref
  10.5 4.4 %shard_map.73 = f32[32,128,128]{2,1,0:T(8,128)} custom-call(s32[512]{0:T(512)} %add_bitcast_fusion.idx_ref, s32[1]{0:T(128)} %bitcast.3.cnt_ref, bf16[128,128,128]{2,1,0:T(8,128)(2,1)} %bitcast.75, bf16[4,128,128]{2,1,0:T(8,128)(2,1)} %bitcast.85, bf16[2,2,128,128]{3,2,1,0:T(8,128)(2,1)} %pad_maximum_fusion.3.dep_ref), custom_call_target="tpu_custom_call" | custom-call | tf_op jit(solution)/shard_map/pallas_call | solution.py:109
  15.0 1.7 %fusion.7 = (f32[16,128,128]{2,1,0:T(8,128)S(1)}, f32[16,128,128]{2,1,0:T(8,128)S(1)}) fusion(f32[32,128,128]{2,1,0:T(8,128)} %shard_map.73), kind=kLoop, calls=%fused_computation.46 | loop fusion | bytes 4194304 | tf_op jit(solution)/shard_map/slice | solution.py:50
  16.7 2.7 %collective-permute-start.2 = (f32[2,2,2,2,128,128]{5,4,3,2,1,0:T(8,128)S(1)}, f32[2,2,2,2,128,128]{5,4,3,2,1,0:T(8,128)S(1)}, u32[]{:S(2)}, u32[]{:S(2)}) collective-permute-start(f32[2,2,2,2,128,128]{5,4,3,2,1,0:T(8,128)S(1)} %bitcast.83), channel_id=1, source_target_pairs={{0,1},{1,0},{2,3},{3,2},{4,5},{5,4},{6,7},{7,6},{8,9},{9,8},{10,11... | collective-permute-start | bytes 3145736 | tf_op jit(solution)/shard_map/ppermute | solution.py:31
  19.4 0.1 collective-permute-start.6
  19.5 14.1 %collective-permute-done.6 = bf16[2,2,128,128]{3,2,1,0:T(8,128)(2,1)S(1)} collective-permute-done((bf16[2,2,128,128]{3,2,1,0:T(8,128)(2,1)S(1)}, bf16[2,2,128,128]{3,2,1,0:T(8,128)(2,1)S(1)}, u32[]{:S(2)}, u32[]{:S(2)}) %collective-permute-start.6) | collective-permute-done | bytes 131104 | tf_op jit(solution)/shard_map/ppermute | solution.py:31
  33.6 2.1 %collective-permute-start.7 = (bf16[4,2,128,128]{3,2,1,0:T(8,128)(2,1)S(1)}, bf16[4,2,128,128]{3,2,1,0:T(8,128)(2,1)S(1)}, u32[]{:S(2)}, u32[]{:S(2)}) collective-permute-start(bf16[4,2,128,128]{3,2,1,0:T(8,128)(2,1)S(1)} %pad_maximum_fusion.1), channel_id=1, source_target_pairs={{0,2},{1,3},{2,0},{3,1},{4,6},{5,7},{6,4},{7,5},{8,10},{9,11},{10,... | collective-permute-start | bytes 786440 | tf_op jit(solution)/shard_map/ppermute | solution.py:31
  35.8 4.4 %collective-permute-done.7 = bf16[4,2,128,128]{3,2,1,0:T(8,128)(2,1)S(1)} collective-permute-done((bf16[4,2,128,128]{3,2,1,0:T(8,128)(2,1)S(1)}, bf16[4,2,128,128]{3,2,1,0:T(8,128)(2,1)S(1)}, u32[]{:S(2)}, u32[]{:S(2)}) %collective-permute-start.7) | collective-permute-done | bytes 262176 | tf_op jit(solution)/shard_map/ppermute | solution.py:31
  40.2 0.5 collective-permute-start.8
  40.7 0.2 add.191
  40.9 1.7 %collective-permute-start.3 = (f32[2,2,2,128,128]{4,3,2,1,0:T(8,128)S(1)}, f32[2,2,2,128,128]{4,3,2,1,0:T(8,128)S(1)}, u32[]{:S(2)}, u32[]{:S(2)}) collective-permute-start(f32[2,2,2,128,128]{4,3,2,1,0:T(8,128)S(1)} %slice_bitcast_fusion), channel_id=1, source_target_pairs={{0,2},{1,3},{2,0},{3,1},{4,6},{5,7},{6,4},{7,5},{8,10},{9,11},{10,... | collective-permute-start | bytes 1572872 | tf_op jit(solution)/shard_map/ppermute | solution.py:31
  42.6 6.8 %collective-permute-done.8 = bf16[8,2,128,128]{3,2,1,0:T(8,128)(2,1)S(1)} collective-permute-done((bf16[8,2,128,128]{3,2,1,0:T(8,128)(2,1)S(1)}, bf16[8,2,128,128]{3,2,1,0:T(8,128)(2,1)S(1)}, u32[]{:S(2)}, u32[]{:S(2)}) %collective-permute-start.8) | collective-permute-done | bytes 524320 | tf_op jit(solution)/shard_map/ppermute | solution.py:31
  49.4 0.1 constant_dynamic-update-slice_fusion
  49.5 1.0 %copy-done.1 = bf16[16,2,128,128]{3,2,1,0:T(8,128)(2,1)} copy-done((bf16[16,2,128,128]{3,2,1,0:T(8,128)(2,1)}, bf16[16,2,128,128]{3,2,1,0:T(8,128)(2,1)S(1)}, u32[]{:S(2)}) %copy-start.1) | copy-done | bytes 1048600
  50.5 4.0 %shard_map.74 = f32[4,128,128]{2,1,0:T(8,128)} custom-call(s32[512]{0:T(512)} %add_bitcast_fusion.idx_ref, s32[1]{0:T(128)} %bitcast.3.cnt_ref, bf16[128,128,128]{2,1,0:T(8,128)(2,1)} %bitcast.76, bf16[32,128,128]{2,1,0:T(8,128)(2,1)} %bitcast.82), custom_call_target="tpu_custom_call" | custom-call | tf_op jit(solution)/shard_map/pallas_call | solution.py:151
  54.5 1.0 %slice.53 = f32[2,128,128]{2,1,0:T(8,128)S(1)} slice(f32[4,128,128]{2,1,0:T(8,128)} %shard_map.74), slice={[0:2], [0:128], [0:128]} | slice | bytes 262144 | tf_op jit(solution)/shard_map/slice | solution.py:50
  55.5 3.1 %collective-permute-start.9 = (f32[2,128,128]{2,1,0:T(8,128)S(1)}, f32[2,128,128]{2,1,0:T(8,128)S(1)}, u32[]{:S(2)}, u32[]{:S(2)}) collective-permute-start(f32[2,128,128]{2,1,0:T(8,128)S(1)} %slice.53), channel_id=1, source_target_pairs={{0,16},{16,0},{1,17},{17,1},{2,18},{18,2},{3,19},{19,3},{4,20},{20... | collective-permute-start | bytes 393224 | tf_op jit(solution)/shard_map/ppermute | solution.py:36
  58.7 0.1 collective-permute-start.4
  58.7 0.8 %collective-permute-done.9 = f32[2,128,128]{2,1,0:T(8,128)S(1)} collective-permute-done((f32[2,128,128]{2,1,0:T(8,128)S(1)}, f32[2,128,128]{2,1,0:T(8,128)S(1)}, u32[]{:S(2)}, u32[]{:S(2)}) %collective-permute-start.9) | collective-permute-done | bytes 131104 | tf_op jit(solution)/shard_map/ppermute | solution.py:36
  59.6 0.1 copy.9
  59.7 5.4 %collective-permute-done.4 = f32[2,2,128,128]{3,2,1,0:T(8,128)S(1)} collective-permute-done((f32[2,2,128,128]{3,2,1,0:T(8,128)S(1)}, f32[2,2,128,128]{3,2,1,0:T(8,128)S(1)}, u32[]{:S(2)}, u32[]{:S(2)}) %collective-permute-start.4) | collective-permute-done | bytes 262176 | tf_op jit(solution)/shard_map/ppermute | solution.py:31
  65.1 0.1 collective-permute-start.5
  65.2 0.2 fusion.8
  65.5 6.6 %collective-permute-done.5 = f32[2,128,128]{2,1,0:T(8,128)S(1)} collective-permute-done((f32[2,128,128]{2,1,0:T(8,128)S(1)}, f32[2,128,128]{2,1,0:T(8,128)S(1)}, u32[]{:S(2)}, u32[]{:S(2)}) %collective-permute-start.5) | collective-permute-done | bytes 131104 | tf_op jit(solution)/shard_map/ppermute | solution.py:31
  72.1 0.9 %fusion = bf16[256,256]{1,0:T(8,128)(2,1)} fusion(f32[256,256]{1,0:T(8,128)S(1)} %fusion.8, f32[256,128]{1,0:T(8,128)S(1)} %bitcast.86, bf16[128,256]{1,0:T(8,128)(2,1)S(1)} %copy-done.4), kind=kOutput, calls=%fused_computation.1 | convolution fusion | flops 100794368 | bytes 589824 | tf_op jit(solution)/shard_map/dot_general | solution.py:214
  (27 shorter events, 0.4 us)
Async XLA Ops:
  0.0 65.2 %copy-start = (bf16[128,256]{1,0:T(8,128)(2,1)S(1)}, bf16[128,256]{1,0:T(8,128)(2,1)}, u32[]{:S(2)}) copy-start(bf16[128,256]{1,0:T(8,128)(2,1)} %param.13) | copy-start | bytes 196612
  1.0 8.9 %collective-permute-start.1 = (bf16[1,2,128,128]{3,2,1,0:T(8,128)(2,1)S(1)}, bf16[1,2,128,128]{3,2,1,0:T(8,128)(2,1)S(1)}, u32[]{:S(2)}, u32[]{:S(2)}) collective-permute-start(bf16[1,2,128,128]{3,2,1,0:T(8,128)(2,1)S(1)} %bitcast.78), channel_id=1, source_target_pairs={{0,8},{1,9},{2,10},{3,11},{4,12},{5,13},{6,14},{7,15},{8,0},{9,1},... | collective-permute-start | bytes 196616 | tf_op jit(solution)/shard_map/ppermute | solution.py:31
  5.1 3.2 %collective-permute-start = (bf16[1,256,128]{2,1,0:T(8,128)(2,1)}, bf16[1,256,128]{2,1,0:T(8,128)(2,1)S(1)}, u32[]{:S(2)}, u32[]{:S(2)}) collective-permute-start(bf16[1,256,128]{2,1,0:T(8,128)(2,1)} %bitcast.88), channel_id=1, source_target_pairs={{0,16},{16,0},{1,17},{17,1},{2,18},{18,2},{3,19},{19,3},{4,20},{20... | collective-permute-start | bytes 196616 | tf_op jit(solution)/shard_map/ppermute | solution.py:36
  15.0 4.5 %copy-start.3 = (bf16[2,2,128,128]{3,2,1,0:T(8,128)(2,1)S(1)}, bf16[2,2,128,128]{3,2,1,0:T(8,128)(2,1)}, u32[]{:S(2)}) copy-start(bf16[2,2,128,128]{3,2,1,0:T(8,128)(2,1)} %pad_maximum_fusion.3.dep_ref) | copy-start | bytes 393220
  16.7 24.0 %collective-permute-start.2 = (f32[2,2,2,2,128,128]{5,4,3,2,1,0:T(8,128)S(1)}, f32[2,2,2,2,128,128]{5,4,3,2,1,0:T(8,128)S(1)}, u32[]{:S(2)}, u32[]{:S(2)}) collective-permute-start(f32[2,2,2,2,128,128]{5,4,3,2,1,0:T(8,128)S(1)} %bitcast.83), channel_id=1, source_target_pairs={{0,1},{1,0},{2,3},{3,2},{4,5},{5,4},{6,7},{7,6},{8,9},{9,8},{10,11... | collective-permute-start | bytes 3145736 | tf_op jit(solution)/shard_map/ppermute | solution.py:31
  19.4 14.2 %collective-permute-start.6 = (bf16[2,2,128,128]{3,2,1,0:T(8,128)(2,1)S(1)}, bf16[2,2,128,128]{3,2,1,0:T(8,128)(2,1)S(1)}, u32[]{:S(2)}, u32[]{:S(2)}) collective-permute-start(bf16[2,2,128,128]{3,2,1,0:T(8,128)(2,1)S(1)} %copy-done.3), channel_id=1, source_target_pairs={{0,1},{1,0},{2,3},{3,2},{4,5},{5,4},{6,7},{7,6},{8,9},{9,8},{10,11... | collective-permute-start | bytes 393224 | tf_op jit(solution)/shard_map/ppermute | solution.py:31
  33.6 6.5 %collective-permute-start.7 = (bf16[4,2,128,128]{3,2,1,0:T(8,128)(2,1)S(1)}, bf16[4,2,128,128]{3,2,1,0:T(8,128)(2,1)S(1)}, u32[]{:S(2)}, u32[]{:S(2)}) collective-permute-start(bf16[4,2,128,128]{3,2,1,0:T(8,128)(2,1)S(1)} %pad_maximum_fusion.1), channel_id=1, source_target_pairs={{0,2},{1,3},{2,0},{3,1},{4,6},{5,7},{6,4},{7,5},{8,10},{9,11},{10,... | collective-permute-start | bytes 786440 | tf_op jit(solution)/shard_map/ppermute | solution.py:31
  40.2 9.2 %collective-permute-start.8 = (bf16[8,2,128,128]{3,2,1,0:T(8,128)(2,1)S(1)}, bf16[8,2,128,128]{3,2,1,0:T(8,128)(2,1)S(1)}, u32[]{:S(2)}, u32[]{:S(2)}) collective-permute-start(bf16[8,2,128,128]{3,2,1,0:T(8,128)(2,1)S(1)} %pad_maximum_fusion), channel_id=1, source_target_pairs={{0,4},{1,5},{2,6},{3,7},{4,0},{5,1},{6,2},{7,3},{8,12},{9,13},{10,... | collective-permute-start | bytes 1572872 | tf_op jit(solution)/shard_map/ppermute | solution.py:31
  40.9 17.7 %collective-permute-start.3 = (f32[2,2,2,128,128]{4,3,2,1,0:T(8,128)S(1)}, f32[2,2,2,128,128]{4,3,2,1,0:T(8,128)S(1)}, u32[]{:S(2)}, u32[]{:S(2)}) collective-permute-start(f32[2,2,2,128,128]{4,3,2,1,0:T(8,128)S(1)} %slice_bitcast_fusion), channel_id=1, source_target_pairs={{0,2},{1,3},{2,0},{3,1},{4,6},{5,7},{6,4},{7,5},{8,10},{9,11},{10,... | collective-permute-start | bytes 1572872 | tf_op jit(solution)/shard_map/ppermute | solution.py:31
  49.5 1.0 %copy-start.1 = (bf16[16,2,128,128]{3,2,1,0:T(8,128)(2,1)}, bf16[16,2,128,128]{3,2,1,0:T(8,128)(2,1)S(1)}, u32[]{:S(2)}) copy-start(bf16[16,2,128,128]{3,2,1,0:T(8,128)(2,1)S(1)} %constant_dynamic-update-slice_fusion) | copy-start | bytes 3145732
  54.5 5.1 %copy-start.2 = (f32[4,128,128]{2,1,0:T(8,128)S(1)}, f32[4,128,128]{2,1,0:T(8,128)}, u32[]{:S(2)}) copy-start(f32[4,128,128]{2,1,0:T(8,128)} %shard_map.74) | copy-start | bytes 786436
  55.5 16.6 %copy-start.4 = (bf16[128,256]{1,0:T(8,128)(2,1)S(1)}, bf16[128,256]{1,0:T(8,128)(2,1)}, u32[]{:S(2)}) copy-start(bf16[128,256]{1,0:T(8,128)(2,1)} %param.12) | copy-start | bytes 196612
  55.5 4.1 %collective-permute-start.9 = (f32[2,128,128]{2,1,0:T(8,128)S(1)}, f32[2,128,128]{2,1,0:T(8,128)S(1)}, u32[]{:S(2)}, u32[]{:S(2)}) collective-permute-start(f32[2,128,128]{2,1,0:T(8,128)S(1)} %slice.53), channel_id=1, source_target_pairs={{0,16},{16,0},{1,17},{17,1},{2,18},{18,2},{3,19},{19,3},{4,20},{20... | collective-permute-start | bytes 393224 | tf_op jit(solution)/shard_map/ppermute | solution.py:36
  58.7 6.4 %collective-permute-start.4 = (f32[2,2,128,128]{3,2,1,0:T(8,128)S(1)}, f32[2,2,128,128]{3,2,1,0:T(8,128)S(1)}, u32[]{:S(2)}, u32[]{:S(2)}) collective-permute-start(f32[2,2,128,128]{3,2,1,0:T(8,128)S(1)} %slice_bitcast_fusion.2), channel_id=1, source_target_pairs={{0,4},{1,5},{2,6},{3,7},{4,0},{5,1},{6,2},{7,3},{8,12},{9,13},{10,... | collective-permute-start | bytes 786440 | tf_op jit(solution)/shard_map/ppermute | solution.py:31
  65.1 6.9 %collective-permute-start.5 = (f32[2,128,128]{2,1,0:T(8,128)S(1)}, f32[2,128,128]{2,1,0:T(8,128)S(1)}, u32[]{:S(2)}, u32[]{:S(2)}) collective-permute-start(f32[2,128,128]{2,1,0:T(8,128)S(1)} %slice_bitcast_fusion.4), channel_id=1, source_target_pairs={{0,8},{1,9},{2,10},{3,11},{4,12},{5,13},{6,14},{7,15},{8,0},{9,1},... | collective-permute-start | bytes 393224 | tf_op jit(solution)/shard_map/ppermute | solution.py:31

commit v6 on v5

--- a/solution.py
+++ b/solution.py
@@ -13,7 +13,7 @@
 
 def _orders(nb):
     if nb == 4:
-        return ((0, 1, 2, 3), (2, 0, 1, 3)), ((3, 0, 1, 2), (3, 2, 0, 1))
+        return ((0, 1, 2, 3), (2, 0, 1, 3)), ((3, 1, 2, 0), (3, 1, 0, 2))
     rs = tuple(range(nb))
     return (rs, rs), (rs[::-1], rs[::-1])
 
@@ -202,7 +202,7 @@
     mine_t = jnp.transpose(features.reshape(nbc, side, width), (0, 2, 1))
     stripe_t, stages = gather_blocks(mine_t, nb_c, col_x(ag_order))
     stripe_t = stripe_t.reshape(nrb, width, side)
-    fwd_parts = along_call(idx, cnt, values, group, nrb, stages[0])
+    fwd_parts = along_call(idx, cnt, values, group, nrb, stages[min(1, nb_c - 1)])
     along = scatter_blocks(fwd_parts.reshape((2,) * nb_c + (nbc, side, width)), nb_c, col_x(rs_order))
 
     bwd_t = against_call(idx, cnt, values, stripe_t, ncb)

time: 74.4 us -> 70.5 us (0.948)
  waiting for transfers between devices: 38.1 us -> 29.8 us
  starting transfers between devices: 14.5 us -> 20.1 us
  Pallas kernels: 8.44 us -> 7.52 us
    ppermute x8, starting transfers between devices: 11.4 us -> 20 us  [_swap_col(): return lax.ppermute(x, ('row', 'col'), perm)]
    ppermute x8, waiting for transfers between devices: 37.2 us -> 29.8 us  [_swap_col(): return lax.ppermute(x, ('row', 'col'), perm)]
    ppermute x2, starting transfers between devices: 3.09 us -> 0.07 us  [_swap_row(): return lax.ppermute(x, 'row', perm)]
    ppermute x2, waiting for transfers between devices: 0.82 us -> 0.01 us  [_swap_row(): return lax.ppermute(x, 'row', perm)]
  transfers between devices with their start and end apart: 10 -> 10, of which waited for: 6 -> 7; matrix products, arithmetic and copies ran while one was open for 8% -> 9% of each run, Pallas kernels for 5% -> 5%
where the time goes in v6:
time: 70.5 us; the launch traced here: 69.6 us
  waiting for transfers between devices  29.8 us (42%)
  starting transfers between devices  20.1 us (29%)
  Pallas kernels  7.52 us (11%)
  other arithmetic  5.2 us (7%)
  local copies, waits for them, and re-layouts  4.98 us (7%)
  matrix products  1.16 us (2%)
  between operations  0.83 us (1%)
    ppermute x8, waiting for transfers between devices, _swap_col(): return lax.ppermute(x, ('row', 'col'), perm)  29.8 us
    ppermute x8, starting transfers between devices, _swap_col(): return lax.ppermute(x, ('row', 'col'), perm)  20 us
    pallas_call x1, Pallas kernels, along_call(): pl.pallas_call(kernel, grid_spec=spec, out_shape=jax.ShapeDtypeStruct((nr...  3.98 us
    pallas_call x1, Pallas kernels, against_call(): pl.pallas_call(kernel, grid_spec=spec, out_shape=jax.ShapeDtypeStruct((nc...  3.54 us
    slice x2, local copies, waits for them, and re-layouts, scatter_blocks(): data = data[1] + xchg(data[0], t)  2.71 us
    concatenate x4, other arithmetic, gather_blocks(): have = jnp.concatenate([have, xchg(have, t)], axis=0)  2.32 us
  transfers between devices with their start and end apart: 10, of which 7 were waited for; matrix products, arithmetic and copies ran while one was open for 9% of the time, Pallas kernels for 5%

profile of v6, /device:TPU:0, one launch (start us, length us, event | category | flops | bytes accessed | tf_op | source)
XLA Modules:
  0.0 69.6 jit_solution(16686760021917743268)
XLA Ops:
  0.0 1.0 %copy.8 = bf16[2,128,128]{1,2,0:T(8,128)(2,1)S(1)} copy(bf16[2,128,128]{2,1,0:T(8,128)(2,1)} %bitcast.87) | data formatting | bytes 131072 | tf_op jit(solution)/shard_map/reshape | solution.py:202
  1.0 4.1 %collective-permute-start.1 = (bf16[1,2,128,128]{3,2,1,0:T(8,128)(2,1)S(1)}, bf16[1,2,128,128]{3,2,1,0:T(8,128)(2,1)S(1)}, u32[]{:S(2)}, u32[]{:S(2)}) collective-permute-start(bf16[1,2,128,128]{3,2,1,0:T(8,128)(2,1)S(1)} %bitcast.78), channel_id=1, source_target_pairs={{0,8},{1,9},{2,10},{3,11},{4,12},{5,13},{6,14},{7,15},{8,0},{9,1},... | collective-permute-start | bytes 196616 | tf_op jit(solution)/shard_map/ppermute | solution.py:31
  5.1 0.7 multiply_add_fusion.2
  5.8 0.7 multiply_add_fusion.3
  6.5 0.7 multiply_add_fusion
  7.1 1.6 %collective-permute-done.1 = bf16[1,2,128,128]{3,2,1,0:T(8,128)(2,1)S(1)} collective-permute-done((bf16[1,2,128,128]{3,2,1,0:T(8,128)(2,1)S(1)}, bf16[1,2,128,128]{3,2,1,0:T(8,128)(2,1)S(1)}, u32[]{:S(2)}, u32[]{:S(2)}) %collective-permute-start.1) | collective-permute-done | bytes 65568 | tf_op jit(solution)/shard_map/ppermute | solution.py:31
  8.8 1.8 %collective-permute-start.2 = (bf16[2,2,128,128]{3,2,1,0:T(8,128)(2,1)S(1)}, bf16[2,2,128,128]{3,2,1,0:T(8,128)(2,1)S(1)}, u32[]{:S(2)}, u32[]{:S(2)}) collective-permute-start(bf16[2,2,128,128]{3,2,1,0:T(8,128)(2,1)S(1)} %pad_maximum_fusion.3), channel_id=1, source_target_pairs={{0,2},{1,3},{2,0},{3,1},{4,6},{5,7},{6,4},{7,5},{8,10},{9,11},{10,... | collective-permute-start | bytes 393224 | tf_op jit(solution)/shard_map/ppermute | solution.py:31
  10.6 0.6 add_bitcast_fusion.idx_ref
  11.8 1.5 %pad_maximum_fusion.2 = bf16[2,256,128]{2,1,0:T(8,128)(2,1)} fusion(bf16[1,256,128]{2,1,0:T(8,128)(2,1)S(1)} %collective-permute-done, bf16[1,256,128]{2,1,0:T(8,128)(2,1)} %bitcast.89), kind=kLoop, calls=%fused_computation.15 | loop fusion | flops 65536 | bytes 262144 | tf_op jit(solution)/shard_map/concatenate | solution.py:43
  13.3 0.5 collective-permute-done.2
  13.8 0.7 %pad_maximum_fusion.1.dep_ref = bf16[4,2,128,128]{3,2,1,0:T(8,128)(2,1)} fusion(bf16[2,2,128,128]{3,2,1,0:T(8,128)(2,1)S(1)} %collective-permute-done.2, bf16[1,2,128,128]{3,2,1,0:T(8,128)(2,1)S(1)} %collective-permute-done.1, bf16[1,2,128,128]{3,2,1,0:T(8,128)(2,1)S(1)} %bitcast.80), kind=kLoop, calls=%fused_computation.9 | loop fusion | flops 262144 | bytes 524288 | tf_op jit(solution)/shard_map/concatenate | solution.py:43
  14.5 4.0 %shard_map.73 = f32[32,128,128]{2,1,0:T(8,128)} custom-call(s32[512]{0:T(512)} %add_bitcast_fusion.idx_ref, s32[1]{0:T(128)} %bitcast.3.cnt_ref, bf16[128,128,128]{2,1,0:T(8,128)(2,1)} %bitcast.75, bf16[4,128,128]{2,1,0:T(8,128)(2,1)} %bitcast.85, bf16[4,2,128,128]{3,2,1,0:T(8,128)(2,1)} %pad_maximum_fusion.1.dep_ref), custom_call_target="tpu_custom_call" | custom-call | tf_op jit(solution)/shard_map/pallas_call | solution.py:109
  18.5 1.7 %fusion.7 = (f32[16,128,128]{2,1,0:T(8,128)S(1)}, f32[16,128,128]{2,1,0:T(8,128)S(1)}) fusion(f32[32,128,128]{2,1,0:T(8,128)} %shard_map.73), kind=kLoop, calls=%fused_computation.44 | loop fusion | bytes 4194304 | tf_op jit(solution)/shard_map/slice | solution.py:50
  20.2 1.8 %collective-permute-start.3 = (f32[2,2,2,2,128,128]{5,4,3,2,1,0:T(8,128)S(1)}, f32[2,2,2,2,128,128]{5,4,3,2,1,0:T(8,128)S(1)}, u32[]{:S(2)}, u32[]{:S(2)}) collective-permute-start(f32[2,2,2,2,128,128]{5,4,3,2,1,0:T(8,128)S(1)} %bitcast.83), channel_id=1, source_target_pairs={{0,1},{1,0},{2,3},{3,2},{4,5},{5,4},{6,7},{7,6},{8,9},{9,8},{10,11... | collective-permute-start | bytes 3145736 | tf_op jit(solution)/shard_map/ppermute | solution.py:31
  22.0 2.9 %collective-permute-start.7 = (bf16[4,2,128,128]{3,2,1,0:T(8,128)(2,1)S(1)}, bf16[4,2,128,128]{3,2,1,0:T(8,128)(2,1)S(1)}, u32[]{:S(2)}, u32[]{:S(2)}) collective-permute-start(bf16[4,2,128,128]{3,2,1,0:T(8,128)(2,1)S(1)} %copy-done.2), channel_id=1, source_target_pairs={{0,4},{1,5},{2,6},{3,7},{4,0},{5,1},{6,2},{7,3},{8,12},{9,13},{10,... | collective-permute-start | bytes 786440 | tf_op jit(solution)/shard_map/ppermute | solution.py:31
  24.9 7.2 %collective-permute-done.7 = bf16[4,2,128,128]{3,2,1,0:T(8,128)(2,1)S(1)} collective-permute-done((bf16[4,2,128,128]{3,2,1,0:T(8,128)(2,1)S(1)}, bf16[4,2,128,128]{3,2,1,0:T(8,128)(2,1)S(1)}, u32[]{:S(2)}, u32[]{:S(2)}) %collective-permute-start.7) | collective-permute-done | bytes 262176 | tf_op jit(solution)/shard_map/ppermute | solution.py:31
  32.2 0.2 collective-permute-start.8
  32.3 4.6 %collective-permute-done.3 = f32[2,2,2,2,128,128]{5,4,3,2,1,0:T(8,128)S(1)} collective-permute-done((f32[2,2,2,2,128,128]{5,4,3,2,1,0:T(8,128)S(1)}, f32[2,2,2,2,128,128]{5,4,3,2,1,0:T(8,128)S(1)}, u32[]{:S(2)}, u32[]{:S(2)}) %collective-permute-start.3) | collective-permute-done | bytes 1048608 | tf_op jit(solution)/shard_map/ppermute | solution.py:31
  36.9 0.2 add.191
  37.1 2.7 %collective-permute-start.4 = (f32[2,2,2,128,128]{4,3,2,1,0:T(8,128)S(1)}, f32[2,2,2,128,128]{4,3,2,1,0:T(8,128)S(1)}, u32[]{:S(2)}, u32[]{:S(2)}) collective-permute-start(f32[2,2,2,128,128]{4,3,2,1,0:T(8,128)S(1)} %slice_bitcast_fusion), channel_id=1, source_target_pairs={{0,2},{1,3},{2,0},{3,1},{4,6},{5,7},{6,4},{7,5},{8,10},{9,11},{10,... | collective-permute-start | bytes 1572872 | tf_op jit(solution)/shard_map/ppermute | solution.py:31
  39.9 5.3 %collective-permute-done.8 = bf16[8,2,128,128]{3,2,1,0:T(8,128)(2,1)S(1)} collective-permute-done((bf16[8,2,128,128]{3,2,1,0:T(8,128)(2,1)S(1)}, bf16[8,2,128,128]{3,2,1,0:T(8,128)(2,1)S(1)}, u32[]{:S(2)}, u32[]{:S(2)}) %collective-permute-start.8) | collective-permute-done | bytes 524320 | tf_op jit(solution)/shard_map/ppermute | solution.py:31
  45.3 1.0 %copy-done.1 = bf16[16,2,128,128]{3,2,1,0:T(8,128)(2,1)} copy-done((bf16[16,2,128,128]{3,2,1,0:T(8,128)(2,1)}, bf16[16,2,128,128]{3,2,1,0:T(8,128)(2,1)S(1)}, u32[]{:S(2)}) %copy-start.1) | copy-done | bytes 1048600
  46.2 3.5 %shard_map.74 = f32[4,128,128]{2,1,0:T(8,128)} custom-call(s32[512]{0:T(512)} %add_bitcast_fusion.idx_ref, s32[1]{0:T(128)} %bitcast.3.cnt_ref, bf16[128,128,128]{2,1,0:T(8,128)(2,1)} %bitcast.76, bf16[32,128,128]{2,1,0:T(8,128)(2,1)} %bitcast.82), custom_call_target="tpu_custom_call" | custom-call | tf_op jit(solution)/shard_map/pallas_call | solution.py:151
  49.8 1.0 %slice.53 = f32[2,128,128]{2,1,0:T(8,128)S(1)} slice(f32[4,128,128]{2,1,0:T(8,128)} %shard_map.74), slice={[0:2], [0:128], [0:128]} | slice | bytes 262144 | tf_op jit(solution)/shard_map/slice | solution.py:50
  50.8 0.1 collective-permute-start.9
  51.0 3.6 %collective-permute-start.5 = (f32[2,2,128,128]{3,2,1,0:T(8,128)S(1)}, f32[2,2,128,128]{3,2,1,0:T(8,128)S(1)}, u32[]{:S(2)}, u32[]{:S(2)}) collective-permute-start(f32[2,2,128,128]{3,2,1,0:T(8,128)S(1)} %slice_bitcast_fusion.2), channel_id=1, source_target_pairs={{0,4},{1,5},{2,6},{3,7},{4,0},{5,1},{6,2},{7,3},{8,12},{9,13},{10,... | collective-permute-start | bytes 786440 | tf_op jit(solution)/shard_map/ppermute | solution.py:31
  54.5 0.1 copy.9
  54.6 4.2 %collective-permute-done.5 = f32[2,2,128,128]{3,2,1,0:T(8,128)S(1)} collective-permute-done((f32[2,2,128,128]{3,2,1,0:T(8,128)S(1)}, f32[2,2,128,128]{3,2,1,0:T(8,128)S(1)}, u32[]{:S(2)}, u32[]{:S(2)}) %collective-permute-start.5) | collective-permute-done | bytes 262176 | tf_op jit(solution)/shard_map/ppermute | solution.py:31
  58.9 3.1 %collective-permute-start.6 = (f32[2,128,128]{2,1,0:T(8,128)S(1)}, f32[2,128,128]{2,1,0:T(8,128)S(1)}, u32[]{:S(2)}, u32[]{:S(2)}) collective-permute-start(f32[2,128,128]{2,1,0:T(8,128)S(1)} %slice_bitcast_fusion.4), channel_id=1, source_target_pairs={{0,8},{1,9},{2,10},{3,11},{4,12},{5,13},{6,14},{7,15},{8,0},{9,1},... | collective-permute-start | bytes 393224 | tf_op jit(solution)/shard_map/ppermute | solution.py:31
  62.0 0.2 fusion.8
  62.2 6.4 %collective-permute-done.6 = f32[2,128,128]{2,1,0:T(8,128)S(1)} collective-permute-done((f32[2,128,128]{2,1,0:T(8,128)S(1)}, f32[2,128,128]{2,1,0:T(8,128)S(1)}, u32[]{:S(2)}, u32[]{:S(2)}) %collective-permute-start.6) | collective-permute-done | bytes 131104 | tf_op jit(solution)/shard_map/ppermute | solution.py:31
  68.7 0.9 %fusion = bf16[256,256]{1,0:T(8,128)(2,1)} fusion(f32[256,256]{1,0:T(8,128)S(1)} %fusion.8, f32[256,128]{1,0:T(8,128)S(1)} %bitcast.86, bf16[128,256]{1,0:T(8,128)(2,1)S(1)} %copy-done.4), kind=kOutput, calls=%fused_computation.1 | convolution fusion | flops 100794368 | bytes 589824 | tf_op jit(solution)/shard_map/dot_general | solution.py:214
  (27 shorter events, 0.4 us)
Async XLA Ops:
  0.0 62.0 %copy-start = (bf16[128,256]{1,0:T(8,128)(2,1)S(1)}, bf16[128,256]{1,0:T(8,128)(2,1)}, u32[]{:S(2)}) copy-start(bf16[128,256]{1,0:T(8,128)(2,1)} %param.13) | copy-start | bytes 196612
  1.0 7.8 %collective-permute-start.1 = (bf16[1,2,128,128]{3,2,1,0:T(8,128)(2,1)S(1)}, bf16[1,2,128,128]{3,2,1,0:T(8,128)(2,1)S(1)}, u32[]{:S(2)}, u32[]{:S(2)}) collective-permute-start(bf16[1,2,128,128]{3,2,1,0:T(8,128)(2,1)S(1)} %bitcast.78), channel_id=1, source_target_pairs={{0,8},{1,9},{2,10},{3,11},{4,12},{5,13},{6,14},{7,15},{8,0},{9,1},... | collective-permute-start | bytes 196616 | tf_op jit(solution)/shard_map/ppermute | solution.py:31
  5.1 6.7 %collective-permute-start = (bf16[1,256,128]{2,1,0:T(8,128)(2,1)}, bf16[1,256,128]{2,1,0:T(8,128)(2,1)S(1)}, u32[]{:S(2)}, u32[]{:S(2)}) collective-permute-start(bf16[1,256,128]{2,1,0:T(8,128)(2,1)} %bitcast.88), channel_id=1, source_target_pairs={{0,16},{16,0},{1,17},{17,1},{2,18},{18,2},{3,19},{19,3},{4,20},{20... | collective-permute-start | bytes 196616 | tf_op jit(solution)/shard_map/ppermute | solution.py:36
  8.8 5.0 %collective-permute-start.2 = (bf16[2,2,128,128]{3,2,1,0:T(8,128)(2,1)S(1)}, bf16[2,2,128,128]{3,2,1,0:T(8,128)(2,1)S(1)}, u32[]{:S(2)}, u32[]{:S(2)}) collective-permute-start(bf16[2,2,128,128]{3,2,1,0:T(8,128)(2,1)S(1)} %pad_maximum_fusion.3), channel_id=1, source_target_pairs={{0,2},{1,3},{2,0},{3,1},{4,6},{5,7},{6,4},{7,5},{8,10},{9,11},{10,... | collective-permute-start | bytes 393224 | tf_op jit(solution)/shard_map/ppermute | solution.py:31
  18.5 3.5 %copy-start.2 = (bf16[4,2,128,128]{3,2,1,0:T(8,128)(2,1)S(1)}, bf16[4,2,128,128]{3,2,1,0:T(8,128)(2,1)}, u32[]{:S(2)}) copy-start(bf16[4,2,128,128]{3,2,1,0:T(8,128)(2,1)} %pad_maximum_fusion.1.dep_ref) | copy-start | bytes 786436
  20.2 16.7 %collective-permute-start.3 = (f32[2,2,2,2,128,128]{5,4,3,2,1,0:T(8,128)S(1)}, f32[2,2,2,2,128,128]{5,4,3,2,1,0:T(8,128)S(1)}, u32[]{:S(2)}, u32[]{:S(2)}) collective-permute-start(f32[2,2,2,2,128,128]{5,4,3,2,1,0:T(8,128)S(1)} %bitcast.83), channel_id=1, source_target_pairs={{0,1},{1,0},{2,3},{3,2},{4,5},{5,4},{6,7},{7,6},{8,9},{9,8},{10,11... | collective-permute-start | bytes 3145736 | tf_op jit(solution)/shard_map/ppermute | solution.py:31
  22.0 10.1 %collective-permute-start.7 = (bf16[4,2,128,128]{3,2,1,0:T(8,128)(2,1)S(1)}, bf16[4,2,128,128]{3,2,1,0:T(8,128)(2,1)S(1)}, u32[]{:S(2)}, u32[]{:S(2)}) collective-permute-start(bf16[4,2,128,128]{3,2,1,0:T(8,128)(2,1)S(1)} %copy-done.2), channel_id=1, source_target_pairs={{0,4},{1,5},{2,6},{3,7},{4,0},{5,1},{6,2},{7,3},{8,12},{9,13},{10,... | collective-permute-start | bytes 786440 | tf_op jit(solution)/shard_map/ppermute | solution.py:31
  32.2 13.0 %collective-permute-start.8 = (bf16[8,2,128,128]{3,2,1,0:T(8,128)(2,1)S(1)}, bf16[8,2,128,128]{3,2,1,0:T(8,128)(2,1)S(1)}, u32[]{:S(2)}, u32[]{:S(2)}) collective-permute-start(bf16[8,2,128,128]{3,2,1,0:T(8,128)(2,1)S(1)} %pad_maximum_fusion), channel_id=1, source_target_pairs={{0,1},{1,0},{2,3},{3,2},{4,5},{5,4},{6,7},{7,6},{8,9},{9,8},{10,11... | collective-permute-start | bytes 1572872 | tf_op jit(solution)/shard_map/ppermute | solution.py:31
  37.1 13.8 %collective-permute-start.4 = (f32[2,2,2,128,128]{4,3,2,1,0:T(8,128)S(1)}, f32[2,2,2,128,128]{4,3,2,1,0:T(8,128)S(1)}, u32[]{:S(2)}, u32[]{:S(2)}) collective-permute-start(f32[2,2,2,128,128]{4,3,2,1,0:T(8,128)S(1)} %slice_bitcast_fusion), channel_id=1, source_target_pairs={{0,2},{1,3},{2,0},{3,1},{4,6},{5,7},{6,4},{7,5},{8,10},{9,11},{10,... | collective-permute-start | bytes 1572872 | tf_op jit(solution)/shard_map/ppermute | solution.py:31
  45.2 1.0 %copy-start.1 = (bf16[16,2,128,128]{3,2,1,0:T(8,128)(2,1)}, bf16[16,2,128,128]{3,2,1,0:T(8,128)(2,1)S(1)}, u32[]{:S(2)}) copy-start(bf16[16,2,128,128]{3,2,1,0:T(8,128)(2,1)S(1)} %constant_dynamic-update-slice_fusion) | copy-start | bytes 3145732
  49.8 4.7 %copy-start.3 = (f32[4,128,128]{2,1,0:T(8,128)S(1)}, f32[4,128,128]{2,1,0:T(8,128)}, u32[]{:S(2)}) copy-start(f32[4,128,128]{2,1,0:T(8,128)} %shard_map.74) | copy-start | bytes 786436
  50.8 17.9 %copy-start.4 = (bf16[128,256]{1,0:T(8,128)(2,1)S(1)}, bf16[128,256]{1,0:T(8,128)(2,1)}, u32[]{:S(2)}) copy-start(bf16[128,256]{1,0:T(8,128)(2,1)} %param.12) | copy-start | bytes 196612
  50.8 3.7 %collective-permute-start.9 = (f32[2,128,128]{2,1,0:T(8,128)S(1)}, f32[2,128,128]{2,1,0:T(8,128)S(1)}, u32[]{:S(2)}, u32[]{:S(2)}) collective-permute-start(f32[2,128,128]{2,1,0:T(8,128)S(1)} %slice.53), channel_id=1, source_target_pairs={{0,16},{16,0},{1,17},{17,1},{2,18},{18,2},{3,19},{19,3},{4,20},{20... | collective-permute-start | bytes 393224 | tf_op jit(solution)/shard_map/ppermute | solution.py:36
  51.0 7.9 %collective-permute-start.5 = (f32[2,2,128,128]{3,2,1,0:T(8,128)S(1)}, f32[2,2,128,128]{3,2,1,0:T(8,128)S(1)}, u32[]{:S(2)}, u32[]{:S(2)}) collective-permute-start(f32[2,2,128,128]{3,2,1,0:T(8,128)S(1)} %slice_bitcast_fusion.2), channel_id=1, source_target_pairs={{0,4},{1,5},{2,6},{3,7},{4,0},{5,1},{6,2},{7,3},{8,12},{9,13},{10,... | collective-permute-start | bytes 786440 | tf_op jit(solution)/shard_map/ppermute | solution.py:31
  58.9 9.7 %collective-permute-start.6 = (f32[2,128,128]{2,1,0:T(8,128)S(1)}, f32[2,128,128]{2,1,0:T(8,128)S(1)}, u32[]{:S(2)}, u32[]{:S(2)}) collective-permute-start(f32[2,128,128]{2,1,0:T(8,128)S(1)} %slice_bitcast_fusion.4), channel_id=1, source_target_pairs={{0,8},{1,9},{2,10},{3,11},{4,12},{5,13},{6,14},{7,15},{8,0},{9,1},... | collective-permute-start | bytes 393224 | tf_op jit(solution)/shard_map/ppermute | solution.py:31

commit v7 on v6

--- a/solution.py
+++ b/solution.py
@@ -70,18 +70,21 @@
     return 32 if slots % 32 == 0 else slots
 
 
-def along_call(idx, cnt, values, group, nrb, dep):
+def along_call(idx, cnt, values, grp_a, grp_b, nrb, dep):
     slots, side, _ = values.shape
-    width = group.shape[-1]
+    width = grp_a.shape[-1]
+    half = grp_a.shape[0]
     k = _chunk(slots)
 
-    def kernel(idx_ref, cnt_ref, vals_ref, grp_ref, dep_ref, out_ref):
+    def kernel(idx_ref, cnt_ref, vals_ref, ga_ref, gb_ref, dep_ref, out_ref, grp_ref):
         i = pl.program_id(0)
         n = cnt_ref[0]
 
         @pl.when(i == 0)
         def _():
             out_ref[...] = jnp.zeros(out_ref.shape, out_ref.dtype)
+            grp_ref[:half] = ga_ref[...]
+            grp_ref[half:] = gb_ref[...]
 
         @pl.when(i * k < n)
         def _():
@@ -101,24 +104,26 @@
         grid=(slots // k,),
         in_specs=[
             pl.BlockSpec((k, side, side), vals_map),
-            pl.BlockSpec(group.shape, lambda i, *_: (0, 0, 0)),
+            pl.BlockSpec(grp_a.shape, lambda i, *_: (0, 0, 0)),
+            pl.BlockSpec(grp_b.shape, lambda i, *_: (0, 0, 0)),
             pl.BlockSpec(memory_space=pl.ANY),
         ],
         out_specs=pl.BlockSpec((nrb, side, width), lambda i, *_: (0, 0, 0)),
+        scratch_shapes=[pltpu.VMEM((2 * half, side, width), grp_a.dtype)],
     )
     return pl.pallas_call(
         kernel,
         grid_spec=spec,
         out_shape=jax.ShapeDtypeStruct((nrb, side, width), jnp.float32),
-    )(idx, cnt, values, group, dep)
-
-
-def against_call(idx, cnt, values, stripe_t, ncb):
+    )(idx, cnt, values, grp_a, grp_b, dep)
+
+
+def against_call(idx, cnt, values, stripe_t, ncb, dep):
     slots, side, _ = values.shape
     width = stripe_t.shape[1]
     k = _chunk(slots)
 
-    def kernel(idx_ref, cnt_ref, vals_ref, st_ref, out_ref):
+    def kernel(idx_ref, cnt_ref, vals_ref, st_ref, dep_ref, out_ref):
         i = pl.program_id(0)
         n = cnt_ref[0]
 
@@ -145,6 +150,7 @@
         in_specs=[
             pl.BlockSpec((k, side, side), vals_map),
             pl.BlockSpec(stripe_t.shape, lambda i, *_: (0, 0, 0)),
+            pl.BlockSpec(memory_space=pl.ANY),
         ],
         out_specs=pl.BlockSpec((ncb, width, side), lambda i, *_: (0, 0, 0)),
     )
@@ -152,7 +158,7 @@
         kernel,
         grid_spec=spec,
         out_shape=jax.ShapeDtypeStruct((ncb, width, side), jnp.float32),
-    )(idx, cnt, values, stripe_t)
+    )(idx, cnt, values, stripe_t, dep)
 
 
 def local(features, tile_vals, tile_rows, tile_cols, tile_count, w_fwd, w_bwd):
@@ -186,11 +192,17 @@
     csub = colblk % nbc
     rs_bits = [_pick(parity, rs_order, t) for t in range(nb_c)]
     ag_bits = [_pick(parity, ag_order, t) for t in range(nb_c)]
+    which = lax.broadcasted_iota(jnp.int32, (4, slots), 0)
+    dest = jnp.broadcast_to(dest, (4, slots))
+    sub = jnp.broadcast_to(sub, (4, slots))
+    src = jnp.broadcast_to(src, (4, slots))
+    csub = jnp.broadcast_to(csub, (4, slots))
     rows_fwd = scatter_pos(dest, me_c, rs_bits) * nbc + sub
     rows_bwd = gather_pos(dest, me_c, ag_bits) * nbc + sub
     cols_fwd = gather_pos(src, me_r, row_bits) * nbc + csub
     cols_bwd = scatter_pos(src, me_r, row_bits) * nbc + csub
-    idx = jnp.stack([rows_fwd, cols_fwd, rows_bwd, cols_bwd]).reshape(-1)
+    idx = jnp.where(which == 0, rows_fwd, jnp.where(which == 1, cols_fwd, jnp.where(which == 2, rows_bwd, cols_bwd)))
+    idx = idx.reshape(-1)
 
     def col_x(order):
         return lambda x, t: _swap_col(x, row_size, col_size, (order[0][t], order[1][t]))
@@ -198,14 +210,17 @@
     def row_x(x, t):
         return _swap_row(x, row_size, row_bits[t])
 
-    group = gather_blocks(features, nb_r, row_x)[0].reshape(ncb, side, width)
+    grp_a, _ = gather_blocks(features, nb_r - 1, row_x)
+    grp_b = row_x(grp_a, nb_r - 1)
+    grp_a = grp_a.reshape(-1, side, width)
+    grp_b = grp_b.reshape(-1, side, width)
     mine_t = jnp.transpose(features.reshape(nbc, side, width), (0, 2, 1))
     stripe_t, stages = gather_blocks(mine_t, nb_c, col_x(ag_order))
     stripe_t = stripe_t.reshape(nrb, width, side)
-    fwd_parts = along_call(idx, cnt, values, group, nrb, stages[min(1, nb_c - 1)])
+    fwd_parts = along_call(idx, cnt, values, grp_a, grp_b, nrb, stages[min(1, nb_c - 1)])
     along = scatter_blocks(fwd_parts.reshape((2,) * nb_c + (nbc, side, width)), nb_c, col_x(rs_order))
 
-    bwd_t = against_call(idx, cnt, values, stripe_t, ncb)
+    bwd_t = against_call(idx, cnt, values, stripe_t, ncb, along)
     against_t = scatter_blocks(bwd_t.reshape((2,) * nb_r + (nbc, width, side)), nb_r, row_x)
     against = jnp.transpose(against_t, (0, 2, 1))
 

time: 70.5 us -> 75.6 us (1.072)
  waiting for transfers between devices: 29.8 us -> 36.8 us
  starting transfers between devices: 20.1 us -> 18.9 us
    ppermute x8, waiting for transfers between devices: 29.8 us -> 35.5 us  [_swap_col(): return lax.ppermute(x, ('row', 'col'), perm)]
    concatenate x4 -> x3, other arithmetic: 2.32 us -> 0.81 us  [gather_blocks(): have = jnp.concatenate([have, xchg(have, t)], axis=0)]
    ppermute x2, waiting for transfers between devices: 0.01 us -> 1.34 us  [_swap_row(): return lax.ppermute(x, 'row', perm)]
    ppermute x8, starting transfers between devices: 20 us -> 18.8 us  [_swap_col(): return lax.ppermute(x, ('row', 'col'), perm)]
    another operation x0 -> x1, local copies, waits for them, and re-layouts: none -> 0.98 us  [local(): grp_a = grp_a.reshape(-1, side, width)]
    reshape x1 -> x0, local copies, waits for them, and re-layouts: 0.98 us -> none  [local(): mine_t = jnp.transpose(features.reshape(nbc, side, width), (0, 2, 1))]
    transpose x1, other arithmetic: 0.02 us -> 0.93 us  [local(): against = jnp.transpose(against_t, (0, 2, 1))]
  transfers between devices with their start and end apart: 10 -> 10, of which waited for: 7 -> 8; matrix products, arithmetic and copies ran while one was open for 9% -> 4% of each run, Pallas kernels for 5% -> 0%
where the time goes in v7:
time: 75.6 us; the launch traced here: 74.5 us
  waiting for transfers between devices  36.8 us (49%)
  starting transfers between devices  18.9 us (25%)
  Pallas kernels  7.67 us (10%)
  other arithmetic  4.69 us (6%)
  local copies, waits for them, and re-layouts  4.52 us (6%)
  matrix products  1.16 us (2%)
  between operations  0.86 us (1%)
    ppermute x8, waiting for transfers between devices, _swap_col(): return lax.ppermute(x, ('row', 'col'), perm)  35.5 us
    ppermute x8, starting transfers between devices, _swap_col(): return lax.ppermute(x, ('row', 'col'), perm)  18.8 us
    pallas_call x1, Pallas kernels, along_call(): pl.pallas_call(kernel, grid_spec=spec, out_shape=jax.ShapeDtypeStruct((nr...  3.99 us
    pallas_call x1, Pallas kernels, against_call(): pl.pallas_call(kernel, grid_spec=spec, out_shape=jax.ShapeDtypeStruct((nc...  3.67 us
    slice x2, local copies, waits for them, and re-layouts, scatter_blocks(): data = data[1] + xchg(data[0], t)  2.59 us
  transfers between devices with their start and end apart: 10, of which 8 were waited for; matrix products, arithmetic and copies ran while one was open for 4% of the time, Pallas kernels for 0%

profile of v7, /device:TPU:0, one launch (start us, length us, event | category | flops | bytes accessed | tf_op | source)
XLA Modules:
  0.0 74.5 jit_solution(8670850809743901397)
XLA Ops:
  0.0 1.0 %copy.9 = bf16[2,128,128]{1,2,0:T(8,128)(2,1)S(1)} copy(bf16[2,128,128]{2,1,0:T(8,128)(2,1)} %bitcast.86) | data formatting | bytes 131072 | tf_op jit(solution)/shard_map/reshape;broadcast_in_dim | solution.py:215
  1.0 4.1 %collective-permute-start.1 = (bf16[1,2,128,128]{3,2,1,0:T(8,128)(2,1)S(1)}, bf16[1,2,128,128]{3,2,1,0:T(8,128)(2,1)S(1)}, u32[]{:S(2)}, u32[]{:S(2)}) collective-permute-start(bf16[1,2,128,128]{3,2,1,0:T(8,128)(2,1)S(1)} %bitcast.78), channel_id=1, source_target_pairs={{0,8},{1,9},{2,10},{3,11},{4,12},{5,13},{6,14},{7,15},{8,0},{9,1},... | collective-permute-start | bytes 196616 | tf_op jit(solution)/shard_map/ppermute | solution.py:31
  5.8 0.7 multiply_add_fusion
  6.5 0.7 multiply_add_fusion.2
  7.2 1.6 %collective-permute-done.1 = bf16[1,2,128,128]{3,2,1,0:T(8,128)(2,1)S(1)} collective-permute-done((bf16[1,2,128,128]{3,2,1,0:T(8,128)(2,1)S(1)}, bf16[1,2,128,128]{3,2,1,0:T(8,128)(2,1)S(1)}, u32[]{:S(2)}, u32[]{:S(2)}) %collective-permute-start.1) | collective-permute-done | bytes 65568 | tf_op jit(solution)/shard_map/ppermute | solution.py:31
  8.8 1.8 %collective-permute-start.2 = (bf16[2,2,128,128]{3,2,1,0:T(8,128)(2,1)S(1)}, bf16[2,2,128,128]{3,2,1,0:T(8,128)(2,1)S(1)}, u32[]{:S(2)}, u32[]{:S(2)}) collective-permute-start(bf16[2,2,128,128]{3,2,1,0:T(8,128)(2,1)S(1)} %pad_maximum_fusion.2), channel_id=1, source_target_pairs={{0,2},{1,3},{2,0},{3,1},{4,6},{5,7},{6,4},{7,5},{8,10},{9,11},{10,... | collective-permute-start | bytes 393224 | tf_op jit(solution)/shard_map/ppermute | solution.py:31
  10.6 0.6 select_bitcast_fusion.idx_ref
  11.2 2.6 %collective-permute-done.2 = bf16[2,2,128,128]{3,2,1,0:T(8,128)(2,1)S(1)} collective-permute-done((bf16[2,2,128,128]{3,2,1,0:T(8,128)(2,1)S(1)}, bf16[2,2,128,128]{3,2,1,0:T(8,128)(2,1)S(1)}, u32[]{:S(2)}, u32[]{:S(2)}) %collective-permute-start.2) | collective-permute-done | bytes 131104 | tf_op jit(solution)/shard_map/ppermute | solution.py:31
  13.8 0.7 pad_maximum_fusion.1.dep_ref
  14.5 0.6 copy-done.4
  15.2 4.0 %shard_map.73 = f32[32,128,128]{2,1,0:T(8,128)} custom-call(s32[512]{0:T(512)} %select_bitcast_fusion.idx_ref, s32[1]{0:T(128)} %bitcast.3.cnt_ref, bf16[128,128,128]{2,1,0:T(8,128)(2,1)} %bitcast.75, bf16[2,128,128]{2,1,0:T(8,128)(2,1)} %bitcast.88, bf16[2,128,128]{2,1,0:T(8,128)(2,1)} %bitcast.89, bf16[4,2,128,128]{3,2,1,0:T(8,128)(2,1)} %pad_maximum_fusion.1.dep_ref), custom_call_target="tpu_custom_call" | custom-call | tf_op jit(solution)/shard_map/pallas_call | solution.py:114
  19.2 1.7 %fusion.7 = (f32[16,128,128]{2,1,0:T(8,128)S(1)}, f32[16,128,128]{2,1,0:T(8,128)S(1)}) fusion(f32[32,128,128]{2,1,0:T(8,128)} %shard_map.73), kind=kLoop, calls=%fused_computation.46 | loop fusion | bytes 4194304 | tf_op jit(solution)/shard_map/slice | solution.py:50
  20.8 1.8 %collective-permute-start.3 = (f32[2,2,2,2,128,128]{5,4,3,2,1,0:T(8,128)S(1)}, f32[2,2,2,2,128,128]{5,4,3,2,1,0:T(8,128)S(1)}, u32[]{:S(2)}, u32[]{:S(2)}) collective-permute-start(f32[2,2,2,2,128,128]{5,4,3,2,1,0:T(8,128)S(1)} %bitcast.84), channel_id=1, source_target_pairs={{0,1},{1,0},{2,3},{3,2},{4,5},{5,4},{6,7},{7,6},{8,9},{9,8},{10,11... | collective-permute-start | bytes 3145736 | tf_op jit(solution)/shard_map/ppermute | solution.py:31
  22.6 13.1 %collective-permute-done.3 = f32[2,2,2,2,128,128]{5,4,3,2,1,0:T(8,128)S(1)} collective-permute-done((f32[2,2,2,2,128,128]{5,4,3,2,1,0:T(8,128)S(1)}, f32[2,2,2,2,128,128]{5,4,3,2,1,0:T(8,128)S(1)}, u32[]{:S(2)}, u32[]{:S(2)}) %collective-permute-start.3) | collective-permute-done | bytes 1048608 | tf_op jit(solution)/shard_map/ppermute | solution.py:31
  35.7 0.2 add.101
  35.9 2.2 %collective-permute-start.4 = (f32[2,2,2,128,128]{4,3,2,1,0:T(8,128)S(1)}, f32[2,2,2,128,128]{4,3,2,1,0:T(8,128)S(1)}, u32[]{:S(2)}, u32[]{:S(2)}) collective-permute-start(f32[2,2,2,128,128]{4,3,2,1,0:T(8,128)S(1)} %slice_bitcast_fusion), channel_id=1, source_target_pairs={{0,2},{1,3},{2,0},{3,1},{4,6},{5,7},{6,4},{7,5},{8,10},{9,11},{10,... | collective-permute-start | bytes 1572872 | tf_op jit(solution)/shard_map/ppermute | solution.py:31
  38.2 3.1 %collective-permute-start.7 = (bf16[4,2,128,128]{3,2,1,0:T(8,128)(2,1)S(1)}, bf16[4,2,128,128]{3,2,1,0:T(8,128)(2,1)S(1)}, u32[]{:S(2)}, u32[]{:S(2)}) collective-permute-start(bf16[4,2,128,128]{3,2,1,0:T(8,128)(2,1)S(1)} %copy-done.3), channel_id=1, source_target_pairs={{0,4},{1,5},{2,6},{3,7},{4,0},{5,1},{6,2},{7,3},{8,12},{9,13},{10,... | collective-permute-start | bytes 786440 | tf_op jit(solution)/shard_map/ppermute | solution.py:31
  41.3 4.4 %collective-permute-done.4 = f32[2,2,2,128,128]{4,3,2,1,0:T(8,128)S(1)} collective-permute-done((f32[2,2,2,128,128]{4,3,2,1,0:T(8,128)S(1)}, f32[2,2,2,128,128]{4,3,2,1,0:T(8,128)S(1)}, u32[]{:S(2)}, u32[]{:S(2)}) %collective-permute-start.4) | collective-permute-done | bytes 524320 | tf_op jit(solution)/shard_map/ppermute | solution.py:31
  45.7 5.6 %collective-permute-start.5 = (f32[2,2,128,128]{3,2,1,0:T(8,128)S(1)}, f32[2,2,128,128]{3,2,1,0:T(8,128)S(1)}, u32[]{:S(2)}, u32[]{:S(2)}) collective-permute-start(f32[2,2,128,128]{3,2,1,0:T(8,128)S(1)} %slice_bitcast_fusion.2), channel_id=1, source_target_pairs={{0,4},{1,5},{2,6},{3,7},{4,0},{5,1},{6,2},{7,3},{8,12},{9,13},{10,... | collective-permute-start | bytes 786440 | tf_op jit(solution)/shard_map/ppermute | solution.py:31
  51.5 0.1 collective-permute-start.8
  51.6 6.7 %collective-permute-done.5 = f32[2,2,128,128]{3,2,1,0:T(8,128)S(1)} collective-permute-done((f32[2,2,128,128]{3,2,1,0:T(8,128)S(1)}, f32[2,2,128,128]{3,2,1,0:T(8,128)S(1)}, u32[]{:S(2)}, u32[]{:S(2)}) %collective-permute-start.5) | collective-permute-done | bytes 262176 | tf_op jit(solution)/shard_map/ppermute | solution.py:31
  58.3 0.1 collective-permute-start.6
  58.4 2.3 %collective-permute-done.8 = bf16[8,2,128,128]{3,2,1,0:T(8,128)(2,1)S(1)} collective-permute-done((bf16[8,2,128,128]{3,2,1,0:T(8,128)(2,1)S(1)}, bf16[8,2,128,128]{3,2,1,0:T(8,128)(2,1)S(1)}, u32[]{:S(2)}, u32[]{:S(2)}) %collective-permute-start.8) | collective-permute-done | bytes 524320 | tf_op jit(solution)/shard_map/ppermute | solution.py:31
  60.8 4.8 %collective-permute-done.6 = f32[2,128,128]{2,1,0:T(8,128)S(1)} collective-permute-done((f32[2,128,128]{2,1,0:T(8,128)S(1)}, f32[2,128,128]{2,1,0:T(8,128)S(1)}, u32[]{:S(2)}, u32[]{:S(2)}) %collective-permute-start.6) | collective-permute-done | bytes 131104 | tf_op jit(solution)/shard_map/ppermute | solution.py:31
  65.6 0.7 fusion.4.dep_ref
  66.3 3.7 %shard_map.74 = f32[4,128,128]{2,1,0:T(8,128)} custom-call(s32[512]{0:T(512)} %select_bitcast_fusion.idx_ref, s32[1]{0:T(128)} %bitcast.3.cnt_ref, bf16[128,128,128]{2,1,0:T(8,128)(2,1)} %bitcast.76, bf16[32,128,128]{2,1,0:T(8,128)(2,1)} %bitcast.82, f32[2,128,128]{2,1,0:T(8,128)} %fusion.4.dep_ref), custom_call_target="tpu_custom_call" | custom-call | tf_op jit(solution)/shard_map/pallas_call | solution.py:157
  70.0 0.9 %slice.53 = f32[2,128,128]{2,1,0:T(8,128)S(1)} slice(f32[4,128,128]{2,1,0:T(8,128)} %shard_map.74), slice={[0:2], [0:128], [0:128]} | slice | bytes 262144 | tf_op jit(solution)/shard_map/slice | solution.py:50
  71.0 1.3 %collective-permute-done.9 = f32[2,128,128]{2,1,0:T(8,128)S(1)} collective-permute-done((f32[2,128,128]{2,1,0:T(8,128)S(1)}, f32[2,128,128]{2,1,0:T(8,128)S(1)}, u32[]{:S(2)}, u32[]{:S(2)}) %collective-permute-start.9) | collective-permute-done | bytes 131104 | tf_op jit(solution)/shard_map/ppermute | solution.py:36
  72.3 0.9 %fusion.3 = f32[2,128,128]{1,2,0:T(8,128)S(1)} fusion(f32[2,128,128]{2,1,0:T(8,128)S(1)} %collective-permute-done.9, f32[4,128,128]{2,1,0:T(8,128)} %shard_map.74), kind=kLoop, calls=%fused_computation.11 | loop fusion | flops 32768 | bytes 393216 | tf_op jit(solution)/shard_map/transpose | solution.py:225
  73.2 0.1 copy.10
  73.3 0.2 fusion.8
  73.6 0.9 %fusion = bf16[256,256]{1,0:T(8,128)(2,1)} fusion(f32[256,256]{1,0:T(8,128)S(1)} %fusion.8, f32[256,128]{1,0:T(8,128)S(1)} %bitcast.83, bf16[128,256]{1,0:T(8,128)(2,1)S(1)} %copy-done.5), kind=kOutput, calls=%fused_computation.1 | convolution fusion | flops 100794368 | bytes 589824 | tf_op jit(solution)/shard_map/dot_general | solution.py:229
  (30 shorter events, 0.5 us)
Async XLA Ops:
  0.0 73.3 %copy-start = (bf16[128,256]{1,0:T(8,128)(2,1)S(1)}, bf16[128,256]{1,0:T(8,128)(2,1)}, u32[]{:S(2)}) copy-start(bf16[128,256]{1,0:T(8,128)(2,1)} %param.13) | copy-start | bytes 196612
  1.0 7.8 %collective-permute-start.1 = (bf16[1,2,128,128]{3,2,1,0:T(8,128)(2,1)S(1)}, bf16[1,2,128,128]{3,2,1,0:T(8,128)(2,1)S(1)}, u32[]{:S(2)}, u32[]{:S(2)}) collective-permute-start(bf16[1,2,128,128]{3,2,1,0:T(8,128)(2,1)S(1)} %bitcast.78), channel_id=1, source_target_pairs={{0,8},{1,9},{2,10},{3,11},{4,12},{5,13},{6,14},{7,15},{8,0},{9,1},... | collective-permute-start | bytes 196616 | tf_op jit(solution)/shard_map/ppermute | solution.py:31
  5.1 9.4 %collective-permute-start = (bf16[1,256,128]{2,1,0:T(8,128)(2,1)}, bf16[1,256,128]{2,1,0:T(8,128)(2,1)S(1)}, u32[]{:S(2)}, u32[]{:S(2)}) collective-permute-start(bf16[1,256,128]{2,1,0:T(8,128)(2,1)} %bitcast.87), channel_id=1, source_target_pairs={{0,16},{16,0},{1,17},{17,1},{2,18},{18,2},{3,19},{19,3},{4,20},{20... | collective-permute-start | bytes 196616 | tf_op jit(solution)/shard_map/ppermute | solution.py:36
  8.8 5.0 %collective-permute-start.2 = (bf16[2,2,128,128]{3,2,1,0:T(8,128)(2,1)S(1)}, bf16[2,2,128,128]{3,2,1,0:T(8,128)(2,1)S(1)}, u32[]{:S(2)}, u32[]{:S(2)}) collective-permute-start(bf16[2,2,128,128]{3,2,1,0:T(8,128)(2,1)S(1)} %pad_maximum_fusion.2), channel_id=1, source_target_pairs={{0,2},{1,3},{2,0},{3,1},{4,6},{5,7},{6,4},{7,5},{8,10},{9,11},{10,... | collective-permute-start | bytes 393224 | tf_op jit(solution)/shard_map/ppermute | solution.py:31
  14.5 0.6 copy-start.4
  20.8 14.9 %collective-permute-start.3 = (f32[2,2,2,2,128,128]{5,4,3,2,1,0:T(8,128)S(1)}, f32[2,2,2,2,128,128]{5,4,3,2,1,0:T(8,128)S(1)}, u32[]{:S(2)}, u32[]{:S(2)}) collective-permute-start(f32[2,2,2,2,128,128]{5,4,3,2,1,0:T(8,128)S(1)} %bitcast.84), channel_id=1, source_target_pairs={{0,1},{1,0},{2,3},{3,2},{4,5},{5,4},{6,7},{7,6},{8,9},{9,8},{10,11... | collective-permute-start | bytes 3145736 | tf_op jit(solution)/shard_map/ppermute | solution.py:31
  35.7 2.5 %copy-start.3 = (bf16[4,2,128,128]{3,2,1,0:T(8,128)(2,1)S(1)}, bf16[4,2,128,128]{3,2,1,0:T(8,128)(2,1)}, u32[]{:S(2)}) copy-start(bf16[4,2,128,128]{3,2,1,0:T(8,128)(2,1)} %pad_maximum_fusion.1.dep_ref) | copy-start | bytes 786436
  35.9 9.7 %collective-permute-start.4 = (f32[2,2,2,128,128]{4,3,2,1,0:T(8,128)S(1)}, f32[2,2,2,128,128]{4,3,2,1,0:T(8,128)S(1)}, u32[]{:S(2)}, u32[]{:S(2)}) collective-permute-start(f32[2,2,2,128,128]{4,3,2,1,0:T(8,128)S(1)} %slice_bitcast_fusion), channel_id=1, source_target_pairs={{0,2},{1,3},{2,0},{3,1},{4,6},{5,7},{6,4},{7,5},{8,10},{9,11},{10,... | collective-permute-start | bytes 1572872 | tf_op jit(solution)/shard_map/ppermute | solution.py:31
  38.2 13.2 %collective-permute-start.7 = (bf16[4,2,128,128]{3,2,1,0:T(8,128)(2,1)S(1)}, bf16[4,2,128,128]{3,2,1,0:T(8,128)(2,1)S(1)}, u32[]{:S(2)}, u32[]{:S(2)}) collective-permute-start(bf16[4,2,128,128]{3,2,1,0:T(8,128)(2,1)S(1)} %copy-done.3), channel_id=1, source_target_pairs={{0,4},{1,5},{2,6},{3,7},{4,0},{5,1},{6,2},{7,3},{8,12},{9,13},{10,... | collective-permute-start | bytes 786440 | tf_op jit(solution)/shard_map/ppermute | solution.py:31
  45.7 12.5 %collective-permute-start.5 = (f32[2,2,128,128]{3,2,1,0:T(8,128)S(1)}, f32[2,2,128,128]{3,2,1,0:T(8,128)S(1)}, u32[]{:S(2)}, u32[]{:S(2)}) collective-permute-start(f32[2,2,128,128]{3,2,1,0:T(8,128)S(1)} %slice_bitcast_fusion.2), channel_id=1, source_target_pairs={{0,4},{1,5},{2,6},{3,7},{4,0},{5,1},{6,2},{7,3},{8,12},{9,13},{10,... | collective-permute-start | bytes 786440 | tf_op jit(solution)/shard_map/ppermute | solution.py:31
  51.5 9.2 %collective-permute-start.8 = (bf16[8,2,128,128]{3,2,1,0:T(8,128)(2,1)S(1)}, bf16[8,2,128,128]{3,2,1,0:T(8,128)(2,1)S(1)}, u32[]{:S(2)}, u32[]{:S(2)}) collective-permute-start(bf16[8,2,128,128]{3,2,1,0:T(8,128)(2,1)S(1)} %pad_maximum_fusion), channel_id=1, source_target_pairs={{0,1},{1,0},{2,3},{3,2},{4,5},{5,4},{6,7},{7,6},{8,9},{9,8},{10,11... | collective-permute-start | bytes 1572872 | tf_op jit(solution)/shard_map/ppermute | solution.py:31
  58.3 7.3 %collective-permute-start.6 = (f32[2,128,128]{2,1,0:T(8,128)S(1)}, f32[2,128,128]{2,1,0:T(8,128)S(1)}, u32[]{:S(2)}, u32[]{:S(2)}) collective-permute-start(f32[2,128,128]{2,1,0:T(8,128)S(1)} %slice_bitcast_fusion.4), channel_id=1, source_target_pairs={{0,8},{1,9},{2,10},{3,11},{4,12},{5,13},{6,14},{7,15},{8,0},{9,1},... | collective-permute-start | bytes 393224 | tf_op jit(solution)/shard_map/ppermute | solution.py:31
  60.8 5.5 %copy-start.1 = (bf16[16,2,128,128]{3,2,1,0:T(8,128)(2,1)}, bf16[16,2,128,128]{3,2,1,0:T(8,128)(2,1)S(1)}, u32[]{:S(2)}) copy-start(bf16[16,2,128,128]{3,2,1,0:T(8,128)(2,1)S(1)} %constant_dynamic-update-slice_fusion) | copy-start | bytes 3145732
  66.3 7.3 %copy-start.2 = (f32[2,128,128]{2,1,0:T(8,128)S(1)}, f32[2,128,128]{2,1,0:T(8,128)}, u32[]{:S(2)}) copy-start(f32[2,128,128]{2,1,0:T(8,128)} %fusion.4.dep_ref) | copy-start | bytes 393220
  66.3 7.3 %copy-start.5 = (bf16[128,256]{1,0:T(8,128)(2,1)S(1)}, bf16[128,256]{1,0:T(8,128)(2,1)}, u32[]{:S(2)}) copy-start(bf16[128,256]{1,0:T(8,128)(2,1)} %param.12) | copy-start | bytes 196612
  70.9 1.4 %collective-permute-start.9 = (f32[2,128,128]{2,1,0:T(8,128)S(1)}, f32[2,128,128]{2,1,0:T(8,128)S(1)}, u32[]{:S(2)}, u32[]{:S(2)}) collective-permute-start(f32[2,128,128]{2,1,0:T(8,128)S(1)} %slice.53), channel_id=1, source_target_pairs={{0,16},{16,0},{1,17},{17,1},{2,18},{18,2},{3,19},{19,3},{4,20},{20... | collective-permute-start | bytes 393224 | tf_op jit(solution)/shard_map/ppermute | solution.py:36

commit v8 on v3

--- a/solution.py
+++ b/solution.py
@@ -13,7 +13,7 @@
 
 def _orders(nb):
     if nb == 4:
-        return ((0, 1, 2, 3), (2, 0, 1, 3)), ((3, 0, 1, 2), (3, 2, 0, 1))
+        return ((0, 1, 2, 3), (2, 0, 1, 3)), ((3, 0, 1, 2), (3, 0, 1, 2))
     rs = tuple(range(nb))
     return (rs, rs), (rs[::-1], rs[::-1])
 

time: 62.8 us -> 68 us (1.083); the launches traced: 63.7 us -> 68.2 us
  starting transfers between devices: 17.4 us -> 19.5 us
  waiting for transfers between devices: 23.6 us -> 25.1 us
  Pallas kernels: 7.53 us -> 8.47 us
    ppermute x8, starting transfers between devices: 15.7 us -> 18.9 us  [_swap_col(): return lax.ppermute(x, ('row', 'col'), perm)]
    ppermute x8, waiting for transfers between devices: 23.6 us -> 25.1 us  [_swap_col(): return lax.ppermute(x, ('row', 'col'), perm)]
    ppermute x2, starting transfers between devices: 1.7 us -> 0.52 us  [_swap(): return lax.ppermute(x, axis, perm)]
  transfers between devices with their start and end apart: 10 -> 10, of which waited for: 6 -> 6; matrix products, arithmetic and copies ran while one was open for 21% -> 20% of each run, Pallas kernels for 12% -> 12%
where the time goes in v8:
time: 68 us; the launch traced here: 68.2 us
  waiting for transfers between devices  25.1 us (37%)
  starting transfers between devices  19.5 us (29%)
  other arithmetic  9.72 us (14%)
  Pallas kernels  8.47 us (12%)
  local copies, waits for them, and re-layouts  3.42 us (5%)
  matrix products  1.16 us (2%)
  between operations  0.84 us (1%)
    ppermute x8, waiting for transfers between devices, _swap_col(): return lax.ppermute(x, ('row', 'col'), perm)  25.1 us
    ppermute x8, starting transfers between devices, _swap_col(): return lax.ppermute(x, ('row', 'col'), perm)  18.9 us
    pallas_call x1, Pallas kernels, along_call(): pl.pallas_call(kernel, grid_spec=spec, out_shape=jax.ShapeDtypeStruct((nr...  4.44 us
    pallas_call x1, Pallas kernels, against_call(): pl.pallas_call(kernel, grid_spec=spec, out_shape=jax.ShapeDtypeStruct((nc...  4.03 us
    another operation x7, other arithmetic, gather_col(): have = jnp.stack([lo, hi], axis=0).reshape((-1,) + have.shape[1:])  3.12 us
    another operation x2, other arithmetic, gather_row(): have = jnp.stack([lo, hi], axis=0).reshape((-1,) + have.shape[1:])  1.51 us
    add x4, other arithmetic, scatter_sum_col(): keep + _swap_col(other, row_size, col_size, (order[0][t], order[1][t]))  1.44 us
    squeeze x4, local copies, waits for them, and re-layouts, scatter_sum_col(): other = lax.dynamic_index_in_dim(data, 1 - mine, axis=0, keepdims=False)  1.38 us
  transfers between devices with their start and end apart: 10, of which 6 were waited for; matrix products, arithmetic and copies ran while one was open for 20% of the time, Pallas kernels for 12%

profile of v8, /device:TPU:0, one launch (start us, length us, event | category | flops | bytes accessed | tf_op | source)
XLA Modules:
  0.0 68.2 jit_solution(17217865602647045865)
XLA Ops:
  0.0 0.5 collective-permute-start
  0.5 3.7 %collective-permute-start.5 = (bf16[1,2,128,128]{2,3,1,0:T(8,128)(2,1)}, bf16[1,2,128,128]{2,3,1,0:T(8,128)(2,1)S(1)}, u32[]{:S(2)}, u32[]{:S(2)}) collective-permute-start(bf16[1,2,128,128]{2,3,1,0:T(8,128)(2,1)} %bitcast.98), channel_id=1, source_target_pairs={{0,8},{1,9},{2,10},{3,11},{4,12},{5,13},{6,14},{7,15},{8,0},{9,1},... | collective-permute-start | bytes 196616 | tf_op jit(solution)/shard_map/ppermute | solution.py:31
  4.1 1.2 %multiply_add_fusion.1 = (s32[128]{0:T(128)}, s32[128]{0:T(128)S(1)}, s32[128]{0:T(128)S(1)}) fusion(s32[]{:T(128)S(6)} %select_n.143, s32[]{:T(128)S(6)} %select_n.142, s32[]{:T(128)S(6)} %select_n.141, s32[1,1,128]{2,1,0:T(1,128)} %param.9), kind=kLoop, calls=%fused_computation.36 | loop fusion | flops 4736 | bytes 2060 | tf_op jit(solution)/shard_map/add | solution.py:223
  5.3 1.2 %clamp_bitcast_fusion.cols_ref = s32[128]{0:T(128)} fusion(s32[1,1,128]{2,1,0:T(1,128)} %param.10), kind=kLoop, calls=%fused_computation.35 | loop fusion | flops 128 | bytes 1024 | tf_op jit(solution)/shard_map/jit(clip)/min | solution.py:210
  7.2 1.2 %collective-permute-done.5 = bf16[1,2,128,128]{2,3,1,0:T(8,128)(2,1)S(1)} collective-permute-done((bf16[1,2,128,128]{2,3,1,0:T(8,128)(2,1)}, bf16[1,2,128,128]{2,3,1,0:T(8,128)(2,1)S(1)}, u32[]{:S(2)}, u32[]{:S(2)}) %collective-permute-start.5) | collective-permute-done | bytes 65568 | tf_op jit(solution)/shard_map/ppermute | solution.py:31
  8.4 0.9 %select_bitcast_fusion.7 = (bf16[1,1,2,128,128]{3,4,2,1,0:T(8,128)(2,1)S(1)}, bf16[1,1,2,128,128]{3,4,2,1,0:T(8,128)(2,1)S(1)}) fusion(bf16[1,2,128,128]{2,3,1,0:T(8,128)(2,1)} %bitcast.99, bf16[1,2,128,128]{2,3,1,0:T(8,128)(2,1)S(1)} %collective-permute-done.5, pred[]{:T(512)S(6)} %eq.23), kind=kLoop, calls=%fused_computation.23 | loop fusion | flops 65536 | bytes 262145 | tf_op jit(solution)/shard_map/stack | solution.py:90
  9.3 0.7 maximum_bitcast_fusion
  9.9 1.5 %collective-permute-start.6 = (bf16[2,2,128,128]{2,3,1,0:T(8,128)(2,1)}, bf16[2,2,128,128]{2,3,1,0:T(8,128)(2,1)S(1)}, u32[]{:S(2)}, u32[]{:S(2)}) collective-permute-start(bf16[2,2,128,128]{2,3,1,0:T(8,128)(2,1)} %maximum_bitcast_fusion), channel_id=1, source_target_pairs={{0,1},{1,0},{2,3},{3,2},{4,5},{5,4},{6,7},{7,6},{8,9},{9,8},{10,11... | collective-permute-start | bytes 393224 | tf_op jit(solution)/shard_map/ppermute | solution.py:31
  11.5 0.9 %select_bitcast_fusion.9 = (bf16[1,1,256,128]{3,2,1,0:T(8,128)(2,1)S(1)}, bf16[1,1,256,128]{3,2,1,0:T(8,128)(2,1)S(1)}) fusion(bf16[1,256,128]{2,1,0:T(8,128)(2,1)S(1)} %collective-permute-done, pred[]{:T(512)S(6)} %eq.19, bf16[256,128]{1,0:T(8,128)(2,1)} %param.7), kind=kLoop, calls=%fused_computation.25 | loop fusion | flops 65536 | bytes 262145 | tf_op jit(solution)/shard_map/stack | solution.py:52
  12.3 0.7 pad_maximum_fusion.3
  13.0 4.4 %shard_map.73 = f32[32,128,128]{2,1,0:T(8,128)} custom-call(s32[128]{0:T(128)} %get-tuple-element.5.rows_ref, s32[128]{0:T(128)} %clamp_bitcast_fusion.cols_ref, s32[1]{0:T(128)} %bitcast.2.cnt_ref, bf16[128,128,128]{2,1,0:T(8,128)(2,1)} %bitcast.86, bf16[4,128,128]{2,1,0:T(8,128)(2,1)} %bitcast.95), custom_call_target="tpu_custom_call" | custom-call | tf_op jit(solution)/shard_map/pallas_call | solution.py:147
  17.5 1.3 %dynamic-slice_bitcast_fusion = f32[2,2,2,2,128,128]{5,4,3,2,1,0:T(8,128)S(1)} fusion(f32[2,2,2,2,2,128,128]{6,5,4,3,2,1,0:T(8,128)} %bitcast.88, s32[]{:T(128)S(6)} %select_n.149), kind=kLoop, calls=%fused_computation.4 | loop fusion | bytes 2097156 | tf_op jit(solution)/shard_map/jit(dynamic_index_in_dim)/squeeze | solution.py:103
  18.8 2.3 %collective-permute-start.1 = (f32[2,2,2,2,128,128]{5,4,3,2,1,0:T(8,128)S(1)}, f32[2,2,2,2,128,128]{5,4,3,2,1,0:T(8,128)}, u32[]{:S(2)}, u32[]{:S(2)}) collective-permute-start(f32[2,2,2,2,128,128]{5,4,3,2,1,0:T(8,128)S(1)} %dynamic-slice_bitcast_fusion), channel_id=1, source_target_pairs={{0,1},{1,0},{2,3},{3,2},{4,5},{5,4},{6,7},{7,6},{8,9},{9,8},{10,11... | collective-permute-start | bytes 3145736 | tf_op jit(solution)/shard_map/ppermute | solution.py:31
  21.1 0.9 %copy.12 = bf16[4,2,128,128]{3,2,1,0:T(8,128)(2,1)} copy(bf16[4,2,128,128]{2,3,1,0:T(8,128)(2,1)S(1)} %bitcast.93) | data formatting | bytes 524288 | tf_op jit(solution)/shard_map/reshape | solution.py:90
  21.9 0.5 collective-permute-start.7
  22.5 6.1 %collective-permute-done.7 = bf16[4,2,128,128]{3,2,1,0:T(8,128)(2,1)S(1)} collective-permute-done((bf16[4,2,128,128]{3,2,1,0:T(8,128)(2,1)}, bf16[4,2,128,128]{3,2,1,0:T(8,128)(2,1)S(1)}, u32[]{:S(2)}, u32[]{:S(2)}) %collective-permute-start.7) | collective-permute-done | bytes 262176 | tf_op jit(solution)/shard_map/ppermute | solution.py:31
  28.5 1.0 %select_bitcast_fusion.3 = (bf16[1,4,2,128,128]{4,3,2,1,0:T(8,128)(2,1)S(1)}, bf16[1,4,2,128,128]{4,3,2,1,0:T(8,128)(2,1)S(1)}) fusion(bf16[4,2,128,128]{3,2,1,0:T(8,128)(2,1)} %copy.12, bf16[4,2,128,128]{3,2,1,0:T(8,128)(2,1)S(1)} %collective-permute-done.7, pred[]{:T(512)S(6)} %eq.21), kind=kLoop, calls=%fused_computation.13 | loop fusion | flops 262144 | bytes 1048577 | tf_op jit(solution)/shard_map/stack | solution.py:90
  29.6 0.4 collective-permute-start.8
  30.0 0.5 multiply_add_fusion.rows_ref
  30.5 3.4 %collective-permute-done.1 = f32[2,2,2,2,128,128]{5,4,3,2,1,0:T(8,128)} collective-permute-done((f32[2,2,2,2,128,128]{5,4,3,2,1,0:T(8,128)S(1)}, f32[2,2,2,2,128,128]{5,4,3,2,1,0:T(8,128)}, u32[]{:S(2)}, u32[]{:S(2)}) %collective-permute-start.1) | collective-permute-done | bytes 1048608 | tf_op jit(solution)/shard_map/ppermute | solution.py:31
  33.9 1.3 %bitcast_add_fusion = f32[2,2,2,2,128,128]{5,4,3,2,1,0:T(8,128)S(1)} fusion(f32[2,2,2,2,128,128]{5,4,3,2,1,0:T(8,128)} %collective-permute-done.1, f32[2,2,2,2,2,128,128]{6,5,4,3,2,1,0:T(8,128)S(1)} %bitcast.89, s32[]{:T(128)S(6)} %select_n.148), kind=kLoop, calls=%fused_computation.3 | loop fusion | flops 262144 | bytes 3145732 | tf_op jit(solution)/shard_map/add | solution.py:104
  35.3 2.6 %collective-permute-start.2 = (f32[2,2,2,128,128]{4,3,2,1,0:T(8,128)S(1)}, f32[2,2,2,128,128]{4,3,2,1,0:T(8,128)S(1)}, u32[]{:S(2)}, u32[]{:S(2)}) collective-permute-start(f32[2,2,2,128,128]{4,3,2,1,0:T(8,128)S(1)} %dynamic-slice_bitcast_fusion.1), channel_id=1, source_target_pairs={{0,2},{1,3},{2,0},{3,1},{4,6},{5,7},{6,4},{7,5},{8,10},{9,11},{10,... | collective-permute-start | bytes 1572872 | tf_op jit(solution)/shard_map/ppermute | solution.py:31
  37.9 4.8 %collective-permute-done.8 = bf16[8,2,128,128]{3,2,1,0:T(8,128)(2,1)S(1)} collective-permute-done((bf16[8,2,128,128]{3,2,1,0:T(8,128)(2,1)S(1)}, bf16[8,2,128,128]{3,2,1,0:T(8,128)(2,1)S(1)}, u32[]{:S(2)}, u32[]{:S(2)}) %collective-permute-start.8) | collective-permute-done | bytes 524320 | tf_op jit(solution)/shard_map/ppermute | solution.py:31
  42.8 1.1 %pad_maximum_fusion = bf16[2,8,2,128,128]{4,3,2,1,0:T(8,128)(2,1)} fusion(bf16[1,8,2,128,128]{4,3,2,1,0:T(8,128)(2,1)S(1)} %get-tuple-element.9, bf16[1,8,2,128,128]{4,3,2,1,0:T(8,128)(2,1)S(1)} %get-tuple-element.8), kind=kLoop, calls=%fused_computation.2 | loop fusion | flops 524288 | bytes 2097152 | tf_op jit(solution)/shard_map/stack | solution.py:90
  43.9 4.0 %shard_map.74 = f32[4,128,128]{2,1,0:T(8,128)} custom-call(s32[128]{0:T(128)} %multiply_add_fusion.rows_ref, s32[128]{0:T(128)} %clamp_bitcast_fusion.cols_ref, s32[1]{0:T(128)} %bitcast.2.cnt_ref, bf16[128,128,128]{2,1,0:T(8,128)(2,1)} %bitcast.87, bf16[32,128,128]{2,1,0:T(8,128)(2,1)} %bitcast.90), custom_call_target="tpu_custom_call" | custom-call | tf_op jit(solution)/shard_map/pallas_call | solution.py:189
  47.9 1.0 %constant_dynamic-slice_fusion.1 = (f32[1,2,128,128]{3,2,1,0:T(8,128)S(1)}, f32[1,2,128,128]{3,2,1,0:T(8,128)S(1)}) fusion(f32[2,2,128,128]{3,2,1,0:T(8,128)} %bitcast.92, s32[]{:T(128)S(6)} %select_n.168, s32[]{:T(128)S(6)} %select_n.169), kind=kLoop, calls=%fused_computation.27 | loop fusion | bytes 524296 | tf_op jit(solution)/shard_map/jit(dynamic_index_in_dim)/dynamic_slice | solution.py:71
  49.2 3.5 %collective-permute-start.3 = (f32[2,2,128,128]{3,2,1,0:T(8,128)S(1)}, f32[2,2,128,128]{3,2,1,0:T(8,128)S(1)}, u32[]{:S(2)}, u32[]{:S(2)}) collective-permute-start(f32[2,2,128,128]{3,2,1,0:T(8,128)S(1)} %dynamic-slice_bitcast_fusion.2), channel_id=1, source_target_pairs={{0,4},{1,5},{2,6},{3,7},{4,0},{5,1},{6,2},{7,3},{8,12},{9,13},{10,... | collective-permute-start | bytes 786440 | tf_op jit(solution)/shard_map/ppermute | solution.py:31
  52.9 4.2 %collective-permute-done.3 = f32[2,2,128,128]{3,2,1,0:T(8,128)S(1)} collective-permute-done((f32[2,2,128,128]{3,2,1,0:T(8,128)S(1)}, f32[2,2,128,128]{3,2,1,0:T(8,128)S(1)}, u32[]{:S(2)}, u32[]{:S(2)}) %collective-permute-start.3) | collective-permute-done | bytes 262176 | tf_op jit(solution)/shard_map/ppermute | solution.py:31
  57.2 4.4 %collective-permute-start.4 = (f32[2,128,128]{2,1,0:T(8,128)S(1)}, f32[2,128,128]{2,1,0:T(8,128)S(1)}, u32[]{:S(2)}, u32[]{:S(2)}) collective-permute-start(f32[2,128,128]{2,1,0:T(8,128)S(1)} %dynamic-slice_bitcast_fusion.3), channel_id=1, source_target_pairs={{0,8},{1,9},{2,10},{3,11},{4,12},{5,13},{6,14},{7,15},{8,0},{9,1},... | collective-permute-start | bytes 393224 | tf_op jit(solution)/shard_map/ppermute | solution.py:31
  61.6 0.2 fusion.1
  61.9 5.4 %collective-permute-done.4 = f32[2,128,128]{2,1,0:T(8,128)S(1)} collective-permute-done((f32[2,128,128]{2,1,0:T(8,128)S(1)}, f32[2,128,128]{2,1,0:T(8,128)S(1)}, u32[]{:S(2)}, u32[]{:S(2)}) %collective-permute-start.4) | collective-permute-done | bytes 131104 | tf_op jit(solution)/shard_map/ppermute | solution.py:31
  67.3 0.9 %fusion = bf16[256,256]{1,0:T(8,128)(2,1)} fusion(f32[256,256]{1,0:T(8,128)S(1)} %fusion.1, f32[256,128]{1,0:T(8,128)S(1)} %bitcast.96, bf16[128,256]{1,0:T(8,128)(2,1)S(1)} %copy-done.2), kind=kOutput, calls=%fused_computation.1 | convolution fusion | flops 100794368 | bytes 589824 | tf_op jit(solution)/shard_map/dot_general | solution.py:246
  (24 shorter events, 0.7 us)
Async XLA Ops:
  0.0 61.6 %copy-start = (bf16[128,256]{1,0:T(8,128)(2,1)S(1)}, bf16[128,256]{1,0:T(8,128)(2,1)}, u32[]{:S(2)}) copy-start(bf16[128,256]{1,0:T(8,128)(2,1)} %param.13) | copy-start | bytes 196612
  0.0 11.5 %collective-permute-start = (bf16[1,256,128]{2,1,0:T(8,128)(2,1)}, bf16[1,256,128]{2,1,0:T(8,128)(2,1)S(1)}, u32[]{:S(2)}, u32[]{:S(2)}) collective-permute-start(bf16[1,256,128]{2,1,0:T(8,128)(2,1)} %bitcast.97), channel_id=1, source_target_pairs={{0,16},{16,0},{1,17},{17,1},{2,18},{18,2},{3,19},{19,3},{4,20},{20... | collective-permute-start | bytes 196616 | tf_op jit(solution)/shard_map/ppermute | solution.py:36
  0.5 8.0 %collective-permute-start.5 = (bf16[1,2,128,128]{2,3,1,0:T(8,128)(2,1)}, bf16[1,2,128,128]{2,3,1,0:T(8,128)(2,1)S(1)}, u32[]{:S(2)}, u32[]{:S(2)}) collective-permute-start(bf16[1,2,128,128]{2,3,1,0:T(8,128)(2,1)} %bitcast.98), channel_id=1, source_target_pairs={{0,8},{1,9},{2,10},{3,11},{4,12},{5,13},{6,14},{7,15},{8,0},{9,1},... | collective-permute-start | bytes 196616 | tf_op jit(solution)/shard_map/ppermute | solution.py:31
  9.9 11.1 %collective-permute-start.6 = (bf16[2,2,128,128]{2,3,1,0:T(8,128)(2,1)}, bf16[2,2,128,128]{2,3,1,0:T(8,128)(2,1)S(1)}, u32[]{:S(2)}, u32[]{:S(2)}) collective-permute-start(bf16[2,2,128,128]{2,3,1,0:T(8,128)(2,1)} %maximum_bitcast_fusion), channel_id=1, source_target_pairs={{0,1},{1,0},{2,3},{3,2},{4,5},{5,4},{6,7},{7,6},{8,9},{9,8},{10,11... | collective-permute-start | bytes 393224 | tf_op jit(solution)/shard_map/ppermute | solution.py:31
  18.8 15.2 %copy-start.1 = (f32[32,128,128]{2,1,0:T(8,128)S(1)}, f32[32,128,128]{2,1,0:T(8,128)}, u32[]{:S(2)}) copy-start(f32[32,128,128]{2,1,0:T(8,128)} %shard_map.73) | copy-start | bytes 6291460
  18.8 15.1 %collective-permute-start.1 = (f32[2,2,2,2,128,128]{5,4,3,2,1,0:T(8,128)S(1)}, f32[2,2,2,2,128,128]{5,4,3,2,1,0:T(8,128)}, u32[]{:S(2)}, u32[]{:S(2)}) collective-permute-start(f32[2,2,2,2,128,128]{5,4,3,2,1,0:T(8,128)S(1)} %dynamic-slice_bitcast_fusion), channel_id=1, source_target_pairs={{0,1},{1,0},{2,3},{3,2},{4,5},{5,4},{6,7},{7,6},{8,9},{9,8},{10,11... | collective-permute-start | bytes 3145736 | tf_op jit(solution)/shard_map/ppermute | solution.py:31
  21.9 6.6 %collective-permute-start.7 = (bf16[4,2,128,128]{3,2,1,0:T(8,128)(2,1)}, bf16[4,2,128,128]{3,2,1,0:T(8,128)(2,1)S(1)}, u32[]{:S(2)}, u32[]{:S(2)}) collective-permute-start(bf16[4,2,128,128]{3,2,1,0:T(8,128)(2,1)} %copy.12), channel_id=1, source_target_pairs={{0,2},{1,3},{2,0},{3,1},{4,6},{5,7},{6,4},{7,5},{8,10},{9,11},{10,... | collective-permute-start | bytes 786440 | tf_op jit(solution)/shard_map/ppermute | solution.py:31
  29.6 13.1 %collective-permute-start.8 = (bf16[8,2,128,128]{3,2,1,0:T(8,128)(2,1)S(1)}, bf16[8,2,128,128]{3,2,1,0:T(8,128)(2,1)S(1)}, u32[]{:S(2)}, u32[]{:S(2)}) collective-permute-start(bf16[8,2,128,128]{3,2,1,0:T(8,128)(2,1)S(1)} %bitcast.91), channel_id=1, source_target_pairs={{0,4},{1,5},{2,6},{3,7},{4,0},{5,1},{6,2},{7,3},{8,12},{9,13},{10,... | collective-permute-start | bytes 1572872 | tf_op jit(solution)/shard_map/ppermute | solution.py:31
  35.3 13.8 %collective-permute-start.2 = (f32[2,2,2,128,128]{4,3,2,1,0:T(8,128)S(1)}, f32[2,2,2,128,128]{4,3,2,1,0:T(8,128)S(1)}, u32[]{:S(2)}, u32[]{:S(2)}) collective-permute-start(f32[2,2,2,128,128]{4,3,2,1,0:T(8,128)S(1)} %dynamic-slice_bitcast_fusion.1), channel_id=1, source_target_pairs={{0,2},{1,3},{2,0},{3,1},{4,6},{5,7},{6,4},{7,5},{8,10},{9,11},{10,... | collective-permute-start | bytes 1572872 | tf_op jit(solution)/shard_map/ppermute | solution.py:31
  49.0 18.2 %copy-start.2 = (bf16[128,256]{1,0:T(8,128)(2,1)S(1)}, bf16[128,256]{1,0:T(8,128)(2,1)}, u32[]{:S(2)}) copy-start(bf16[128,256]{1,0:T(8,128)(2,1)} %param.12) | copy-start | bytes 196612
  49.0 3.8 %collective-permute-start.9 = (f32[2,128,128]{1,2,0:T(8,128)S(1)}, f32[2,128,128]{1,2,0:T(8,128)S(1)}, u32[]{:S(2)}, u32[]{:S(2)}) collective-permute-start(f32[2,128,128]{1,2,0:T(8,128)S(1)} %bitcast.100), channel_id=1, source_target_pairs={{0,16},{16,0},{1,17},{17,1},{2,18},{18,2},{3,19},{19,3},{4,20},{20... | collective-permute-start | bytes 393224 | tf_op jit(solution)/shard_map/ppermute | solution.py:36
  49.2 7.9 %collective-permute-start.3 = (f32[2,2,128,128]{3,2,1,0:T(8,128)S(1)}, f32[2,2,128,128]{3,2,1,0:T(8,128)S(1)}, u32[]{:S(2)}, u32[]{:S(2)}) collective-permute-start(f32[2,2,128,128]{3,2,1,0:T(8,128)S(1)} %dynamic-slice_bitcast_fusion.2), channel_id=1, source_target_pairs={{0,4},{1,5},{2,6},{3,7},{4,0},{5,1},{6,2},{7,3},{8,12},{9,13},{10,... | collective-permute-start | bytes 786440 | tf_op jit(solution)/shard_map/ppermute | solution.py:31
  57.2 10.1 %collective-permute-start.4 = (f32[2,128,128]{2,1,0:T(8,128)S(1)}, f32[2,128,128]{2,1,0:T(8,128)S(1)}, u32[]{:S(2)}, u32[]{:S(2)}) collective-permute-start(f32[2,128,128]{2,1,0:T(8,128)S(1)} %dynamic-slice_bitcast_fusion.3), channel_id=1, source_target_pairs={{0,8},{1,9},{2,10},{3,11},{4,12},{5,13},{6,14},{7,15},{8,0},{9,1},... | collective-permute-start | bytes 393224 | tf_op jit(solution)/shard_map/ppermute | solution.py:31

commit v9 on v3

--- a/solution.py
+++ b/solution.py
@@ -109,14 +109,14 @@
     return 32 if slots % 32 == 0 else slots
 
 
-def along_call(rows, cols, cnt, values, group, nrb):
+def along_call(rows, cols, cnt, values, group, nrb, fwd_index):
     slots, side, _ = values.shape
     width = group.shape[-1]
     k = _chunk(slots)
 
     def kernel(rows_ref, cols_ref, cnt_ref, vals_ref, grp_ref, out_ref):
         i = pl.program_id(0)
-        n = cnt_ref[0]
+        n = jnp.clip(cnt_ref[0], 0, slots)
 
         @pl.when(i == 0)
         def _():
@@ -127,12 +127,11 @@
             for t in range(k):
                 s = i * k + t
                 tile = jnp.where(s < n, vals_ref[t], jnp.zeros((side, side), vals_ref.dtype))
-                r = rows_ref[s]
-                c = cols_ref[s]
+                r, c = fwd_index(rows_ref[s], cols_ref[s])
                 out_ref[r] += jnp.dot(tile, grp_ref[c], preferred_element_type=jnp.float32)
 
     def vals_map(i, rows_ref, cols_ref, cnt_ref):
-        last = jnp.maximum(cnt_ref[0] - 1, 0) // k
+        last = jnp.clip(cnt_ref[0] - 1, 0, slots - 1) // k
         return (jnp.minimum(i, last), 0, 0)
 
     spec = pltpu.PrefetchScalarGridSpec(
@@ -151,14 +150,14 @@
     )(rows, cols, cnt, values, group)
 
 
-def against_call(rows, cols, cnt, values, stripe_t, ncb):
+def against_call(rows, cols, cnt, values, stripe_t, ncb, bwd_index):
     slots, side, _ = values.shape
     width = stripe_t.shape[1]
     k = _chunk(slots)
 
     def kernel(rows_ref, cols_ref, cnt_ref, vals_ref, st_ref, out_ref):
         i = pl.program_id(0)
-        n = cnt_ref[0]
+        n = jnp.clip(cnt_ref[0], 0, slots)
 
         @pl.when(i == 0)
         def _():
@@ -169,12 +168,11 @@
             for t in range(k):
                 s = i * k + t
                 tile = jnp.where(s < n, vals_ref[t], jnp.zeros((side, side), vals_ref.dtype))
-                r = rows_ref[s]
-                c = cols_ref[s]
+                r, c = bwd_index(rows_ref[s], cols_ref[s])
                 out_ref[c] += jnp.dot(st_ref[r], tile, preferred_element_type=jnp.float32)
 
     def vals_map(i, rows_ref, cols_ref, cnt_ref):
-        last = jnp.maximum(cnt_ref[0] - 1, 0) // k
+        last = jnp.clip(cnt_ref[0] - 1, 0, slots - 1) // k
         return (jnp.minimum(i, last), 0, 0)
 
     spec = pltpu.PrefetchScalarGridSpec(
@@ -206,28 +204,37 @@
     ncb = row_size * nbc
     parity = lax.axis_index("row") % 2
 
-    rowblk = jnp.clip(tile_rows[0, 0], 0, nrb - 1)
-    colblk = jnp.clip(tile_cols[0, 0], 0, ncb - 1)
-    cnt = jnp.clip(tile_count[0, 0], 0, slots).reshape(1).astype(jnp.int32)
+    rows = tile_rows.reshape(slots)
+    cols = tile_cols.reshape(slots)
+    cnt = tile_count.reshape(1)
 
     nb = _nbits(col_size)
     if nb is not None:
         rs_order, ag_order = _orders(nb)
+
+    def block_pos(rowblk, order, msb_first):
+        if nb is None:
+            return rowblk
+        par = lax.axis_index("row") % 2
         dest = rowblk // nbc
-        sub = rowblk % nbc
-        rs_pos = jnp.zeros_like(dest)
-        ag_pos = jnp.zeros_like(dest)
+        pos = 0
         for t in range(nb):
-            rs_pos = rs_pos + (((dest >> _pick(parity, rs_order, t)) & 1) << (nb - 1 - t))
-            ag_pos = ag_pos + (((dest >> _pick(parity, ag_order, t)) & 1) << t)
-        rows_fwd = rs_pos * nbc + sub
-        rows_bwd = ag_pos * nbc + sub
-    else:
-        rows_fwd = rowblk
-        rows_bwd = rowblk
+            bit = (dest >> _pick(par, order, t)) & 1
+            pos = pos + (bit << ((nb - 1 - t) if msb_first else t))
+        return pos * nbc + rowblk % nbc
+
+    def fwd_index(r, c):
+        r = jnp.clip(r, 0, nrb - 1)
+        c = jnp.clip(c, 0, ncb - 1)
+        return block_pos(r, rs_order if nb is not None else None, True), c
+
+    def bwd_index(r, c):
+        r = jnp.clip(r, 0, nrb - 1)
+        c = jnp.clip(c, 0, ncb - 1)
+        return block_pos(r, ag_order if nb is not None else None, False), c
 
     group = gather_row(features).reshape(ncb, side, width)
-    fwd_parts = along_call(rows_fwd, colblk, cnt, values, group, nrb)
+    fwd_parts = along_call(rows, cols, cnt, values, group, nrb, fwd_index)
 
     mine_t = jnp.transpose(features.reshape(nbc, side, width), (0, 2, 1))
     if nb is not None:
@@ -237,7 +244,7 @@
         stripe_t = lax.all_gather(mine_t, "col", axis=0, tiled=True)
         along = lax.psum_scatter(fwd_parts, "col", scatter_dimension=0, tiled=True)
 
-    bwd_t = against_call(rows_bwd, colblk, cnt, values, stripe_t, ncb)
+    bwd_t = against_call(rows, cols, cnt, values, stripe_t, ncb, bwd_index)
     against_t = scatter_sum_row(bwd_t)
     against = jnp.transpose(against_t, (0, 2, 1))
 

time: 62.8 us -> 63.7 us (1.014); the launches traced: 63.7 us -> 63.9 us
  other arithmetic: 9.73 us -> 8.73 us
  waiting for transfers between devices: 23.6 us -> 24.6 us
    another operation x7, other arithmetic: 3.13 us -> 5.08 us  [gather_col(): have = jnp.stack([lo, hi], axis=0).reshape((-1,) + have.shape[1:])]
    add x2 -> x0, other arithmetic: 1.72 us -> none  [the longest x1 1.19 us: local(): rows_fwd = rs_pos * nbc + sub]
    ppermute x2, starting transfers between devices: 1.7 us -> 0.07 us  [_swap(): return lax.ppermute(x, axis, perm)]
    ppermute x8, starting transfers between devices: 15.7 us -> 17.2 us  [_swap_col(): return lax.ppermute(x, ('row', 'col'), perm)]
    min x1 -> x0, other arithmetic: 1.25 us -> none  [local(): colblk = jnp.clip(tile_cols[0, 0], 0, ncb - 1)]
    ppermute x8, waiting for transfers between devices: 23.6 us -> 24.6 us  [_swap_col(): return lax.ppermute(x, ('row', 'col'), perm)]
  transfers between devices with their start and end apart: 10 -> 10, of which waited for: 6 -> 6; matrix products, arithmetic and copies ran while one was open for 21% -> 19% of each run, Pallas kernels for 12% -> 12%
where the time goes in v9:
time: 63.7 us; the launch traced here: 63.9 us
  waiting for transfers between devices  24.6 us (39%)
  starting transfers between devices  17.3 us (27%)
  other arithmetic  8.73 us (14%)
  Pallas kernels  7.87 us (12%)
  local copies, waits for them, and re-layouts  3.44 us (5%)
  matrix products  1.16 us (2%)
  between operations  0.81 us (1%)
    ppermute x8, waiting for transfers between devices, _swap_col(): return lax.ppermute(x, ('row', 'col'), perm)  24.6 us
    ppermute x8, starting transfers between devices, _swap_col(): return lax.ppermute(x, ('row', 'col'), perm)  17.2 us
    another operation x7, other arithmetic, gather_col(): have = jnp.stack([lo, hi], axis=0).reshape((-1,) + have.shape[1:])  5.08 us
    pallas_call x1, Pallas kernels, along_call(): pl.pallas_call(kernel, grid_spec=spec, out_shape=jax.ShapeDtypeStruct((nr...  4.16 us
    pallas_call x1, Pallas kernels, against_call(): pl.pallas_call(kernel, grid_spec=spec, out_shape=jax.ShapeDtypeStruct((nc...  3.7 us
    another operation x2, other arithmetic, gather_row(): have = jnp.stack([lo, hi], axis=0).reshape((-1,) + have.shape[1:])  1.52 us
    add x4, other arithmetic, scatter_sum_col(): keep + _swap_col(other, row_size, col_size, (order[0][t], order[1][t]))  1.44 us
    squeeze x4, local copies, waits for them, and re-layouts, scatter_sum_col(): other = lax.dynamic_index_in_dim(data, 1 - mine, axis=0, keepdims=False)  1.38 us
  transfers between devices with their start and end apart: 10, of which 6 were waited for; matrix products, arithmetic and copies ran while one was open for 19% of the time, Pallas kernels for 12%

profile of v9, /device:TPU:0, one launch (start us, length us, event | category | flops | bytes accessed | tf_op | source)
XLA Modules:
  0.0 63.9 jit_solution(15156290272079179718)
XLA Ops:
  0.0 4.0 %collective-permute-start.5 = (bf16[1,2,128,128]{2,3,1,0:T(8,128)(2,1)}, bf16[1,2,128,128]{2,3,1,0:T(8,128)(2,1)S(1)}, u32[]{:S(2)}, u32[]{:S(2)}) collective-permute-start(bf16[1,2,128,128]{2,3,1,0:T(8,128)(2,1)} %bitcast.85), channel_id=1, source_target_pairs={{0,8},{1,9},{2,10},{3,11},{4,12},{5,13},{6,14},{7,15},{8,0},{9,1},... | collective-permute-start | bytes 196616 | tf_op jit(solution)/shard_map/ppermute | solution.py:31
  4.7 3.2 %collective-permute-done.5 = bf16[1,2,128,128]{2,3,1,0:T(8,128)(2,1)S(1)} collective-permute-done((bf16[1,2,128,128]{2,3,1,0:T(8,128)(2,1)}, bf16[1,2,128,128]{2,3,1,0:T(8,128)(2,1)S(1)}, u32[]{:S(2)}, u32[]{:S(2)}) %collective-permute-start.5) | collective-permute-done | bytes 65568 | tf_op jit(solution)/shard_map/ppermute | solution.py:31
  7.9 0.9 %select_bitcast_fusion.7 = (bf16[1,1,2,128,128]{3,4,2,1,0:T(8,128)(2,1)S(1)}, bf16[1,1,2,128,128]{3,4,2,1,0:T(8,128)(2,1)S(1)}) fusion(bf16[1,2,128,128]{2,3,1,0:T(8,128)(2,1)} %bitcast.87, bf16[1,2,128,128]{2,3,1,0:T(8,128)(2,1)S(1)} %collective-permute-done.5, pred[]{:T(512)S(6)} %eq.38), kind=kLoop, calls=%fused_computation.23 | loop fusion | flops 65536 | bytes 262145 | tf_op jit(solution)/shard_map/stack | solution.py:90
  8.8 0.7 %maximum_bitcast_fusion = bf16[2,2,128,128]{2,3,1,0:T(8,128)(2,1)} fusion(bf16[1,1,2,128,128]{3,4,2,1,0:T(8,128)(2,1)S(1)} %get-tuple-element.16, bf16[1,1,2,128,128]{3,4,2,1,0:T(8,128)(2,1)S(1)} %get-tuple-element.15), kind=kLoop, calls=%fused_computation.16 | loop fusion | flops 65536 | bytes 262144 | tf_op jit(solution)/shard_map/reshape | solution.py:90
  9.4 1.7 %collective-permute-start.6 = (bf16[2,2,128,128]{2,3,1,0:T(8,128)(2,1)}, bf16[2,2,128,128]{2,3,1,0:T(8,128)(2,1)S(1)}, u32[]{:S(2)}, u32[]{:S(2)}) collective-permute-start(bf16[2,2,128,128]{2,3,1,0:T(8,128)(2,1)} %maximum_bitcast_fusion), channel_id=1, source_target_pairs={{0,1},{1,0},{2,3},{3,2},{4,5},{5,4},{6,7},{7,6},{8,9},{9,8},{10,11... | collective-permute-start | bytes 393224 | tf_op jit(solution)/shard_map/ppermute | solution.py:31
  11.1 0.9 %select_bitcast_fusion.9 = (bf16[1,1,256,128]{3,2,1,0:T(8,128)(2,1)S(1)}, bf16[1,1,256,128]{3,2,1,0:T(8,128)(2,1)S(1)}) fusion(bf16[1,256,128]{2,1,0:T(8,128)(2,1)S(1)} %collective-permute-done, pred[]{:T(512)S(6)} %eq.15, bf16[256,128]{1,0:T(8,128)(2,1)} %param.7), kind=kLoop, calls=%fused_computation.25 | loop fusion | flops 65536 | bytes 262145 | tf_op jit(solution)/shard_map/stack | solution.py:52
  12.0 0.7 %pad_maximum_fusion.3 = bf16[2,1,256,128]{3,2,1,0:T(8,128)(2,1)} fusion(bf16[1,1,256,128]{3,2,1,0:T(8,128)(2,1)S(1)} %get-tuple-element.14, bf16[1,1,256,128]{3,2,1,0:T(8,128)(2,1)S(1)} %get-tuple-element.13), kind=kLoop, calls=%fused_computation.15 | loop fusion | flops 65536 | bytes 262144 | tf_op jit(solution)/shard_map/stack | solution.py:52
  12.7 4.2 %shard_map.73 = f32[32,128,128]{2,1,0:T(8,128)} custom-call(s32[128]{0:T(128)} %bitcast.89, s32[128]{0:T(128)} %bitcast.91, s32[1]{0:T(128)} %bitcast.73.cnt_ref, bf16[128,128,128]{2,1,0:T(8,128)(2,1)} %bitcast.75, bf16[4,128,128]{2,1,0:T(8,128)(2,1)} %bitcast.83), custom_call_target="tpu_custom_call" | custom-call | tf_op jit(solution)/shard_map/pallas_call | solution.py:146
  16.8 1.3 %dynamic-slice_bitcast_fusion = f32[2,2,2,2,128,128]{5,4,3,2,1,0:T(8,128)S(1)} fusion(f32[2,2,2,2,2,128,128]{6,5,4,3,2,1,0:T(8,128)} %bitcast.77, s32[]{:T(128)S(6)} %select_n.124), kind=kLoop, calls=%fused_computation.4 | loop fusion | bytes 2097156 | tf_op jit(solution)/shard_map/jit(dynamic_index_in_dim)/squeeze | solution.py:103
  18.1 1.0 %collective-permute-start.1 = (f32[2,2,2,2,128,128]{5,4,3,2,1,0:T(8,128)S(1)}, f32[2,2,2,2,128,128]{5,4,3,2,1,0:T(8,128)}, u32[]{:S(2)}, u32[]{:S(2)}) collective-permute-start(f32[2,2,2,2,128,128]{5,4,3,2,1,0:T(8,128)S(1)} %dynamic-slice_bitcast_fusion), channel_id=1, source_target_pairs={{0,1},{1,0},{2,3},{3,2},{4,5},{5,4},{6,7},{7,6},{8,9},{9,8},{10,11... | collective-permute-start | bytes 3145736 | tf_op jit(solution)/shard_map/ppermute | solution.py:31
  19.2 0.9 %copy.12 = bf16[4,2,128,128]{3,2,1,0:T(8,128)(2,1)} copy(bf16[4,2,128,128]{2,3,1,0:T(8,128)(2,1)S(1)} %bitcast.81) | data formatting | bytes 524288 | tf_op jit(solution)/shard_map/reshape | solution.py:90
  20.1 1.7 %collective-permute-start.7 = (bf16[4,2,128,128]{3,2,1,0:T(8,128)(2,1)}, bf16[4,2,128,128]{3,2,1,0:T(8,128)(2,1)S(1)}, u32[]{:S(2)}, u32[]{:S(2)}) collective-permute-start(bf16[4,2,128,128]{3,2,1,0:T(8,128)(2,1)} %copy.12), channel_id=1, source_target_pairs={{0,2},{1,3},{2,0},{3,1},{4,6},{5,7},{6,4},{7,5},{8,10},{9,11},{10,... | collective-permute-start | bytes 786440 | tf_op jit(solution)/shard_map/ppermute | solution.py:31
  21.8 4.9 %collective-permute-done.7 = bf16[4,2,128,128]{3,2,1,0:T(8,128)(2,1)S(1)} collective-permute-done((bf16[4,2,128,128]{3,2,1,0:T(8,128)(2,1)}, bf16[4,2,128,128]{3,2,1,0:T(8,128)(2,1)S(1)}, u32[]{:S(2)}, u32[]{:S(2)}) %collective-permute-start.7) | collective-permute-done | bytes 262176 | tf_op jit(solution)/shard_map/ppermute | solution.py:31
  26.7 1.0 %select_bitcast_fusion.3 = (bf16[1,4,2,128,128]{4,3,2,1,0:T(8,128)(2,1)S(1)}, bf16[1,4,2,128,128]{4,3,2,1,0:T(8,128)(2,1)S(1)}) fusion(bf16[4,2,128,128]{3,2,1,0:T(8,128)(2,1)} %copy.12, bf16[4,2,128,128]{3,2,1,0:T(8,128)(2,1)S(1)} %collective-permute-done.7, pred[]{:T(512)S(6)} %eq.18), kind=kLoop, calls=%fused_computation.13 | loop fusion | flops 262144 | bytes 1048577 | tf_op jit(solution)/shard_map/stack | solution.py:90
  27.7 0.8 %pad_maximum_fusion.1 = bf16[2,4,2,128,128]{4,3,2,1,0:T(8,128)(2,1)} fusion(bf16[1,4,2,128,128]{4,3,2,1,0:T(8,128)(2,1)S(1)} %get-tuple-element.8, bf16[1,4,2,128,128]{4,3,2,1,0:T(8,128)(2,1)S(1)} %get-tuple-element.7), kind=kLoop, calls=%fused_computation.5 | loop fusion | flops 262144 | bytes 1048576 | tf_op jit(solution)/shard_map/stack | solution.py:90
  28.5 2.6 %collective-permute-start.8 = (bf16[8,2,128,128]{3,2,1,0:T(8,128)(2,1)}, bf16[8,2,128,128]{3,2,1,0:T(8,128)(2,1)}, u32[]{:S(2)}, u32[]{:S(2)}) collective-permute-start(bf16[8,2,128,128]{3,2,1,0:T(8,128)(2,1)} %bitcast.31), channel_id=1, source_target_pairs={{0,4},{1,5},{2,6},{3,7},{4,0},{5,1},{6,2},{7,3},{8,12},{9,13},{10,... | collective-permute-start | bytes 1572872 | tf_op jit(solution)/shard_map/ppermute | solution.py:31
  31.1 5.0 %collective-permute-done.1 = f32[2,2,2,2,128,128]{5,4,3,2,1,0:T(8,128)} collective-permute-done((f32[2,2,2,2,128,128]{5,4,3,2,1,0:T(8,128)S(1)}, f32[2,2,2,2,128,128]{5,4,3,2,1,0:T(8,128)}, u32[]{:S(2)}, u32[]{:S(2)}) %collective-permute-start.1) | collective-permute-done | bytes 1048608 | tf_op jit(solution)/shard_map/ppermute | solution.py:31
  36.1 1.3 %bitcast_add_fusion = f32[2,2,2,2,128,128]{5,4,3,2,1,0:T(8,128)S(1)} fusion(f32[2,2,2,2,128,128]{5,4,3,2,1,0:T(8,128)} %collective-permute-done.1, f32[2,2,2,2,2,128,128]{6,5,4,3,2,1,0:T(8,128)S(1)} %bitcast.78, s32[]{:T(128)S(6)} %select_n.123), kind=kLoop, calls=%fused_computation.3 | loop fusion | flops 262144 | bytes 3145732 | tf_op jit(solution)/shard_map/add | solution.py:104
  37.5 1.4 %collective-permute-start.2 = (f32[2,2,2,128,128]{4,3,2,1,0:T(8,128)S(1)}, f32[2,2,2,128,128]{4,3,2,1,0:T(8,128)S(1)}, u32[]{:S(2)}, u32[]{:S(2)}) collective-permute-start(f32[2,2,2,128,128]{4,3,2,1,0:T(8,128)S(1)} %dynamic-slice_bitcast_fusion.1), channel_id=1, source_target_pairs={{0,2},{1,3},{2,0},{3,1},{4,6},{5,7},{6,4},{7,5},{8,10},{9,11},{10,... | collective-permute-start | bytes 1572872 | tf_op jit(solution)/shard_map/ppermute | solution.py:31
  38.9 1.3 %select_bitcast_fusion.1 = (bf16[1,8,2,128,128]{4,3,2,1,0:T(8,128)(2,1)S(1)}, bf16[1,8,2,128,128]{4,3,2,1,0:T(8,128)(2,1)S(1)}) fusion(bf16[8,2,128,128]{3,2,1,0:T(8,128)(2,1)} %collective-permute-done.8, pred[]{:T(512)S(6)} %eq.17, bf16[2,4,2,128,128]{4,3,2,1,0:T(8,128)(2,1)} %pad_maximum_fusion.1), kind=kLoop, calls=%fused_computation.8 | loop fusion | flops 524288 | bytes 2097153 | tf_op jit(solution)/shard_map/stack | solution.py:90
  40.2 1.1 %pad_maximum_fusion = bf16[2,8,2,128,128]{4,3,2,1,0:T(8,128)(2,1)} fusion(bf16[1,8,2,128,128]{4,3,2,1,0:T(8,128)(2,1)S(1)} %get-tuple-element.6, bf16[1,8,2,128,128]{4,3,2,1,0:T(8,128)(2,1)S(1)} %get-tuple-element.5), kind=kLoop, calls=%fused_computation.2 | loop fusion | flops 524288 | bytes 2097152 | tf_op jit(solution)/shard_map/stack | solution.py:90
  41.2 3.7 %shard_map.74 = f32[4,128,128]{2,1,0:T(8,128)} custom-call(s32[128]{0:T(128)} %bitcast.90, s32[128]{0:T(128)} %bitcast.92, s32[1]{0:T(128)} %bitcast.74.cnt_ref, bf16[128,128,128]{2,1,0:T(8,128)(2,1)} %bitcast.76, bf16[32,128,128]{2,1,0:T(8,128)(2,1)} %bitcast.79), custom_call_target="tpu_custom_call" | custom-call | tf_op jit(solution)/shard_map/pallas_call | solution.py:187
  44.9 1.0 %constant_dynamic-slice_fusion.1 = (f32[1,2,128,128]{3,2,1,0:T(8,128)S(1)}, f32[1,2,128,128]{3,2,1,0:T(8,128)S(1)}) fusion(f32[2,2,128,128]{3,2,1,0:T(8,128)} %bitcast.80, s32[]{:T(128)S(6)} %select_n.145, s32[]{:T(128)S(6)} %select_n.146), kind=kLoop, calls=%fused_computation.27 | loop fusion | bytes 524296 | tf_op jit(solution)/shard_map/jit(dynamic_index_in_dim)/dynamic_slice | solution.py:71
  45.9 0.1 copy.15
  46.1 0.6 collective-permute-done.2
  46.8 3.4 %collective-permute-start.3 = (f32[2,2,128,128]{3,2,1,0:T(8,128)S(1)}, f32[2,2,128,128]{3,2,1,0:T(8,128)S(1)}, u32[]{:S(2)}, u32[]{:S(2)}) collective-permute-start(f32[2,2,128,128]{3,2,1,0:T(8,128)S(1)} %dynamic-slice_bitcast_fusion.2), channel_id=1, source_target_pairs={{0,4},{1,5},{2,6},{3,7},{4,0},{5,1},{6,2},{7,3},{8,12},{9,13},{10,... | collective-permute-start | bytes 786440 | tf_op jit(solution)/shard_map/ppermute | solution.py:31
  50.2 0.1 copy.14
  50.3 4.2 %collective-permute-done.3 = f32[2,2,128,128]{3,2,1,0:T(8,128)S(1)} collective-permute-done((f32[2,2,128,128]{3,2,1,0:T(8,128)S(1)}, f32[2,2,128,128]{3,2,1,0:T(8,128)S(1)}, u32[]{:S(2)}, u32[]{:S(2)}) %collective-permute-start.3) | collective-permute-done | bytes 262176 | tf_op jit(solution)/shard_map/ppermute | solution.py:31
  54.6 1.4 %collective-permute-start.4 = (f32[2,128,128]{2,1,0:T(8,128)S(1)}, f32[2,128,128]{2,1,0:T(8,128)S(1)}, u32[]{:S(2)}, u32[]{:S(2)}) collective-permute-start(f32[2,128,128]{2,1,0:T(8,128)S(1)} %dynamic-slice_bitcast_fusion.3), channel_id=1, source_target_pairs={{0,8},{1,9},{2,10},{3,11},{4,12},{5,13},{6,14},{7,15},{8,0},{9,1},... | collective-permute-start | bytes 393224 | tf_op jit(solution)/shard_map/ppermute | solution.py:31
  55.9 0.2 fusion.1
  56.2 6.8 %collective-permute-done.4 = f32[2,128,128]{2,1,0:T(8,128)S(1)} collective-permute-done((f32[2,128,128]{2,1,0:T(8,128)S(1)}, f32[2,128,128]{2,1,0:T(8,128)S(1)}, u32[]{:S(2)}, u32[]{:S(2)}) %collective-permute-start.4) | collective-permute-done | bytes 131104 | tf_op jit(solution)/shard_map/ppermute | solution.py:31
  63.0 0.9 %fusion = bf16[256,256]{1,0:T(8,128)(2,1)} fusion(f32[256,256]{1,0:T(8,128)S(1)} %fusion.1, f32[256,128]{1,0:T(8,128)S(1)} %bitcast.84, bf16[128,256]{1,0:T(8,128)(2,1)S(1)} %copy-done.2), kind=kOutput, calls=%fused_computation.1 | convolution fusion | flops 100794368 | bytes 589824 | tf_op jit(solution)/shard_map/dot_general | solution.py:253
  (21 shorter events, 0.4 us)
Async XLA Ops:
  0.0 55.9 %copy-start = (bf16[128,256]{1,0:T(8,128)(2,1)S(1)}, bf16[128,256]{1,0:T(8,128)(2,1)}, u32[]{:S(2)}) copy-start(bf16[128,256]{1,0:T(8,128)(2,1)} %param.13) | copy-start | bytes 196612
  0.0 7.9 %collective-permute-start.5 = (bf16[1,2,128,128]{2,3,1,0:T(8,128)(2,1)}, bf16[1,2,128,128]{2,3,1,0:T(8,128)(2,1)S(1)}, u32[]{:S(2)}, u32[]{:S(2)}) collective-permute-start(bf16[1,2,128,128]{2,3,1,0:T(8,128)(2,1)} %bitcast.85), channel_id=1, source_target_pairs={{0,8},{1,9},{2,10},{3,11},{4,12},{5,13},{6,14},{7,15},{8,0},{9,1},... | collective-permute-start | bytes 196616 | tf_op jit(solution)/shard_map/ppermute | solution.py:31
  4.0 7.1 %collective-permute-start = (bf16[1,256,128]{2,1,0:T(8,128)(2,1)}, bf16[1,256,128]{2,1,0:T(8,128)(2,1)S(1)}, u32[]{:S(2)}, u32[]{:S(2)}) collective-permute-start(bf16[1,256,128]{2,1,0:T(8,128)(2,1)} %bitcast.86), channel_id=1, source_target_pairs={{0,16},{16,0},{1,17},{17,1},{2,18},{18,2},{3,19},{19,3},{4,20},{20... | collective-permute-start | bytes 196616 | tf_op jit(solution)/shard_map/ppermute | solution.py:36
  9.4 9.7 %collective-permute-start.6 = (bf16[2,2,128,128]{2,3,1,0:T(8,128)(2,1)}, bf16[2,2,128,128]{2,3,1,0:T(8,128)(2,1)S(1)}, u32[]{:S(2)}, u32[]{:S(2)}) collective-permute-start(bf16[2,2,128,128]{2,3,1,0:T(8,128)(2,1)} %maximum_bitcast_fusion), channel_id=1, source_target_pairs={{0,1},{1,0},{2,3},{3,2},{4,5},{5,4},{6,7},{7,6},{8,9},{9,8},{10,11... | collective-permute-start | bytes 393224 | tf_op jit(solution)/shard_map/ppermute | solution.py:31
  18.1 17.9 %copy-start.1 = (f32[32,128,128]{2,1,0:T(8,128)S(1)}, f32[32,128,128]{2,1,0:T(8,128)}, u32[]{:S(2)}) copy-start(f32[32,128,128]{2,1,0:T(8,128)} %shard_map.73) | copy-start | bytes 6291460
  18.1 17.9 %collective-permute-start.1 = (f32[2,2,2,2,128,128]{5,4,3,2,1,0:T(8,128)S(1)}, f32[2,2,2,2,128,128]{5,4,3,2,1,0:T(8,128)}, u32[]{:S(2)}, u32[]{:S(2)}) collective-permute-start(f32[2,2,2,2,128,128]{5,4,3,2,1,0:T(8,128)S(1)} %dynamic-slice_bitcast_fusion), channel_id=1, source_target_pairs={{0,1},{1,0},{2,3},{3,2},{4,5},{5,4},{6,7},{7,6},{8,9},{9,8},{10,11... | collective-permute-start | bytes 3145736 | tf_op jit(solution)/shard_map/ppermute | solution.py:31
  20.1 6.6 %collective-permute-start.7 = (bf16[4,2,128,128]{3,2,1,0:T(8,128)(2,1)}, bf16[4,2,128,128]{3,2,1,0:T(8,128)(2,1)S(1)}, u32[]{:S(2)}, u32[]{:S(2)}) collective-permute-start(bf16[4,2,128,128]{3,2,1,0:T(8,128)(2,1)} %copy.12), channel_id=1, source_target_pairs={{0,2},{1,3},{2,0},{3,1},{4,6},{5,7},{6,4},{7,5},{8,10},{9,11},{10,... | collective-permute-start | bytes 786440 | tf_op jit(solution)/shard_map/ppermute | solution.py:31
  28.5 10.4 %collective-permute-start.8 = (bf16[8,2,128,128]{3,2,1,0:T(8,128)(2,1)}, bf16[8,2,128,128]{3,2,1,0:T(8,128)(2,1)}, u32[]{:S(2)}, u32[]{:S(2)}) collective-permute-start(bf16[8,2,128,128]{3,2,1,0:T(8,128)(2,1)} %bitcast.31), channel_id=1, source_target_pairs={{0,4},{1,5},{2,6},{3,7},{4,0},{5,1},{6,2},{7,3},{8,12},{9,13},{10,... | collective-permute-start | bytes 1572872 | tf_op jit(solution)/shard_map/ppermute | solution.py:31
  37.5 9.2 %collective-permute-start.2 = (f32[2,2,2,128,128]{4,3,2,1,0:T(8,128)S(1)}, f32[2,2,2,128,128]{4,3,2,1,0:T(8,128)S(1)}, u32[]{:S(2)}, u32[]{:S(2)}) collective-permute-start(f32[2,2,2,128,128]{4,3,2,1,0:T(8,128)S(1)} %dynamic-slice_bitcast_fusion.1), channel_id=1, source_target_pairs={{0,2},{1,3},{2,0},{3,1},{4,6},{5,7},{6,4},{7,5},{8,10},{9,11},{10,... | collective-permute-start | bytes 1572872 | tf_op jit(solution)/shard_map/ppermute | solution.py:31
  46.0 17.0 %copy-start.2 = (bf16[128,256]{1,0:T(8,128)(2,1)S(1)}, bf16[128,256]{1,0:T(8,128)(2,1)}, u32[]{:S(2)}) copy-start(bf16[128,256]{1,0:T(8,128)(2,1)} %param.12) | copy-start | bytes 196612
  46.1 4.2 %collective-permute-start.9 = (f32[2,128,128]{1,2,0:T(8,128)S(1)}, f32[2,128,128]{1,2,0:T(8,128)S(1)}, u32[]{:S(2)}, u32[]{:S(2)}) collective-permute-start(f32[2,128,128]{1,2,0:T(8,128)S(1)} %bitcast.88), channel_id=1, source_target_pairs={{0,16},{16,0},{1,17},{17,1},{2,18},{18,2},{3,19},{19,3},{4,20},{20... | collective-permute-start | bytes 393224 | tf_op jit(solution)/shard_map/ppermute | solution.py:36
  46.8 7.7 %collective-permute-start.3 = (f32[2,2,128,128]{3,2,1,0:T(8,128)S(1)}, f32[2,2,128,128]{3,2,1,0:T(8,128)S(1)}, u32[]{:S(2)}, u32[]{:S(2)}) collective-permute-start(f32[2,2,128,128]{3,2,1,0:T(8,128)S(1)} %dynamic-slice_bitcast_fusion.2), channel_id=1, source_target_pairs={{0,4},{1,5},{2,6},{3,7},{4,0},{5,1},{6,2},{7,3},{8,12},{9,13},{10,... | collective-permute-start | bytes 786440 | tf_op jit(solution)/shard_map/ppermute | solution.py:31
  54.6 8.4 %collective-permute-start.4 = (f32[2,128,128]{2,1,0:T(8,128)S(1)}, f32[2,128,128]{2,1,0:T(8,128)S(1)}, u32[]{:S(2)}, u32[]{:S(2)}) collective-permute-start(f32[2,128,128]{2,1,0:T(8,128)S(1)} %dynamic-slice_bitcast_fusion.3), channel_id=1, source_target_pairs={{0,8},{1,9},{2,10},{3,11},{4,12},{5,13},{6,14},{7,15},{8,0},{9,1},... | collective-permute-start | bytes 393224 | tf_op jit(solution)/shard_map/ppermute | solution.py:31

commit v10 on v9

--- a/solution.py
+++ b/solution.py
@@ -237,6 +237,7 @@
     fwd_parts = along_call(rows, cols, cnt, values, group, nrb, fwd_index)
 
     mine_t = jnp.transpose(features.reshape(nbc, side, width), (0, 2, 1))
+    mine_t, fwd_parts = lax.optimization_barrier((mine_t, fwd_parts))
     if nb is not None:
         stripe_t = gather_col(mine_t, ag_order).reshape(nrb, width, side)
         along = scatter_sum_col(fwd_parts.reshape((2,) * nb + (nbc, side, width)), rs_order)

time: 63.7 us -> 66.3 us (1.041)
  starting transfers between devices: 17.3 us -> 19.1 us
  waiting for transfers between devices: 24.6 us -> 26.3 us
  other arithmetic: 8.73 us -> 7.23 us
    ppermute x2, starting transfers between devices: 0.07 us -> 1.94 us  [_swap(): return lax.ppermute(x, axis, perm)]
    ppermute x8, waiting for transfers between devices: 24.6 us -> 25.9 us  [_swap_col(): return lax.ppermute(x, ('row', 'col'), perm)]
    another operation x7, other arithmetic: 5.08 us -> 4.23 us  [gather_col(): have = jnp.stack([lo, hi], axis=0).reshape((-1,) + have.shape[1:])]
  transfers between devices with their start and end apart: 10 -> 10, of which waited for: 6 -> 8; matrix products, arithmetic and copies ran while one was open for 19% -> 14% of each run, Pallas kernels for 12% -> 6%
where the time goes in v10:
time: 66.3 us; the launch traced here: 66 us
  waiting for transfers between devices  26.3 us (40%)
  starting transfers between devices  19.1 us (29%)
  Pallas kernels  8.02 us (12%)
  other arithmetic  7.23 us (11%)
  local copies, waits for them, and re-layouts  3.43 us (5%)
  matrix products  1.16 us (2%)
  between operations  0.81 us (1%)
    ppermute x8, waiting for transfers between devices, _swap_col(): return lax.ppermute(x, ('row', 'col'), perm)  25.9 us
    ppermute x8, starting transfers between devices, _swap_col(): return lax.ppermute(x, ('row', 'col'), perm)  17.1 us
    pallas_call x1, Pallas kernels, along_call(): pl.pallas_call(kernel, grid_spec=spec, out_shape=jax.ShapeDtypeStruct((nr...  4.3 us
    another operation x7, other arithmetic, gather_col(): have = jnp.stack([lo, hi], axis=0).reshape((-1,) + have.shape[1:])  4.23 us
    pallas_call x1, Pallas kernels, against_call(): pl.pallas_call(kernel, grid_spec=spec, out_shape=jax.ShapeDtypeStruct((nc...  3.72 us
    ppermute x2, starting transfers between devices, _swap(): return lax.ppermute(x, axis, perm)  1.94 us
    another operation x2, other arithmetic, gather_row(): have = jnp.stack([lo, hi], axis=0).reshape((-1,) + have.shape[1:])  1.52 us
    add x4, other arithmetic, scatter_sum_col(): keep + _swap_col(other, row_size, col_size, (order[0][t], order[1][t]))  1.44 us
  transfers between devices with their start and end apart: 10, of which 8 were waited for; matrix products, arithmetic and copies ran while one was open for 14% of the time, Pallas kernels for 6%

profile of v10, /device:TPU:0, one launch (start us, length us, event | category | flops | bytes accessed | tf_op | source)
XLA Modules:
  0.0 66.0 jit_solution(18427485813361663994)
XLA Ops:
  0.0 0.5 collective-permute-start
  1.1 0.5 collective-permute-done
  1.6 0.9 %select_bitcast_fusion.9 = (bf16[1,1,256,128]{3,2,1,0:T(8,128)(2,1)S(1)}, bf16[1,1,256,128]{3,2,1,0:T(8,128)(2,1)S(1)}) fusion(bf16[1,256,128]{2,1,0:T(8,128)(2,1)S(1)} %collective-permute-done, pred[]{:T(512)S(6)} %eq.15, bf16[256,128]{1,0:T(8,128)(2,1)} %param.7), kind=kLoop, calls=%fused_computation.25 | loop fusion | flops 65536 | bytes 262145 | tf_op jit(solution)/shard_map/stack | solution.py:52
  2.4 0.7 %pad_maximum_fusion.3 = bf16[2,1,256,128]{3,2,1,0:T(8,128)(2,1)} fusion(bf16[1,1,256,128]{3,2,1,0:T(8,128)(2,1)S(1)} %get-tuple-element.20, bf16[1,1,256,128]{3,2,1,0:T(8,128)(2,1)S(1)} %get-tuple-element.19), kind=kLoop, calls=%fused_computation.15 | loop fusion | flops 65536 | bytes 262144 | tf_op jit(solution)/shard_map/stack | solution.py:52
  3.1 4.3 %shard_map.73 = f32[32,128,128]{2,1,0:T(8,128)} custom-call(s32[128]{0:T(128)} %bitcast.90, s32[128]{0:T(128)} %bitcast.92, s32[1]{0:T(128)} %bitcast.74.cnt_ref, bf16[128,128,128]{2,1,0:T(8,128)(2,1)} %bitcast.76, bf16[4,128,128]{2,1,0:T(8,128)(2,1)} %bitcast.84), custom_call_target="tpu_custom_call" | custom-call | tf_op jit(solution)/shard_map/pallas_call | solution.py:146
  7.4 3.9 %collective-permute-start.5 = (bf16[1,2,128,128]{2,3,1,0:T(8,128)(2,1)S(1)}, bf16[1,2,128,128]{2,3,1,0:T(8,128)(2,1)S(1)}, u32[]{:S(2)}, u32[]{:S(2)}) collective-permute-start(bf16[1,2,128,128]{2,3,1,0:T(8,128)(2,1)S(1)} %bitcast.87), channel_id=1, source_target_pairs={{0,8},{1,9},{2,10},{3,11},{4,12},{5,13},{6,14},{7,15},{8,0},{9,1},... | collective-permute-start | bytes 196616 | tf_op jit(solution)/shard_map/ppermute | solution.py:31
  11.3 2.2 %collective-permute-done.5 = bf16[1,2,128,128]{2,3,1,0:T(8,128)(2,1)S(1)} collective-permute-done((bf16[1,2,128,128]{2,3,1,0:T(8,128)(2,1)S(1)}, bf16[1,2,128,128]{2,3,1,0:T(8,128)(2,1)S(1)}, u32[]{:S(2)}, u32[]{:S(2)}) %collective-permute-start.5) | collective-permute-done | bytes 65568 | tf_op jit(solution)/shard_map/ppermute | solution.py:31
  13.6 3.3 %collective-permute-start.6 = (bf16[2,2,128,128]{2,3,1,0:T(8,128)(2,1)S(1)}, bf16[2,2,128,128]{2,3,1,0:T(8,128)(2,1)S(1)}, u32[]{:S(2)}, u32[]{:S(2)}) collective-permute-start(bf16[2,2,128,128]{2,3,1,0:T(8,128)(2,1)S(1)} %maximum_bitcast_fusion), channel_id=1, source_target_pairs={{0,1},{1,0},{2,3},{3,2},{4,5},{5,4},{6,7},{7,6},{8,9},{9,8},{10,11... | collective-permute-start | bytes 393224 | tf_op jit(solution)/shard_map/ppermute | solution.py:31
  16.9 1.3 %dynamic-slice_bitcast_fusion = f32[2,2,2,2,128,128]{5,4,3,2,1,0:T(8,128)S(1)} fusion(f32[2,2,2,2,2,128,128]{6,5,4,3,2,1,0:T(8,128)} %bitcast.78, s32[]{:T(128)S(6)} %select_n.124), kind=kLoop, calls=%fused_computation.4 | loop fusion | bytes 2097156 | tf_op jit(solution)/shard_map/jit(dynamic_index_in_dim)/squeeze | solution.py:103
  18.3 1.5 %collective-permute-done.6 = bf16[2,2,128,128]{2,3,1,0:T(8,128)(2,1)S(1)} collective-permute-done((bf16[2,2,128,128]{2,3,1,0:T(8,128)(2,1)S(1)}, bf16[2,2,128,128]{2,3,1,0:T(8,128)(2,1)S(1)}, u32[]{:S(2)}, u32[]{:S(2)}) %collective-permute-start.6) | collective-permute-done | bytes 131104 | tf_op jit(solution)/shard_map/ppermute | solution.py:31
  19.9 0.9 %copy.12 = bf16[4,2,128,128]{3,2,1,0:T(8,128)(2,1)} copy(bf16[4,2,128,128]{2,3,1,0:T(8,128)(2,1)S(1)} %bitcast.82) | data formatting | bytes 524288 | tf_op jit(solution)/shard_map/reshape | solution.py:90
  20.8 1.3 %collective-permute-start.7 = (bf16[4,2,128,128]{3,2,1,0:T(8,128)(2,1)}, bf16[4,2,128,128]{3,2,1,0:T(8,128)(2,1)S(1)}, u32[]{:S(2)}, u32[]{:S(2)}) collective-permute-start(bf16[4,2,128,128]{3,2,1,0:T(8,128)(2,1)} %copy.12), channel_id=1, source_target_pairs={{0,2},{1,3},{2,0},{3,1},{4,6},{5,7},{6,4},{7,5},{8,10},{9,11},{10,... | collective-permute-start | bytes 786440 | tf_op jit(solution)/shard_map/ppermute | solution.py:31
  22.1 5.2 %collective-permute-done.7 = bf16[4,2,128,128]{3,2,1,0:T(8,128)(2,1)S(1)} collective-permute-done((bf16[4,2,128,128]{3,2,1,0:T(8,128)(2,1)}, bf16[4,2,128,128]{3,2,1,0:T(8,128)(2,1)S(1)}, u32[]{:S(2)}, u32[]{:S(2)}) %collective-permute-start.7) | collective-permute-done | bytes 262176 | tf_op jit(solution)/shard_map/ppermute | solution.py:31
  27.4 1.0 %select_bitcast_fusion.3 = (bf16[1,4,2,128,128]{4,3,2,1,0:T(8,128)(2,1)S(1)}, bf16[1,4,2,128,128]{4,3,2,1,0:T(8,128)(2,1)S(1)}) fusion(bf16[4,2,128,128]{3,2,1,0:T(8,128)(2,1)} %copy.12, bf16[4,2,128,128]{3,2,1,0:T(8,128)(2,1)S(1)} %collective-permute-done.7, pred[]{:T(512)S(6)} %eq.18), kind=kLoop, calls=%fused_computation.13 | loop fusion | flops 262144 | bytes 1048577 | tf_op jit(solution)/shard_map/stack | solution.py:90
  28.4 0.8 %pad_maximum_fusion.1 = bf16[2,4,2,128,128]{4,3,2,1,0:T(8,128)(2,1)} fusion(bf16[1,4,2,128,128]{4,3,2,1,0:T(8,128)(2,1)S(1)} %get-tuple-element.12, bf16[1,4,2,128,128]{4,3,2,1,0:T(8,128)(2,1)S(1)} %get-tuple-element.11), kind=kLoop, calls=%fused_computation.5 | loop fusion | flops 262144 | bytes 1048576 | tf_op jit(solution)/shard_map/stack | solution.py:90
  29.2 3.2 %collective-permute-start.8 = (bf16[8,2,128,128]{3,2,1,0:T(8,128)(2,1)}, bf16[8,2,128,128]{3,2,1,0:T(8,128)(2,1)}, u32[]{:S(2)}, u32[]{:S(2)}) collective-permute-start(bf16[8,2,128,128]{3,2,1,0:T(8,128)(2,1)} %bitcast.29), channel_id=1, source_target_pairs={{0,4},{1,5},{2,6},{3,7},{4,0},{5,1},{6,2},{7,3},{8,12},{9,13},{10,... | collective-permute-start | bytes 1572872 | tf_op jit(solution)/shard_map/ppermute | solution.py:31
  32.4 3.6 %collective-permute-done.1 = f32[2,2,2,2,128,128]{5,4,3,2,1,0:T(8,128)} collective-permute-done((f32[2,2,2,2,128,128]{5,4,3,2,1,0:T(8,128)S(1)}, f32[2,2,2,2,128,128]{5,4,3,2,1,0:T(8,128)}, u32[]{:S(2)}, u32[]{:S(2)}) %collective-permute-start.1) | collective-permute-done | bytes 1048608 | tf_op jit(solution)/shard_map/ppermute | solution.py:31
  36.1 1.3 %bitcast_add_fusion = f32[2,2,2,2,128,128]{5,4,3,2,1,0:T(8,128)S(1)} fusion(f32[2,2,2,2,128,128]{5,4,3,2,1,0:T(8,128)} %collective-permute-done.1, f32[2,2,2,2,2,128,128]{6,5,4,3,2,1,0:T(8,128)S(1)} %bitcast.79, s32[]{:T(128)S(6)} %select_n.123), kind=kLoop, calls=%fused_computation.3 | loop fusion | flops 262144 | bytes 3145732 | tf_op jit(solution)/shard_map/add | solution.py:104
  37.4 1.5 %collective-permute-start.2 = (f32[2,2,2,128,128]{4,3,2,1,0:T(8,128)S(1)}, f32[2,2,2,128,128]{4,3,2,1,0:T(8,128)S(1)}, u32[]{:S(2)}, u32[]{:S(2)}) collective-permute-start(f32[2,2,2,128,128]{4,3,2,1,0:T(8,128)S(1)} %dynamic-slice_bitcast_fusion.1), channel_id=1, source_target_pairs={{0,2},{1,3},{2,0},{3,1},{4,6},{5,7},{6,4},{7,5},{8,10},{9,11},{10,... | collective-permute-start | bytes 1572872 | tf_op jit(solution)/shard_map/ppermute | solution.py:31
  38.9 1.0 %collective-permute-done.8 = bf16[8,2,128,128]{3,2,1,0:T(8,128)(2,1)} collective-permute-done((bf16[8,2,128,128]{3,2,1,0:T(8,128)(2,1)}, bf16[8,2,128,128]{3,2,1,0:T(8,128)(2,1)}, u32[]{:S(2)}, u32[]{:S(2)}) %collective-permute-start.8) | collective-permute-done | bytes 524320 | tf_op jit(solution)/shard_map/ppermute | solution.py:31
  39.9 1.3 %select_bitcast_fusion.1 = (bf16[1,8,2,128,128]{4,3,2,1,0:T(8,128)(2,1)S(1)}, bf16[1,8,2,128,128]{4,3,2,1,0:T(8,128)(2,1)S(1)}) fusion(bf16[8,2,128,128]{3,2,1,0:T(8,128)(2,1)} %collective-permute-done.8, pred[]{:T(512)S(6)} %eq.17, bf16[2,4,2,128,128]{4,3,2,1,0:T(8,128)(2,1)} %pad_maximum_fusion.1), kind=kLoop, calls=%fused_computation.8 | loop fusion | flops 524288 | bytes 2097153 | tf_op jit(solution)/shard_map/stack | solution.py:90
  41.2 1.1 %pad_maximum_fusion = bf16[2,8,2,128,128]{4,3,2,1,0:T(8,128)(2,1)} fusion(bf16[1,8,2,128,128]{4,3,2,1,0:T(8,128)(2,1)S(1)} %get-tuple-element.10, bf16[1,8,2,128,128]{4,3,2,1,0:T(8,128)(2,1)S(1)} %get-tuple-element.9), kind=kLoop, calls=%fused_computation.2 | loop fusion | flops 524288 | bytes 2097152 | tf_op jit(solution)/shard_map/stack | solution.py:90
  42.2 3.7 %shard_map.74 = f32[4,128,128]{2,1,0:T(8,128)} custom-call(s32[128]{0:T(128)} %bitcast.91, s32[128]{0:T(128)} %bitcast.93, s32[1]{0:T(128)} %bitcast.75.cnt_ref, bf16[128,128,128]{2,1,0:T(8,128)(2,1)} %bitcast.77, bf16[32,128,128]{2,1,0:T(8,128)(2,1)} %bitcast.80), custom_call_target="tpu_custom_call" | custom-call | tf_op jit(solution)/shard_map/pallas_call | solution.py:187
  46.0 1.0 %constant_dynamic-slice_fusion.1 = (f32[1,2,128,128]{3,2,1,0:T(8,128)S(1)}, f32[1,2,128,128]{3,2,1,0:T(8,128)S(1)}) fusion(f32[2,2,128,128]{3,2,1,0:T(8,128)} %bitcast.81, s32[]{:T(128)S(6)} %select_n.145, s32[]{:T(128)S(6)} %select_n.146), kind=kLoop, calls=%fused_computation.27 | loop fusion | bytes 524296 | tf_op jit(solution)/shard_map/jit(dynamic_index_in_dim)/dynamic_slice | solution.py:71
  46.9 0.1 copy.15
  47.1 1.5 %collective-permute-start.9 = (f32[2,128,128]{1,2,0:T(8,128)S(1)}, f32[2,128,128]{1,2,0:T(8,128)S(1)}, u32[]{:S(2)}, u32[]{:S(2)}) collective-permute-start(f32[2,128,128]{1,2,0:T(8,128)S(1)} %bitcast.89), channel_id=1, source_target_pairs={{0,16},{16,0},{1,17},{17,1},{2,18},{18,2},{3,19},{19,3},{4,20},{20... | collective-permute-start | bytes 393224 | tf_op jit(solution)/shard_map/ppermute | solution.py:36
  48.6 3.2 %collective-permute-start.3 = (f32[2,2,128,128]{3,2,1,0:T(8,128)S(1)}, f32[2,2,128,128]{3,2,1,0:T(8,128)S(1)}, u32[]{:S(2)}, u32[]{:S(2)}) collective-permute-start(f32[2,2,128,128]{3,2,1,0:T(8,128)S(1)} %dynamic-slice_bitcast_fusion.2), channel_id=1, source_target_pairs={{0,4},{1,5},{2,6},{3,7},{4,0},{5,1},{6,2},{7,3},{8,12},{9,13},{10,... | collective-permute-start | bytes 786440 | tf_op jit(solution)/shard_map/ppermute | solution.py:31
  52.0 4.6 %collective-permute-done.3 = f32[2,2,128,128]{3,2,1,0:T(8,128)S(1)} collective-permute-done((f32[2,2,128,128]{3,2,1,0:T(8,128)S(1)}, f32[2,2,128,128]{3,2,1,0:T(8,128)S(1)}, u32[]{:S(2)}, u32[]{:S(2)}) %collective-permute-start.3) | collective-permute-done | bytes 262176 | tf_op jit(solution)/shard_map/ppermute | solution.py:31
  56.7 0.6 collective-permute-start.4
  57.3 0.2 fusion.1
  57.5 7.6 %collective-permute-done.4 = f32[2,128,128]{2,1,0:T(8,128)S(1)} collective-permute-done((f32[2,128,128]{2,1,0:T(8,128)S(1)}, f32[2,128,128]{2,1,0:T(8,128)S(1)}, u32[]{:S(2)}, u32[]{:S(2)}) %collective-permute-start.4) | collective-permute-done | bytes 131104 | tf_op jit(solution)/shard_map/ppermute | solution.py:31
  65.1 0.9 %fusion = bf16[256,256]{1,0:T(8,128)(2,1)} fusion(f32[256,256]{1,0:T(8,128)S(1)} %fusion.1, f32[256,128]{1,0:T(8,128)S(1)} %bitcast.85, bf16[128,256]{1,0:T(8,128)(2,1)S(1)} %copy-done.3), kind=kOutput, calls=%fused_computation.1 | convolution fusion | flops 100794368 | bytes 589824 | tf_op jit(solution)/shard_map/dot_general | solution.py:254
  (23 shorter events, 0.5 us)
Async XLA Ops:
  0.0 57.3 %copy-start = (bf16[128,256]{1,0:T(8,128)(2,1)S(1)}, bf16[128,256]{1,0:T(8,128)(2,1)}, u32[]{:S(2)}) copy-start(bf16[128,256]{1,0:T(8,128)(2,1)} %param.13) | copy-start | bytes 196612
  0.0 1.6 %collective-permute-start = (bf16[1,256,128]{2,1,0:T(8,128)(2,1)}, bf16[1,256,128]{2,1,0:T(8,128)(2,1)S(1)}, u32[]{:S(2)}, u32[]{:S(2)}) collective-permute-start(bf16[1,256,128]{2,1,0:T(8,128)(2,1)} %bitcast.86), channel_id=1, source_target_pairs={{0,16},{16,0},{1,17},{17,1},{2,18},{18,2},{3,19},{19,3},{4,20},{20... | collective-permute-start | bytes 196616 | tf_op jit(solution)/shard_map/ppermute | solution.py:36
  3.1 4.3 %copy-start.2 = (bf16[256,128]{1,0:T(8,128)(2,1)S(1)}, bf16[256,128]{1,0:T(8,128)(2,1)}, u32[]{:S(2)}) copy-start(bf16[256,128]{1,0:T(8,128)(2,1)} %param.7) | copy-start | bytes 196612
  7.4 6.2 %collective-permute-start.5 = (bf16[1,2,128,128]{2,3,1,0:T(8,128)(2,1)S(1)}, bf16[1,2,128,128]{2,3,1,0:T(8,128)(2,1)S(1)}, u32[]{:S(2)}, u32[]{:S(2)}) collective-permute-start(bf16[1,2,128,128]{2,3,1,0:T(8,128)(2,1)S(1)} %bitcast.87), channel_id=1, source_target_pairs={{0,8},{1,9},{2,10},{3,11},{4,12},{5,13},{6,14},{7,15},{8,0},{9,1},... | collective-permute-start | bytes 196616 | tf_op jit(solution)/shard_map/ppermute | solution.py:31
  13.6 6.2 %collective-permute-start.6 = (bf16[2,2,128,128]{2,3,1,0:T(8,128)(2,1)S(1)}, bf16[2,2,128,128]{2,3,1,0:T(8,128)(2,1)S(1)}, u32[]{:S(2)}, u32[]{:S(2)}) collective-permute-start(bf16[2,2,128,128]{2,3,1,0:T(8,128)(2,1)S(1)} %maximum_bitcast_fusion), channel_id=1, source_target_pairs={{0,1},{1,0},{2,3},{3,2},{4,5},{5,4},{6,7},{7,6},{8,9},{9,8},{10,11... | collective-permute-start | bytes 393224 | tf_op jit(solution)/shard_map/ppermute | solution.py:31
  18.2 17.8 %copy-start.1 = (f32[32,128,128]{2,1,0:T(8,128)S(1)}, f32[32,128,128]{2,1,0:T(8,128)}, u32[]{:S(2)}) copy-start(f32[32,128,128]{2,1,0:T(8,128)} %shard_map.73) | copy-start | bytes 6291460
  18.2 17.8 %collective-permute-start.1 = (f32[2,2,2,2,128,128]{5,4,3,2,1,0:T(8,128)S(1)}, f32[2,2,2,2,128,128]{5,4,3,2,1,0:T(8,128)}, u32[]{:S(2)}, u32[]{:S(2)}) collective-permute-start(f32[2,2,2,2,128,128]{5,4,3,2,1,0:T(8,128)S(1)} %dynamic-slice_bitcast_fusion), channel_id=1, source_target_pairs={{0,1},{1,0},{2,3},{3,2},{4,5},{5,4},{6,7},{7,6},{8,9},{9,8},{10,11... | collective-permute-start | bytes 3145736 | tf_op jit(solution)/shard_map/ppermute | solution.py:31
  20.8 6.6 %collective-permute-start.7 = (bf16[4,2,128,128]{3,2,1,0:T(8,128)(2,1)}, bf16[4,2,128,128]{3,2,1,0:T(8,128)(2,1)S(1)}, u32[]{:S(2)}, u32[]{:S(2)}) collective-permute-start(bf16[4,2,128,128]{3,2,1,0:T(8,128)(2,1)} %copy.12), channel_id=1, source_target_pairs={{0,2},{1,3},{2,0},{3,1},{4,6},{5,7},{6,4},{7,5},{8,10},{9,11},{10,... | collective-permute-start | bytes 786440 | tf_op jit(solution)/shard_map/ppermute | solution.py:31
  29.2 10.7 %collective-permute-start.8 = (bf16[8,2,128,128]{3,2,1,0:T(8,128)(2,1)}, bf16[8,2,128,128]{3,2,1,0:T(8,128)(2,1)}, u32[]{:S(2)}, u32[]{:S(2)}) collective-permute-start(bf16[8,2,128,128]{3,2,1,0:T(8,128)(2,1)} %bitcast.29), channel_id=1, source_target_pairs={{0,4},{1,5},{2,6},{3,7},{4,0},{5,1},{6,2},{7,3},{8,12},{9,13},{10,... | collective-permute-start | bytes 1572872 | tf_op jit(solution)/shard_map/ppermute | solution.py:31
  37.4 11.1 %collective-permute-start.2 = (f32[2,2,2,128,128]{4,3,2,1,0:T(8,128)S(1)}, f32[2,2,2,128,128]{4,3,2,1,0:T(8,128)S(1)}, u32[]{:S(2)}, u32[]{:S(2)}) collective-permute-start(f32[2,2,2,128,128]{4,3,2,1,0:T(8,128)S(1)} %dynamic-slice_bitcast_fusion.1), channel_id=1, source_target_pairs={{0,2},{1,3},{2,0},{3,1},{4,6},{5,7},{6,4},{7,5},{8,10},{9,11},{10,... | collective-permute-start | bytes 1572872 | tf_op jit(solution)/shard_map/ppermute | solution.py:31
  47.1 18.1 %copy-start.3 = (bf16[128,256]{1,0:T(8,128)(2,1)S(1)}, bf16[128,256]{1,0:T(8,128)(2,1)}, u32[]{:S(2)}) copy-start(bf16[128,256]{1,0:T(8,128)(2,1)} %param.12) | copy-start | bytes 196612
  47.1 4.9 %collective-permute-start.9 = (f32[2,128,128]{1,2,0:T(8,128)S(1)}, f32[2,128,128]{1,2,0:T(8,128)S(1)}, u32[]{:S(2)}, u32[]{:S(2)}) collective-permute-start(f32[2,128,128]{1,2,0:T(8,128)S(1)} %bitcast.89), channel_id=1, source_target_pairs={{0,16},{16,0},{1,17},{17,1},{2,18},{18,2},{3,19},{19,3},{4,20},{20... | collective-permute-start | bytes 393224 | tf_op jit(solution)/shard_map/ppermute | solution.py:36
  48.6 8.0 %collective-permute-start.3 = (f32[2,2,128,128]{3,2,1,0:T(8,128)S(1)}, f32[2,2,128,128]{3,2,1,0:T(8,128)S(1)}, u32[]{:S(2)}, u32[]{:S(2)}) collective-permute-start(f32[2,2,128,128]{3,2,1,0:T(8,128)S(1)} %dynamic-slice_bitcast_fusion.2), channel_id=1, source_target_pairs={{0,4},{1,5},{2,6},{3,7},{4,0},{5,1},{6,2},{7,3},{8,12},{9,13},{10,... | collective-permute-start | bytes 786440 | tf_op jit(solution)/shard_map/ppermute | solution.py:31
  56.7 8.4 %collective-permute-start.4 = (f32[2,128,128]{2,1,0:T(8,128)S(1)}, f32[2,128,128]{2,1,0:T(8,128)S(1)}, u32[]{:S(2)}, u32[]{:S(2)}) collective-permute-start(f32[2,128,128]{2,1,0:T(8,128)S(1)} %dynamic-slice_bitcast_fusion.3), channel_id=1, source_target_pairs={{0,8},{1,9},{2,10},{3,11},{4,12},{5,13},{6,14},{7,15},{8,0},{9,1},... | collective-permute-start | bytes 393224 | tf_op jit(solution)/shard_map/ppermute | solution.py:31

commit v11 on v9

--- a/solution.py
+++ b/solution.py
@@ -91,13 +91,13 @@
     return have
 
 
-def scatter_sum_col(data, order):
+def scatter_sum_col(data, order, first=0, stop=None):
     row_size = lax.axis_size("row")
     col_size = lax.axis_size("col")
     nb = len(order[0])
     me = lax.axis_index("col")
     parity = lax.axis_index("row") % 2
-    for t in range(nb):
+    for t in range(first, nb if stop is None else stop):
         mine = (me >> _pick(parity, order, t)) & 1
         keep = lax.dynamic_index_in_dim(data, mine, axis=0, keepdims=False)
         other = lax.dynamic_index_in_dim(data, 1 - mine, axis=0, keepdims=False)
@@ -238,8 +238,10 @@
 
     mine_t = jnp.transpose(features.reshape(nbc, side, width), (0, 2, 1))
     if nb is not None:
+        along = scatter_sum_col(fwd_parts.reshape((2,) * nb + (nbc, side, width)), rs_order, 0, 1)
+        mine_t, along = lax.optimization_barrier((mine_t, along))
         stripe_t = gather_col(mine_t, ag_order).reshape(nrb, width, side)
-        along = scatter_sum_col(fwd_parts.reshape((2,) * nb + (nbc, side, width)), rs_order)
+        along = scatter_sum_col(along, rs_order, 1)
     else:
         stripe_t = lax.all_gather(mine_t, "col", axis=0, tiled=True)
         along = lax.psum_scatter(fwd_parts, "col", scatter_dimension=0, tiled=True)

time: 63.7 us -> 73.1 us (1.15); the launches traced: 63.9 us -> 72.2 us
  waiting for transfers between devices: 24.6 us -> 41.4 us
  other arithmetic: 8.73 us -> 4.33 us
  starting transfers between devices: 17.3 us -> 13.7 us
    ppermute x8, waiting for transfers between devices: 24.6 us -> 39.7 us  [_swap_col(): return lax.ppermute(x, ('row', 'col'), perm)]
    ppermute x8, starting transfers between devices: 17.2 us -> 13.2 us  [_swap_col(): return lax.ppermute(x, ('row', 'col'), perm)]
    another operation x7, other arithmetic: 5.08 us -> 1.33 us  [gather_col(): have = jnp.stack([lo, hi], axis=0).reshape((-1,) + have.shape[1:])]
    ppermute x2, waiting for transfers between devices: 0.01 us -> 1.66 us  [_swap(): return lax.ppermute(x, axis, perm)]
  transfers between devices with their start and end apart: 10 -> 10, of which waited for: 6 -> 8; matrix products, arithmetic and copies ran while one was open for 19% -> 4% of each run, Pallas kernels for 12% -> 5%
where the time goes in v11:
time: 73.1 us; the launch traced here: 72.2 us
  waiting for transfers between devices  41.4 us (57%)
  starting transfers between devices  13.7 us (19%)
  Pallas kernels  7.89 us (11%)
  other arithmetic  4.33 us (6%)
  local copies, waits for them, and re-layouts  2.93 us (4%)
  matrix products  1.16 us (2%)
  between operations  0.84 us (1%)
    ppermute x8, waiting for transfers between devices, _swap_col(): return lax.ppermute(x, ('row', 'col'), perm)  39.7 us
    ppermute x8, starting transfers between devices, _swap_col(): return lax.ppermute(x, ('row', 'col'), perm)  13.2 us
    pallas_call x1, Pallas kernels, along_call(): pl.pallas_call(kernel, grid_spec=spec, out_shape=jax.ShapeDtypeStruct((nr...  4.17 us
    pallas_call x1, Pallas kernels, against_call(): pl.pallas_call(kernel, grid_spec=spec, out_shape=jax.ShapeDtypeStruct((nc...  3.72 us
    ppermute x2, waiting for transfers between devices, _swap(): return lax.ppermute(x, axis, perm)  1.66 us
    squeeze x4, local copies, waits for them, and re-layouts, scatter_sum_col(): other = lax.dynamic_index_in_dim(data, 1 - mine, axis=0, keepdims=False)  1.52 us
    another operation x2, other arithmetic, gather_row(): have = jnp.stack([lo, hi], axis=0).reshape((-1,) + have.shape[1:])  1.52 us
  transfers between devices with their start and end apart: 10, of which 8 were waited for; matrix products, arithmetic and copies ran while one was open for 4% of the time, Pallas kernels for 5%

profile of v11, /device:TPU:0, one launch (start us, length us, event | category | flops | bytes accessed | tf_op | source)
XLA Modules:
  0.0 72.2 jit_solution(18365822428776585978)
XLA Ops:
  0.0 0.5 collective-permute-start
  1.1 0.5 collective-permute-done
  1.6 0.9 %select_bitcast_fusion.9 = (bf16[1,1,256,128]{3,2,1,0:T(8,128)(2,1)S(1)}, bf16[1,1,256,128]{3,2,1,0:T(8,128)(2,1)S(1)}) fusion(bf16[1,256,128]{2,1,0:T(8,128)(2,1)S(1)} %collective-permute-done, pred[]{:T(512)S(6)} %eq.16, bf16[256,128]{1,0:T(8,128)(2,1)} %param.7), kind=kLoop, calls=%fused_computation.25 | loop fusion | flops 65536 | bytes 262145 | tf_op jit(solution)/shard_map/stack | solution.py:52
  2.4 0.7 pad_maximum_fusion.3
  3.1 4.2 %shard_map.73 = f32[32,128,128]{2,1,0:T(8,128)} custom-call(s32[128]{0:T(128)} %bitcast.91, s32[128]{0:T(128)} %bitcast.93, s32[1]{0:T(128)} %bitcast.74.cnt_ref, bf16[128,128,128]{2,1,0:T(8,128)(2,1)} %bitcast.76, bf16[4,128,128]{2,1,0:T(8,128)(2,1)} %bitcast.85), custom_call_target="tpu_custom_call" | custom-call | tf_op jit(solution)/shard_map/pallas_call | solution.py:146
  7.3 1.4 %dynamic-slice_bitcast_fusion = f32[2,2,2,2,128,128]{5,4,3,2,1,0:T(8,128)S(1)} fusion(f32[2,2,2,2,2,128,128]{6,5,4,3,2,1,0:T(8,128)} %bitcast.78, s32[]{:T(128)S(6)} %select_n.126), kind=kLoop, calls=%fused_computation.4 | loop fusion | bytes 2097156 | tf_op jit(solution)/shard_map/jit(dynamic_index_in_dim)/squeeze | solution.py:103
  8.7 5.4 %collective-permute-start.1 = (f32[2,2,2,2,128,128]{5,4,3,2,1,0:T(8,128)S(1)}, f32[2,2,2,2,128,128]{5,4,3,2,1,0:T(8,128)}, u32[]{:S(2)}, u32[]{:S(2)}) collective-permute-start(f32[2,2,2,2,128,128]{5,4,3,2,1,0:T(8,128)S(1)} %dynamic-slice_bitcast_fusion), channel_id=1, source_target_pairs={{0,1},{1,0},{2,3},{3,2},{4,5},{5,4},{6,7},{7,6},{8,9},{9,8},{10,11... | collective-permute-start | bytes 3145736 | tf_op jit(solution)/shard_map/ppermute | solution.py:31
  14.2 12.9 %collective-permute-done.1 = f32[2,2,2,2,128,128]{5,4,3,2,1,0:T(8,128)} collective-permute-done((f32[2,2,2,2,128,128]{5,4,3,2,1,0:T(8,128)S(1)}, f32[2,2,2,2,128,128]{5,4,3,2,1,0:T(8,128)}, u32[]{:S(2)}, u32[]{:S(2)}) %collective-permute-start.1) | collective-permute-done | bytes 1048608 | tf_op jit(solution)/shard_map/ppermute | solution.py:31
  27.0 1.3 %bitcast_add_fusion = f32[2,2,2,2,128,128]{5,4,3,2,1,0:T(8,128)S(1)} fusion(f32[2,2,2,2,128,128]{5,4,3,2,1,0:T(8,128)} %collective-permute-done.1, f32[2,2,2,2,2,128,128]{6,5,4,3,2,1,0:T(8,128)S(1)} %bitcast.79, s32[]{:T(128)S(6)} %select_n.125), kind=kLoop, calls=%fused_computation.3 | loop fusion | flops 262144 | bytes 3145732 | tf_op jit(solution)/shard_map/add | solution.py:104
  28.4 1.9 %collective-permute-start.5 = (bf16[1,2,128,128]{2,3,1,0:T(8,128)(2,1)S(1)}, bf16[1,2,128,128]{2,3,1,0:T(8,128)(2,1)S(1)}, u32[]{:S(2)}, u32[]{:S(2)}) collective-permute-start(bf16[1,2,128,128]{2,3,1,0:T(8,128)(2,1)S(1)} %bitcast.88), channel_id=1, source_target_pairs={{0,8},{1,9},{2,10},{3,11},{4,12},{5,13},{6,14},{7,15},{8,0},{9,1},... | collective-permute-start | bytes 196616 | tf_op jit(solution)/shard_map/ppermute | solution.py:31
  30.3 4.2 %collective-permute-done.5 = bf16[1,2,128,128]{2,3,1,0:T(8,128)(2,1)S(1)} collective-permute-done((bf16[1,2,128,128]{2,3,1,0:T(8,128)(2,1)S(1)}, bf16[1,2,128,128]{2,3,1,0:T(8,128)(2,1)S(1)}, u32[]{:S(2)}, u32[]{:S(2)}) %collective-permute-start.5) | collective-permute-done | bytes 65568 | tf_op jit(solution)/shard_map/ppermute | solution.py:31
  34.6 1.8 %collective-permute-start.6 = (bf16[2,2,128,128]{2,3,1,0:T(8,128)(2,1)S(1)}, bf16[2,2,128,128]{2,3,1,0:T(8,128)(2,1)S(1)}, u32[]{:S(2)}, u32[]{:S(2)}) collective-permute-start(bf16[2,2,128,128]{2,3,1,0:T(8,128)(2,1)S(1)} %maximum_bitcast_fusion), channel_id=1, source_target_pairs={{0,1},{1,0},{2,3},{3,2},{4,5},{5,4},{6,7},{7,6},{8,9},{9,8},{10,11... | collective-permute-start | bytes 393224 | tf_op jit(solution)/shard_map/ppermute | solution.py:31
  36.5 0.1 collective-permute-start.2
  36.6 4.4 %collective-permute-done.6 = bf16[2,2,128,128]{2,3,1,0:T(8,128)(2,1)S(1)} collective-permute-done((bf16[2,2,128,128]{2,3,1,0:T(8,128)(2,1)S(1)}, bf16[2,2,128,128]{2,3,1,0:T(8,128)(2,1)S(1)}, u32[]{:S(2)}, u32[]{:S(2)}) %collective-permute-start.6) | collective-permute-done | bytes 131104 | tf_op jit(solution)/shard_map/ppermute | solution.py:31
  41.1 0.2 copy.12
  41.3 0.4 collective-permute-start.7
  41.6 6.9 %collective-permute-done.7 = bf16[4,2,128,128]{3,2,1,0:T(8,128)(2,1)S(1)} collective-permute-done((bf16[4,2,128,128]{3,2,1,0:T(8,128)(2,1)S(1)}, bf16[4,2,128,128]{3,2,1,0:T(8,128)(2,1)S(1)}, u32[]{:S(2)}, u32[]{:S(2)}) %collective-permute-start.7) | collective-permute-done | bytes 262176 | tf_op jit(solution)/shard_map/ppermute | solution.py:31
  48.7 0.3 collective-permute-start.3
  49.1 1.8 %collective-permute-start.8 = (bf16[8,2,128,128]{3,2,1,0:T(8,128)(2,1)S(1)}, bf16[8,2,128,128]{3,2,1,0:T(8,128)(2,1)S(1)}, u32[]{:S(2)}, u32[]{:S(2)}) collective-permute-start(bf16[8,2,128,128]{3,2,1,0:T(8,128)(2,1)S(1)} %bitcast.81), channel_id=1, source_target_pairs={{0,4},{1,5},{2,6},{3,7},{4,0},{5,1},{6,2},{7,3},{8,12},{9,13},{10,... | collective-permute-start | bytes 1572872 | tf_op jit(solution)/shard_map/ppermute | solution.py:31
  50.9 4.2 %collective-permute-done.3 = f32[2,2,128,128]{3,2,1,0:T(8,128)S(1)} collective-permute-done((f32[2,2,128,128]{3,2,1,0:T(8,128)S(1)}, f32[2,2,128,128]{3,2,1,0:T(8,128)S(1)}, u32[]{:S(2)}, u32[]{:S(2)}) %collective-permute-start.3) | collective-permute-done | bytes 262176 | tf_op jit(solution)/shard_map/ppermute | solution.py:31
  55.2 1.3 %collective-permute-start.4 = (f32[2,128,128]{2,1,0:T(8,128)S(1)}, f32[2,128,128]{2,1,0:T(8,128)S(1)}, u32[]{:S(2)}, u32[]{:S(2)}) collective-permute-start(f32[2,128,128]{2,1,0:T(8,128)S(1)} %dynamic-slice_bitcast_fusion.3), channel_id=1, source_target_pairs={{0,8},{1,9},{2,10},{3,11},{4,12},{5,13},{6,14},{7,15},{8,0},{9,1},... | collective-permute-start | bytes 393224 | tf_op jit(solution)/shard_map/ppermute | solution.py:31
  56.5 7.1 %collective-permute-done.8 = bf16[8,2,128,128]{3,2,1,0:T(8,128)(2,1)S(1)} collective-permute-done((bf16[8,2,128,128]{3,2,1,0:T(8,128)(2,1)S(1)}, bf16[8,2,128,128]{3,2,1,0:T(8,128)(2,1)S(1)}, u32[]{:S(2)}, u32[]{:S(2)}) %collective-permute-start.8) | collective-permute-done | bytes 524320 | tf_op jit(solution)/shard_map/ppermute | solution.py:31
  63.6 0.1 select_bitcast_fusion.1
  63.7 1.1 %pad_maximum_fusion = bf16[2,8,2,128,128]{4,3,2,1,0:T(8,128)(2,1)} fusion(bf16[1,8,2,128,128]{4,3,2,1,0:T(8,128)(2,1)S(1)} %get-tuple-element.10, bf16[1,8,2,128,128]{4,3,2,1,0:T(8,128)(2,1)S(1)} %get-tuple-element.9), kind=kLoop, calls=%fused_computation.2 | loop fusion | flops 524288 | bytes 2097152 | tf_op jit(solution)/shard_map/stack | solution.py:90
  64.7 3.7 %shard_map.74 = f32[4,128,128]{2,1,0:T(8,128)} custom-call(s32[128]{0:T(128)} %bitcast.92, s32[128]{0:T(128)} %bitcast.94, s32[1]{0:T(128)} %bitcast.75.cnt_ref, bf16[128,128,128]{2,1,0:T(8,128)(2,1)} %bitcast.77, bf16[32,128,128]{2,1,0:T(8,128)(2,1)} %bitcast.80), custom_call_target="tpu_custom_call" | custom-call | tf_op jit(solution)/shard_map/pallas_call | solution.py:187
  68.5 1.0 %constant_dynamic-slice_fusion.1 = (f32[1,2,128,128]{3,2,1,0:T(8,128)S(1)}, f32[1,2,128,128]{3,2,1,0:T(8,128)S(1)}) fusion(f32[2,2,128,128]{3,2,1,0:T(8,128)} %bitcast.82, s32[]{:T(128)S(6)} %select_n.147, s32[]{:T(128)S(6)} %select_n.148), kind=kLoop, calls=%fused_computation.27 | loop fusion | bytes 524296 | tf_op jit(solution)/shard_map/jit(dynamic_index_in_dim)/dynamic_slice | solution.py:71
  69.5 0.1 copy.15
  69.6 0.1 collective-permute-start.9
  69.7 0.1 copy.14
  69.8 1.2 %collective-permute-done.9 = f32[2,128,128]{1,2,0:T(8,128)S(1)} collective-permute-done((f32[2,128,128]{1,2,0:T(8,128)S(1)}, f32[2,128,128]{1,2,0:T(8,128)S(1)}, u32[]{:S(2)}, u32[]{:S(2)}) %collective-permute-start.9) | collective-permute-done | bytes 131104 | tf_op jit(solution)/shard_map/ppermute | solution.py:36
  71.0 0.3 fusion.1
  71.3 0.9 %fusion = bf16[256,256]{1,0:T(8,128)(2,1)} fusion(f32[256,256]{1,0:T(8,128)S(1)} %fusion.1, f32[256,128]{1,0:T(8,128)S(1)} %bitcast.86, bf16[128,256]{1,0:T(8,128)(2,1)S(1)} %copy-done.3), kind=kOutput, calls=%fused_computation.1 | convolution fusion | flops 100794368 | bytes 589824 | tf_op jit(solution)/shard_map/dot_general | solution.py:255
  (23 shorter events, 0.4 us)
Async XLA Ops:
  0.0 71.0 %copy-start = (bf16[128,256]{1,0:T(8,128)(2,1)S(1)}, bf16[128,256]{1,0:T(8,128)(2,1)}, u32[]{:S(2)}) copy-start(bf16[128,256]{1,0:T(8,128)(2,1)} %param.13) | copy-start | bytes 196612
  0.0 1.6 %collective-permute-start = (bf16[1,256,128]{2,1,0:T(8,128)(2,1)}, bf16[1,256,128]{2,1,0:T(8,128)(2,1)S(1)}, u32[]{:S(2)}, u32[]{:S(2)}) collective-permute-start(bf16[1,256,128]{2,1,0:T(8,128)(2,1)} %bitcast.87), channel_id=1, source_target_pairs={{0,16},{16,0},{1,17},{17,1},{2,18},{18,2},{3,19},{19,3},{4,20},{20... | collective-permute-start | bytes 196616 | tf_op jit(solution)/shard_map/ppermute | solution.py:36
  7.3 19.8 %copy-start.1 = (f32[32,128,128]{2,1,0:T(8,128)S(1)}, f32[32,128,128]{2,1,0:T(8,128)}, u32[]{:S(2)}) copy-start(f32[32,128,128]{2,1,0:T(8,128)} %shard_map.73) | copy-start | bytes 6291460
  8.7 19.7 %copy-start.2 = (bf16[256,128]{1,0:T(8,128)(2,1)S(1)}, bf16[256,128]{1,0:T(8,128)(2,1)}, u32[]{:S(2)}) copy-start(bf16[256,128]{1,0:T(8,128)(2,1)} %param.7) | copy-start | bytes 196612
  8.7 18.3 %collective-permute-start.1 = (f32[2,2,2,2,128,128]{5,4,3,2,1,0:T(8,128)S(1)}, f32[2,2,2,2,128,128]{5,4,3,2,1,0:T(8,128)}, u32[]{:S(2)}, u32[]{:S(2)}) collective-permute-start(f32[2,2,2,2,128,128]{5,4,3,2,1,0:T(8,128)S(1)} %dynamic-slice_bitcast_fusion), channel_id=1, source_target_pairs={{0,1},{1,0},{2,3},{3,2},{4,5},{5,4},{6,7},{7,6},{8,9},{9,8},{10,11... | collective-permute-start | bytes 3145736 | tf_op jit(solution)/shard_map/ppermute | solution.py:31
  28.4 6.2 %collective-permute-start.5 = (bf16[1,2,128,128]{2,3,1,0:T(8,128)(2,1)S(1)}, bf16[1,2,128,128]{2,3,1,0:T(8,128)(2,1)S(1)}, u32[]{:S(2)}, u32[]{:S(2)}) collective-permute-start(bf16[1,2,128,128]{2,3,1,0:T(8,128)(2,1)S(1)} %bitcast.88), channel_id=1, source_target_pairs={{0,8},{1,9},{2,10},{3,11},{4,12},{5,13},{6,14},{7,15},{8,0},{9,1},... | collective-permute-start | bytes 196616 | tf_op jit(solution)/shard_map/ppermute | solution.py:31
  34.6 6.4 %collective-permute-start.6 = (bf16[2,2,128,128]{2,3,1,0:T(8,128)(2,1)S(1)}, bf16[2,2,128,128]{2,3,1,0:T(8,128)(2,1)S(1)}, u32[]{:S(2)}, u32[]{:S(2)}) collective-permute-start(bf16[2,2,128,128]{2,3,1,0:T(8,128)(2,1)S(1)} %maximum_bitcast_fusion), channel_id=1, source_target_pairs={{0,1},{1,0},{2,3},{3,2},{4,5},{5,4},{6,7},{7,6},{8,9},{9,8},{10,11... | collective-permute-start | bytes 393224 | tf_op jit(solution)/shard_map/ppermute | solution.py:31
  36.5 12.1 %collective-permute-start.2 = (f32[2,2,2,128,128]{4,3,2,1,0:T(8,128)S(1)}, f32[2,2,2,128,128]{4,3,2,1,0:T(8,128)S(1)}, u32[]{:S(2)}, u32[]{:S(2)}) collective-permute-start(f32[2,2,2,128,128]{4,3,2,1,0:T(8,128)S(1)} %dynamic-slice_bitcast_fusion.1), channel_id=1, source_target_pairs={{0,2},{1,3},{2,0},{3,1},{4,6},{5,7},{6,4},{7,5},{8,10},{9,11},{10,... | collective-permute-start | bytes 1572872 | tf_op jit(solution)/shard_map/ppermute | solution.py:31
  41.3 7.3 %collective-permute-start.7 = (bf16[4,2,128,128]{3,2,1,0:T(8,128)(2,1)S(1)}, bf16[4,2,128,128]{3,2,1,0:T(8,128)(2,1)S(1)}, u32[]{:S(2)}, u32[]{:S(2)}) collective-permute-start(bf16[4,2,128,128]{3,2,1,0:T(8,128)(2,1)S(1)} %copy.12), channel_id=1, source_target_pairs={{0,2},{1,3},{2,0},{3,1},{4,6},{5,7},{6,4},{7,5},{8,10},{9,11},{10,... | collective-permute-start | bytes 786440 | tf_op jit(solution)/shard_map/ppermute | solution.py:31
  48.7 6.4 %collective-permute-start.3 = (f32[2,2,128,128]{3,2,1,0:T(8,128)S(1)}, f32[2,2,128,128]{3,2,1,0:T(8,128)S(1)}, u32[]{:S(2)}, u32[]{:S(2)}) collective-permute-start(f32[2,2,128,128]{3,2,1,0:T(8,128)S(1)} %dynamic-slice_bitcast_fusion.2), channel_id=1, source_target_pairs={{0,4},{1,5},{2,6},{3,7},{4,0},{5,1},{6,2},{7,3},{8,12},{9,13},{10,... | collective-permute-start | bytes 786440 | tf_op jit(solution)/shard_map/ppermute | solution.py:31
  49.1 14.5 %collective-permute-start.8 = (bf16[8,2,128,128]{3,2,1,0:T(8,128)(2,1)S(1)}, bf16[8,2,128,128]{3,2,1,0:T(8,128)(2,1)S(1)}, u32[]{:S(2)}, u32[]{:S(2)}) collective-permute-start(bf16[8,2,128,128]{3,2,1,0:T(8,128)(2,1)S(1)} %bitcast.81), channel_id=1, source_target_pairs={{0,4},{1,5},{2,6},{3,7},{4,0},{5,1},{6,2},{7,3},{8,12},{9,13},{10,... | collective-permute-start | bytes 1572872 | tf_op jit(solution)/shard_map/ppermute | solution.py:31
  55.2 14.5 %collective-permute-start.4 = (f32[2,128,128]{2,1,0:T(8,128)S(1)}, f32[2,128,128]{2,1,0:T(8,128)S(1)}, u32[]{:S(2)}, u32[]{:S(2)}) collective-permute-start(f32[2,128,128]{2,1,0:T(8,128)S(1)} %dynamic-slice_bitcast_fusion.3), channel_id=1, source_target_pairs={{0,8},{1,9},{2,10},{3,11},{4,12},{5,13},{6,14},{7,15},{8,0},{9,1},... | collective-permute-start | bytes 393224 | tf_op jit(solution)/shard_map/ppermute | solution.py:31
  68.5 2.8 %copy-start.3 = (bf16[128,256]{1,0:T(8,128)(2,1)S(1)}, bf16[128,256]{1,0:T(8,128)(2,1)}, u32[]{:S(2)}) copy-start(bf16[128,256]{1,0:T(8,128)(2,1)} %param.12) | copy-start | bytes 196612
  69.6 1.4 %collective-permute-start.9 = (f32[2,128,128]{1,2,0:T(8,128)S(1)}, f32[2,128,128]{1,2,0:T(8,128)S(1)}, u32[]{:S(2)}, u32[]{:S(2)}) collective-permute-start(f32[2,128,128]{1,2,0:T(8,128)S(1)} %bitcast.90), channel_id=1, source_target_pairs={{0,16},{16,0},{1,17},{17,1},{2,18},{18,2},{3,19},{19,3},{4,20},{20... | collective-permute-start | bytes 393224 | tf_op jit(solution)/shard_map/ppermute | solution.py:36

commit v12 on v3

--- a/solution.py
+++ b/solution.py
@@ -101,7 +101,15 @@
         mine = (me >> _pick(parity, order, t)) & 1
         keep = lax.dynamic_index_in_dim(data, mine, axis=0, keepdims=False)
         other = lax.dynamic_index_in_dim(data, 1 - mine, axis=0, keepdims=False)
-        data = keep + _swap_col(other, row_size, col_size, (order[0][t], order[1][t]))
+        bits = (order[0][t], order[1][t])
+        if other.shape[0] % 2 == 0:
+            half = other.shape[0] // 2
+            got = jnp.concatenate(
+                [_swap_col(other[:half], row_size, col_size, bits),
+                 _swap_col(other[half:], row_size, col_size, bits)], axis=0)
+        else:
+            got = _swap_col(other, row_size, col_size, bits)
+        data = keep + got
     return data
 
 

time: 62.8 us -> 71 us (1.13); the launches traced: 63.7 us -> 70.4 us
  waiting for transfers between devices: 23.6 us -> 30.9 us
  Pallas kernels: 7.53 us -> 10.8 us
  other arithmetic: 9.73 us -> 7.07 us
  starting transfers between devices: 17.4 us -> 15.7 us
    ppermute x8 -> x12, waiting for transfers between devices: 23.6 us -> 29.7 us  [_swap_col(): return lax.ppermute(x, ('row', 'col'), perm)]
    slice x0 -> x4, local copies, waits for them, and re-layouts: none -> 2.52 us  [scatter_sum_col(): other[:half]]
    another operation x7, other arithmetic: 3.13 us -> 1.34 us  [gather_col(): have = jnp.stack([lo, hi], axis=0).reshape((-1,) + have.shape[1:])]
    pallas_call x1, Pallas kernels: 3.97 us -> 5.61 us  [along_call(): pl.pallas_call(kernel, grid_spec=spec, out_shape=jax.ShapeDtypeStruct((nr...]
    pallas_call x1, Pallas kernels: 3.56 us -> 5.17 us  [against_call(): pl.pallas_call(kernel, grid_spec=spec, out_shape=jax.ShapeDtypeStruct((nc...]
    squeeze x4 -> x0, local copies, waits for them, and re-layouts: 1.38 us -> none  [scatter_sum_col(): other = lax.dynamic_index_in_dim(data, 1 - mine, axis=0, keepdims=False)]
    ppermute x2, starting transfers between devices: 1.7 us -> 0.52 us  [_swap(): return lax.ppermute(x, axis, perm)]
    ppermute x2, waiting for transfers between devices: 0.01 us -> 1.17 us  [_swap(): return lax.ppermute(x, axis, perm)]
  transfers between devices with their start and end apart: 10 -> 14, of which waited for: 6 -> 7; matrix products, arithmetic and copies ran while one was open for 21% -> 16% of each run, Pallas kernels for 12% -> 15%
where the time goes in v12:
time: 71 us; the launch traced here: 70.4 us
  waiting for transfers between devices  30.9 us (44%)
  starting transfers between devices  15.7 us (22%)
  Pallas kernels  10.8 us (15%)
  other arithmetic  7.07 us (10%)
  local copies, waits for them, and re-layouts  3.94 us (6%)
  matrix products  1.16 us (2%)
  between operations  0.9 us (1%)
    ppermute x12, waiting for transfers between devices, _swap_col(): return lax.ppermute(x, ('row', 'col'), perm)  29.7 us
    ppermute x12, starting transfers between devices, _swap_col(): return lax.ppermute(x, ('row', 'col'), perm)  15.1 us
    pallas_call x1, Pallas kernels, along_call(): pl.pallas_call(kernel, grid_spec=spec, out_shape=jax.ShapeDtypeStruct((nr...  5.61 us
    pallas_call x1, Pallas kernels, against_call(): pl.pallas_call(kernel, grid_spec=spec, out_shape=jax.ShapeDtypeStruct((nc...  5.17 us
    slice x4, local copies, waits for them, and re-layouts, scatter_sum_col(): other[:half]  2.52 us
    another operation x2, other arithmetic, gather_row(): have = jnp.stack([lo, hi], axis=0).reshape((-1,) + have.shape[1:])  1.52 us
  transfers between devices with their start and end apart: 14, of which 7 were waited for; matrix products, arithmetic and copies ran while one was open for 16% of the time, Pallas kernels for 15%

profile of v12, /device:TPU:0, one launch (start us, length us, event | category | flops | bytes accessed | tf_op | source)
XLA Modules:
  0.0 70.4 jit_solution(4601852897383207886)
XLA Ops:
  0.0 0.5 collective-permute-start
  0.5 3.7 %collective-permute-start.9 = (bf16[1,2,128,128]{2,3,1,0:T(8,128)(2,1)}, bf16[1,2,128,128]{2,3,1,0:T(8,128)(2,1)S(1)}, u32[]{:S(2)}, u32[]{:S(2)}) collective-permute-start(bf16[1,2,128,128]{2,3,1,0:T(8,128)(2,1)} %bitcast.111), channel_id=1, source_target_pairs={{0,8},{1,9},{2,10},{3,11},{4,12},{5,13},{6,14},{7,15},{8,0},{9,1},... | collective-permute-start | bytes 196616 | tf_op jit(solution)/shard_map/ppermute | solution.py:31
  4.1 1.2 %multiply_add_fusion.1 = (s32[128]{0:T(128)}, s32[128]{0:T(128)S(1)}) fusion(s32[]{:T(128)S(6)} %select_n.141, s32[]{:T(128)S(6)} %select_n.143, s32[]{:T(128)S(6)} %select_n.142, s32[1,1,128]{2,1,0:T(1,128)} %param.9), kind=kLoop, calls=%fused_computation.42 | loop fusion | flops 4736 | bytes 1548 | tf_op jit(solution)/shard_map/add | solution.py:231
  5.3 1.2 %clamp_bitcast_fusion.cols_ref = s32[128]{0:T(128)} fusion(s32[1,1,128]{2,1,0:T(1,128)} %param.10), kind=kLoop, calls=%fused_computation.41 | loop fusion | flops 128 | bytes 1024 | tf_op jit(solution)/shard_map/jit(clip)/min | solution.py:218
  7.2 0.9 %select_bitcast_fusion.9 = (bf16[1,1,256,128]{3,2,1,0:T(8,128)(2,1)S(1)}, bf16[1,1,256,128]{3,2,1,0:T(8,128)(2,1)S(1)}) fusion(bf16[1,256,128]{2,1,0:T(8,128)(2,1)S(1)} %collective-permute-done, pred[]{:T(512)S(6)} %eq.19, bf16[256,128]{1,0:T(8,128)(2,1)} %param.7), kind=kLoop, calls=%fused_computation.30 | loop fusion | flops 65536 | bytes 262145 | tf_op jit(solution)/shard_map/stack | solution.py:52
  8.0 0.7 pad_maximum_fusion.3
  8.7 5.6 %shard_map.73 = f32[32,128,128]{2,1,0:T(8,128)} custom-call(s32[128]{0:T(128)} %get-tuple-element.5.rows_ref, s32[128]{0:T(128)} %clamp_bitcast_fusion.cols_ref, s32[1]{0:T(128)} %bitcast.2.cnt_ref, bf16[128,128,128]{2,1,0:T(8,128)(2,1)} %bitcast.100, bf16[4,128,128]{2,1,0:T(8,128)(2,1)} %bitcast.109), custom_call_target="tpu_custom_call" | custom-call | tf_op jit(solution)/shard_map/pallas_call | solution.py:155
  14.3 2.4 %dynamic-slice_bitcast_fusion.1 = (f32[1,2,2,2,128,128]{5,4,3,2,1,0:T(8,128)}, f32[1,2,2,2,128,128]{5,4,3,2,1,0:T(8,128)}) fusion(f32[2,2,2,2,2,128,128]{6,5,4,3,2,1,0:T(8,128)} %bitcast.102, s32[]{:T(128)S(6)} %select_n.149, s32[]{:T(128)S(6)} %add.121), kind=kLoop, calls=%fused_computation.5 | loop fusion | bytes 2097160 | tf_op jit(solution)/shard_map/slice | solution.py:108
  16.7 2.0 %collective-permute-start.2 = (f32[1,2,2,2,128,128]{5,4,3,2,1,0:T(8,128)}, f32[1,2,2,2,128,128]{5,4,3,2,1,0:T(8,128)}, u32[]{:S(2)}, u32[]{:S(2)}) collective-permute-start(f32[1,2,2,2,128,128]{5,4,3,2,1,0:T(8,128)} %get-tuple-element.8), channel_id=1, source_target_pairs={{0,1},{1,0},{2,3},{3,2},{4,5},{5,4},{6,7},{7,6},{8,9},{9,8},{10,11... | collective-permute-start | bytes 1572872 | tf_op jit(solution)/shard_map/ppermute | solution.py:31
  18.8 0.1 collective-permute-start.10
  18.9 14.2 %collective-permute-done.10 = bf16[2,2,128,128]{2,3,1,0:T(8,128)(2,1)S(1)} collective-permute-done((bf16[2,2,128,128]{2,3,1,0:T(8,128)(2,1)S(1)}, bf16[2,2,128,128]{2,3,1,0:T(8,128)(2,1)S(1)}, u32[]{:S(2)}, u32[]{:S(2)}) %collective-permute-start.10) | collective-permute-done | bytes 131104 | tf_op jit(solution)/shard_map/ppermute | solution.py:31
  33.2 0.2 copy.12
  33.4 2.1 %collective-permute-start.11 = (bf16[4,2,128,128]{3,2,1,0:T(8,128)(2,1)S(1)}, bf16[4,2,128,128]{3,2,1,0:T(8,128)(2,1)S(1)}, u32[]{:S(2)}, u32[]{:S(2)}) collective-permute-start(bf16[4,2,128,128]{3,2,1,0:T(8,128)(2,1)S(1)} %copy.12), channel_id=1, source_target_pairs={{0,2},{1,3},{2,0},{3,1},{4,6},{5,7},{6,4},{7,5},{8,10},{9,11},{10,... | collective-permute-start | bytes 786440 | tf_op jit(solution)/shard_map/ppermute | solution.py:31
  35.5 1.2 %maximum_add_fusion = f32[2,2,2,2,128,128]{5,4,3,2,1,0:T(8,128)S(1)} fusion(f32[1,2,2,2,128,128]{5,4,3,2,1,0:T(8,128)} %collective-permute-done.2, f32[1,2,2,2,128,128]{5,4,3,2,1,0:T(8,128)S(1)} %collective-permute-done.1, f32[2,2,2,2,2,128,128]{6,5,4,3,2,1,0:T(8,128)S(1)} %bitcast.103, s32[]{:T(128)S(6)} %select_n.148), kind=kLoop, calls=%fused_computation.2 | loop fusion | flops 524288 | bytes 3145732 | tf_op jit(solution)/shard_map/add | solution.py:112
  36.7 0.1 collective-permute-start.3
  36.8 2.0 %collective-permute-start.4 = (f32[1,2,2,128,128]{4,3,2,1,0:T(8,128)S(1)}, f32[1,2,2,128,128]{4,3,2,1,0:T(8,128)S(1)}, u32[]{:S(2)}, u32[]{:S(2)}) collective-permute-start(f32[1,2,2,128,128]{4,3,2,1,0:T(8,128)S(1)} %get-tuple-element.10), channel_id=1, source_target_pairs={{0,2},{1,3},{2,0},{3,1},{4,6},{5,7},{6,4},{7,5},{8,10},{9,11},{10,... | collective-permute-start | bytes 786440 | tf_op jit(solution)/shard_map/ppermute | solution.py:31
  38.8 1.0 %collective-permute-done.11 = bf16[4,2,128,128]{3,2,1,0:T(8,128)(2,1)S(1)} collective-permute-done((bf16[4,2,128,128]{3,2,1,0:T(8,128)(2,1)S(1)}, bf16[4,2,128,128]{3,2,1,0:T(8,128)(2,1)S(1)}, u32[]{:S(2)}, u32[]{:S(2)}) %collective-permute-start.11) | collective-permute-done | bytes 262176 | tf_op jit(solution)/shard_map/ppermute | solution.py:31
  40.0 5.0 %collective-permute-done.3 = f32[1,2,2,128,128]{4,3,2,1,0:T(8,128)S(1)} collective-permute-done((f32[1,2,2,128,128]{4,3,2,1,0:T(8,128)S(1)}, f32[1,2,2,128,128]{4,3,2,1,0:T(8,128)S(1)}, u32[]{:S(2)}, u32[]{:S(2)}) %collective-permute-start.3) | collective-permute-done | bytes 262176 | tf_op jit(solution)/shard_map/ppermute | solution.py:31
  45.0 5.6 %collective-permute-done.4 = f32[1,2,2,128,128]{4,3,2,1,0:T(8,128)S(1)} collective-permute-done((f32[1,2,2,128,128]{4,3,2,1,0:T(8,128)S(1)}, f32[1,2,2,128,128]{4,3,2,1,0:T(8,128)S(1)}, u32[]{:S(2)}, u32[]{:S(2)}) %collective-permute-start.4) | collective-permute-done | bytes 262176 | tf_op jit(solution)/shard_map/ppermute | solution.py:31
  50.8 2.0 %collective-permute-start.6 = (f32[1,2,128,128]{3,2,1,0:T(8,128)S(1)}, f32[1,2,128,128]{3,2,1,0:T(8,128)S(1)}, u32[]{:S(2)}, u32[]{:S(2)}) collective-permute-start(f32[1,2,128,128]{3,2,1,0:T(8,128)S(1)} %get-tuple-element.14), channel_id=1, source_target_pairs={{0,4},{1,5},{2,6},{3,7},{4,0},{5,1},{6,2},{7,3},{8,12},{9,13},{10,... | collective-permute-start | bytes 393224 | tf_op jit(solution)/shard_map/ppermute | solution.py:31
  52.8 0.5 multiply_add_fusion.rows_ref
  53.3 2.4 %collective-permute-done.5 = f32[1,2,128,128]{3,2,1,0:T(8,128)S(1)} collective-permute-done((f32[1,2,128,128]{3,2,1,0:T(8,128)S(1)}, f32[1,2,128,128]{3,2,1,0:T(8,128)S(1)}, u32[]{:S(2)}, u32[]{:S(2)}) %collective-permute-start.5) | collective-permute-done | bytes 131104 | tf_op jit(solution)/shard_map/ppermute | solution.py:31
  55.8 1.4 %collective-permute-done.6 = f32[1,2,128,128]{3,2,1,0:T(8,128)S(1)} collective-permute-done((f32[1,2,128,128]{3,2,1,0:T(8,128)S(1)}, f32[1,2,128,128]{3,2,1,0:T(8,128)S(1)}, u32[]{:S(2)}, u32[]{:S(2)}) %collective-permute-start.6) | collective-permute-done | bytes 131104 | tf_op jit(solution)/shard_map/ppermute | solution.py:31
  57.2 0.8 %collective-permute-start.7 = (f32[1,128,128]{2,1,0:T(8,128)S(1)}, f32[1,128,128]{2,1,0:T(8,128)S(1)}, u32[]{:S(2)}, u32[]{:S(2)}) collective-permute-start(f32[1,128,128]{2,1,0:T(8,128)S(1)} %get-tuple-element.17), channel_id=1, source_target_pairs={{0,8},{1,9},{2,10},{3,11},{4,12},{5,13},{6,14},{7,15},{8,0},{9,1},... | collective-permute-start | bytes 196616 | tf_op jit(solution)/shard_map/ppermute | solution.py:31
  58.0 2.2 %collective-permute-start.8 = (f32[1,128,128]{2,1,0:T(8,128)S(1)}, f32[1,128,128]{2,1,0:T(8,128)S(1)}, u32[]{:S(2)}, u32[]{:S(2)}) collective-permute-start(f32[1,128,128]{2,1,0:T(8,128)S(1)} %get-tuple-element.18), channel_id=1, source_target_pairs={{0,8},{1,9},{2,10},{3,11},{4,12},{5,13},{6,14},{7,15},{8,0},{9,1},... | collective-permute-start | bytes 196616 | tf_op jit(solution)/shard_map/ppermute | solution.py:31
  60.2 0.1 select_bitcast_fusion.1
  60.4 1.1 %pad_maximum_fusion = bf16[2,8,2,128,128]{4,3,2,1,0:T(8,128)(2,1)} fusion(bf16[1,8,2,128,128]{4,3,2,1,0:T(8,128)(2,1)S(1)} %get-tuple-element.12, bf16[1,8,2,128,128]{4,3,2,1,0:T(8,128)(2,1)S(1)} %get-tuple-element.11), kind=kLoop, calls=%fused_computation.3 | loop fusion | flops 524288 | bytes 2097152 | tf_op jit(solution)/shard_map/stack | solution.py:90
  61.4 5.2 %shard_map.74 = f32[4,128,128]{2,1,0:T(8,128)} custom-call(s32[128]{0:T(128)} %multiply_add_fusion.rows_ref, s32[128]{0:T(128)} %clamp_bitcast_fusion.cols_ref, s32[1]{0:T(128)} %bitcast.2.cnt_ref, bf16[128,128,128]{2,1,0:T(8,128)(2,1)} %bitcast.101, bf16[32,128,128]{2,1,0:T(8,128)(2,1)} %bitcast.104), custom_call_target="tpu_custom_call" | custom-call | tf_op jit(solution)/shard_map/pallas_call | solution.py:197
  66.6 1.0 %constant_dynamic-slice_fusion.1 = (f32[1,2,128,128]{3,2,1,0:T(8,128)S(1)}, f32[1,2,128,128]{3,2,1,0:T(8,128)S(1)}) fusion(f32[2,2,128,128]{3,2,1,0:T(8,128)} %bitcast.106, s32[]{:T(128)S(6)} %select_n.168, s32[]{:T(128)S(6)} %select_n.169), kind=kLoop, calls=%fused_computation.32 | loop fusion | bytes 524296 | tf_op jit(solution)/shard_map/jit(dynamic_index_in_dim)/dynamic_slice | solution.py:71
  68.0 1.2 %collective-permute-done.13 = f32[2,128,128]{1,2,0:T(8,128)S(1)} collective-permute-done((f32[2,128,128]{1,2,0:T(8,128)S(1)}, f32[2,128,128]{1,2,0:T(8,128)S(1)}, u32[]{:S(2)}, u32[]{:S(2)}) %collective-permute-start.13) | collective-permute-done | bytes 131104 | tf_op jit(solution)/shard_map/ppermute | solution.py:36
  69.2 0.3 fusion.1
  69.5 0.9 %fusion = bf16[256,256]{1,0:T(8,128)(2,1)} fusion(f32[256,256]{1,0:T(8,128)S(1)} %fusion.1, f32[256,128]{1,0:T(8,128)S(1)} %bitcast_add_fusion.1, bf16[128,256]{1,0:T(8,128)(2,1)S(1)} %copy-done.3), kind=kOutput, calls=%fused_computation.1 | convolution fusion | flops 100794368 | bytes 589824 | tf_op jit(solution)/shard_map/dot_general | solution.py:254
  (38 shorter events, 0.8 us)
Async XLA Ops:
  0.0 69.2 %copy-start = (bf16[128,256]{1,0:T(8,128)(2,1)S(1)}, bf16[128,256]{1,0:T(8,128)(2,1)}, u32[]{:S(2)}) copy-start(bf16[128,256]{1,0:T(8,128)(2,1)} %param.13) | copy-start | bytes 196612
  0.0 7.1 %collective-permute-start = (bf16[1,256,128]{2,1,0:T(8,128)(2,1)}, bf16[1,256,128]{2,1,0:T(8,128)(2,1)S(1)}, u32[]{:S(2)}, u32[]{:S(2)}) collective-permute-start(bf16[1,256,128]{2,1,0:T(8,128)(2,1)} %bitcast.110), channel_id=1, source_target_pairs={{0,16},{16,0},{1,17},{17,1},{2,18},{18,2},{3,19},{19,3},{4,20},{20... | collective-permute-start | bytes 196616 | tf_op jit(solution)/shard_map/ppermute | solution.py:36
  0.5 18.3 %collective-permute-start.9 = (bf16[1,2,128,128]{2,3,1,0:T(8,128)(2,1)}, bf16[1,2,128,128]{2,3,1,0:T(8,128)(2,1)S(1)}, u32[]{:S(2)}, u32[]{:S(2)}) collective-permute-start(bf16[1,2,128,128]{2,3,1,0:T(8,128)(2,1)} %bitcast.111), channel_id=1, source_target_pairs={{0,8},{1,9},{2,10},{3,11},{4,12},{5,13},{6,14},{7,15},{8,0},{9,1},... | collective-permute-start | bytes 196616 | tf_op jit(solution)/shard_map/ppermute | solution.py:31
  14.3 4.5 %copy-start.2 = (bf16[256,128]{1,0:T(8,128)(2,1)S(1)}, bf16[256,128]{1,0:T(8,128)(2,1)}, u32[]{:S(2)}) copy-start(bf16[256,128]{1,0:T(8,128)(2,1)} %param.7) | copy-start | bytes 196612
  14.3 21.2 %copy-start.1 = (f32[32,128,128]{2,1,0:T(8,128)S(1)}, f32[32,128,128]{2,1,0:T(8,128)}, u32[]{:S(2)}) copy-start(f32[32,128,128]{2,1,0:T(8,128)} %shard_map.73) | copy-start | bytes 6291460
  16.7 18.8 %collective-permute-start.1 = (f32[1,2,2,2,128,128]{5,4,3,2,1,0:T(8,128)}, f32[1,2,2,2,128,128]{5,4,3,2,1,0:T(8,128)S(1)}, u32[]{:S(2)}, u32[]{:S(2)}) collective-permute-start(f32[1,2,2,2,128,128]{5,4,3,2,1,0:T(8,128)} %get-tuple-element.7), channel_id=1, source_target_pairs={{0,1},{1,0},{2,3},{3,2},{4,5},{5,4},{6,7},{7,6},{8,9},{9,8},{10,11... | collective-permute-start | bytes 1572872 | tf_op jit(solution)/shard_map/ppermute | solution.py:31
  16.7 18.8 %collective-permute-start.2 = (f32[1,2,2,2,128,128]{5,4,3,2,1,0:T(8,128)}, f32[1,2,2,2,128,128]{5,4,3,2,1,0:T(8,128)}, u32[]{:S(2)}, u32[]{:S(2)}) collective-permute-start(f32[1,2,2,2,128,128]{5,4,3,2,1,0:T(8,128)} %get-tuple-element.8), channel_id=1, source_target_pairs={{0,1},{1,0},{2,3},{3,2},{4,5},{5,4},{6,7},{7,6},{8,9},{9,8},{10,11... | collective-permute-start | bytes 1572872 | tf_op jit(solution)/shard_map/ppermute | solution.py:31
  18.8 14.3 %collective-permute-start.10 = (bf16[2,2,128,128]{2,3,1,0:T(8,128)(2,1)S(1)}, bf16[2,2,128,128]{2,3,1,0:T(8,128)(2,1)S(1)}, u32[]{:S(2)}, u32[]{:S(2)}) collective-permute-start(bf16[2,2,128,128]{2,3,1,0:T(8,128)(2,1)S(1)} %maximum_bitcast_fusion), channel_id=1, source_target_pairs={{0,1},{1,0},{2,3},{3,2},{4,5},{5,4},{6,7},{7,6},{8,9},{9,8},{10,11... | collective-permute-start | bytes 393224 | tf_op jit(solution)/shard_map/ppermute | solution.py:31
  33.4 6.5 %collective-permute-start.11 = (bf16[4,2,128,128]{3,2,1,0:T(8,128)(2,1)S(1)}, bf16[4,2,128,128]{3,2,1,0:T(8,128)(2,1)S(1)}, u32[]{:S(2)}, u32[]{:S(2)}) collective-permute-start(bf16[4,2,128,128]{3,2,1,0:T(8,128)(2,1)S(1)} %copy.12), channel_id=1, source_target_pairs={{0,2},{1,3},{2,0},{3,1},{4,6},{5,7},{6,4},{7,5},{8,10},{9,11},{10,... | collective-permute-start | bytes 786440 | tf_op jit(solution)/shard_map/ppermute | solution.py:31
  36.7 8.3 %collective-permute-start.3 = (f32[1,2,2,128,128]{4,3,2,1,0:T(8,128)S(1)}, f32[1,2,2,128,128]{4,3,2,1,0:T(8,128)S(1)}, u32[]{:S(2)}, u32[]{:S(2)}) collective-permute-start(f32[1,2,2,128,128]{4,3,2,1,0:T(8,128)S(1)} %get-tuple-element.9), channel_id=1, source_target_pairs={{0,2},{1,3},{2,0},{3,1},{4,6},{5,7},{6,4},{7,5},{8,10},{9,11},{10,... | collective-permute-start | bytes 786440 | tf_op jit(solution)/shard_map/ppermute | solution.py:31
  36.8 16.0 %copy-start.4 = (s32[1,1,128]{2,1,0:T(1,128)S(1)}, s32[1,1,128]{2,1,0:T(1,128)}, u32[]{:S(2)}) copy-start(s32[1,1,128]{2,1,0:T(1,128)} %param.9) | copy-start | bytes 1540
  36.8 13.8 %collective-permute-start.4 = (f32[1,2,2,128,128]{4,3,2,1,0:T(8,128)S(1)}, f32[1,2,2,128,128]{4,3,2,1,0:T(8,128)S(1)}, u32[]{:S(2)}, u32[]{:S(2)}) collective-permute-start(f32[1,2,2,128,128]{4,3,2,1,0:T(8,128)S(1)} %get-tuple-element.10), channel_id=1, source_target_pairs={{0,2},{1,3},{2,0},{3,1},{4,6},{5,7},{6,4},{7,5},{8,10},{9,11},{10,... | collective-permute-start | bytes 786440 | tf_op jit(solution)/shard_map/ppermute | solution.py:31
  40.0 20.3 %collective-permute-start.12 = (bf16[8,2,128,128]{3,2,1,0:T(8,128)(2,1)S(1)}, bf16[8,2,128,128]{3,2,1,0:T(8,128)(2,1)S(1)}, u32[]{:S(2)}, u32[]{:S(2)}) collective-permute-start(bf16[8,2,128,128]{3,2,1,0:T(8,128)(2,1)S(1)} %bitcast.105), channel_id=1, source_target_pairs={{0,4},{1,5},{2,6},{3,7},{4,0},{5,1},{6,2},{7,3},{8,12},{9,13},{10,... | collective-permute-start | bytes 1572872 | tf_op jit(solution)/shard_map/ppermute | solution.py:31
  50.7 5.0 %collective-permute-start.5 = (f32[1,2,128,128]{3,2,1,0:T(8,128)S(1)}, f32[1,2,128,128]{3,2,1,0:T(8,128)S(1)}, u32[]{:S(2)}, u32[]{:S(2)}) collective-permute-start(f32[1,2,128,128]{3,2,1,0:T(8,128)S(1)} %get-tuple-element.13), channel_id=1, source_target_pairs={{0,4},{1,5},{2,6},{3,7},{4,0},{5,1},{6,2},{7,3},{8,12},{9,13},{10,... | collective-permute-start | bytes 393224 | tf_op jit(solution)/shard_map/ppermute | solution.py:31
  50.8 6.4 %collective-permute-start.6 = (f32[1,2,128,128]{3,2,1,0:T(8,128)S(1)}, f32[1,2,128,128]{3,2,1,0:T(8,128)S(1)}, u32[]{:S(2)}, u32[]{:S(2)}) collective-permute-start(f32[1,2,128,128]{3,2,1,0:T(8,128)S(1)} %get-tuple-element.14), channel_id=1, source_target_pairs={{0,4},{1,5},{2,6},{3,7},{4,0},{5,1},{6,2},{7,3},{8,12},{9,13},{10,... | collective-permute-start | bytes 393224 | tf_op jit(solution)/shard_map/ppermute | solution.py:31
  57.2 10.7 %collective-permute-start.7 = (f32[1,128,128]{2,1,0:T(8,128)S(1)}, f32[1,128,128]{2,1,0:T(8,128)S(1)}, u32[]{:S(2)}, u32[]{:S(2)}) collective-permute-start(f32[1,128,128]{2,1,0:T(8,128)S(1)} %get-tuple-element.17), channel_id=1, source_target_pairs={{0,8},{1,9},{2,10},{3,11},{4,12},{5,13},{6,14},{7,15},{8,0},{9,1},... | collective-permute-start | bytes 196616 | tf_op jit(solution)/shard_map/ppermute | solution.py:31
  58.0 9.9 %collective-permute-start.8 = (f32[1,128,128]{2,1,0:T(8,128)S(1)}, f32[1,128,128]{2,1,0:T(8,128)S(1)}, u32[]{:S(2)}, u32[]{:S(2)}) collective-permute-start(f32[1,128,128]{2,1,0:T(8,128)S(1)} %get-tuple-element.18), channel_id=1, source_target_pairs={{0,8},{1,9},{2,10},{3,11},{4,12},{5,13},{6,14},{7,15},{8,0},{9,1},... | collective-permute-start | bytes 196616 | tf_op jit(solution)/shard_map/ppermute | solution.py:31
  66.6 2.8 %copy-start.3 = (bf16[128,256]{1,0:T(8,128)(2,1)S(1)}, bf16[128,256]{1,0:T(8,128)(2,1)}, u32[]{:S(2)}) copy-start(bf16[128,256]{1,0:T(8,128)(2,1)} %param.12) | copy-start | bytes 196612
  67.7 1.4 %collective-permute-start.13 = (f32[2,128,128]{1,2,0:T(8,128)S(1)}, f32[2,128,128]{1,2,0:T(8,128)S(1)}, u32[]{:S(2)}, u32[]{:S(2)}) collective-permute-start(f32[2,128,128]{1,2,0:T(8,128)S(1)} %bitcast.113), channel_id=1, source_target_pairs={{0,16},{16,0},{1,17},{17,1},{2,18},{18,2},{3,19},{19,3},{4,20},{20... | collective-permute-start | bytes 393224 | tf_op jit(solution)/shard_map/ppermute | solution.py:36

commit v13 on v3

--- a/solution.py
+++ b/solution.py
@@ -232,7 +232,18 @@
     mine_t = jnp.transpose(features.reshape(nbc, side, width), (0, 2, 1))
     if nb is not None:
         stripe_t = gather_col(mine_t, ag_order).reshape(nrb, width, side)
-        along = scatter_sum_col(fwd_parts.reshape((2,) * nb + (nbc, side, width)), rs_order)
+        cut = side // 4
+        parts = fwd_parts.reshape((2,) * nb + (nbc, side, width))
+        quarter = parts[..., :cut, :]
+        canon = []
+        for p in range(2):
+            order = rs_order[p]
+            perm = [order.index(b) for b in range(nb - 1, -1, -1)]
+            canon.append(jnp.transpose(quarter, perm + list(range(nb, nb + 3))))
+        quarter = jnp.where(parity == 0, canon[0], canon[1]).reshape(-1, width)
+        sc_part = lax.psum_scatter(quarter, "col", scatter_dimension=0, tiled=True)
+        rest = scatter_sum_col(parts[..., cut:, :], rs_order)
+        along = jnp.concatenate([sc_part.reshape(nbc, cut, width), rest], axis=1)
     else:
         stripe_t = lax.all_gather(mine_t, "col", axis=0, tiled=True)
         along = lax.psum_scatter(fwd_parts, "col", scatter_dimension=0, tiled=True)

time: 62.8 us -> 123 us (1.96); the launches traced: 63.7 us -> 123 us
  waiting for transfers between devices: 23.6 us -> 65 us
  between operations: 0.83 us -> 14.2 us
  local copies, waits for them, and re-layouts: 3.43 us -> 5.83 us
    reduce_scatter x0 -> x1, waiting for transfers between devices: none -> 48.5 us  [local(): sc_part = lax.psum_scatter(quarter, 'col', scatter_dimension=0, tiled=True)]
    ppermute x8, waiting for transfers between devices: 23.6 us -> 16.5 us  [_swap_col(): return lax.ppermute(x, ('row', 'col'), perm)]
    slice x0 -> x2, local copies, waits for them, and re-layouts: none -> 2.65 us  [the longest x1 1.54 us: local(): rest = scatter_sum_col(parts[..., cut:, :], rs_order)]
    ppermute x8, starting transfers between devices: 15.7 us -> 18.1 us  [_swap_col(): return lax.ppermute(x, ('row', 'col'), perm)]
  transfers between devices with their start and end apart: 10 -> 11, of which waited for: 6 -> 7; matrix products, arithmetic and copies ran while one was open for 21% -> 13% of each run, Pallas kernels for 12% -> 6%
where the time goes in v13:
time: 123 us
  waiting for transfers between devices  65 us (53%)
  starting transfers between devices  18.6 us (15%)
  between operations  14.2 us (12%)
  other arithmetic  10.4 us (8%)
  Pallas kernels  7.51 us (6%)
  local copies, waits for them, and re-layouts  5.83 us (5%)
    reduce_scatter x1, waiting for transfers between devices, local(): sc_part = lax.psum_scatter(quarter, 'col', scatter_dimension=0, tiled=True)  48.5 us
    ppermute x8, starting transfers between devices, _swap_col(): return lax.ppermute(x, ('row', 'col'), perm)  18.1 us
    ppermute x8, waiting for transfers between devices, _swap_col(): return lax.ppermute(x, ('row', 'col'), perm)  16.5 us
    pallas_call x1, Pallas kernels, along_call(): pl.pallas_call(kernel, grid_spec=spec, out_shape=jax.ShapeDtypeStruct((nr...  3.98 us
    pallas_call x1, Pallas kernels, against_call(): pl.pallas_call(kernel, grid_spec=spec, out_shape=jax.ShapeDtypeStruct((nc...  3.53 us
  transfers between devices with their start and end apart: 11, of which 7 were waited for; matrix products, arithmetic and copies ran while one was open for 13% of the time, Pallas kernels for 6%

profile of v13, /device:TPU:0, one launch (start us, length us, event | category | flops | bytes accessed | tf_op | source)
XLA Modules:
  0.0 122.7 jit_solution(16374749283940535809)
XLA Ops:
  7.0 3.6 %collective-permute-start.5 = (bf16[1,2,128,128]{2,3,1,0:T(8,128)(2,1)}, bf16[1,2,128,128]{2,3,1,0:T(8,128)(2,1)S(1)}, u32[]{:S(2)}, u32[]{:S(2)}) collective-permute-start(bf16[1,2,128,128]{2,3,1,0:T(8,128)(2,1)} %bitcast.113), channel_id=1, source_target_pairs={{0,8},{1,9},{2,10},{3,11},{4,12},{5,13},{6,14},{7,15},{8,0},{9,1},... | collective-permute-start | bytes 196616 | tf_op jit(solution)/shard_map/ppermute | solution.py:31
  10.6 1.2 multiply_add_fusion.1
  11.8 1.2 %multiply_add_fusion.rows_ref = s32[128]{0:T(128)} fusion(s32[128]{0:T(128)S(1)} %get-tuple-element.6, s32[]{:T(128)S(6)} %select_n.151, s32[]{:T(128)S(6)} %select_n.153, s32[]{:T(128)S(6)} %select_n.152, s32[1,1,128]{2,1,0:T(1,128)} %param.9), kind=kLoop, calls=%fused_computation.37 | loop fusion | flops 3712 | bytes 1548 | tf_op jit(solution)/shard_map/add | solution.py:224
  13.0 1.2 %clamp_bitcast_fusion.cols_ref = s32[128]{0:T(128)} fusion(s32[1,1,128]{2,1,0:T(1,128)} %param.10), kind=kLoop, calls=%fused_computation.38 | loop fusion | flops 128 | bytes 1024 | tf_op jit(solution)/shard_map/jit(clip)/min | solution.py:210
  15.0 0.9 select_bitcast_fusion.7
  15.8 1.6 %collective-permute-start.6 = (bf16[2,2,128,128]{2,3,1,0:T(8,128)(2,1)S(1)}, bf16[2,2,128,128]{2,3,1,0:T(8,128)(2,1)S(1)}, u32[]{:S(2)}, u32[]{:S(2)}) collective-permute-start(bf16[2,2,128,128]{2,3,1,0:T(8,128)(2,1)S(1)} %maximum_bitcast_fusion), channel_id=1, source_target_pairs={{0,1},{1,0},{2,3},{3,2},{4,5},{5,4},{6,7},{7,6},{8,9},{9,8},{10,11... | collective-permute-start | bytes 393224 | tf_op jit(solution)/shard_map/ppermute | solution.py:31
  17.4 0.9 select_bitcast_fusion.9
  18.3 0.7 pad_maximum_fusion.3
  19.0 4.0 %shard_map.73 = f32[32,128,128]{2,1,0:T(8,128)} custom-call(s32[128]{0:T(128)} %get-tuple-element.5.rows_ref, s32[128]{0:T(128)} %clamp_bitcast_fusion.cols_ref, s32[1]{0:T(128)} %bitcast.2.cnt_ref, bf16[128,128,128]{2,1,0:T(8,128)(2,1)} %bitcast.100, bf16[4,128,128]{2,1,0:T(8,128)(2,1)} %bitcast.110), custom_call_target="tpu_custom_call" | custom-call | tf_op jit(solution)/shard_map/pallas_call | solution.py:147
  22.9 1.5 %slice.9 = f32[2,2,2,2,2,96,128]{6,5,4,3,2,1,0:T(8,128)S(1)} slice(f32[2,2,2,2,2,128,128]{6,5,4,3,2,1,0:T(8,128)} %bitcast.102), slice={[0:2], [0:2], [0:2], [0:2], [0:2], [32:128], [0:128]} | slice | bytes 3145728 | tf_op jit(solution)/shard_map/slice | solution.py:245
  24.5 1.0 dynamic-slice_bitcast_fusion
  25.5 0.5 collective-permute-start.1
  26.2 2.1 %collective-permute-start.7 = (bf16[4,2,128,128]{3,2,1,0:T(8,128)(2,1)S(1)}, bf16[4,2,128,128]{3,2,1,0:T(8,128)(2,1)S(1)}, u32[]{:S(2)}, u32[]{:S(2)}) collective-permute-start(bf16[4,2,128,128]{3,2,1,0:T(8,128)(2,1)S(1)} %copy.15), channel_id=1, source_target_pairs={{0,2},{1,3},{2,0},{3,1},{4,6},{5,7},{6,4},{7,5},{8,10},{9,11},{10,... | collective-permute-start | bytes 786440 | tf_op jit(solution)/shard_map/ppermute | solution.py:31
  28.3 1.1 fusion.1
  29.4 3.2 %collective-permute-done.7 = bf16[4,2,128,128]{3,2,1,0:T(8,128)(2,1)S(1)} collective-permute-done((bf16[4,2,128,128]{3,2,1,0:T(8,128)(2,1)S(1)}, bf16[4,2,128,128]{3,2,1,0:T(8,128)(2,1)S(1)}, u32[]{:S(2)}, u32[]{:S(2)}) %collective-permute-start.7) | collective-permute-done | bytes 262176 | tf_op jit(solution)/shard_map/ppermute | solution.py:31
  32.8 3.2 %collective-permute-start.8 = (bf16[8,2,128,128]{3,2,1,0:T(8,128)(2,1)S(1)}, bf16[8,2,128,128]{3,2,1,0:T(8,128)(2,1)S(1)}, u32[]{:S(2)}, u32[]{:S(2)}) collective-permute-start(bf16[8,2,128,128]{3,2,1,0:T(8,128)(2,1)S(1)} %bitcast.105), channel_id=1, source_target_pairs={{0,4},{1,5},{2,6},{3,7},{4,0},{5,1},{6,2},{7,3},{8,12},{9,13},{10,... | collective-permute-start | bytes 1572872 | tf_op jit(solution)/shard_map/ppermute | solution.py:31
  36.0 0.9 copy_select_fusion
  36.9 2.9 %collective-permute-done.1 = f32[2,2,2,2,96,128]{5,4,3,2,1,0:T(8,128)} collective-permute-done((f32[2,2,2,2,96,128]{5,4,3,2,1,0:T(8,128)}, f32[2,2,2,2,96,128]{5,4,3,2,1,0:T(8,128)}, u32[]{:S(2)}, u32[]{:S(2)}) %collective-permute-start.1) | collective-permute-done | bytes 786464 | tf_op jit(solution)/shard_map/ppermute | solution.py:31
  39.8 1.2 bitcast_add_fusion
  41.0 0.8 dynamic-slice_bitcast_fusion.1
  41.8 1.5 %collective-permute-start.2 = (f32[2,2,2,96,128]{4,3,2,1,0:T(8,128)}, f32[2,2,2,96,128]{4,3,2,1,0:T(8,128)S(1)}, u32[]{:S(2)}, u32[]{:S(2)}) collective-permute-start(f32[2,2,2,96,128]{4,3,2,1,0:T(8,128)} %dynamic-slice_bitcast_fusion.1), channel_id=1, source_target_pairs={{0,2},{1,3},{2,0},{3,1},{4,6},{5,7},{6,4},{7,5},{8,10},{9,11},{10,... | collective-permute-start | bytes 1179656 | tf_op jit(solution)/shard_map/ppermute | solution.py:31
  43.4 1.1 pad_maximum_fusion
  44.5 3.5 %shard_map.74 = f32[4,128,128]{2,1,0:T(8,128)} custom-call(s32[128]{0:T(128)} %multiply_add_fusion.rows_ref, s32[128]{0:T(128)} %clamp_bitcast_fusion.cols_ref, s32[1]{0:T(128)} %bitcast.2.cnt_ref, bf16[128,128,128]{2,1,0:T(8,128)(2,1)} %bitcast.101, bf16[32,128,128]{2,1,0:T(8,128)(2,1)} %bitcast.104), custom_call_target="tpu_custom_call" | custom-call | tf_op jit(solution)/shard_map/pallas_call | solution.py:189
  48.1 1.0 constant_dynamic-slice_fusion.1
  49.3 0.8 collective-permute-done.2
  50.2 3.3 %collective-permute-start.3 = (f32[2,2,96,128]{3,2,1,0:T(8,128)S(1)}, f32[2,2,96,128]{3,2,1,0:T(8,128)S(1)}, u32[]{:S(2)}, u32[]{:S(2)}) collective-permute-start(f32[2,2,96,128]{3,2,1,0:T(8,128)S(1)} %dynamic-slice_bitcast_fusion.2), channel_id=1, source_target_pairs={{0,4},{1,5},{2,6},{3,7},{4,0},{5,1},{6,2},{7,3},{8,12},{9,13},{10,... | collective-permute-start | bytes 589832 | tf_op jit(solution)/shard_map/ppermute | solution.py:31
  53.5 3.8 %collective-permute-done.3 = f32[2,2,96,128]{3,2,1,0:T(8,128)S(1)} collective-permute-done((f32[2,2,96,128]{3,2,1,0:T(8,128)S(1)}, f32[2,2,96,128]{3,2,1,0:T(8,128)S(1)}, u32[]{:S(2)}, u32[]{:S(2)}) %collective-permute-start.3) | collective-permute-done | bytes 196640 | tf_op jit(solution)/shard_map/ppermute | solution.py:31
  57.4 2.3 %collective-permute-start.4 = (f32[2,96,128]{2,1,0:T(8,128)S(1)}, f32[2,96,128]{2,1,0:T(8,128)S(1)}, u32[]{:S(2)}, u32[]{:S(2)}) collective-permute-start(f32[2,96,128]{2,1,0:T(8,128)S(1)} %dynamic-slice_bitcast_fusion.3), channel_id=1, source_target_pairs={{0,8},{1,9},{2,10},{3,11},{4,12},{5,13},{6,14},{7,15},{8,0},{9,1},... | collective-permute-start | bytes 294920 | tf_op jit(solution)/shard_map/ppermute | solution.py:31
  60.0 5.6 %collective-permute-done.4 = f32[2,96,128]{2,1,0:T(8,128)S(1)} collective-permute-done((f32[2,96,128]{2,1,0:T(8,128)S(1)}, f32[2,96,128]{2,1,0:T(8,128)S(1)}, u32[]{:S(2)}, u32[]{:S(2)}) %collective-permute-start.4) | collective-permute-done | bytes 98336 | tf_op jit(solution)/shard_map/ppermute | solution.py:31
  65.6 48.5 %reduce-scatter.2.cloned.1.call-done = f32[64,128]{1,0:T(8,128)} async-done(((f32[1024,128]{1,0:T(8,128)}), f32[64,128]{1,0:T(8,128)}) %reduce-scatter.2.cloned.1.call-update) | async-done | bytes 32784 | tf_op jit(solution)/shard_map/reduce_scatter | solution.py:244
  114.1 0.8 pad_maximum_fusion.4
  114.9 0.9 fusion
  (29 shorter events, 1.7 us)
Async XLA Ops:
  6.5 53.2 %copy-start = (bf16[128,256]{1,0:T(8,128)(2,1)S(1)}, bf16[128,256]{1,0:T(8,128)(2,1)}, u32[]{:S(2)}) copy-start(bf16[128,256]{1,0:T(8,128)(2,1)} %param.13) | copy-start | bytes 196612
  6.5 107.6 %reduce-scatter.2.cloned.1.call-start = ((), (), s32[]{:S(2)}) async-start(), calls=%async_computation.1 | async-start | bytes 557056 | tf_op jit(solution)/shard_map/reduce_scatter | solution.py:244
  6.5 10.9 %collective-permute-start = (bf16[1,256,128]{2,1,0:T(8,128)(2,1)}, bf16[1,256,128]{2,1,0:T(8,128)(2,1)S(1)}, u32[]{:S(2)}, u32[]{:S(2)}) collective-permute-start(bf16[1,256,128]{2,1,0:T(8,128)(2,1)} %bitcast.112), channel_id=1, source_target_pairs={{0,16},{16,0},{1,17},{17,1},{2,18},{18,2},{3,19},{19,3},{4,20},{20... | collective-permute-start | bytes 196616 | tf_op jit(solution)/shard_map/ppermute | solution.py:36
  7.0 8.0 %collective-permute-start.5 = (bf16[1,2,128,128]{2,3,1,0:T(8,128)(2,1)}, bf16[1,2,128,128]{2,3,1,0:T(8,128)(2,1)S(1)}, u32[]{:S(2)}, u32[]{:S(2)}) collective-permute-start(bf16[1,2,128,128]{2,3,1,0:T(8,128)(2,1)} %bitcast.113), channel_id=1, source_target_pairs={{0,8},{1,9},{2,10},{3,11},{4,12},{5,13},{6,14},{7,15},{8,0},{9,1},... | collective-permute-start | bytes 196616 | tf_op jit(solution)/shard_map/ppermute | solution.py:31
  15.8 10.1 %collective-permute-start.6 = (bf16[2,2,128,128]{2,3,1,0:T(8,128)(2,1)S(1)}, bf16[2,2,128,128]{2,3,1,0:T(8,128)(2,1)S(1)}, u32[]{:S(2)}, u32[]{:S(2)}) collective-permute-start(bf16[2,2,128,128]{2,3,1,0:T(8,128)(2,1)S(1)} %maximum_bitcast_fusion), channel_id=1, source_target_pairs={{0,1},{1,0},{2,3},{3,2},{4,5},{5,4},{6,7},{7,6},{8,9},{9,8},{10,11... | collective-permute-start | bytes 393224 | tf_op jit(solution)/shard_map/ppermute | solution.py:31
  25.5 14.3 %collective-permute-start.1 = (f32[2,2,2,2,96,128]{5,4,3,2,1,0:T(8,128)}, f32[2,2,2,2,96,128]{5,4,3,2,1,0:T(8,128)}, u32[]{:S(2)}, u32[]{:S(2)}) collective-permute-start(f32[2,2,2,2,96,128]{5,4,3,2,1,0:T(8,128)} %dynamic-slice_bitcast_fusion), channel_id=1, source_target_pairs={{0,1},{1,0},{2,3},{3,2},{4,5},{5,4},{6,7},{7,6},{8,9},{9,8},{10,11... | collective-permute-start | bytes 2359304 | tf_op jit(solution)/shard_map/ppermute | solution.py:31
  26.2 6.5 %collective-permute-start.7 = (bf16[4,2,128,128]{3,2,1,0:T(8,128)(2,1)S(1)}, bf16[4,2,128,128]{3,2,1,0:T(8,128)(2,1)S(1)}, u32[]{:S(2)}, u32[]{:S(2)}) collective-permute-start(bf16[4,2,128,128]{3,2,1,0:T(8,128)(2,1)S(1)} %copy.15), channel_id=1, source_target_pairs={{0,2},{1,3},{2,0},{3,1},{4,6},{5,7},{6,4},{7,5},{8,10},{9,11},{10,... | collective-permute-start | bytes 786440 | tf_op jit(solution)/shard_map/ppermute | solution.py:31
  32.8 10.6 %collective-permute-start.8 = (bf16[8,2,128,128]{3,2,1,0:T(8,128)(2,1)S(1)}, bf16[8,2,128,128]{3,2,1,0:T(8,128)(2,1)S(1)}, u32[]{:S(2)}, u32[]{:S(2)}) collective-permute-start(bf16[8,2,128,128]{3,2,1,0:T(8,128)(2,1)S(1)} %bitcast.105), channel_id=1, source_target_pairs={{0,4},{1,5},{2,6},{3,7},{4,0},{5,1},{6,2},{7,3},{8,12},{9,13},{10,... | collective-permute-start | bytes 1572872 | tf_op jit(solution)/shard_map/ppermute | solution.py:31
  41.8 8.3 %collective-permute-start.2 = (f32[2,2,2,96,128]{4,3,2,1,0:T(8,128)}, f32[2,2,2,96,128]{4,3,2,1,0:T(8,128)S(1)}, u32[]{:S(2)}, u32[]{:S(2)}) collective-permute-start(f32[2,2,2,96,128]{4,3,2,1,0:T(8,128)} %dynamic-slice_bitcast_fusion.1), channel_id=1, source_target_pairs={{0,2},{1,3},{2,0},{3,1},{4,6},{5,7},{6,4},{7,5},{8,10},{9,11},{10,... | collective-permute-start | bytes 1179656 | tf_op jit(solution)/shard_map/ppermute | solution.py:31
  49.1 65.8 %copy-start.1 = (bf16[128,256]{1,0:T(8,128)(2,1)S(1)}, bf16[128,256]{1,0:T(8,128)(2,1)}, u32[]{:S(2)}) copy-start(bf16[128,256]{1,0:T(8,128)(2,1)} %param.12) | copy-start | bytes 196612
  49.3 4.3 %collective-permute-start.9 = (f32[2,128,128]{1,2,0:T(8,128)S(1)}, f32[2,128,128]{1,2,0:T(8,128)S(1)}, u32[]{:S(2)}, u32[]{:S(2)}) collective-permute-start(f32[2,128,128]{1,2,0:T(8,128)S(1)} %bitcast.115), channel_id=1, source_target_pairs={{0,16},{16,0},{1,17},{17,1},{2,18},{18,2},{3,19},{19,3},{4,20},{20... | collective-permute-start | bytes 393224 | tf_op jit(solution)/shard_map/ppermute | solution.py:36
  50.2 7.2 %collective-permute-start.3 = (f32[2,2,96,128]{3,2,1,0:T(8,128)S(1)}, f32[2,2,96,128]{3,2,1,0:T(8,128)S(1)}, u32[]{:S(2)}, u32[]{:S(2)}) collective-permute-start(f32[2,2,96,128]{3,2,1,0:T(8,128)S(1)} %dynamic-slice_bitcast_fusion.2), channel_id=1, source_target_pairs={{0,4},{1,5},{2,6},{3,7},{4,0},{5,1},{6,2},{7,3},{8,12},{9,13},{10,... | collective-permute-start | bytes 589832 | tf_op jit(solution)/shard_map/ppermute | solution.py:31
  57.4 8.2 %collective-permute-start.4 = (f32[2,96,128]{2,1,0:T(8,128)S(1)}, f32[2,96,128]{2,1,0:T(8,128)S(1)}, u32[]{:S(2)}, u32[]{:S(2)}) collective-permute-start(f32[2,96,128]{2,1,0:T(8,128)S(1)} %dynamic-slice_bitcast_fusion.3), channel_id=1, source_target_pairs={{0,8},{1,9},{2,10},{3,11},{4,12},{5,13},{6,14},{7,15},{8,0},{9,1},... | collective-permute-start | bytes 294920 | tf_op jit(solution)/shard_map/ppermute | solution.py:31
Sparse Core Ops, SparseCore 0:
  37.0 77.0 reduce-scatter.1

commit v14 on v3

--- a/solution.py
+++ b/solution.py
@@ -106,7 +106,7 @@
 
 
 def _chunk(slots):
-    return 32 if slots % 32 == 0 else slots
+    return 64 if slots % 64 == 0 else slots
 
 
 def along_call(rows, cols, cnt, values, group, nrb):

time: 62.8 us -> 63.3 us (level); the launches traced: 63.7 us -> 62.4 us
  starting transfers between devices: 17.4 us -> 13.2 us
  waiting for transfers between devices: 23.6 us -> 25.3 us
  Pallas kernels: 7.53 us -> 8.74 us
    ppermute x8, starting transfers between devices: 15.7 us -> 12.7 us  [_swap_col(): return lax.ppermute(x, ('row', 'col'), perm)]
    ppermute x8, waiting for transfers between devices: 23.6 us -> 25.2 us  [_swap_col(): return lax.ppermute(x, ('row', 'col'), perm)]
    ppermute x2, starting transfers between devices: 1.7 us -> 0.52 us  [_swap(): return lax.ppermute(x, axis, perm)]
    pallas_call x1, Pallas kernels: 3.97 us -> 4.61 us  [along_call(): pl.pallas_call(kernel, grid_spec=spec, out_shape=jax.ShapeDtypeStruct((nr...]
  transfers between devices with their start and end apart: 10 -> 10, of which waited for: 6 -> 6; matrix products, arithmetic and copies ran while one was open for 21% -> 21% of each run, Pallas kernels for 12% -> 14%
where the time goes in v14:
time: 63.3 us; the launch traced here: 62.4 us
  waiting for transfers between devices  25.3 us (40%)
  starting transfers between devices  13.2 us (21%)
  other arithmetic  9.73 us (15%)
  Pallas kernels  8.74 us (14%)
  local copies, waits for them, and re-layouts  3.43 us (5%)
  matrix products  1.16 us (2%)
  between operations  0.84 us (1%)
    ppermute x8, waiting for transfers between devices, _swap_col(): return lax.ppermute(x, ('row', 'col'), perm)  25.2 us
    ppermute x8, starting transfers between devices, _swap_col(): return lax.ppermute(x, ('row', 'col'), perm)  12.7 us
    pallas_call x1, Pallas kernels, along_call(): pl.pallas_call(kernel, grid_spec=spec, out_shape=jax.ShapeDtypeStruct((nr...  4.61 us
    pallas_call x1, Pallas kernels, against_call(): pl.pallas_call(kernel, grid_spec=spec, out_shape=jax.ShapeDtypeStruct((nc...  4.13 us
    another operation x7, other arithmetic, gather_col(): have = jnp.stack([lo, hi], axis=0).reshape((-1,) + have.shape[1:])  3.13 us
    another operation x2, other arithmetic, gather_row(): have = jnp.stack([lo, hi], axis=0).reshape((-1,) + have.shape[1:])  1.51 us
    add x4, other arithmetic, scatter_sum_col(): keep + _swap_col(other, row_size, col_size, (order[0][t], order[1][t]))  1.44 us
    squeeze x4, local copies, waits for them, and re-layouts, scatter_sum_col(): other = lax.dynamic_index_in_dim(data, 1 - mine, axis=0, keepdims=False)  1.38 us
  transfers between devices with their start and end apart: 10, of which 6 were waited for; matrix products, arithmetic and copies ran while one was open for 21% of the time, Pallas kernels for 14%

profile of v14, /device:TPU:0, one launch (start us, length us, event | category | flops | bytes accessed | tf_op | source)
XLA Modules:
  0.0 62.4 jit_solution(11849773345653559197)
XLA Ops:
  0.0 0.5 collective-permute-start
  0.5 3.7 %collective-permute-start.5 = (bf16[1,2,128,128]{2,3,1,0:T(8,128)(2,1)}, bf16[1,2,128,128]{2,3,1,0:T(8,128)(2,1)S(1)}, u32[]{:S(2)}, u32[]{:S(2)}) collective-permute-start(bf16[1,2,128,128]{2,3,1,0:T(8,128)(2,1)} %bitcast.103), channel_id=1, source_target_pairs={{0,8},{1,9},{2,10},{3,11},{4,12},{5,13},{6,14},{7,15},{8,0},{9,1},... | collective-permute-start | bytes 196616 | tf_op jit(solution)/shard_map/ppermute | solution.py:31
  4.1 1.2 %multiply_add_fusion.1 = (s32[128]{0:T(128)}, s32[128]{0:T(128)S(1)}) fusion(s32[]{:T(128)S(6)} %select_n.141, s32[]{:T(128)S(6)} %select_n.143, s32[]{:T(128)S(6)} %select_n.142, s32[1,1,128]{2,1,0:T(1,128)} %param.9), kind=kLoop, calls=%fused_computation.36 | loop fusion | flops 4736 | bytes 1548 | tf_op jit(solution)/shard_map/add | solution.py:223
  5.3 1.2 %clamp_bitcast_fusion.cols_ref = s32[128]{0:T(128)} fusion(s32[1,1,128]{2,1,0:T(1,128)} %param.10), kind=kLoop, calls=%fused_computation.35 | loop fusion | flops 128 | bytes 1024 | tf_op jit(solution)/shard_map/jit(clip)/min | solution.py:210
  7.2 1.2 %collective-permute-done.5 = bf16[1,2,128,128]{2,3,1,0:T(8,128)(2,1)S(1)} collective-permute-done((bf16[1,2,128,128]{2,3,1,0:T(8,128)(2,1)}, bf16[1,2,128,128]{2,3,1,0:T(8,128)(2,1)S(1)}, u32[]{:S(2)}, u32[]{:S(2)}) %collective-permute-start.5) | collective-permute-done | bytes 65568 | tf_op jit(solution)/shard_map/ppermute | solution.py:31
  8.4 0.9 %select_bitcast_fusion.7 = (bf16[1,1,2,128,128]{3,4,2,1,0:T(8,128)(2,1)S(1)}, bf16[1,1,2,128,128]{3,4,2,1,0:T(8,128)(2,1)S(1)}) fusion(bf16[1,2,128,128]{2,3,1,0:T(8,128)(2,1)} %bitcast.104, bf16[1,2,128,128]{2,3,1,0:T(8,128)(2,1)S(1)} %collective-permute-done.5, pred[]{:T(512)S(6)} %eq.23), kind=kLoop, calls=%fused_computation.23 | loop fusion | flops 65536 | bytes 262145 | tf_op jit(solution)/shard_map/stack | solution.py:90
  9.3 0.7 %maximum_bitcast_fusion = bf16[2,2,128,128]{2,3,1,0:T(8,128)(2,1)} fusion(bf16[1,1,2,128,128]{3,4,2,1,0:T(8,128)(2,1)S(1)} %get-tuple-element.18, bf16[1,1,2,128,128]{3,4,2,1,0:T(8,128)(2,1)S(1)} %get-tuple-element.17), kind=kLoop, calls=%fused_computation.16 | loop fusion | flops 65536 | bytes 262144 | tf_op jit(solution)/shard_map/reshape | solution.py:90
  9.9 1.5 %collective-permute-start.6 = (bf16[2,2,128,128]{2,3,1,0:T(8,128)(2,1)}, bf16[2,2,128,128]{2,3,1,0:T(8,128)(2,1)S(1)}, u32[]{:S(2)}, u32[]{:S(2)}) collective-permute-start(bf16[2,2,128,128]{2,3,1,0:T(8,128)(2,1)} %maximum_bitcast_fusion), channel_id=1, source_target_pairs={{0,1},{1,0},{2,3},{3,2},{4,5},{5,4},{6,7},{7,6},{8,9},{9,8},{10,11... | collective-permute-start | bytes 393224 | tf_op jit(solution)/shard_map/ppermute | solution.py:31
  11.5 0.9 %select_bitcast_fusion.9 = (bf16[1,1,256,128]{3,2,1,0:T(8,128)(2,1)S(1)}, bf16[1,1,256,128]{3,2,1,0:T(8,128)(2,1)S(1)}) fusion(bf16[1,256,128]{2,1,0:T(8,128)(2,1)S(1)} %collective-permute-done, pred[]{:T(512)S(6)} %eq.19, bf16[256,128]{1,0:T(8,128)(2,1)} %param.7), kind=kLoop, calls=%fused_computation.25 | loop fusion | flops 65536 | bytes 262145 | tf_op jit(solution)/shard_map/stack | solution.py:52
  12.3 0.7 %pad_maximum_fusion.3 = bf16[2,1,256,128]{3,2,1,0:T(8,128)(2,1)} fusion(bf16[1,1,256,128]{3,2,1,0:T(8,128)(2,1)S(1)} %get-tuple-element.16, bf16[1,1,256,128]{3,2,1,0:T(8,128)(2,1)S(1)} %get-tuple-element.15), kind=kLoop, calls=%fused_computation.15 | loop fusion | flops 65536 | bytes 262144 | tf_op jit(solution)/shard_map/stack | solution.py:52
  13.0 4.6 %shard_map.73 = f32[32,128,128]{2,1,0:T(8,128)} custom-call(s32[128]{0:T(128)} %get-tuple-element.5.rows_ref, s32[128]{0:T(128)} %clamp_bitcast_fusion.cols_ref, s32[1]{0:T(128)} %bitcast.2.cnt_ref, bf16[128,128,128]{2,1,0:T(8,128)(2,1)} %bitcast.91, bf16[4,128,128]{2,1,0:T(8,128)(2,1)} %bitcast.100), custom_call_target="tpu_custom_call" | custom-call | tf_op jit(solution)/shard_map/pallas_call | solution.py:147
  17.6 1.3 %dynamic-slice_bitcast_fusion = f32[2,2,2,2,128,128]{5,4,3,2,1,0:T(8,128)S(1)} fusion(f32[2,2,2,2,2,128,128]{6,5,4,3,2,1,0:T(8,128)} %bitcast.93, s32[]{:T(128)S(6)} %select_n.149), kind=kLoop, calls=%fused_computation.4 | loop fusion | bytes 2097156 | tf_op jit(solution)/shard_map/jit(dynamic_index_in_dim)/squeeze | solution.py:103
  18.9 0.5 collective-permute-start.1
  19.6 0.8 %copy.12 = bf16[4,2,128,128]{3,2,1,0:T(8,128)(2,1)} copy(bf16[4,2,128,128]{2,3,1,0:T(8,128)(2,1)S(1)} %bitcast.98) | data formatting | bytes 524288 | tf_op jit(solution)/shard_map/reshape | solution.py:90
  20.4 1.6 %collective-permute-start.7 = (bf16[4,2,128,128]{3,2,1,0:T(8,128)(2,1)}, bf16[4,2,128,128]{3,2,1,0:T(8,128)(2,1)S(1)}, u32[]{:S(2)}, u32[]{:S(2)}) collective-permute-start(bf16[4,2,128,128]{3,2,1,0:T(8,128)(2,1)} %copy.12), channel_id=1, source_target_pairs={{0,2},{1,3},{2,0},{3,1},{4,6},{5,7},{6,4},{7,5},{8,10},{9,11},{10,... | collective-permute-start | bytes 786440 | tf_op jit(solution)/shard_map/ppermute | solution.py:31
  22.0 5.0 %collective-permute-done.7 = bf16[4,2,128,128]{3,2,1,0:T(8,128)(2,1)S(1)} collective-permute-done((bf16[4,2,128,128]{3,2,1,0:T(8,128)(2,1)}, bf16[4,2,128,128]{3,2,1,0:T(8,128)(2,1)S(1)}, u32[]{:S(2)}, u32[]{:S(2)}) %collective-permute-start.7) | collective-permute-done | bytes 262176 | tf_op jit(solution)/shard_map/ppermute | solution.py:31
  27.0 1.0 %select_bitcast_fusion.3 = (bf16[1,4,2,128,128]{4,3,2,1,0:T(8,128)(2,1)S(1)}, bf16[1,4,2,128,128]{4,3,2,1,0:T(8,128)(2,1)S(1)}) fusion(bf16[4,2,128,128]{3,2,1,0:T(8,128)(2,1)} %copy.12, bf16[4,2,128,128]{3,2,1,0:T(8,128)(2,1)S(1)} %collective-permute-done.7, pred[]{:T(512)S(6)} %eq.21), kind=kLoop, calls=%fused_computation.13 | loop fusion | flops 262144 | bytes 1048577 | tf_op jit(solution)/shard_map/stack | solution.py:90
  28.0 0.9 %collective-permute-start.8 = (bf16[8,2,128,128]{3,2,1,0:T(8,128)(2,1)S(1)}, bf16[8,2,128,128]{3,2,1,0:T(8,128)(2,1)S(1)}, u32[]{:S(2)}, u32[]{:S(2)}) collective-permute-start(bf16[8,2,128,128]{3,2,1,0:T(8,128)(2,1)S(1)} %bitcast.96), channel_id=1, source_target_pairs={{0,4},{1,5},{2,6},{3,7},{4,0},{5,1},{6,2},{7,3},{8,12},{9,13},{10,... | collective-permute-start | bytes 1572872 | tf_op jit(solution)/shard_map/ppermute | solution.py:31
  28.9 0.5 multiply_add_fusion.rows_ref
  29.5 7.3 %collective-permute-done.1 = f32[2,2,2,2,128,128]{5,4,3,2,1,0:T(8,128)} collective-permute-done((f32[2,2,2,2,128,128]{5,4,3,2,1,0:T(8,128)S(1)}, f32[2,2,2,2,128,128]{5,4,3,2,1,0:T(8,128)}, u32[]{:S(2)}, u32[]{:S(2)}) %collective-permute-start.1) | collective-permute-done | bytes 1048608 | tf_op jit(solution)/shard_map/ppermute | solution.py:31
  36.7 1.3 %bitcast_add_fusion = f32[2,2,2,2,128,128]{5,4,3,2,1,0:T(8,128)S(1)} fusion(f32[2,2,2,2,128,128]{5,4,3,2,1,0:T(8,128)} %collective-permute-done.1, f32[2,2,2,2,2,128,128]{6,5,4,3,2,1,0:T(8,128)S(1)} %bitcast.94, s32[]{:T(128)S(6)} %select_n.148), kind=kLoop, calls=%fused_computation.3 | loop fusion | flops 262144 | bytes 3145732 | tf_op jit(solution)/shard_map/add | solution.py:104
  38.1 0.8 %collective-permute-start.2 = (f32[2,2,2,128,128]{4,3,2,1,0:T(8,128)S(1)}, f32[2,2,2,128,128]{4,3,2,1,0:T(8,128)S(1)}, u32[]{:S(2)}, u32[]{:S(2)}) collective-permute-start(f32[2,2,2,128,128]{4,3,2,1,0:T(8,128)S(1)} %dynamic-slice_bitcast_fusion.1), channel_id=1, source_target_pairs={{0,2},{1,3},{2,0},{3,1},{4,6},{5,7},{6,4},{7,5},{8,10},{9,11},{10,... | collective-permute-start | bytes 1572872 | tf_op jit(solution)/shard_map/ppermute | solution.py:31
  39.1 1.1 %pad_maximum_fusion = bf16[2,8,2,128,128]{4,3,2,1,0:T(8,128)(2,1)} fusion(bf16[1,8,2,128,128]{4,3,2,1,0:T(8,128)(2,1)S(1)} %get-tuple-element.8, bf16[1,8,2,128,128]{4,3,2,1,0:T(8,128)(2,1)S(1)} %get-tuple-element.7), kind=kLoop, calls=%fused_computation.2 | loop fusion | flops 524288 | bytes 2097152 | tf_op jit(solution)/shard_map/stack | solution.py:90
  40.2 4.1 %shard_map.74 = f32[4,128,128]{2,1,0:T(8,128)} custom-call(s32[128]{0:T(128)} %multiply_add_fusion.rows_ref, s32[128]{0:T(128)} %clamp_bitcast_fusion.cols_ref, s32[1]{0:T(128)} %bitcast.2.cnt_ref, bf16[128,128,128]{2,1,0:T(8,128)(2,1)} %bitcast.92, bf16[32,128,128]{2,1,0:T(8,128)(2,1)} %bitcast.95), custom_call_target="tpu_custom_call" | custom-call | tf_op jit(solution)/shard_map/pallas_call | solution.py:189
  44.3 1.0 %constant_dynamic-slice_fusion.1 = (f32[1,2,128,128]{3,2,1,0:T(8,128)S(1)}, f32[1,2,128,128]{3,2,1,0:T(8,128)S(1)}) fusion(f32[2,2,128,128]{3,2,1,0:T(8,128)} %bitcast.97, s32[]{:T(128)S(6)} %select_n.168, s32[]{:T(128)S(6)} %select_n.169), kind=kLoop, calls=%fused_computation.27 | loop fusion | bytes 524296 | tf_op jit(solution)/shard_map/jit(dynamic_index_in_dim)/dynamic_slice | solution.py:71
  45.5 1.9 %collective-permute-done.2 = f32[2,2,2,128,128]{4,3,2,1,0:T(8,128)S(1)} collective-permute-done((f32[2,2,2,128,128]{4,3,2,1,0:T(8,128)S(1)}, f32[2,2,2,128,128]{4,3,2,1,0:T(8,128)S(1)}, u32[]{:S(2)}, u32[]{:S(2)}) %collective-permute-start.2) | collective-permute-done | bytes 524320 | tf_op jit(solution)/shard_map/ppermute | solution.py:31
  47.5 1.2 %collective-permute-start.3 = (f32[2,2,128,128]{3,2,1,0:T(8,128)S(1)}, f32[2,2,128,128]{3,2,1,0:T(8,128)S(1)}, u32[]{:S(2)}, u32[]{:S(2)}) collective-permute-start(f32[2,2,128,128]{3,2,1,0:T(8,128)S(1)} %dynamic-slice_bitcast_fusion.2), channel_id=1, source_target_pairs={{0,4},{1,5},{2,6},{3,7},{4,0},{5,1},{6,2},{7,3},{8,12},{9,13},{10,... | collective-permute-start | bytes 786440 | tf_op jit(solution)/shard_map/ppermute | solution.py:31
  48.8 5.1 %collective-permute-done.3 = f32[2,2,128,128]{3,2,1,0:T(8,128)S(1)} collective-permute-done((f32[2,2,128,128]{3,2,1,0:T(8,128)S(1)}, f32[2,2,128,128]{3,2,1,0:T(8,128)S(1)}, u32[]{:S(2)}, u32[]{:S(2)}) %collective-permute-start.3) | collective-permute-done | bytes 262176 | tf_op jit(solution)/shard_map/ppermute | solution.py:31
  54.0 2.4 %collective-permute-start.4 = (f32[2,128,128]{2,1,0:T(8,128)S(1)}, f32[2,128,128]{2,1,0:T(8,128)S(1)}, u32[]{:S(2)}, u32[]{:S(2)}) collective-permute-start(f32[2,128,128]{2,1,0:T(8,128)S(1)} %dynamic-slice_bitcast_fusion.3), channel_id=1, source_target_pairs={{0,8},{1,9},{2,10},{3,11},{4,12},{5,13},{6,14},{7,15},{8,0},{9,1},... | collective-permute-start | bytes 393224 | tf_op jit(solution)/shard_map/ppermute | solution.py:31
  56.4 0.2 fusion.1
  56.7 4.8 %collective-permute-done.4 = f32[2,128,128]{2,1,0:T(8,128)S(1)} collective-permute-done((f32[2,128,128]{2,1,0:T(8,128)S(1)}, f32[2,128,128]{2,1,0:T(8,128)S(1)}, u32[]{:S(2)}, u32[]{:S(2)}) %collective-permute-start.4) | collective-permute-done | bytes 131104 | tf_op jit(solution)/shard_map/ppermute | solution.py:31
  61.4 0.9 %fusion = bf16[256,256]{1,0:T(8,128)(2,1)} fusion(f32[256,256]{1,0:T(8,128)S(1)} %fusion.1, f32[256,128]{1,0:T(8,128)S(1)} %bitcast.101, bf16[128,256]{1,0:T(8,128)(2,1)S(1)} %copy-done.2), kind=kOutput, calls=%fused_computation.1 | convolution fusion | flops 100794368 | bytes 589824 | tf_op jit(solution)/shard_map/dot_general | solution.py:246
  (26 shorter events, 0.7 us)
Async XLA Ops:
  0.0 56.4 %copy-start = (bf16[128,256]{1,0:T(8,128)(2,1)S(1)}, bf16[128,256]{1,0:T(8,128)(2,1)}, u32[]{:S(2)}) copy-start(bf16[128,256]{1,0:T(8,128)(2,1)} %param.13) | copy-start | bytes 196612
  0.0 11.5 %collective-permute-start = (bf16[1,256,128]{2,1,0:T(8,128)(2,1)}, bf16[1,256,128]{2,1,0:T(8,128)(2,1)S(1)}, u32[]{:S(2)}, u32[]{:S(2)}) collective-permute-start(bf16[1,256,128]{2,1,0:T(8,128)(2,1)} %bitcast.102), channel_id=1, source_target_pairs={{0,16},{16,0},{1,17},{17,1},{2,18},{18,2},{3,19},{19,3},{4,20},{20... | collective-permute-start | bytes 196616 | tf_op jit(solution)/shard_map/ppermute | solution.py:36
  0.5 8.0 %collective-permute-start.5 = (bf16[1,2,128,128]{2,3,1,0:T(8,128)(2,1)}, bf16[1,2,128,128]{2,3,1,0:T(8,128)(2,1)S(1)}, u32[]{:S(2)}, u32[]{:S(2)}) collective-permute-start(bf16[1,2,128,128]{2,3,1,0:T(8,128)(2,1)} %bitcast.103), channel_id=1, source_target_pairs={{0,8},{1,9},{2,10},{3,11},{4,12},{5,13},{6,14},{7,15},{8,0},{9,1},... | collective-permute-start | bytes 196616 | tf_op jit(solution)/shard_map/ppermute | solution.py:31
  9.9 9.5 %collective-permute-start.6 = (bf16[2,2,128,128]{2,3,1,0:T(8,128)(2,1)}, bf16[2,2,128,128]{2,3,1,0:T(8,128)(2,1)S(1)}, u32[]{:S(2)}, u32[]{:S(2)}) collective-permute-start(bf16[2,2,128,128]{2,3,1,0:T(8,128)(2,1)} %maximum_bitcast_fusion), channel_id=1, source_target_pairs={{0,1},{1,0},{2,3},{3,2},{4,5},{5,4},{6,7},{7,6},{8,9},{9,8},{10,11... | collective-permute-start | bytes 393224 | tf_op jit(solution)/shard_map/ppermute | solution.py:31
  18.9 10.0 %copy-start.3 = (s32[1,1,128]{2,1,0:T(1,128)S(1)}, s32[1,1,128]{2,1,0:T(1,128)}, u32[]{:S(2)}) copy-start(s32[1,1,128]{2,1,0:T(1,128)} %param.9) | copy-start | bytes 1540
  18.9 17.8 %copy-start.1 = (f32[32,128,128]{2,1,0:T(8,128)S(1)}, f32[32,128,128]{2,1,0:T(8,128)}, u32[]{:S(2)}) copy-start(f32[32,128,128]{2,1,0:T(8,128)} %shard_map.73) | copy-start | bytes 6291460
  18.9 17.8 %collective-permute-start.1 = (f32[2,2,2,2,128,128]{5,4,3,2,1,0:T(8,128)S(1)}, f32[2,2,2,2,128,128]{5,4,3,2,1,0:T(8,128)}, u32[]{:S(2)}, u32[]{:S(2)}) collective-permute-start(f32[2,2,2,2,128,128]{5,4,3,2,1,0:T(8,128)S(1)} %dynamic-slice_bitcast_fusion), channel_id=1, source_target_pairs={{0,1},{1,0},{2,3},{3,2},{4,5},{5,4},{6,7},{7,6},{8,9},{9,8},{10,11... | collective-permute-start | bytes 3145736 | tf_op jit(solution)/shard_map/ppermute | solution.py:31
  20.4 6.6 %collective-permute-start.7 = (bf16[4,2,128,128]{3,2,1,0:T(8,128)(2,1)}, bf16[4,2,128,128]{3,2,1,0:T(8,128)(2,1)S(1)}, u32[]{:S(2)}, u32[]{:S(2)}) collective-permute-start(bf16[4,2,128,128]{3,2,1,0:T(8,128)(2,1)} %copy.12), channel_id=1, source_target_pairs={{0,2},{1,3},{2,0},{3,1},{4,6},{5,7},{6,4},{7,5},{8,10},{9,11},{10,... | collective-permute-start | bytes 786440 | tf_op jit(solution)/shard_map/ppermute | solution.py:31
  28.0 10.9 %collective-permute-start.8 = (bf16[8,2,128,128]{3,2,1,0:T(8,128)(2,1)S(1)}, bf16[8,2,128,128]{3,2,1,0:T(8,128)(2,1)S(1)}, u32[]{:S(2)}, u32[]{:S(2)}) collective-permute-start(bf16[8,2,128,128]{3,2,1,0:T(8,128)(2,1)S(1)} %bitcast.96), channel_id=1, source_target_pairs={{0,4},{1,5},{2,6},{3,7},{4,0},{5,1},{6,2},{7,3},{8,12},{9,13},{10,... | collective-permute-start | bytes 1572872 | tf_op jit(solution)/shard_map/ppermute | solution.py:31
  38.1 9.2 %collective-permute-start.2 = (f32[2,2,2,128,128]{4,3,2,1,0:T(8,128)S(1)}, f32[2,2,2,128,128]{4,3,2,1,0:T(8,128)S(1)}, u32[]{:S(2)}, u32[]{:S(2)}) collective-permute-start(f32[2,2,2,128,128]{4,3,2,1,0:T(8,128)S(1)} %dynamic-slice_bitcast_fusion.1), channel_id=1, source_target_pairs={{0,2},{1,3},{2,0},{3,1},{4,6},{5,7},{6,4},{7,5},{8,10},{9,11},{10,... | collective-permute-start | bytes 1572872 | tf_op jit(solution)/shard_map/ppermute | solution.py:31
  45.4 16.1 %copy-start.2 = (bf16[128,256]{1,0:T(8,128)(2,1)S(1)}, bf16[128,256]{1,0:T(8,128)(2,1)}, u32[]{:S(2)}) copy-start(bf16[128,256]{1,0:T(8,128)(2,1)} %param.12) | copy-start | bytes 196612
  45.4 3.4 %collective-permute-start.9 = (f32[2,128,128]{1,2,0:T(8,128)S(1)}, f32[2,128,128]{1,2,0:T(8,128)S(1)}, u32[]{:S(2)}, u32[]{:S(2)}) collective-permute-start(f32[2,128,128]{1,2,0:T(8,128)S(1)} %bitcast.105), channel_id=1, source_target_pairs={{0,16},{16,0},{1,17},{17,1},{2,18},{18,2},{3,19},{19,3},{4,20},{20... | collective-permute-start | bytes 393224 | tf_op jit(solution)/shard_map/ppermute | solution.py:36
  47.5 6.4 %collective-permute-start.3 = (f32[2,2,128,128]{3,2,1,0:T(8,128)S(1)}, f32[2,2,128,128]{3,2,1,0:T(8,128)S(1)}, u32[]{:S(2)}, u32[]{:S(2)}) collective-permute-start(f32[2,2,128,128]{3,2,1,0:T(8,128)S(1)} %dynamic-slice_bitcast_fusion.2), channel_id=1, source_target_pairs={{0,4},{1,5},{2,6},{3,7},{4,0},{5,1},{6,2},{7,3},{8,12},{9,13},{10,... | collective-permute-start | bytes 786440 | tf_op jit(solution)/shard_map/ppermute | solution.py:31
  54.0 7.5 %collective-permute-start.4 = (f32[2,128,128]{2,1,0:T(8,128)S(1)}, f32[2,128,128]{2,1,0:T(8,128)S(1)}, u32[]{:S(2)}, u32[]{:S(2)}) collective-permute-start(f32[2,128,128]{2,1,0:T(8,128)S(1)} %dynamic-slice_bitcast_fusion.3), channel_id=1, source_target_pairs={{0,8},{1,9},{2,10},{3,11},{4,12},{5,13},{6,14},{7,15},{8,0},{9,1},... | collective-permute-start | bytes 393224 | tf_op jit(solution)/shard_map/ppermute | solution.py:31

commit v15 on v11

--- a/solution.py
+++ b/solution.py
@@ -238,10 +238,15 @@
 
     mine_t = jnp.transpose(features.reshape(nbc, side, width), (0, 2, 1))
     if nb is not None:
-        along = scatter_sum_col(fwd_parts.reshape((2,) * nb + (nbc, side, width)), rs_order, 0, 1)
-        mine_t, along = lax.optimization_barrier((mine_t, along))
+        parts = fwd_parts.reshape((2,) * nb + (nbc, side, width))
+        par = lax.axis_index("row") % 2
+        mine0 = (lax.axis_index("col") >> _pick(par, rs_order, 0)) & 1
+        keep0 = lax.dynamic_index_in_dim(parts, mine0, axis=0, keepdims=False)
+        send0 = lax.dynamic_index_in_dim(parts, 1 - mine0, axis=0, keepdims=False)
+        mine_t, send0 = lax.optimization_barrier((mine_t, send0))
+        got0 = _swap_col(send0, row_size, col_size, (rs_order[0][0], rs_order[1][0]))
         stripe_t = gather_col(mine_t, ag_order).reshape(nrb, width, side)
-        along = scatter_sum_col(along, rs_order, 1)
+        along = scatter_sum_col(keep0 + got0, rs_order, 1)
     else:
         stripe_t = lax.all_gather(mine_t, "col", axis=0, tiled=True)
         along = lax.psum_scatter(fwd_parts, "col", scatter_dimension=0, tiled=True)

time: 73.1 us -> 68.3 us (0.934)
  waiting for transfers between devices: 41.4 us -> 28.7 us
  starting transfers between devices: 13.7 us -> 17.5 us
  other arithmetic: 4.33 us -> 7.88 us
    ppermute x8, waiting for transfers between devices: 39.7 us -> 28.1 us  [_swap_col(): return lax.ppermute(x, ('row', 'col'), perm)]
    another operation x7, other arithmetic: 1.33 us -> 4.23 us  [gather_col(): have = jnp.stack([lo, hi], axis=0).reshape((-1,) + have.shape[1:])]
    ppermute x8, starting transfers between devices: 13.2 us -> 15.9 us  [_swap_col(): return lax.ppermute(x, ('row', 'col'), perm)]
    squeeze x4 -> x3, local copies, waits for them, and re-layouts: 1.52 us -> 0.09 us  [scatter_sum_col(): other = lax.dynamic_index_in_dim(data, 1 - mine, axis=0, keepdims=False)]
    add x4 -> x3, other arithmetic: 1.45 us -> 0.1 us  [scatter_sum_col(): keep + _swap_col(other, row_size, col_size, (order[0][t], order[1][t]))]
    add x0 -> x1, other arithmetic: none -> 1.34 us  [local(): along = scatter_sum_col(keep0 + got0, rs_order, 1)]
    squeeze x0 -> x1, local copies, waits for them, and re-layouts: none -> 1.33 us  [local(): send0 = lax.dynamic_index_in_dim(parts, 1 - mine0, axis=0, keepdims=False)]
    ppermute x2, starting transfers between devices: 0.52 us -> 1.63 us  [_swap(): return lax.ppermute(x, axis, perm)]
  transfers between devices with their start and end apart: 10 -> 10, of which waited for: 8 -> 9; matrix products, arithmetic and copies ran while one was open for 4% -> 12% of each run, Pallas kernels for 5% -> 6%
where the time goes in v15:
time: 68.3 us; the launch traced here: 67.4 us
  waiting for transfers between devices  28.7 us (42%)
  starting transfers between devices  17.5 us (26%)
  Pallas kernels  7.89 us (12%)
  other arithmetic  7.88 us (12%)
  local copies, waits for them, and re-layouts  3.46 us (5%)
  matrix products  1.16 us (2%)
  between operations  0.79 us (1%)
    ppermute x8, waiting for transfers between devices, _swap_col(): return lax.ppermute(x, ('row', 'col'), perm)  28.1 us
    ppermute x8, starting transfers between devices, _swap_col(): return lax.ppermute(x, ('row', 'col'), perm)  15.9 us
    another operation x7, other arithmetic, gather_col(): have = jnp.stack([lo, hi], axis=0).reshape((-1,) + have.shape[1:])  4.23 us
    pallas_call x1, Pallas kernels, along_call(): pl.pallas_call(kernel, grid_spec=spec, out_shape=jax.ShapeDtypeStruct((nr...  4.17 us
    pallas_call x1, Pallas kernels, against_call(): pl.pallas_call(kernel, grid_spec=spec, out_shape=jax.ShapeDtypeStruct((nc...  3.72 us
    ppermute x2, starting transfers between devices, _swap(): return lax.ppermute(x, axis, perm)  1.63 us
    another operation x2, other arithmetic, gather_row(): have = jnp.stack([lo, hi], axis=0).reshape((-1,) + have.shape[1:])  1.52 us
  transfers between devices with their start and end apart: 10, of which 9 were waited for; matrix products, arithmetic and copies ran while one was open for 12% of the time, Pallas kernels for 6%

profile of v15, /device:TPU:0, one launch (start us, length us, event | category | flops | bytes accessed | tf_op | source)
XLA Modules:
  0.0 67.4 jit_solution(3158969752866281700)
XLA Ops:
  0.0 0.5 collective-permute-start
  1.1 0.5 collective-permute-done
  1.6 0.9 %select_bitcast_fusion.9 = (bf16[1,1,256,128]{3,2,1,0:T(8,128)(2,1)S(1)}, bf16[1,1,256,128]{3,2,1,0:T(8,128)(2,1)S(1)}) fusion(bf16[1,256,128]{2,1,0:T(8,128)(2,1)S(1)} %collective-permute-done, pred[]{:T(512)S(6)} %eq.16, bf16[256,128]{1,0:T(8,128)(2,1)} %param.7), kind=kLoop, calls=%fused_computation.25 | loop fusion | flops 65536 | bytes 262145 | tf_op jit(solution)/shard_map/stack | solution.py:52
  2.4 0.7 pad_maximum_fusion.3
  3.1 4.2 %shard_map.73 = f32[32,128,128]{2,1,0:T(8,128)} custom-call(s32[128]{0:T(128)} %bitcast.90, s32[128]{0:T(128)} %bitcast.92, s32[1]{0:T(128)} %bitcast.74.cnt_ref, bf16[128,128,128]{2,1,0:T(8,128)(2,1)} %bitcast.76, bf16[4,128,128]{2,1,0:T(8,128)(2,1)} %bitcast.84), custom_call_target="tpu_custom_call" | custom-call | tf_op jit(solution)/shard_map/pallas_call | solution.py:146
  7.3 1.3 %dynamic-slice_bitcast_fusion = f32[2,2,2,2,128,128]{5,4,3,2,1,0:T(8,128)S(1)} fusion(f32[2,2,2,2,2,128,128]{6,5,4,3,2,1,0:T(8,128)} %bitcast.78, s32[]{:T(128)S(6)} %select_n.126), kind=kLoop, calls=%fused_computation.4 | loop fusion | bytes 2097156 | tf_op jit(solution)/shard_map/jit(dynamic_index_in_dim)/squeeze | solution.py:245
  8.6 4.6 %collective-permute-start.5 = (bf16[1,2,128,128]{2,3,1,0:T(8,128)(2,1)S(1)}, bf16[1,2,128,128]{2,3,1,0:T(8,128)(2,1)S(1)}, u32[]{:S(2)}, u32[]{:S(2)}) collective-permute-start(bf16[1,2,128,128]{2,3,1,0:T(8,128)(2,1)S(1)} %bitcast.87), channel_id=1, source_target_pairs={{0,8},{1,9},{2,10},{3,11},{4,12},{5,13},{6,14},{7,15},{8,0},{9,1},... | collective-permute-start | bytes 196616 | tf_op jit(solution)/shard_map/ppermute | solution.py:31
  13.3 3.7 %collective-permute-done.5 = bf16[1,2,128,128]{2,3,1,0:T(8,128)(2,1)S(1)} collective-permute-done((bf16[1,2,128,128]{2,3,1,0:T(8,128)(2,1)S(1)}, bf16[1,2,128,128]{2,3,1,0:T(8,128)(2,1)S(1)}, u32[]{:S(2)}, u32[]{:S(2)}) %collective-permute-start.5) | collective-permute-done | bytes 65568 | tf_op jit(solution)/shard_map/ppermute | solution.py:31
  16.9 0.7 maximum_bitcast_fusion
  17.6 2.0 %collective-permute-start.1 = (f32[2,2,2,2,128,128]{5,4,3,2,1,0:T(8,128)S(1)}, f32[2,2,2,2,128,128]{5,4,3,2,1,0:T(8,128)}, u32[]{:S(2)}, u32[]{:S(2)}) collective-permute-start(f32[2,2,2,2,128,128]{5,4,3,2,1,0:T(8,128)S(1)} %dynamic-slice_bitcast_fusion), channel_id=1, source_target_pairs={{0,1},{1,0},{2,3},{3,2},{4,5},{5,4},{6,7},{7,6},{8,9},{9,8},{10,11... | collective-permute-start | bytes 3145736 | tf_op jit(solution)/shard_map/ppermute | solution.py:31
  19.6 3.2 %collective-permute-done.6 = bf16[2,2,128,128]{2,3,1,0:T(8,128)(2,1)S(1)} collective-permute-done((bf16[2,2,128,128]{2,3,1,0:T(8,128)(2,1)}, bf16[2,2,128,128]{2,3,1,0:T(8,128)(2,1)S(1)}, u32[]{:S(2)}, u32[]{:S(2)}) %collective-permute-start.6) | collective-permute-done | bytes 131104 | tf_op jit(solution)/shard_map/ppermute | solution.py:31
  22.8 0.9 %copy.12 = bf16[4,2,128,128]{3,2,1,0:T(8,128)(2,1)} copy(bf16[4,2,128,128]{2,3,1,0:T(8,128)(2,1)S(1)} %bitcast.82) | data formatting | bytes 524288 | tf_op jit(solution)/shard_map/reshape | solution.py:90
  23.7 1.8 %collective-permute-start.7 = (bf16[4,2,128,128]{3,2,1,0:T(8,128)(2,1)}, bf16[4,2,128,128]{3,2,1,0:T(8,128)(2,1)S(1)}, u32[]{:S(2)}, u32[]{:S(2)}) collective-permute-start(bf16[4,2,128,128]{3,2,1,0:T(8,128)(2,1)} %copy.12), channel_id=1, source_target_pairs={{0,2},{1,3},{2,0},{3,1},{4,6},{5,7},{6,4},{7,5},{8,10},{9,11},{10,... | collective-permute-start | bytes 786440 | tf_op jit(solution)/shard_map/ppermute | solution.py:31
  25.5 4.8 %collective-permute-done.7 = bf16[4,2,128,128]{3,2,1,0:T(8,128)(2,1)S(1)} collective-permute-done((bf16[4,2,128,128]{3,2,1,0:T(8,128)(2,1)}, bf16[4,2,128,128]{3,2,1,0:T(8,128)(2,1)S(1)}, u32[]{:S(2)}, u32[]{:S(2)}) %collective-permute-start.7) | collective-permute-done | bytes 262176 | tf_op jit(solution)/shard_map/ppermute | solution.py:31
  30.3 1.0 %select_bitcast_fusion.3 = (bf16[1,4,2,128,128]{4,3,2,1,0:T(8,128)(2,1)S(1)}, bf16[1,4,2,128,128]{4,3,2,1,0:T(8,128)(2,1)S(1)}) fusion(bf16[4,2,128,128]{3,2,1,0:T(8,128)(2,1)} %copy.12, bf16[4,2,128,128]{3,2,1,0:T(8,128)(2,1)S(1)} %collective-permute-done.7, pred[]{:T(512)S(6)} %eq.19), kind=kLoop, calls=%fused_computation.13 | loop fusion | flops 262144 | bytes 1048577 | tf_op jit(solution)/shard_map/stack | solution.py:90
  31.3 0.8 %pad_maximum_fusion.1 = bf16[2,4,2,128,128]{4,3,2,1,0:T(8,128)(2,1)} fusion(bf16[1,4,2,128,128]{4,3,2,1,0:T(8,128)(2,1)S(1)} %get-tuple-element.12, bf16[1,4,2,128,128]{4,3,2,1,0:T(8,128)(2,1)S(1)} %get-tuple-element.11), kind=kLoop, calls=%fused_computation.5 | loop fusion | flops 262144 | bytes 1048576 | tf_op jit(solution)/shard_map/stack | solution.py:90
  32.1 1.0 %collective-permute-start.8 = (bf16[8,2,128,128]{3,2,1,0:T(8,128)(2,1)}, bf16[8,2,128,128]{3,2,1,0:T(8,128)(2,1)}, u32[]{:S(2)}, u32[]{:S(2)}) collective-permute-start(bf16[8,2,128,128]{3,2,1,0:T(8,128)(2,1)} %bitcast.29), channel_id=1, source_target_pairs={{0,4},{1,5},{2,6},{3,7},{4,0},{5,1},{6,2},{7,3},{8,12},{9,13},{10,... | collective-permute-start | bytes 1572872 | tf_op jit(solution)/shard_map/ppermute | solution.py:31
  33.1 3.8 %collective-permute-done.1 = f32[2,2,2,2,128,128]{5,4,3,2,1,0:T(8,128)} collective-permute-done((f32[2,2,2,2,128,128]{5,4,3,2,1,0:T(8,128)S(1)}, f32[2,2,2,2,128,128]{5,4,3,2,1,0:T(8,128)}, u32[]{:S(2)}, u32[]{:S(2)}) %collective-permute-start.1) | collective-permute-done | bytes 1048608 | tf_op jit(solution)/shard_map/ppermute | solution.py:31
  36.9 1.3 %bitcast_add_fusion = f32[2,2,2,2,128,128]{5,4,3,2,1,0:T(8,128)S(1)} fusion(f32[2,2,2,2,128,128]{5,4,3,2,1,0:T(8,128)} %collective-permute-done.1, f32[2,2,2,2,2,128,128]{6,5,4,3,2,1,0:T(8,128)S(1)} %bitcast.79, s32[]{:T(128)S(6)} %select_n.125), kind=kLoop, calls=%fused_computation.3 | loop fusion | flops 262144 | bytes 3145732 | tf_op jit(solution)/shard_map/add | solution.py:249
  38.3 1.5 %collective-permute-start.2 = (f32[2,2,2,128,128]{4,3,2,1,0:T(8,128)S(1)}, f32[2,2,2,128,128]{4,3,2,1,0:T(8,128)S(1)}, u32[]{:S(2)}, u32[]{:S(2)}) collective-permute-start(f32[2,2,2,128,128]{4,3,2,1,0:T(8,128)S(1)} %dynamic-slice_bitcast_fusion.1), channel_id=1, source_target_pairs={{0,2},{1,3},{2,0},{3,1},{4,6},{5,7},{6,4},{7,5},{8,10},{9,11},{10,... | collective-permute-start | bytes 1572872 | tf_op jit(solution)/shard_map/ppermute | solution.py:31
  39.8 1.8 %collective-permute-done.8 = bf16[8,2,128,128]{3,2,1,0:T(8,128)(2,1)} collective-permute-done((bf16[8,2,128,128]{3,2,1,0:T(8,128)(2,1)}, bf16[8,2,128,128]{3,2,1,0:T(8,128)(2,1)}, u32[]{:S(2)}, u32[]{:S(2)}) %collective-permute-start.8) | collective-permute-done | bytes 524320 | tf_op jit(solution)/shard_map/ppermute | solution.py:31
  41.6 1.3 %select_bitcast_fusion.1 = (bf16[1,8,2,128,128]{4,3,2,1,0:T(8,128)(2,1)S(1)}, bf16[1,8,2,128,128]{4,3,2,1,0:T(8,128)(2,1)S(1)}) fusion(bf16[8,2,128,128]{3,2,1,0:T(8,128)(2,1)} %collective-permute-done.8, pred[]{:T(512)S(6)} %eq.18, bf16[2,4,2,128,128]{4,3,2,1,0:T(8,128)(2,1)} %pad_maximum_fusion.1), kind=kLoop, calls=%fused_computation.8 | loop fusion | flops 524288 | bytes 2097153 | tf_op jit(solution)/shard_map/stack | solution.py:90
  42.9 1.1 %pad_maximum_fusion = bf16[2,8,2,128,128]{4,3,2,1,0:T(8,128)(2,1)} fusion(bf16[1,8,2,128,128]{4,3,2,1,0:T(8,128)(2,1)S(1)} %get-tuple-element.10, bf16[1,8,2,128,128]{4,3,2,1,0:T(8,128)(2,1)S(1)} %get-tuple-element.9), kind=kLoop, calls=%fused_computation.2 | loop fusion | flops 524288 | bytes 2097152 | tf_op jit(solution)/shard_map/stack | solution.py:90
  44.0 3.7 %shard_map.74 = f32[4,128,128]{2,1,0:T(8,128)} custom-call(s32[128]{0:T(128)} %bitcast.91, s32[128]{0:T(128)} %bitcast.93, s32[1]{0:T(128)} %bitcast.75.cnt_ref, bf16[128,128,128]{2,1,0:T(8,128)(2,1)} %bitcast.77, bf16[32,128,128]{2,1,0:T(8,128)(2,1)} %bitcast.80), custom_call_target="tpu_custom_call" | custom-call | tf_op jit(solution)/shard_map/pallas_call | solution.py:187
  47.7 1.0 %constant_dynamic-slice_fusion.1 = (f32[1,2,128,128]{3,2,1,0:T(8,128)S(1)}, f32[1,2,128,128]{3,2,1,0:T(8,128)S(1)}) fusion(f32[2,2,128,128]{3,2,1,0:T(8,128)} %bitcast.81, s32[]{:T(128)S(6)} %select_n.147, s32[]{:T(128)S(6)} %select_n.148), kind=kLoop, calls=%fused_computation.27 | loop fusion | bytes 524296 | tf_op jit(solution)/shard_map/jit(dynamic_index_in_dim)/dynamic_slice | solution.py:71
  48.8 1.2 %collective-permute-start.9 = (f32[2,128,128]{1,2,0:T(8,128)S(1)}, f32[2,128,128]{1,2,0:T(8,128)S(1)}, u32[]{:S(2)}, u32[]{:S(2)}) collective-permute-start(f32[2,128,128]{1,2,0:T(8,128)S(1)} %bitcast.89), channel_id=1, source_target_pairs={{0,16},{16,0},{1,17},{17,1},{2,18},{18,2},{3,19},{19,3},{4,20},{20... | collective-permute-start | bytes 393224 | tf_op jit(solution)/shard_map/ppermute | solution.py:36
  50.0 0.6 collective-permute-start.3
  51.0 5.5 %collective-permute-done.3 = f32[2,2,128,128]{3,2,1,0:T(8,128)S(1)} collective-permute-done((f32[2,2,128,128]{3,2,1,0:T(8,128)S(1)}, f32[2,2,128,128]{3,2,1,0:T(8,128)S(1)}, u32[]{:S(2)}, u32[]{:S(2)}) %collective-permute-start.3) | collective-permute-done | bytes 262176 | tf_op jit(solution)/shard_map/ppermute | solution.py:31
  56.5 4.3 %collective-permute-start.4 = (f32[2,128,128]{2,1,0:T(8,128)S(1)}, f32[2,128,128]{2,1,0:T(8,128)S(1)}, u32[]{:S(2)}, u32[]{:S(2)}) collective-permute-start(f32[2,128,128]{2,1,0:T(8,128)S(1)} %dynamic-slice_bitcast_fusion.3), channel_id=1, source_target_pairs={{0,8},{1,9},{2,10},{3,11},{4,12},{5,13},{6,14},{7,15},{8,0},{9,1},... | collective-permute-start | bytes 393224 | tf_op jit(solution)/shard_map/ppermute | solution.py:31
  60.8 0.2 fusion.1
  61.1 5.4 %collective-permute-done.4 = f32[2,128,128]{2,1,0:T(8,128)S(1)} collective-permute-done((f32[2,128,128]{2,1,0:T(8,128)S(1)}, f32[2,128,128]{2,1,0:T(8,128)S(1)}, u32[]{:S(2)}, u32[]{:S(2)}) %collective-permute-start.4) | collective-permute-done | bytes 131104 | tf_op jit(solution)/shard_map/ppermute | solution.py:31
  66.5 0.9 %fusion = bf16[256,256]{1,0:T(8,128)(2,1)} fusion(f32[256,256]{1,0:T(8,128)S(1)} %fusion.1, f32[256,128]{1,0:T(8,128)S(1)} %bitcast.85, bf16[128,256]{1,0:T(8,128)(2,1)S(1)} %copy-done.3), kind=kOutput, calls=%fused_computation.1 | convolution fusion | flops 100794368 | bytes 589824 | tf_op jit(solution)/shard_map/dot_general | solution.py:260
  (23 shorter events, 0.7 us)
Async XLA Ops:
  0.0 60.8 %copy-start = (bf16[128,256]{1,0:T(8,128)(2,1)S(1)}, bf16[128,256]{1,0:T(8,128)(2,1)}, u32[]{:S(2)}) copy-start(bf16[128,256]{1,0:T(8,128)(2,1)} %param.13) | copy-start | bytes 196612
  0.0 1.6 %collective-permute-start = (bf16[1,256,128]{2,1,0:T(8,128)(2,1)}, bf16[1,256,128]{2,1,0:T(8,128)(2,1)S(1)}, u32[]{:S(2)}, u32[]{:S(2)}) collective-permute-start(bf16[1,256,128]{2,1,0:T(8,128)(2,1)} %bitcast.86), channel_id=1, source_target_pairs={{0,16},{16,0},{1,17},{17,1},{2,18},{18,2},{3,19},{19,3},{4,20},{20... | collective-permute-start | bytes 196616 | tf_op jit(solution)/shard_map/ppermute | solution.py:36
  7.3 1.3 %copy-start.2 = (bf16[256,128]{1,0:T(8,128)(2,1)S(1)}, bf16[256,128]{1,0:T(8,128)(2,1)}, u32[]{:S(2)}) copy-start(bf16[256,128]{1,0:T(8,128)(2,1)} %param.7) | copy-start | bytes 196612
  8.6 8.3 %collective-permute-start.5 = (bf16[1,2,128,128]{2,3,1,0:T(8,128)(2,1)S(1)}, bf16[1,2,128,128]{2,3,1,0:T(8,128)(2,1)S(1)}, u32[]{:S(2)}, u32[]{:S(2)}) collective-permute-start(bf16[1,2,128,128]{2,3,1,0:T(8,128)(2,1)S(1)} %bitcast.87), channel_id=1, source_target_pairs={{0,8},{1,9},{2,10},{3,11},{4,12},{5,13},{6,14},{7,15},{8,0},{9,1},... | collective-permute-start | bytes 196616 | tf_op jit(solution)/shard_map/ppermute | solution.py:31
  13.3 23.7 %copy-start.1 = (f32[32,128,128]{2,1,0:T(8,128)S(1)}, f32[32,128,128]{2,1,0:T(8,128)}, u32[]{:S(2)}) copy-start(f32[32,128,128]{2,1,0:T(8,128)} %shard_map.73) | copy-start | bytes 6291460
  17.6 5.2 %collective-permute-start.6 = (bf16[2,2,128,128]{2,3,1,0:T(8,128)(2,1)}, bf16[2,2,128,128]{2,3,1,0:T(8,128)(2,1)S(1)}, u32[]{:S(2)}, u32[]{:S(2)}) collective-permute-start(bf16[2,2,128,128]{2,3,1,0:T(8,128)(2,1)} %maximum_bitcast_fusion), channel_id=1, source_target_pairs={{0,1},{1,0},{2,3},{3,2},{4,5},{5,4},{6,7},{7,6},{8,9},{9,8},{10,11... | collective-permute-start | bytes 393224 | tf_op jit(solution)/shard_map/ppermute | solution.py:31
  17.6 19.3 %collective-permute-start.1 = (f32[2,2,2,2,128,128]{5,4,3,2,1,0:T(8,128)S(1)}, f32[2,2,2,2,128,128]{5,4,3,2,1,0:T(8,128)}, u32[]{:S(2)}, u32[]{:S(2)}) collective-permute-start(f32[2,2,2,2,128,128]{5,4,3,2,1,0:T(8,128)S(1)} %dynamic-slice_bitcast_fusion), channel_id=1, source_target_pairs={{0,1},{1,0},{2,3},{3,2},{4,5},{5,4},{6,7},{7,6},{8,9},{9,8},{10,11... | collective-permute-start | bytes 3145736 | tf_op jit(solution)/shard_map/ppermute | solution.py:31
  23.7 6.6 %collective-permute-start.7 = (bf16[4,2,128,128]{3,2,1,0:T(8,128)(2,1)}, bf16[4,2,128,128]{3,2,1,0:T(8,128)(2,1)S(1)}, u32[]{:S(2)}, u32[]{:S(2)}) collective-permute-start(bf16[4,2,128,128]{3,2,1,0:T(8,128)(2,1)} %copy.12), channel_id=1, source_target_pairs={{0,2},{1,3},{2,0},{3,1},{4,6},{5,7},{6,4},{7,5},{8,10},{9,11},{10,... | collective-permute-start | bytes 786440 | tf_op jit(solution)/shard_map/ppermute | solution.py:31
  32.1 9.5 %collective-permute-start.8 = (bf16[8,2,128,128]{3,2,1,0:T(8,128)(2,1)}, bf16[8,2,128,128]{3,2,1,0:T(8,128)(2,1)}, u32[]{:S(2)}, u32[]{:S(2)}) collective-permute-start(bf16[8,2,128,128]{3,2,1,0:T(8,128)(2,1)} %bitcast.29), channel_id=1, source_target_pairs={{0,4},{1,5},{2,6},{3,7},{4,0},{5,1},{6,2},{7,3},{8,12},{9,13},{10,... | collective-permute-start | bytes 1572872 | tf_op jit(solution)/shard_map/ppermute | solution.py:31
  38.3 11.6 %collective-permute-start.2 = (f32[2,2,2,128,128]{4,3,2,1,0:T(8,128)S(1)}, f32[2,2,2,128,128]{4,3,2,1,0:T(8,128)S(1)}, u32[]{:S(2)}, u32[]{:S(2)}) collective-permute-start(f32[2,2,2,128,128]{4,3,2,1,0:T(8,128)S(1)} %dynamic-slice_bitcast_fusion.1), channel_id=1, source_target_pairs={{0,2},{1,3},{2,0},{3,1},{4,6},{5,7},{6,4},{7,5},{8,10},{9,11},{10,... | collective-permute-start | bytes 1572872 | tf_op jit(solution)/shard_map/ppermute | solution.py:31
  48.8 17.7 %copy-start.3 = (bf16[128,256]{1,0:T(8,128)(2,1)S(1)}, bf16[128,256]{1,0:T(8,128)(2,1)}, u32[]{:S(2)}) copy-start(bf16[128,256]{1,0:T(8,128)(2,1)} %param.12) | copy-start | bytes 196612
  48.8 2.2 %collective-permute-start.9 = (f32[2,128,128]{1,2,0:T(8,128)S(1)}, f32[2,128,128]{1,2,0:T(8,128)S(1)}, u32[]{:S(2)}, u32[]{:S(2)}) collective-permute-start(f32[2,128,128]{1,2,0:T(8,128)S(1)} %bitcast.89), channel_id=1, source_target_pairs={{0,16},{16,0},{1,17},{17,1},{2,18},{18,2},{3,19},{19,3},{4,20},{20... | collective-permute-start | bytes 393224 | tf_op jit(solution)/shard_map/ppermute | solution.py:36
  50.0 6.4 %collective-permute-start.3 = (f32[2,2,128,128]{3,2,1,0:T(8,128)S(1)}, f32[2,2,128,128]{3,2,1,0:T(8,128)S(1)}, u32[]{:S(2)}, u32[]{:S(2)}) collective-permute-start(f32[2,2,128,128]{3,2,1,0:T(8,128)S(1)} %dynamic-slice_bitcast_fusion.2), channel_id=1, source_target_pairs={{0,4},{1,5},{2,6},{3,7},{4,0},{5,1},{6,2},{7,3},{8,12},{9,13},{10,... | collective-permute-start | bytes 786440 | tf_op jit(solution)/shard_map/ppermute | solution.py:31
  56.5 9.9 %collective-permute-start.4 = (f32[2,128,128]{2,1,0:T(8,128)S(1)}, f32[2,128,128]{2,1,0:T(8,128)S(1)}, u32[]{:S(2)}, u32[]{:S(2)}) collective-permute-start(f32[2,128,128]{2,1,0:T(8,128)S(1)} %dynamic-slice_bitcast_fusion.3), channel_id=1, source_target_pairs={{0,8},{1,9},{2,10},{3,11},{4,12},{5,13},{6,14},{7,15},{8,0},{9,1},... | collective-permute-start | bytes 393224 | tf_op jit(solution)/shard_map/ppermute | solution.py:31

commit v16 on v3

--- a/solution.py
+++ b/solution.py
@@ -98,9 +98,12 @@
     me = lax.axis_index("col")
     parity = lax.axis_index("row") % 2
     for t in range(nb):
-        mine = (me >> _pick(parity, order, t)) & 1
-        keep = lax.dynamic_index_in_dim(data, mine, axis=0, keepdims=False)
-        other = lax.dynamic_index_in_dim(data, 1 - mine, axis=0, keepdims=False)
+        if t == 0:
+            keep, other = data[1], data[0]
+        else:
+            mine = (me >> _pick(parity, order, t)) & 1
+            keep = lax.dynamic_index_in_dim(data, mine, axis=0, keepdims=False)
+            other = lax.dynamic_index_in_dim(data, 1 - mine, axis=0, keepdims=False)
         data = keep + _swap_col(other, row_size, col_size, (order[0][t], order[1][t]))
     return data
 
@@ -218,7 +221,10 @@
         rs_pos = jnp.zeros_like(dest)
         ag_pos = jnp.zeros_like(dest)
         for t in range(nb):
-            rs_pos = rs_pos + (((dest >> _pick(parity, rs_order, t)) & 1) << (nb - 1 - t))
+            bit = (dest >> _pick(parity, rs_order, t)) & 1
+            if t == 0:
+                bit = 1 - (bit ^ ((lax.axis_index("col") >> _pick(parity, rs_order, 0)) & 1))
+            rs_pos = rs_pos + (bit << (nb - 1 - t))
             ag_pos = ag_pos + (((dest >> _pick(parity, ag_order, t)) & 1) << t)
         rows_fwd = rs_pos * nbc + sub
         rows_bwd = ag_pos * nbc + sub

time: 62.8 us -> 64.7 us (1.030); the launches traced: 63.7 us -> 63.8 us
  local copies, waits for them, and re-layouts: 3.43 us -> 5.15 us
  other arithmetic: 9.73 us -> 8.18 us
    slice x0 -> x1, local copies, waits for them, and re-layouts: none -> 2.7 us  [scatter_sum_col(): keep, other = (data[1], data[0])]
    squeeze x4 -> x3, local copies, waits for them, and re-layouts: 1.38 us -> 0.09 us  [scatter_sum_col(): other = lax.dynamic_index_in_dim(data, 1 - mine, axis=0, keepdims=False)]
    ppermute x2, starting transfers between devices: 1.7 us -> 0.52 us  [_swap(): return lax.ppermute(x, axis, perm)]
    unnamed x8, local copies, waits for them, and re-layouts: 0.02 us -> 1 us
    another operation x7, other arithmetic: 3.13 us -> 2.18 us  [gather_col(): have = jnp.stack([lo, hi], axis=0).reshape((-1,) + have.shape[1:])]
    reshape x1, local copies, waits for them, and re-layouts: 0.85 us -> 0.18 us  [gather_col(): have = jnp.stack([lo, hi], axis=0).reshape((-1,) + have.shape[1:])]
    reshape x1, other arithmetic: 0.67 us -> 0.02 us  [gather_col(): have = jnp.stack([lo, hi], axis=0).reshape((-1,) + have.shape[1:])]
  transfers between devices with their start and end apart: 10 -> 10, of which waited for: 6 -> 6; matrix products, arithmetic and copies ran while one was open for 21% -> 20% of each run, Pallas kernels for 12% -> 12%
where the time goes in v16:
time: 64.7 us; the launch traced here: 63.8 us
  waiting for transfers between devices  24.1 us (37%)
  starting transfers between devices  16.9 us (26%)
  other arithmetic  8.18 us (13%)
  Pallas kernels  7.51 us (12%)
  local copies, waits for them, and re-layouts  5.15 us (8%)
  matrix products  1.16 us (2%)
  between operations  0.83 us (1%)
    ppermute x8, waiting for transfers between devices, _swap_col(): return lax.ppermute(x, ('row', 'col'), perm)  24.1 us
    ppermute x8, starting transfers between devices, _swap_col(): return lax.ppermute(x, ('row', 'col'), perm)  16.3 us
    pallas_call x1, Pallas kernels, along_call(): pl.pallas_call(kernel, grid_spec=spec, out_shape=jax.ShapeDtypeStruct((nr...  3.97 us
    pallas_call x1, Pallas kernels, against_call(): pl.pallas_call(kernel, grid_spec=spec, out_shape=jax.ShapeDtypeStruct((nc...  3.54 us
    slice x1, local copies, waits for them, and re-layouts, scatter_sum_col(): keep, other = (data[1], data[0])  2.7 us
    another operation x7, other arithmetic, gather_col(): have = jnp.stack([lo, hi], axis=0).reshape((-1,) + have.shape[1:])  2.18 us
    another operation x2, other arithmetic, gather_row(): have = jnp.stack([lo, hi], axis=0).reshape((-1,) + have.shape[1:])  1.52 us
    add x4, other arithmetic, scatter_sum_col(): keep + _swap_col(other, row_size, col_size, (order[0][t], order[1][t]))  1.44 us
  transfers between devices with their start and end apart: 10, of which 6 were waited for; matrix products, arithmetic and copies ran while one was open for 20% of the time, Pallas kernels for 12%

profile of v16, /device:TPU:0, one launch (start us, length us, event | category | flops | bytes accessed | tf_op | source)
XLA Modules:
  0.0 63.8 jit_solution(5432489665514898491)
XLA Ops:
  0.0 0.5 collective-permute-start
  0.5 3.7 %collective-permute-start.5 = (bf16[1,2,128,128]{2,3,1,0:T(8,128)(2,1)}, bf16[1,2,128,128]{2,3,1,0:T(8,128)(2,1)S(1)}, u32[]{:S(2)}, u32[]{:S(2)}) collective-permute-start(bf16[1,2,128,128]{2,3,1,0:T(8,128)(2,1)} %bitcast.99), channel_id=1, source_target_pairs={{0,8},{1,9},{2,10},{3,11},{4,12},{5,13},{6,14},{7,15},{8,0},{9,1},... | collective-permute-start | bytes 196616 | tf_op jit(solution)/shard_map/ppermute | solution.py:31
  4.1 1.2 %multiply_add_fusion.1 = (s32[128]{0:T(128)}, s32[128]{0:T(128)S(1)}) fusion(s32[]{:T(128)S(6)} %and.58, s32[]{:T(128)S(6)} %select_n.134, s32[]{:T(128)S(6)} %select_n.136, s32[]{:T(128)S(6)} %select_n.135, s32[1,1,128]{2,1,0:T(1,128)} %param.9), kind=kLoop, calls=%fused_computation.34 | loop fusion | flops 4992 | bytes 1552 | tf_op jit(solution)/shard_map/add | solution.py:229
  5.4 1.2 %clamp_bitcast_fusion.cols_ref = s32[128]{0:T(128)} fusion(s32[1,1,128]{2,1,0:T(1,128)} %param.10), kind=kLoop, calls=%fused_computation.33 | loop fusion | flops 128 | bytes 1024 | tf_op jit(solution)/shard_map/jit(clip)/min | solution.py:213
  7.3 1.2 %collective-permute-done.5 = bf16[1,2,128,128]{2,3,1,0:T(8,128)(2,1)S(1)} collective-permute-done((bf16[1,2,128,128]{2,3,1,0:T(8,128)(2,1)}, bf16[1,2,128,128]{2,3,1,0:T(8,128)(2,1)S(1)}, u32[]{:S(2)}, u32[]{:S(2)}) %collective-permute-start.5) | collective-permute-done | bytes 65568 | tf_op jit(solution)/shard_map/ppermute | solution.py:31
  8.4 0.9 %select_bitcast_fusion.7 = (bf16[1,1,2,128,128]{3,4,2,1,0:T(8,128)(2,1)S(1)}, bf16[1,1,2,128,128]{3,4,2,1,0:T(8,128)(2,1)S(1)}) fusion(bf16[1,2,128,128]{2,3,1,0:T(8,128)(2,1)} %bitcast.100, bf16[1,2,128,128]{2,3,1,0:T(8,128)(2,1)S(1)} %collective-permute-done.5, pred[]{:T(512)S(6)} %eq.23), kind=kLoop, calls=%fused_computation.21 | loop fusion | flops 65536 | bytes 262145 | tf_op jit(solution)/shard_map/stack | solution.py:90
  9.3 1.6 %collective-permute-start.6 = (bf16[2,2,128,128]{2,3,1,0:T(8,128)(2,1)S(1)}, bf16[2,2,128,128]{2,3,1,0:T(8,128)(2,1)S(1)}, u32[]{:S(2)}, u32[]{:S(2)}) collective-permute-start(bf16[2,2,128,128]{2,3,1,0:T(8,128)(2,1)S(1)} %maximum_bitcast_fusion), channel_id=1, source_target_pairs={{0,1},{1,0},{2,3},{3,2},{4,5},{5,4},{6,7},{7,6},{8,9},{9,8},{10,11... | collective-permute-start | bytes 393224 | tf_op jit(solution)/shard_map/ppermute | solution.py:31
  10.9 0.9 %select_bitcast_fusion.9 = (bf16[1,1,256,128]{3,2,1,0:T(8,128)(2,1)S(1)}, bf16[1,1,256,128]{3,2,1,0:T(8,128)(2,1)S(1)}) fusion(bf16[1,256,128]{2,1,0:T(8,128)(2,1)S(1)} %collective-permute-done, pred[]{:T(512)S(6)} %eq.19, bf16[256,128]{1,0:T(8,128)(2,1)} %param.7), kind=kLoop, calls=%fused_computation.23 | loop fusion | flops 65536 | bytes 262145 | tf_op jit(solution)/shard_map/stack | solution.py:52
  11.8 0.7 %pad_maximum_fusion.3 = bf16[2,1,256,128]{3,2,1,0:T(8,128)(2,1)} fusion(bf16[1,1,256,128]{3,2,1,0:T(8,128)(2,1)S(1)} %get-tuple-element.18, bf16[1,1,256,128]{3,2,1,0:T(8,128)(2,1)S(1)} %get-tuple-element.17), kind=kLoop, calls=%fused_computation.13 | loop fusion | flops 65536 | bytes 262144 | tf_op jit(solution)/shard_map/stack | solution.py:52
  12.4 4.0 %shard_map.73 = f32[32,128,128]{2,1,0:T(8,128)} custom-call(s32[128]{0:T(128)} %get-tuple-element.5.rows_ref, s32[128]{0:T(128)} %clamp_bitcast_fusion.cols_ref, s32[1]{0:T(128)} %bitcast.2.cnt_ref, bf16[128,128,128]{2,1,0:T(8,128)(2,1)} %bitcast.88, bf16[4,128,128]{2,1,0:T(8,128)(2,1)} %bitcast.96), custom_call_target="tpu_custom_call" | custom-call | tf_op jit(solution)/shard_map/pallas_call | solution.py:150
  16.4 2.7 %fusion.1 = (f32[16,128,128]{2,1,0:T(8,128)}, f32[16,128,128]{2,1,0:T(8,128)S(1)}) fusion(f32[32,128,128]{2,1,0:T(8,128)} %shard_map.73), kind=kLoop, calls=%fused_computation.39 | loop fusion | bytes 4194304 | tf_op jit(solution)/shard_map/slice | solution.py:102
  19.1 1.0 %collective-permute-start.1 = (f32[2,2,2,2,128,128]{5,4,3,2,1,0:T(8,128)}, f32[2,2,2,2,128,128]{5,4,3,2,1,0:T(8,128)S(1)}, u32[]{:S(2)}, u32[]{:S(2)}) collective-permute-start(f32[2,2,2,2,128,128]{5,4,3,2,1,0:T(8,128)} %bitcast.9), channel_id=1, source_target_pairs={{0,1},{1,0},{2,3},{3,2},{4,5},{5,4},{6,7},{7,6},{8,9},{9,8},{10,11... | collective-permute-start | bytes 3145736 | tf_op jit(solution)/shard_map/ppermute | solution.py:31
  20.1 0.2 copy.12
  20.3 1.2 %collective-permute-start.7 = (bf16[4,2,128,128]{3,2,1,0:T(8,128)(2,1)S(1)}, bf16[4,2,128,128]{3,2,1,0:T(8,128)(2,1)S(1)}, u32[]{:S(2)}, u32[]{:S(2)}) collective-permute-start(bf16[4,2,128,128]{3,2,1,0:T(8,128)(2,1)S(1)} %copy.12), channel_id=1, source_target_pairs={{0,2},{1,3},{2,0},{3,1},{4,6},{5,7},{6,4},{7,5},{8,10},{9,11},{10,... | collective-permute-start | bytes 786440 | tf_op jit(solution)/shard_map/ppermute | solution.py:31
  21.5 5.3 %collective-permute-done.7 = bf16[4,2,128,128]{3,2,1,0:T(8,128)(2,1)S(1)} collective-permute-done((bf16[4,2,128,128]{3,2,1,0:T(8,128)(2,1)S(1)}, bf16[4,2,128,128]{3,2,1,0:T(8,128)(2,1)S(1)}, u32[]{:S(2)}, u32[]{:S(2)}) %collective-permute-start.7) | collective-permute-done | bytes 262176 | tf_op jit(solution)/shard_map/ppermute | solution.py:31
  26.9 1.6 %collective-permute-start.8 = (bf16[8,2,128,128]{3,2,1,0:T(8,128)(2,1)S(1)}, bf16[8,2,128,128]{3,2,1,0:T(8,128)(2,1)S(1)}, u32[]{:S(2)}, u32[]{:S(2)}) collective-permute-start(bf16[8,2,128,128]{3,2,1,0:T(8,128)(2,1)S(1)} %bitcast.92), channel_id=1, source_target_pairs={{0,4},{1,5},{2,6},{3,7},{4,0},{5,1},{6,2},{7,3},{8,12},{9,13},{10,... | collective-permute-start | bytes 1572872 | tf_op jit(solution)/shard_map/ppermute | solution.py:31
  28.4 0.5 multiply_add_fusion.rows_ref
  29.0 6.2 %collective-permute-done.1 = f32[2,2,2,2,128,128]{5,4,3,2,1,0:T(8,128)S(1)} collective-permute-done((f32[2,2,2,2,128,128]{5,4,3,2,1,0:T(8,128)}, f32[2,2,2,2,128,128]{5,4,3,2,1,0:T(8,128)S(1)}, u32[]{:S(2)}, u32[]{:S(2)}) %collective-permute-start.1) | collective-permute-done | bytes 1048608 | tf_op jit(solution)/shard_map/ppermute | solution.py:31
  35.2 1.0 %copy-done.1 = f32[2,2,2,2,128,128]{5,4,3,2,1,0:T(8,128)} copy-done((f32[2,2,2,2,128,128]{5,4,3,2,1,0:T(8,128)}, f32[2,2,2,2,128,128]{5,4,3,2,1,0:T(8,128)S(1)}, u32[]{:S(2)}) %copy-start.1) | copy-done | bytes 1048600
  36.1 1.3 %add.92 = f32[2,2,2,2,128,128]{5,4,3,2,1,0:T(8,128)S(1)} add(f32[2,2,2,2,128,128]{5,4,3,2,1,0:T(8,128)S(1)} %bitcast.91, f32[2,2,2,2,128,128]{5,4,3,2,1,0:T(8,128)} %copy-done.1) | non-fusion elementwise | flops 262144 | bytes 3145728 | tf_op jit(solution)/shard_map/add | solution.py:107
  37.5 2.0 %collective-permute-start.2 = (f32[2,2,2,128,128]{4,3,2,1,0:T(8,128)S(1)}, f32[2,2,2,128,128]{4,3,2,1,0:T(8,128)S(1)}, u32[]{:S(2)}, u32[]{:S(2)}) collective-permute-start(f32[2,2,2,128,128]{4,3,2,1,0:T(8,128)S(1)} %dynamic-slice_bitcast_fusion), channel_id=1, source_target_pairs={{0,2},{1,3},{2,0},{3,1},{4,6},{5,7},{6,4},{7,5},{8,10},{9,11},{10,... | collective-permute-start | bytes 1572872 | tf_op jit(solution)/shard_map/ppermute | solution.py:31
  39.6 0.1 select_bitcast_fusion.1
  39.7 1.1 %pad_maximum_fusion = bf16[2,8,2,128,128]{4,3,2,1,0:T(8,128)(2,1)} fusion(bf16[1,8,2,128,128]{4,3,2,1,0:T(8,128)(2,1)S(1)} %get-tuple-element.10, bf16[1,8,2,128,128]{4,3,2,1,0:T(8,128)(2,1)S(1)} %get-tuple-element.9), kind=kLoop, calls=%fused_computation.2 | loop fusion | flops 524288 | bytes 2097152 | tf_op jit(solution)/shard_map/stack | solution.py:90
  40.8 3.5 %shard_map.74 = f32[4,128,128]{2,1,0:T(8,128)} custom-call(s32[128]{0:T(128)} %multiply_add_fusion.rows_ref, s32[128]{0:T(128)} %clamp_bitcast_fusion.cols_ref, s32[1]{0:T(128)} %bitcast.2.cnt_ref, bf16[128,128,128]{2,1,0:T(8,128)(2,1)} %bitcast.89, bf16[32,128,128]{2,1,0:T(8,128)(2,1)} %bitcast.90), custom_call_target="tpu_custom_call" | custom-call | tf_op jit(solution)/shard_map/pallas_call | solution.py:192
  44.3 1.0 %constant_dynamic-slice_fusion.1 = (f32[1,2,128,128]{3,2,1,0:T(8,128)S(1)}, f32[1,2,128,128]{3,2,1,0:T(8,128)S(1)}) fusion(f32[2,2,128,128]{3,2,1,0:T(8,128)} %bitcast.93, s32[]{:T(128)S(6)} %select_n.159, s32[]{:T(128)S(6)} %select_n.160), kind=kLoop, calls=%fused_computation.25 | loop fusion | bytes 524296 | tf_op jit(solution)/shard_map/jit(dynamic_index_in_dim)/dynamic_slice | solution.py:71
  45.5 1.3 %collective-permute-done.2 = f32[2,2,2,128,128]{4,3,2,1,0:T(8,128)S(1)} collective-permute-done((f32[2,2,2,128,128]{4,3,2,1,0:T(8,128)S(1)}, f32[2,2,2,128,128]{4,3,2,1,0:T(8,128)S(1)}, u32[]{:S(2)}, u32[]{:S(2)}) %collective-permute-start.2) | collective-permute-done | bytes 524320 | tf_op jit(solution)/shard_map/ppermute | solution.py:31
  46.9 1.8 %collective-permute-start.3 = (f32[2,2,128,128]{3,2,1,0:T(8,128)S(1)}, f32[2,2,128,128]{3,2,1,0:T(8,128)S(1)}, u32[]{:S(2)}, u32[]{:S(2)}) collective-permute-start(f32[2,2,128,128]{3,2,1,0:T(8,128)S(1)} %dynamic-slice_bitcast_fusion.1), channel_id=1, source_target_pairs={{0,4},{1,5},{2,6},{3,7},{4,0},{5,1},{6,2},{7,3},{8,12},{9,13},{10,... | collective-permute-start | bytes 786440 | tf_op jit(solution)/shard_map/ppermute | solution.py:31
  48.8 4.5 %collective-permute-done.3 = f32[2,2,128,128]{3,2,1,0:T(8,128)S(1)} collective-permute-done((f32[2,2,128,128]{3,2,1,0:T(8,128)S(1)}, f32[2,2,128,128]{3,2,1,0:T(8,128)S(1)}, u32[]{:S(2)}, u32[]{:S(2)}) %collective-permute-start.3) | collective-permute-done | bytes 262176 | tf_op jit(solution)/shard_map/ppermute | solution.py:31
  53.4 3.5 %collective-permute-start.4 = (f32[2,128,128]{2,1,0:T(8,128)S(1)}, f32[2,128,128]{2,1,0:T(8,128)S(1)}, u32[]{:S(2)}, u32[]{:S(2)}) collective-permute-start(f32[2,128,128]{2,1,0:T(8,128)S(1)} %dynamic-slice_bitcast_fusion.2), channel_id=1, source_target_pairs={{0,8},{1,9},{2,10},{3,11},{4,12},{5,13},{6,14},{7,15},{8,0},{9,1},... | collective-permute-start | bytes 393224 | tf_op jit(solution)/shard_map/ppermute | solution.py:31
  56.9 0.2 fusion.2
  57.2 5.7 %collective-permute-done.4 = f32[2,128,128]{2,1,0:T(8,128)S(1)} collective-permute-done((f32[2,128,128]{2,1,0:T(8,128)S(1)}, f32[2,128,128]{2,1,0:T(8,128)S(1)}, u32[]{:S(2)}, u32[]{:S(2)}) %collective-permute-start.4) | collective-permute-done | bytes 131104 | tf_op jit(solution)/shard_map/ppermute | solution.py:31
  62.9 0.9 %fusion = bf16[256,256]{1,0:T(8,128)(2,1)} fusion(f32[256,256]{1,0:T(8,128)S(1)} %fusion.2, f32[256,128]{1,0:T(8,128)S(1)} %bitcast.97, bf16[128,256]{1,0:T(8,128)(2,1)S(1)} %copy-done.2), kind=kOutput, calls=%fused_computation.1 | convolution fusion | flops 100794368 | bytes 589824 | tf_op jit(solution)/shard_map/dot_general | solution.py:252
  (26 shorter events, 0.7 us)
Async XLA Ops:
  0.0 56.9 %copy-start = (bf16[128,256]{1,0:T(8,128)(2,1)S(1)}, bf16[128,256]{1,0:T(8,128)(2,1)}, u32[]{:S(2)}) copy-start(bf16[128,256]{1,0:T(8,128)(2,1)} %param.13) | copy-start | bytes 196612
  0.0 10.9 %collective-permute-start = (bf16[1,256,128]{2,1,0:T(8,128)(2,1)}, bf16[1,256,128]{2,1,0:T(8,128)(2,1)S(1)}, u32[]{:S(2)}, u32[]{:S(2)}) collective-permute-start(bf16[1,256,128]{2,1,0:T(8,128)(2,1)} %bitcast.98), channel_id=1, source_target_pairs={{0,16},{16,0},{1,17},{17,1},{2,18},{18,2},{3,19},{19,3},{4,20},{20... | collective-permute-start | bytes 196616 | tf_op jit(solution)/shard_map/ppermute | solution.py:36
  0.5 8.0 %collective-permute-start.5 = (bf16[1,2,128,128]{2,3,1,0:T(8,128)(2,1)}, bf16[1,2,128,128]{2,3,1,0:T(8,128)(2,1)S(1)}, u32[]{:S(2)}, u32[]{:S(2)}) collective-permute-start(bf16[1,2,128,128]{2,3,1,0:T(8,128)(2,1)} %bitcast.99), channel_id=1, source_target_pairs={{0,8},{1,9},{2,10},{3,11},{4,12},{5,13},{6,14},{7,15},{8,0},{9,1},... | collective-permute-start | bytes 196616 | tf_op jit(solution)/shard_map/ppermute | solution.py:31
  9.3 10.8 %collective-permute-start.6 = (bf16[2,2,128,128]{2,3,1,0:T(8,128)(2,1)S(1)}, bf16[2,2,128,128]{2,3,1,0:T(8,128)(2,1)S(1)}, u32[]{:S(2)}, u32[]{:S(2)}) collective-permute-start(bf16[2,2,128,128]{2,3,1,0:T(8,128)(2,1)S(1)} %maximum_bitcast_fusion), channel_id=1, source_target_pairs={{0,1},{1,0},{2,3},{3,2},{4,5},{5,4},{6,7},{7,6},{8,9},{9,8},{10,11... | collective-permute-start | bytes 393224 | tf_op jit(solution)/shard_map/ppermute | solution.py:31
  19.1 9.3 %copy-start.3 = (s32[1,1,128]{2,1,0:T(1,128)S(1)}, s32[1,1,128]{2,1,0:T(1,128)}, u32[]{:S(2)}) copy-start(s32[1,1,128]{2,1,0:T(1,128)} %param.9) | copy-start | bytes 1540
  19.1 16.0 %collective-permute-start.1 = (f32[2,2,2,2,128,128]{5,4,3,2,1,0:T(8,128)}, f32[2,2,2,2,128,128]{5,4,3,2,1,0:T(8,128)S(1)}, u32[]{:S(2)}, u32[]{:S(2)}) collective-permute-start(f32[2,2,2,2,128,128]{5,4,3,2,1,0:T(8,128)} %bitcast.9), channel_id=1, source_target_pairs={{0,1},{1,0},{2,3},{3,2},{4,5},{5,4},{6,7},{7,6},{8,9},{9,8},{10,11... | collective-permute-start | bytes 3145736 | tf_op jit(solution)/shard_map/ppermute | solution.py:31
  20.3 6.4 %collective-permute-start.7 = (bf16[4,2,128,128]{3,2,1,0:T(8,128)(2,1)S(1)}, bf16[4,2,128,128]{3,2,1,0:T(8,128)(2,1)S(1)}, u32[]{:S(2)}, u32[]{:S(2)}) collective-permute-start(bf16[4,2,128,128]{3,2,1,0:T(8,128)(2,1)S(1)} %copy.12), channel_id=1, source_target_pairs={{0,2},{1,3},{2,0},{3,1},{4,6},{5,7},{6,4},{7,5},{8,10},{9,11},{10,... | collective-permute-start | bytes 786440 | tf_op jit(solution)/shard_map/ppermute | solution.py:31
  26.9 12.7 %collective-permute-start.8 = (bf16[8,2,128,128]{3,2,1,0:T(8,128)(2,1)S(1)}, bf16[8,2,128,128]{3,2,1,0:T(8,128)(2,1)S(1)}, u32[]{:S(2)}, u32[]{:S(2)}) collective-permute-start(bf16[8,2,128,128]{3,2,1,0:T(8,128)(2,1)S(1)} %bitcast.92), channel_id=1, source_target_pairs={{0,4},{1,5},{2,6},{3,7},{4,0},{5,1},{6,2},{7,3},{8,12},{9,13},{10,... | collective-permute-start | bytes 1572872 | tf_op jit(solution)/shard_map/ppermute | solution.py:31
  35.2 1.0 %copy-start.1 = (f32[2,2,2,2,128,128]{5,4,3,2,1,0:T(8,128)}, f32[2,2,2,2,128,128]{5,4,3,2,1,0:T(8,128)S(1)}, u32[]{:S(2)}) copy-start(f32[2,2,2,2,128,128]{5,4,3,2,1,0:T(8,128)S(1)} %collective-permute-done.1) | copy-start | bytes 3145732
  37.5 9.2 %collective-permute-start.2 = (f32[2,2,2,128,128]{4,3,2,1,0:T(8,128)S(1)}, f32[2,2,2,128,128]{4,3,2,1,0:T(8,128)S(1)}, u32[]{:S(2)}, u32[]{:S(2)}) collective-permute-start(f32[2,2,2,128,128]{4,3,2,1,0:T(8,128)S(1)} %dynamic-slice_bitcast_fusion), channel_id=1, source_target_pairs={{0,2},{1,3},{2,0},{3,1},{4,6},{5,7},{6,4},{7,5},{8,10},{9,11},{10,... | collective-permute-start | bytes 1572872 | tf_op jit(solution)/shard_map/ppermute | solution.py:31
  45.4 17.4 %copy-start.2 = (bf16[128,256]{1,0:T(8,128)(2,1)S(1)}, bf16[128,256]{1,0:T(8,128)(2,1)}, u32[]{:S(2)}) copy-start(bf16[128,256]{1,0:T(8,128)(2,1)} %param.12) | copy-start | bytes 196612
  45.4 3.4 %collective-permute-start.9 = (f32[2,128,128]{1,2,0:T(8,128)S(1)}, f32[2,128,128]{1,2,0:T(8,128)S(1)}, u32[]{:S(2)}, u32[]{:S(2)}) collective-permute-start(f32[2,128,128]{1,2,0:T(8,128)S(1)} %bitcast.101), channel_id=1, source_target_pairs={{0,16},{16,0},{1,17},{17,1},{2,18},{18,2},{3,19},{19,3},{4,20},{20... | collective-permute-start | bytes 393224 | tf_op jit(solution)/shard_map/ppermute | solution.py:36
  46.9 6.4 %collective-permute-start.3 = (f32[2,2,128,128]{3,2,1,0:T(8,128)S(1)}, f32[2,2,128,128]{3,2,1,0:T(8,128)S(1)}, u32[]{:S(2)}, u32[]{:S(2)}) collective-permute-start(f32[2,2,128,128]{3,2,1,0:T(8,128)S(1)} %dynamic-slice_bitcast_fusion.1), channel_id=1, source_target_pairs={{0,4},{1,5},{2,6},{3,7},{4,0},{5,1},{6,2},{7,3},{8,12},{9,13},{10,... | collective-permute-start | bytes 786440 | tf_op jit(solution)/shard_map/ppermute | solution.py:31
  53.4 9.5 %collective-permute-start.4 = (f32[2,128,128]{2,1,0:T(8,128)S(1)}, f32[2,128,128]{2,1,0:T(8,128)S(1)}, u32[]{:S(2)}, u32[]{:S(2)}) collective-permute-start(f32[2,128,128]{2,1,0:T(8,128)S(1)} %dynamic-slice_bitcast_fusion.2), channel_id=1, source_target_pairs={{0,8},{1,9},{2,10},{3,11},{4,12},{5,13},{6,14},{7,15},{8,0},{9,1},... | collective-permute-start | bytes 393224 | tf_op jit(solution)/shard_map/ppermute | solution.py:31

commit v17 on v3

--- a/solution.py
+++ b/solution.py
@@ -226,8 +226,21 @@
         rows_fwd = rowblk
         rows_bwd = rowblk
 
-    group = gather_row(features).reshape(ncb, side, width)
-    fwd_parts = along_call(rows_fwd, colblk, cnt, values, group, nrb)
+    nb_r = _nbits(row_size)
+    if nb_r is not None:
+        me_r = lax.axis_index("row")
+        have = features[None]
+        src = colblk // nbc
+        pos = jnp.zeros_like(src)
+        for t, bit in enumerate(range(nb_r - 1, -1, -1)):
+            have = jnp.concatenate([have, _swap(have, "row", row_size, bit)], axis=0)
+            pos = pos + ((((src ^ me_r) >> bit) & 1) << t)
+        group = have.reshape(ncb, side, width)
+        cols_fwd = pos * nbc + colblk % nbc
+    else:
+        group = gather_row(features).reshape(ncb, side, width)
+        cols_fwd = colblk
+    fwd_parts = along_call(rows_fwd, cols_fwd, cnt, values, group, nrb)
 
     mine_t = jnp.transpose(features.reshape(nbc, side, width), (0, 2, 1))
     if nb is not None:

time: 62.8 us -> 64.6 us (1.029); the launches traced: 63.7 us -> 63.4 us
  starting transfers between devices: 17.4 us -> 9.52 us
  Pallas kernels: 7.53 us -> 11.9 us
  waiting for transfers between devices: 23.6 us -> 27.4 us
  other arithmetic: 9.73 us -> 9.08 us
    ppermute x8, starting transfers between devices: 15.7 us -> 9 us  [_swap_col(): return lax.ppermute(x, ('row', 'col'), perm)]
    ppermute x8, waiting for transfers between devices: 23.6 us -> 27.4 us  [_swap_col(): return lax.ppermute(x, ('row', 'col'), perm)]
    pallas_call x1, Pallas kernels: 3.97 us -> 6.15 us  [along_call(): pl.pallas_call(kernel, grid_spec=spec, out_shape=jax.ShapeDtypeStruct((nr...]
    pallas_call x1, Pallas kernels: 3.56 us -> 5.74 us  [against_call(): pl.pallas_call(kernel, grid_spec=spec, out_shape=jax.ShapeDtypeStruct((nc...]
    another operation x2 -> x0, other arithmetic: 1.51 us -> none  [gather_row(): have = jnp.stack([lo, hi], axis=0).reshape((-1,) + have.shape[1:])]
    concatenate x0 -> x1, other arithmetic: none -> 1.5 us  [local(): have = jnp.concatenate([have, _swap(have, 'row', row_size, bit)], axis=0)]
    ppermute x2, starting transfers between devices: 1.7 us -> 0.52 us  [_swap(): return lax.ppermute(x, axis, perm)]
    min x1, other arithmetic: 1.25 us -> 0.59 us  [local(): colblk = jnp.clip(tile_cols[0, 0], 0, ncb - 1)]
  transfers between devices with their start and end apart: 10 -> 10, of which waited for: 6 -> 6; matrix products, arithmetic and copies ran while one was open for 21% -> 20% of each run, Pallas kernels for 12% -> 19%
where the time goes in v17:
time: 64.6 us; the launch traced here: 63.4 us
  waiting for transfers between devices  27.4 us (42%)
  Pallas kernels  11.9 us (18%)
  starting transfers between devices  9.52 us (15%)
  other arithmetic  9.08 us (14%)
  local copies, waits for them, and re-layouts  3.44 us (5%)
  matrix products  1.16 us (2%)
  between operations  0.85 us (1%)
    ppermute x8, waiting for transfers between devices, _swap_col(): return lax.ppermute(x, ('row', 'col'), perm)  27.4 us
    ppermute x8, starting transfers between devices, _swap_col(): return lax.ppermute(x, ('row', 'col'), perm)  9 us
    pallas_call x1, Pallas kernels, along_call(): pl.pallas_call(kernel, grid_spec=spec, out_shape=jax.ShapeDtypeStruct((nr...  6.15 us
    pallas_call x1, Pallas kernels, against_call(): pl.pallas_call(kernel, grid_spec=spec, out_shape=jax.ShapeDtypeStruct((nc...  5.74 us
    another operation x7, other arithmetic, gather_col(): have = jnp.stack([lo, hi], axis=0).reshape((-1,) + have.shape[1:])  3.13 us
    concatenate x1, other arithmetic, local(): have = jnp.concatenate([have, _swap(have, 'row', row_size, bit)], axis=0)  1.5 us
    add x4, other arithmetic, scatter_sum_col(): keep + _swap_col(other, row_size, col_size, (order[0][t], order[1][t]))  1.44 us
    squeeze x4, local copies, waits for them, and re-layouts, scatter_sum_col(): other = lax.dynamic_index_in_dim(data, 1 - mine, axis=0, keepdims=False)  1.4 us
  transfers between devices with their start and end apart: 10, of which 6 were waited for; matrix products, arithmetic and copies ran while one was open for 20% of the time, Pallas kernels for 19%

profile of v17, /device:TPU:0, one launch (start us, length us, event | category | flops | bytes accessed | tf_op | source)
XLA Modules:
  0.0 63.4 jit_solution(9629078224686030424)
XLA Ops:
  0.0 0.5 collective-permute-start
  0.5 3.7 %collective-permute-start.5 = (bf16[1,2,128,128]{2,3,1,0:T(8,128)(2,1)}, bf16[1,2,128,128]{2,3,1,0:T(8,128)(2,1)S(1)}, u32[]{:S(2)}, u32[]{:S(2)}) collective-permute-start(bf16[1,2,128,128]{2,3,1,0:T(8,128)(2,1)} %bitcast.99), channel_id=1, source_target_pairs={{0,8},{1,9},{2,10},{3,11},{4,12},{5,13},{6,14},{7,15},{8,0},{9,1},... | collective-permute-start | bytes 196616 | tf_op jit(solution)/shard_map/ppermute | solution.py:31
  4.1 1.2 %multiply_add_fusion.1 = (s32[128]{0:T(128)}, s32[128]{0:T(128)S(1)}, s32[128]{0:T(128)}) fusion(s32[]{:T(128)S(6)} %select_n.136, s32[]{:T(128)S(6)} %select_n.138, s32[]{:T(128)S(6)} %select_n.137, s32[1,1,128]{2,1,0:T(1,128)} %param.9, s32[]{:T(128)S(6)} %axis_index.15, s32[1,1,128]{2,1,0:T(1,128)} %param.10), kind=kLoop, calls=%fused_computation.40 | loop fusion | flops 8064 | bytes 2576 | tf_op jit(solution)/shard_map/add | solution.py:223
  6.0 2.4 %collective-permute-done.5 = bf16[1,2,128,128]{2,3,1,0:T(8,128)(2,1)S(1)} collective-permute-done((bf16[1,2,128,128]{2,3,1,0:T(8,128)(2,1)}, bf16[1,2,128,128]{2,3,1,0:T(8,128)(2,1)S(1)}, u32[]{:S(2)}, u32[]{:S(2)}) %collective-permute-start.5) | collective-permute-done | bytes 65568 | tf_op jit(solution)/shard_map/ppermute | solution.py:31
  8.4 0.9 %select_bitcast_fusion.7 = (bf16[1,1,2,128,128]{3,4,2,1,0:T(8,128)(2,1)S(1)}, bf16[1,1,2,128,128]{3,4,2,1,0:T(8,128)(2,1)S(1)}) fusion(bf16[1,2,128,128]{2,3,1,0:T(8,128)(2,1)} %bitcast.100, bf16[1,2,128,128]{2,3,1,0:T(8,128)(2,1)S(1)} %collective-permute-done.5, pred[]{:T(512)S(6)} %eq.21), kind=kLoop, calls=%fused_computation.23 | loop fusion | flops 65536 | bytes 262145 | tf_op jit(solution)/shard_map/stack | solution.py:90
  9.3 0.7 %maximum_bitcast_fusion = bf16[2,2,128,128]{2,3,1,0:T(8,128)(2,1)} fusion(bf16[1,1,2,128,128]{3,4,2,1,0:T(8,128)(2,1)S(1)} %get-tuple-element.16, bf16[1,1,2,128,128]{3,4,2,1,0:T(8,128)(2,1)S(1)} %get-tuple-element.15), kind=kLoop, calls=%fused_computation.16 | loop fusion | flops 65536 | bytes 262144 | tf_op jit(solution)/shard_map/reshape | solution.py:90
  9.9 1.5 %collective-permute-start.6 = (bf16[2,2,128,128]{2,3,1,0:T(8,128)(2,1)}, bf16[2,2,128,128]{2,3,1,0:T(8,128)(2,1)S(1)}, u32[]{:S(2)}, u32[]{:S(2)}) collective-permute-start(bf16[2,2,128,128]{2,3,1,0:T(8,128)(2,1)} %maximum_bitcast_fusion), channel_id=1, source_target_pairs={{0,1},{1,0},{2,3},{3,2},{4,5},{5,4},{6,7},{7,6},{8,9},{9,8},{10,11... | collective-permute-start | bytes 393224 | tf_op jit(solution)/shard_map/ppermute | solution.py:31
  11.5 1.5 %pad_maximum_fusion.3 = bf16[2,256,128]{2,1,0:T(8,128)(2,1)} fusion(bf16[1,256,128]{2,1,0:T(8,128)(2,1)S(1)} %collective-permute-done, bf16[1,256,128]{2,1,0:T(8,128)(2,1)} %bitcast.101), kind=kLoop, calls=%fused_computation.15 | loop fusion | flops 65536 | bytes 262144 | tf_op jit(solution)/shard_map/concatenate | solution.py:236
  13.0 6.2 %shard_map.73 = f32[32,128,128]{2,1,0:T(8,128)} custom-call(s32[128]{0:T(128)} %get-tuple-element.5.rows_ref, s32[128]{0:T(128)} %get-tuple-element.17.cols_ref, s32[1]{0:T(128)} %bitcast.2.cnt_ref, bf16[128,128,128]{2,1,0:T(8,128)(2,1)} %bitcast.87, bf16[4,128,128]{2,1,0:T(8,128)(2,1)} %bitcast.96), custom_call_target="tpu_custom_call" | custom-call | tf_op jit(solution)/shard_map/pallas_call | solution.py:147
  19.1 1.3 %dynamic-slice_bitcast_fusion = f32[2,2,2,2,128,128]{5,4,3,2,1,0:T(8,128)S(1)} fusion(f32[2,2,2,2,2,128,128]{6,5,4,3,2,1,0:T(8,128)} %bitcast.89, s32[]{:T(128)S(6)} %select_n.143), kind=kLoop, calls=%fused_computation.4 | loop fusion | bytes 2097156 | tf_op jit(solution)/shard_map/jit(dynamic_index_in_dim)/squeeze | solution.py:103
  20.5 0.6 collective-permute-start.1
  21.1 0.8 %copy.12 = bf16[4,2,128,128]{3,2,1,0:T(8,128)(2,1)} copy(bf16[4,2,128,128]{2,3,1,0:T(8,128)(2,1)S(1)} %bitcast.94) | data formatting | bytes 524288 | tf_op jit(solution)/shard_map/reshape | solution.py:90
  22.0 0.5 multiply_add_fusion.rows_ref
  22.5 6.1 %collective-permute-done.7 = bf16[4,2,128,128]{3,2,1,0:T(8,128)(2,1)S(1)} collective-permute-done((bf16[4,2,128,128]{3,2,1,0:T(8,128)(2,1)}, bf16[4,2,128,128]{3,2,1,0:T(8,128)(2,1)S(1)}, u32[]{:S(2)}, u32[]{:S(2)}) %collective-permute-start.7) | collective-permute-done | bytes 262176 | tf_op jit(solution)/shard_map/ppermute | solution.py:31
  28.5 1.0 %select_bitcast_fusion.3 = (bf16[1,4,2,128,128]{4,3,2,1,0:T(8,128)(2,1)S(1)}, bf16[1,4,2,128,128]{4,3,2,1,0:T(8,128)(2,1)S(1)}) fusion(bf16[4,2,128,128]{3,2,1,0:T(8,128)(2,1)} %copy.12, bf16[4,2,128,128]{3,2,1,0:T(8,128)(2,1)S(1)} %collective-permute-done.7, pred[]{:T(512)S(6)} %eq.19), kind=kLoop, calls=%fused_computation.13 | loop fusion | flops 262144 | bytes 1048577 | tf_op jit(solution)/shard_map/stack | solution.py:90
  29.7 0.6 clamp_bitcast_fusion.cols_ref
  30.3 7.3 %collective-permute-done.1 = f32[2,2,2,2,128,128]{5,4,3,2,1,0:T(8,128)} collective-permute-done((f32[2,2,2,2,128,128]{5,4,3,2,1,0:T(8,128)S(1)}, f32[2,2,2,2,128,128]{5,4,3,2,1,0:T(8,128)}, u32[]{:S(2)}, u32[]{:S(2)}) %collective-permute-start.1) | collective-permute-done | bytes 1048608 | tf_op jit(solution)/shard_map/ppermute | solution.py:31
  37.5 1.3 %bitcast_add_fusion = f32[2,2,2,2,128,128]{5,4,3,2,1,0:T(8,128)S(1)} fusion(f32[2,2,2,2,128,128]{5,4,3,2,1,0:T(8,128)} %collective-permute-done.1, f32[2,2,2,2,2,128,128]{6,5,4,3,2,1,0:T(8,128)S(1)} %bitcast.90, s32[]{:T(128)S(6)} %select_n.142), kind=kLoop, calls=%fused_computation.3 | loop fusion | flops 262144 | bytes 3145732 | tf_op jit(solution)/shard_map/add | solution.py:104
  38.9 0.1 collective-permute-start.2
  39.1 0.1 select_bitcast_fusion.1
  39.2 1.1 %pad_maximum_fusion = bf16[2,8,2,128,128]{4,3,2,1,0:T(8,128)(2,1)} fusion(bf16[1,8,2,128,128]{4,3,2,1,0:T(8,128)(2,1)S(1)} %get-tuple-element.8, bf16[1,8,2,128,128]{4,3,2,1,0:T(8,128)(2,1)S(1)} %get-tuple-element.7), kind=kLoop, calls=%fused_computation.2 | loop fusion | flops 524288 | bytes 2097152 | tf_op jit(solution)/shard_map/stack | solution.py:90
  40.3 5.7 %shard_map.74 = f32[4,128,128]{2,1,0:T(8,128)} custom-call(s32[128]{0:T(128)} %multiply_add_fusion.rows_ref, s32[128]{0:T(128)} %clamp_bitcast_fusion.cols_ref, s32[1]{0:T(128)} %bitcast.2.cnt_ref, bf16[128,128,128]{2,1,0:T(8,128)(2,1)} %bitcast.88, bf16[32,128,128]{2,1,0:T(8,128)(2,1)} %bitcast.91), custom_call_target="tpu_custom_call" | custom-call | tf_op jit(solution)/shard_map/pallas_call | solution.py:189
  46.0 1.0 %constant_dynamic-slice_fusion.1 = (f32[1,2,128,128]{3,2,1,0:T(8,128)S(1)}, f32[1,2,128,128]{3,2,1,0:T(8,128)S(1)}) fusion(f32[2,2,128,128]{3,2,1,0:T(8,128)} %bitcast.93, s32[]{:T(128)S(6)} %select_n.162, s32[]{:T(128)S(6)} %select_n.163), kind=kLoop, calls=%fused_computation.25 | loop fusion | bytes 524296 | tf_op jit(solution)/shard_map/jit(dynamic_index_in_dim)/dynamic_slice | solution.py:71
  47.0 0.1 copy.15
  47.2 1.0 %collective-permute-done.2 = f32[2,2,2,128,128]{4,3,2,1,0:T(8,128)S(1)} collective-permute-done((f32[2,2,2,128,128]{4,3,2,1,0:T(8,128)S(1)}, f32[2,2,2,128,128]{4,3,2,1,0:T(8,128)S(1)}, u32[]{:S(2)}, u32[]{:S(2)}) %collective-permute-start.2) | collective-permute-done | bytes 524320 | tf_op jit(solution)/shard_map/ppermute | solution.py:31
  48.3 1.0 %collective-permute-start.3 = (f32[2,2,128,128]{3,2,1,0:T(8,128)S(1)}, f32[2,2,128,128]{3,2,1,0:T(8,128)S(1)}, u32[]{:S(2)}, u32[]{:S(2)}) collective-permute-start(f32[2,2,128,128]{3,2,1,0:T(8,128)S(1)} %dynamic-slice_bitcast_fusion.2), channel_id=1, source_target_pairs={{0,4},{1,5},{2,6},{3,7},{4,0},{5,1},{6,2},{7,3},{8,12},{9,13},{10,... | collective-permute-start | bytes 786440 | tf_op jit(solution)/shard_map/ppermute | solution.py:31
  49.3 0.1 copy.14
  49.4 5.3 %collective-permute-done.3 = f32[2,2,128,128]{3,2,1,0:T(8,128)S(1)} collective-permute-done((f32[2,2,128,128]{3,2,1,0:T(8,128)S(1)}, f32[2,2,128,128]{3,2,1,0:T(8,128)S(1)}, u32[]{:S(2)}, u32[]{:S(2)}) %collective-permute-start.3) | collective-permute-done | bytes 262176 | tf_op jit(solution)/shard_map/ppermute | solution.py:31
  54.8 2.0 %collective-permute-start.4 = (f32[2,128,128]{2,1,0:T(8,128)S(1)}, f32[2,128,128]{2,1,0:T(8,128)S(1)}, u32[]{:S(2)}, u32[]{:S(2)}) collective-permute-start(f32[2,128,128]{2,1,0:T(8,128)S(1)} %dynamic-slice_bitcast_fusion.3), channel_id=1, source_target_pairs={{0,8},{1,9},{2,10},{3,11},{4,12},{5,13},{6,14},{7,15},{8,0},{9,1},... | collective-permute-start | bytes 393224 | tf_op jit(solution)/shard_map/ppermute | solution.py:31
  56.8 0.2 fusion.2
  57.0 5.4 %collective-permute-done.4 = f32[2,128,128]{2,1,0:T(8,128)S(1)} collective-permute-done((f32[2,128,128]{2,1,0:T(8,128)S(1)}, f32[2,128,128]{2,1,0:T(8,128)S(1)}, u32[]{:S(2)}, u32[]{:S(2)}) %collective-permute-start.4) | collective-permute-done | bytes 131104 | tf_op jit(solution)/shard_map/ppermute | solution.py:31
  62.4 0.9 %fusion = bf16[256,256]{1,0:T(8,128)(2,1)} fusion(f32[256,256]{1,0:T(8,128)S(1)} %fusion.2, f32[256,128]{1,0:T(8,128)S(1)} %bitcast.97, bf16[128,256]{1,0:T(8,128)(2,1)S(1)} %copy-done.2), kind=kOutput, calls=%fused_computation.1 | convolution fusion | flops 100794368 | bytes 589824 | tf_op jit(solution)/shard_map/dot_general | solution.py:259
  (27 shorter events, 0.5 us)
Async XLA Ops:
  0.0 56.8 %copy-start = (bf16[128,256]{1,0:T(8,128)(2,1)S(1)}, bf16[128,256]{1,0:T(8,128)(2,1)}, u32[]{:S(2)}) copy-start(bf16[128,256]{1,0:T(8,128)(2,1)} %param.13) | copy-start | bytes 196612
  0.0 11.5 %collective-permute-start = (bf16[1,256,128]{2,1,0:T(8,128)(2,1)}, bf16[1,256,128]{2,1,0:T(8,128)(2,1)S(1)}, u32[]{:S(2)}, u32[]{:S(2)}) collective-permute-start(bf16[1,256,128]{2,1,0:T(8,128)(2,1)} %bitcast.98), channel_id=1, source_target_pairs={{0,16},{16,0},{1,17},{17,1},{2,18},{18,2},{3,19},{19,3},{4,20},{20... | collective-permute-start | bytes 196616 | tf_op jit(solution)/shard_map/ppermute | solution.py:36
  0.5 8.0 %collective-permute-start.5 = (bf16[1,2,128,128]{2,3,1,0:T(8,128)(2,1)}, bf16[1,2,128,128]{2,3,1,0:T(8,128)(2,1)S(1)}, u32[]{:S(2)}, u32[]{:S(2)}) collective-permute-start(bf16[1,2,128,128]{2,3,1,0:T(8,128)(2,1)} %bitcast.99), channel_id=1, source_target_pairs={{0,8},{1,9},{2,10},{3,11},{4,12},{5,13},{6,14},{7,15},{8,0},{9,1},... | collective-permute-start | bytes 196616 | tf_op jit(solution)/shard_map/ppermute | solution.py:31
  9.9 11.1 %collective-permute-start.6 = (bf16[2,2,128,128]{2,3,1,0:T(8,128)(2,1)}, bf16[2,2,128,128]{2,3,1,0:T(8,128)(2,1)S(1)}, u32[]{:S(2)}, u32[]{:S(2)}) collective-permute-start(bf16[2,2,128,128]{2,3,1,0:T(8,128)(2,1)} %maximum_bitcast_fusion), channel_id=1, source_target_pairs={{0,1},{1,0},{2,3},{3,2},{4,5},{5,4},{6,7},{7,6},{8,9},{9,8},{10,11... | collective-permute-start | bytes 393224 | tf_op jit(solution)/shard_map/ppermute | solution.py:31
  19.1 2.8 %copy-start.3 = (s32[1,1,128]{2,1,0:T(1,128)S(1)}, s32[1,1,128]{2,1,0:T(1,128)}, u32[]{:S(2)}) copy-start(s32[1,1,128]{2,1,0:T(1,128)} %param.9) | copy-start | bytes 1540
  20.5 9.2 %copy-start.4 = (s32[1,1,128]{2,1,0:T(1,128)S(1)}, s32[1,1,128]{2,1,0:T(1,128)}, u32[]{:S(2)}) copy-start(s32[1,1,128]{2,1,0:T(1,128)} %param.10) | copy-start | bytes 1540
  20.5 17.1 %copy-start.1 = (f32[32,128,128]{2,1,0:T(8,128)S(1)}, f32[32,128,128]{2,1,0:T(8,128)}, u32[]{:S(2)}) copy-start(f32[32,128,128]{2,1,0:T(8,128)} %shard_map.73) | copy-start | bytes 6291460
  20.5 17.0 %collective-permute-start.1 = (f32[2,2,2,2,128,128]{5,4,3,2,1,0:T(8,128)S(1)}, f32[2,2,2,2,128,128]{5,4,3,2,1,0:T(8,128)}, u32[]{:S(2)}, u32[]{:S(2)}) collective-permute-start(f32[2,2,2,2,128,128]{5,4,3,2,1,0:T(8,128)S(1)} %dynamic-slice_bitcast_fusion), channel_id=1, source_target_pairs={{0,1},{1,0},{2,3},{3,2},{4,5},{5,4},{6,7},{7,6},{8,9},{9,8},{10,11... | collective-permute-start | bytes 3145736 | tf_op jit(solution)/shard_map/ppermute | solution.py:31
  22.0 6.6 %collective-permute-start.7 = (bf16[4,2,128,128]{3,2,1,0:T(8,128)(2,1)}, bf16[4,2,128,128]{3,2,1,0:T(8,128)(2,1)S(1)}, u32[]{:S(2)}, u32[]{:S(2)}) collective-permute-start(bf16[4,2,128,128]{3,2,1,0:T(8,128)(2,1)} %copy.12), channel_id=1, source_target_pairs={{0,2},{1,3},{2,0},{3,1},{4,6},{5,7},{6,4},{7,5},{8,10},{9,11},{10,... | collective-permute-start | bytes 786440 | tf_op jit(solution)/shard_map/ppermute | solution.py:31
  29.6 9.5 %collective-permute-start.8 = (bf16[8,2,128,128]{3,2,1,0:T(8,128)(2,1)S(1)}, bf16[8,2,128,128]{3,2,1,0:T(8,128)(2,1)S(1)}, u32[]{:S(2)}, u32[]{:S(2)}) collective-permute-start(bf16[8,2,128,128]{3,2,1,0:T(8,128)(2,1)S(1)} %bitcast.92), channel_id=1, source_target_pairs={{0,4},{1,5},{2,6},{3,7},{4,0},{5,1},{6,2},{7,3},{8,12},{9,13},{10,... | collective-permute-start | bytes 1572872 | tf_op jit(solution)/shard_map/ppermute | solution.py:31
  38.9 9.2 %collective-permute-start.2 = (f32[2,2,2,128,128]{4,3,2,1,0:T(8,128)S(1)}, f32[2,2,2,128,128]{4,3,2,1,0:T(8,128)S(1)}, u32[]{:S(2)}, u32[]{:S(2)}) collective-permute-start(f32[2,2,2,128,128]{4,3,2,1,0:T(8,128)S(1)} %dynamic-slice_bitcast_fusion.1), channel_id=1, source_target_pairs={{0,2},{1,3},{2,0},{3,1},{4,6},{5,7},{6,4},{7,5},{8,10},{9,11},{10,... | collective-permute-start | bytes 1572872 | tf_op jit(solution)/shard_map/ppermute | solution.py:31
  47.1 15.3 %copy-start.2 = (bf16[128,256]{1,0:T(8,128)(2,1)S(1)}, bf16[128,256]{1,0:T(8,128)(2,1)}, u32[]{:S(2)}) copy-start(bf16[128,256]{1,0:T(8,128)(2,1)} %param.12) | copy-start | bytes 196612
  47.1 2.3 %collective-permute-start.9 = (f32[2,128,128]{1,2,0:T(8,128)S(1)}, f32[2,128,128]{1,2,0:T(8,128)S(1)}, u32[]{:S(2)}, u32[]{:S(2)}) collective-permute-start(f32[2,128,128]{1,2,0:T(8,128)S(1)} %bitcast.102), channel_id=1, source_target_pairs={{0,16},{16,0},{1,17},{17,1},{2,18},{18,2},{3,19},{19,3},{4,20},{20... | collective-permute-start | bytes 393224 | tf_op jit(solution)/shard_map/ppermute | solution.py:36
  48.3 6.4 %collective-permute-start.3 = (f32[2,2,128,128]{3,2,1,0:T(8,128)S(1)}, f32[2,2,128,128]{3,2,1,0:T(8,128)S(1)}, u32[]{:S(2)}, u32[]{:S(2)}) collective-permute-start(f32[2,2,128,128]{3,2,1,0:T(8,128)S(1)} %dynamic-slice_bitcast_fusion.2), channel_id=1, source_target_pairs={{0,4},{1,5},{2,6},{3,7},{4,0},{5,1},{6,2},{7,3},{8,12},{9,13},{10,... | collective-permute-start | bytes 786440 | tf_op jit(solution)/shard_map/ppermute | solution.py:31
  54.8 7.7 %collective-permute-start.4 = (f32[2,128,128]{2,1,0:T(8,128)S(1)}, f32[2,128,128]{2,1,0:T(8,128)S(1)}, u32[]{:S(2)}, u32[]{:S(2)}) collective-permute-start(f32[2,128,128]{2,1,0:T(8,128)S(1)} %dynamic-slice_bitcast_fusion.3), channel_id=1, source_target_pairs={{0,8},{1,9},{2,10},{3,11},{4,12},{5,13},{6,14},{7,15},{8,0},{9,1},... | collective-permute-start | bytes 393224 | tf_op jit(solution)/shard_map/ppermute | solution.py:31

commit v18 on v17

--- a/solution.py
+++ b/solution.py
@@ -98,9 +98,12 @@
     me = lax.axis_index("col")
     parity = lax.axis_index("row") % 2
     for t in range(nb):
-        mine = (me >> _pick(parity, order, t)) & 1
-        keep = lax.dynamic_index_in_dim(data, mine, axis=0, keepdims=False)
-        other = lax.dynamic_index_in_dim(data, 1 - mine, axis=0, keepdims=False)
+        if t == 0:
+            keep, other = data[1], data[0]
+        else:
+            mine = (me >> _pick(parity, order, t)) & 1
+            keep = lax.dynamic_index_in_dim(data, mine, axis=0, keepdims=False)
+            other = lax.dynamic_index_in_dim(data, 1 - mine, axis=0, keepdims=False)
         data = keep + _swap_col(other, row_size, col_size, (order[0][t], order[1][t]))
     return data
 
@@ -218,7 +221,10 @@
         rs_pos = jnp.zeros_like(dest)
         ag_pos = jnp.zeros_like(dest)
         for t in range(nb):
-            rs_pos = rs_pos + (((dest >> _pick(parity, rs_order, t)) & 1) << (nb - 1 - t))
+            bit = (dest >> _pick(parity, rs_order, t)) & 1
+            if t == 0:
+                bit = 1 - (bit ^ ((lax.axis_index("col") >> _pick(parity, rs_order, 0)) & 1))
+            rs_pos = rs_pos + (bit << (nb - 1 - t))
             ag_pos = ag_pos + (((dest >> _pick(parity, ag_order, t)) & 1) << t)
         rows_fwd = rs_pos * nbc + sub
         rows_bwd = ag_pos * nbc + sub

time: 64.6 us -> 65.7 us (1.017); the launches traced: 63.4 us -> 65.8 us
  starting transfers between devices: 9.52 us -> 15.5 us
  Pallas kernels: 11.9 us -> 8.47 us
  other arithmetic: 9.08 us -> 6.33 us
  waiting for transfers between devices: 27.4 us -> 29.4 us
  local copies, waits for them, and re-layouts: 3.44 us -> 4.17 us
    ppermute x8, starting transfers between devices: 9 us -> 14 us  [_swap_col(): return lax.ppermute(x, ('row', 'col'), perm)]
    slice x0 -> x1, local copies, waits for them, and re-layouts: none -> 2.71 us  [scatter_sum_col(): keep, other = (data[1], data[0])]
    ppermute x8, waiting for transfers between devices: 27.4 us -> 29.3 us  [_swap_col(): return lax.ppermute(x, ('row', 'col'), perm)]
    pallas_call x1, Pallas kernels: 5.74 us -> 4.02 us  [against_call(): pl.pallas_call(kernel, grid_spec=spec, out_shape=jax.ShapeDtypeStruct((nc...]
    pallas_call x1, Pallas kernels: 6.15 us -> 4.44 us  [along_call(): pl.pallas_call(kernel, grid_spec=spec, out_shape=jax.ShapeDtypeStruct((nr...]
    squeeze x4 -> x3, local copies, waits for them, and re-layouts: 1.4 us -> 0.09 us  [scatter_sum_col(): other = lax.dynamic_index_in_dim(data, 1 - mine, axis=0, keepdims=False)]
    add x4, other arithmetic: 1.44 us -> 0.23 us  [scatter_sum_col(): keep + _swap_col(other, row_size, col_size, (order[0][t], order[1][t]))]
    ppermute x2, starting transfers between devices: 0.52 us -> 1.57 us  [_swap(): return lax.ppermute(x, axis, perm)]
  transfers between devices with their start and end apart: 10 -> 10, of which waited for: 6 -> 7; matrix products, arithmetic and copies ran while one was open for 20% -> 16% of each run, Pallas kernels for 19% -> 13%
where the time goes in v18:
time: 65.7 us; the launch traced here: 65.8 us
  waiting for transfers between devices  29.4 us (45%)
  starting transfers between devices  15.5 us (24%)
  Pallas kernels  8.47 us (13%)
  other arithmetic  6.33 us (10%)
  local copies, waits for them, and re-layouts  4.17 us (6%)
  matrix products  1.16 us (2%)
  between operations  0.81 us (1%)
    ppermute x8, waiting for transfers between devices, _swap_col(): return lax.ppermute(x, ('row', 'col'), perm)  29.3 us
    ppermute x8, starting transfers between devices, _swap_col(): return lax.ppermute(x, ('row', 'col'), perm)  14 us
    pallas_call x1, Pallas kernels, along_call(): pl.pallas_call(kernel, grid_spec=spec, out_shape=jax.ShapeDtypeStruct((nr...  4.44 us
    pallas_call x1, Pallas kernels, against_call(): pl.pallas_call(kernel, grid_spec=spec, out_shape=jax.ShapeDtypeStruct((nc...  4.02 us
    slice x1, local copies, waits for them, and re-layouts, scatter_sum_col(): keep, other = (data[1], data[0])  2.71 us
    another operation x7, other arithmetic, gather_col(): have = jnp.stack([lo, hi], axis=0).reshape((-1,) + have.shape[1:])  2.18 us
    ppermute x2, starting transfers between devices, _swap(): return lax.ppermute(x, axis, perm)  1.57 us
    concatenate x1, other arithmetic, local(): have = jnp.concatenate([have, _swap(have, 'row', row_size, bit)], axis=0)  1.51 us
  transfers between devices with their start and end apart: 10, of which 7 were waited for; matrix products, arithmetic and copies ran while one was open for 16% of the time, Pallas kernels for 13%

profile of v18, /device:TPU:0, one launch (start us, length us, event | category | flops | bytes accessed | tf_op | source)
XLA Modules:
  0.0 65.8 jit_solution(8615307870893648541)
XLA Ops:
  0.0 4.0 %collective-permute-start.5 = (bf16[1,2,128,128]{2,3,1,0:T(8,128)(2,1)}, bf16[1,2,128,128]{2,3,1,0:T(8,128)(2,1)S(1)}, u32[]{:S(2)}, u32[]{:S(2)}) collective-permute-start(bf16[1,2,128,128]{2,3,1,0:T(8,128)(2,1)} %bitcast.94), channel_id=1, source_target_pairs={{0,8},{1,9},{2,10},{3,11},{4,12},{5,13},{6,14},{7,15},{8,0},{9,1},... | collective-permute-start | bytes 196616 | tf_op jit(solution)/shard_map/ppermute | solution.py:31
  4.0 3.9 %collective-permute-done.5 = bf16[1,2,128,128]{2,3,1,0:T(8,128)(2,1)S(1)} collective-permute-done((bf16[1,2,128,128]{2,3,1,0:T(8,128)(2,1)}, bf16[1,2,128,128]{2,3,1,0:T(8,128)(2,1)S(1)}, u32[]{:S(2)}, u32[]{:S(2)}) %collective-permute-start.5) | collective-permute-done | bytes 65568 | tf_op jit(solution)/shard_map/ppermute | solution.py:31
  7.9 0.9 %select_bitcast_fusion.7 = (bf16[1,1,2,128,128]{3,4,2,1,0:T(8,128)(2,1)S(1)}, bf16[1,1,2,128,128]{3,4,2,1,0:T(8,128)(2,1)S(1)}) fusion(bf16[1,2,128,128]{2,3,1,0:T(8,128)(2,1)} %bitcast.96, bf16[1,2,128,128]{2,3,1,0:T(8,128)(2,1)S(1)} %collective-permute-done.5, pred[]{:T(512)S(6)} %eq.21), kind=kLoop, calls=%fused_computation.21 | loop fusion | flops 65536 | bytes 262145 | tf_op jit(solution)/shard_map/stack | solution.py:90
  8.8 1.8 %collective-permute-start.6 = (bf16[2,2,128,128]{2,3,1,0:T(8,128)(2,1)S(1)}, bf16[2,2,128,128]{2,3,1,0:T(8,128)(2,1)S(1)}, u32[]{:S(2)}, u32[]{:S(2)}) collective-permute-start(bf16[2,2,128,128]{2,3,1,0:T(8,128)(2,1)S(1)} %maximum_bitcast_fusion), channel_id=1, source_target_pairs={{0,1},{1,0},{2,3},{3,2},{4,5},{5,4},{6,7},{7,6},{8,9},{9,8},{10,11... | collective-permute-start | bytes 393224 | tf_op jit(solution)/shard_map/ppermute | solution.py:31
  10.5 1.3 %multiply_add_fusion.1 = (s32[128]{0:T(128)}, s32[128]{0:T(128)S(1)}, s32[128]{0:T(128)}) fusion(s32[]{:T(128)S(6)} %and.68, s32[]{:T(128)S(6)} %select_n.129, s32[]{:T(128)S(6)} %select_n.131, s32[]{:T(128)S(6)} %select_n.130, s32[1,1,128]{2,1,0:T(1,128)} %param.9, s32[]{:T(128)S(6)} %axis_index.15, s32[1,1,128]{2,1,0:T(1,128)} %param.10), kind=kLoop, calls=%fused_computation.38 | loop fusion | flops 8320 | bytes 2580 | tf_op jit(solution)/shard_map/add | solution.py:229
  12.5 1.5 %pad_maximum_fusion.3 = bf16[2,256,128]{2,1,0:T(8,128)(2,1)} fusion(bf16[1,256,128]{2,1,0:T(8,128)(2,1)S(1)} %collective-permute-done, bf16[1,256,128]{2,1,0:T(8,128)(2,1)} %bitcast.97), kind=kLoop, calls=%fused_computation.13 | loop fusion | flops 65536 | bytes 262144 | tf_op jit(solution)/shard_map/concatenate | solution.py:242
  14.0 4.4 %shard_map.73 = f32[32,128,128]{2,1,0:T(8,128)} custom-call(s32[128]{0:T(128)} %get-tuple-element.5.rows_ref, s32[128]{0:T(128)} %get-tuple-element.19.cols_ref, s32[1]{0:T(128)} %bitcast.2.cnt_ref, bf16[128,128,128]{2,1,0:T(8,128)(2,1)} %bitcast.84, bf16[4,128,128]{2,1,0:T(8,128)(2,1)} %bitcast.92), custom_call_target="tpu_custom_call" | custom-call | tf_op jit(solution)/shard_map/pallas_call | solution.py:150
  18.5 0.2 copy.12
  18.7 1.1 %collective-permute-start.7 = (bf16[4,2,128,128]{3,2,1,0:T(8,128)(2,1)S(1)}, bf16[4,2,128,128]{3,2,1,0:T(8,128)(2,1)S(1)}, u32[]{:S(2)}, u32[]{:S(2)}) collective-permute-start(bf16[4,2,128,128]{3,2,1,0:T(8,128)(2,1)S(1)} %copy.12), channel_id=1, source_target_pairs={{0,2},{1,3},{2,0},{3,1},{4,6},{5,7},{6,4},{7,5},{8,10},{9,11},{10,... | collective-permute-start | bytes 786440 | tf_op jit(solution)/shard_map/ppermute | solution.py:31
  19.8 2.7 %fusion.2 = (f32[16,128,128]{2,1,0:T(8,128)}, f32[16,128,128]{2,1,0:T(8,128)S(1)}) fusion(f32[32,128,128]{2,1,0:T(8,128)} %shard_map.73), kind=kLoop, calls=%fused_computation.43 | loop fusion | bytes 4194304 | tf_op jit(solution)/shard_map/slice | solution.py:102
  22.5 0.5 collective-permute-start.1
  23.0 2.1 %collective-permute-done.7 = bf16[4,2,128,128]{3,2,1,0:T(8,128)(2,1)S(1)} collective-permute-done((bf16[4,2,128,128]{3,2,1,0:T(8,128)(2,1)S(1)}, bf16[4,2,128,128]{3,2,1,0:T(8,128)(2,1)S(1)}, u32[]{:S(2)}, u32[]{:S(2)}) %collective-permute-start.7) | collective-permute-done | bytes 262176 | tf_op jit(solution)/shard_map/ppermute | solution.py:31
  25.2 0.6 collective-permute-start.8
  25.9 0.6 clamp_bitcast_fusion.cols_ref
  26.5 0.5 multiply_add_fusion.rows_ref
  27.0 10.5 %collective-permute-done.1 = f32[2,2,2,2,128,128]{5,4,3,2,1,0:T(8,128)S(1)} collective-permute-done((f32[2,2,2,2,128,128]{5,4,3,2,1,0:T(8,128)}, f32[2,2,2,2,128,128]{5,4,3,2,1,0:T(8,128)S(1)}, u32[]{:S(2)}, u32[]{:S(2)}) %collective-permute-start.1) | collective-permute-done | bytes 1048608 | tf_op jit(solution)/shard_map/ppermute | solution.py:31
  37.5 0.1 add.102
  37.7 1.0 %collective-permute-start.2 = (f32[2,2,2,128,128]{4,3,2,1,0:T(8,128)S(1)}, f32[2,2,2,128,128]{4,3,2,1,0:T(8,128)S(1)}, u32[]{:S(2)}, u32[]{:S(2)}) collective-permute-start(f32[2,2,2,128,128]{4,3,2,1,0:T(8,128)S(1)} %dynamic-slice_bitcast_fusion), channel_id=1, source_target_pairs={{0,2},{1,3},{2,0},{3,1},{4,6},{5,7},{6,4},{7,5},{8,10},{9,11},{10,... | collective-permute-start | bytes 1572872 | tf_op jit(solution)/shard_map/ppermute | solution.py:31
  38.7 1.4 %collective-permute-done.8 = bf16[8,2,128,128]{3,2,1,0:T(8,128)(2,1)S(1)} collective-permute-done((bf16[8,2,128,128]{3,2,1,0:T(8,128)(2,1)S(1)}, bf16[8,2,128,128]{3,2,1,0:T(8,128)(2,1)S(1)}, u32[]{:S(2)}, u32[]{:S(2)}) %collective-permute-start.8) | collective-permute-done | bytes 524320 | tf_op jit(solution)/shard_map/ppermute | solution.py:31
  40.1 0.1 select_bitcast_fusion.1
  40.2 1.1 %pad_maximum_fusion = bf16[2,8,2,128,128]{4,3,2,1,0:T(8,128)(2,1)} fusion(bf16[1,8,2,128,128]{4,3,2,1,0:T(8,128)(2,1)S(1)} %get-tuple-element.10, bf16[1,8,2,128,128]{4,3,2,1,0:T(8,128)(2,1)S(1)} %get-tuple-element.9), kind=kLoop, calls=%fused_computation.2 | loop fusion | flops 524288 | bytes 2097152 | tf_op jit(solution)/shard_map/stack | solution.py:90
  41.3 4.0 %shard_map.74 = f32[4,128,128]{2,1,0:T(8,128)} custom-call(s32[128]{0:T(128)} %multiply_add_fusion.rows_ref, s32[128]{0:T(128)} %clamp_bitcast_fusion.cols_ref, s32[1]{0:T(128)} %bitcast.2.cnt_ref, bf16[128,128,128]{2,1,0:T(8,128)(2,1)} %bitcast.85, bf16[32,128,128]{2,1,0:T(8,128)(2,1)} %bitcast.86), custom_call_target="tpu_custom_call" | custom-call | tf_op jit(solution)/shard_map/pallas_call | solution.py:192
  45.4 1.0 %constant_dynamic-slice_fusion.1 = (f32[1,2,128,128]{3,2,1,0:T(8,128)S(1)}, f32[1,2,128,128]{3,2,1,0:T(8,128)S(1)}) fusion(f32[2,2,128,128]{3,2,1,0:T(8,128)} %bitcast.89, s32[]{:T(128)S(6)} %select_n.153, s32[]{:T(128)S(6)} %select_n.154), kind=kLoop, calls=%fused_computation.23 | loop fusion | bytes 524296 | tf_op jit(solution)/shard_map/jit(dynamic_index_in_dim)/dynamic_slice | solution.py:71
  46.3 0.1 copy.15
  46.5 1.6 %collective-permute-start.9 = (f32[2,128,128]{1,2,0:T(8,128)S(1)}, f32[2,128,128]{1,2,0:T(8,128)S(1)}, u32[]{:S(2)}, u32[]{:S(2)}) collective-permute-start(f32[2,128,128]{1,2,0:T(8,128)S(1)} %bitcast.98), channel_id=1, source_target_pairs={{0,16},{16,0},{1,17},{17,1},{2,18},{18,2},{3,19},{19,3},{4,20},{20... | collective-permute-start | bytes 393224 | tf_op jit(solution)/shard_map/ppermute | solution.py:36
  48.1 0.7 %collective-permute-start.3 = (f32[2,2,128,128]{3,2,1,0:T(8,128)S(1)}, f32[2,2,128,128]{3,2,1,0:T(8,128)S(1)}, u32[]{:S(2)}, u32[]{:S(2)}) collective-permute-start(f32[2,2,128,128]{3,2,1,0:T(8,128)S(1)} %dynamic-slice_bitcast_fusion.1), channel_id=1, source_target_pairs={{0,4},{1,5},{2,6},{3,7},{4,0},{5,1},{6,2},{7,3},{8,12},{9,13},{10,... | collective-permute-start | bytes 786440 | tf_op jit(solution)/shard_map/ppermute | solution.py:31
  48.9 0.1 copy.14
  49.0 5.5 %collective-permute-done.3 = f32[2,2,128,128]{3,2,1,0:T(8,128)S(1)} collective-permute-done((f32[2,2,128,128]{3,2,1,0:T(8,128)S(1)}, f32[2,2,128,128]{3,2,1,0:T(8,128)S(1)}, u32[]{:S(2)}, u32[]{:S(2)}) %collective-permute-start.3) | collective-permute-done | bytes 262176 | tf_op jit(solution)/shard_map/ppermute | solution.py:31
  54.6 4.1 %collective-permute-start.4 = (f32[2,128,128]{2,1,0:T(8,128)S(1)}, f32[2,128,128]{2,1,0:T(8,128)S(1)}, u32[]{:S(2)}, u32[]{:S(2)}) collective-permute-start(f32[2,128,128]{2,1,0:T(8,128)S(1)} %dynamic-slice_bitcast_fusion.2), channel_id=1, source_target_pairs={{0,8},{1,9},{2,10},{3,11},{4,12},{5,13},{6,14},{7,15},{8,0},{9,1},... | collective-permute-start | bytes 393224 | tf_op jit(solution)/shard_map/ppermute | solution.py:31
  58.7 0.2 fusion.3
  59.0 5.9 %collective-permute-done.4 = f32[2,128,128]{2,1,0:T(8,128)S(1)} collective-permute-done((f32[2,128,128]{2,1,0:T(8,128)S(1)}, f32[2,128,128]{2,1,0:T(8,128)S(1)}, u32[]{:S(2)}, u32[]{:S(2)}) %collective-permute-start.4) | collective-permute-done | bytes 131104 | tf_op jit(solution)/shard_map/ppermute | solution.py:31
  64.9 0.9 %fusion = bf16[256,256]{1,0:T(8,128)(2,1)} fusion(f32[256,256]{1,0:T(8,128)S(1)} %fusion.3, f32[256,128]{1,0:T(8,128)S(1)} %bitcast.93, bf16[128,256]{1,0:T(8,128)(2,1)S(1)} %copy-done.1), kind=kOutput, calls=%fused_computation.1 | convolution fusion | flops 100794368 | bytes 589824 | tf_op jit(solution)/shard_map/dot_general | solution.py:265
  (25 shorter events, 0.5 us)
Async XLA Ops:
  0.0 58.7 %copy-start = (bf16[128,256]{1,0:T(8,128)(2,1)S(1)}, bf16[128,256]{1,0:T(8,128)(2,1)}, u32[]{:S(2)}) copy-start(bf16[128,256]{1,0:T(8,128)(2,1)} %param.13) | copy-start | bytes 196612
  0.0 7.9 %collective-permute-start.5 = (bf16[1,2,128,128]{2,3,1,0:T(8,128)(2,1)}, bf16[1,2,128,128]{2,3,1,0:T(8,128)(2,1)S(1)}, u32[]{:S(2)}, u32[]{:S(2)}) collective-permute-start(bf16[1,2,128,128]{2,3,1,0:T(8,128)(2,1)} %bitcast.94), channel_id=1, source_target_pairs={{0,8},{1,9},{2,10},{3,11},{4,12},{5,13},{6,14},{7,15},{8,0},{9,1},... | collective-permute-start | bytes 196616 | tf_op jit(solution)/shard_map/ppermute | solution.py:31
  4.0 8.4 %collective-permute-start = (bf16[1,256,128]{2,1,0:T(8,128)(2,1)}, bf16[1,256,128]{2,1,0:T(8,128)(2,1)S(1)}, u32[]{:S(2)}, u32[]{:S(2)}) collective-permute-start(bf16[1,256,128]{2,1,0:T(8,128)(2,1)} %bitcast.95), channel_id=1, source_target_pairs={{0,16},{16,0},{1,17},{17,1},{2,18},{18,2},{3,19},{19,3},{4,20},{20... | collective-permute-start | bytes 196616 | tf_op jit(solution)/shard_map/ppermute | solution.py:36
  8.8 9.7 %collective-permute-start.6 = (bf16[2,2,128,128]{2,3,1,0:T(8,128)(2,1)S(1)}, bf16[2,2,128,128]{2,3,1,0:T(8,128)(2,1)S(1)}, u32[]{:S(2)}, u32[]{:S(2)}) collective-permute-start(bf16[2,2,128,128]{2,3,1,0:T(8,128)(2,1)S(1)} %maximum_bitcast_fusion), channel_id=1, source_target_pairs={{0,1},{1,0},{2,3},{3,2},{4,5},{5,4},{6,7},{7,6},{8,9},{9,8},{10,11... | collective-permute-start | bytes 393224 | tf_op jit(solution)/shard_map/ppermute | solution.py:31
  18.7 6.4 %collective-permute-start.7 = (bf16[4,2,128,128]{3,2,1,0:T(8,128)(2,1)S(1)}, bf16[4,2,128,128]{3,2,1,0:T(8,128)(2,1)S(1)}, u32[]{:S(2)}, u32[]{:S(2)}) collective-permute-start(bf16[4,2,128,128]{3,2,1,0:T(8,128)(2,1)S(1)} %copy.12), channel_id=1, source_target_pairs={{0,2},{1,3},{2,0},{3,1},{4,6},{5,7},{6,4},{7,5},{8,10},{9,11},{10,... | collective-permute-start | bytes 786440 | tf_op jit(solution)/shard_map/ppermute | solution.py:31
  22.5 3.4 %copy-start.3 = (s32[1,1,128]{2,1,0:T(1,128)S(1)}, s32[1,1,128]{2,1,0:T(1,128)}, u32[]{:S(2)}) copy-start(s32[1,1,128]{2,1,0:T(1,128)} %param.10) | copy-start | bytes 1540
  22.5 4.0 %copy-start.2 = (s32[1,1,128]{2,1,0:T(1,128)S(1)}, s32[1,1,128]{2,1,0:T(1,128)}, u32[]{:S(2)}) copy-start(s32[1,1,128]{2,1,0:T(1,128)} %param.9) | copy-start | bytes 1540
  22.5 15.0 %collective-permute-start.1 = (f32[2,2,2,2,128,128]{5,4,3,2,1,0:T(8,128)}, f32[2,2,2,2,128,128]{5,4,3,2,1,0:T(8,128)S(1)}, u32[]{:S(2)}, u32[]{:S(2)}) collective-permute-start(f32[2,2,2,2,128,128]{5,4,3,2,1,0:T(8,128)} %bitcast.7), channel_id=1, source_target_pairs={{0,1},{1,0},{2,3},{3,2},{4,5},{5,4},{6,7},{7,6},{8,9},{9,8},{10,11... | collective-permute-start | bytes 3145736 | tf_op jit(solution)/shard_map/ppermute | solution.py:31
  25.2 14.9 %collective-permute-start.8 = (bf16[8,2,128,128]{3,2,1,0:T(8,128)(2,1)S(1)}, bf16[8,2,128,128]{3,2,1,0:T(8,128)(2,1)S(1)}, u32[]{:S(2)}, u32[]{:S(2)}) collective-permute-start(bf16[8,2,128,128]{3,2,1,0:T(8,128)(2,1)S(1)} %bitcast.88), channel_id=1, source_target_pairs={{0,4},{1,5},{2,6},{3,7},{4,0},{5,1},{6,2},{7,3},{8,12},{9,13},{10,... | collective-permute-start | bytes 1572872 | tf_op jit(solution)/shard_map/ppermute | solution.py:31
  37.7 10.3 %collective-permute-start.2 = (f32[2,2,2,128,128]{4,3,2,1,0:T(8,128)S(1)}, f32[2,2,2,128,128]{4,3,2,1,0:T(8,128)S(1)}, u32[]{:S(2)}, u32[]{:S(2)}) collective-permute-start(f32[2,2,2,128,128]{4,3,2,1,0:T(8,128)S(1)} %dynamic-slice_bitcast_fusion), channel_id=1, source_target_pairs={{0,2},{1,3},{2,0},{3,1},{4,6},{5,7},{6,4},{7,5},{8,10},{9,11},{10,... | collective-permute-start | bytes 1572872 | tf_op jit(solution)/shard_map/ppermute | solution.py:31
  46.4 18.5 %copy-start.1 = (bf16[128,256]{1,0:T(8,128)(2,1)S(1)}, bf16[128,256]{1,0:T(8,128)(2,1)}, u32[]{:S(2)}) copy-start(bf16[128,256]{1,0:T(8,128)(2,1)} %param.12) | copy-start | bytes 196612
  46.5 2.6 %collective-permute-start.9 = (f32[2,128,128]{1,2,0:T(8,128)S(1)}, f32[2,128,128]{1,2,0:T(8,128)S(1)}, u32[]{:S(2)}, u32[]{:S(2)}) collective-permute-start(f32[2,128,128]{1,2,0:T(8,128)S(1)} %bitcast.98), channel_id=1, source_target_pairs={{0,16},{16,0},{1,17},{17,1},{2,18},{18,2},{3,19},{19,3},{4,20},{20... | collective-permute-start | bytes 393224 | tf_op jit(solution)/shard_map/ppermute | solution.py:36
  48.1 6.4 %collective-permute-start.3 = (f32[2,2,128,128]{3,2,1,0:T(8,128)S(1)}, f32[2,2,128,128]{3,2,1,0:T(8,128)S(1)}, u32[]{:S(2)}, u32[]{:S(2)}) collective-permute-start(f32[2,2,128,128]{3,2,1,0:T(8,128)S(1)} %dynamic-slice_bitcast_fusion.1), channel_id=1, source_target_pairs={{0,4},{1,5},{2,6},{3,7},{4,0},{5,1},{6,2},{7,3},{8,12},{9,13},{10,... | collective-permute-start | bytes 786440 | tf_op jit(solution)/shard_map/ppermute | solution.py:31
  54.6 10.3 %collective-permute-start.4 = (f32[2,128,128]{2,1,0:T(8,128)S(1)}, f32[2,128,128]{2,1,0:T(8,128)S(1)}, u32[]{:S(2)}, u32[]{:S(2)}) collective-permute-start(f32[2,128,128]{2,1,0:T(8,128)S(1)} %dynamic-slice_bitcast_fusion.2), channel_id=1, source_target_pairs={{0,8},{1,9},{2,10},{3,11},{4,12},{5,13},{6,14},{7,15},{8,0},{9,1},... | collective-permute-start | bytes 393224 | tf_op jit(solution)/shard_map/ppermute | solution.py:31

commit v19 on v14

--- a/solution.py
+++ b/solution.py
@@ -106,7 +106,7 @@
 
 
 def _chunk(slots):
-    return 64 if slots % 64 == 0 else slots
+    return 16 if slots % 16 == 0 else slots
 
 
 def along_call(rows, cols, cnt, values, group, nrb):

time: 63.3 us -> 68.1 us (1.076)
  starting transfers between devices: 13.2 us -> 23.1 us
  waiting for transfers between devices: 25.3 us -> 20.8 us
  Pallas kernels: 8.74 us -> 7.74 us
    ppermute x8, starting transfers between devices: 12.7 us -> 21.3 us  [_swap_col(): return lax.ppermute(x, ('row', 'col'), perm)]
    ppermute x8, waiting for transfers between devices: 25.2 us -> 20.8 us  [_swap_col(): return lax.ppermute(x, ('row', 'col'), perm)]
    ppermute x2, starting transfers between devices: 0.52 us -> 1.77 us  [_swap(): return lax.ppermute(x, axis, perm)]
  transfers between devices with their start and end apart: 10 -> 10, of which waited for: 6 -> 6; matrix products, arithmetic and copies ran while one was open for 21% -> 20% of each run, Pallas kernels for 14% -> 12%
where the time goes in v19:
time: 68.1 us; the launch traced here: 66.7 us
  starting transfers between devices  23.1 us (34%)
  waiting for transfers between devices  20.8 us (31%)
  other arithmetic  9.73 us (14%)
  Pallas kernels  7.74 us (11%)
  local copies, waits for them, and re-layouts  3.43 us (5%)
  matrix products  1.16 us (2%)
  between operations  0.83 us (1%)
    ppermute x8, starting transfers between devices, _swap_col(): return lax.ppermute(x, ('row', 'col'), perm)  21.3 us
    ppermute x8, waiting for transfers between devices, _swap_col(): return lax.ppermute(x, ('row', 'col'), perm)  20.8 us
    pallas_call x1, Pallas kernels, along_call(): pl.pallas_call(kernel, grid_spec=spec, out_shape=jax.ShapeDtypeStruct((nr...  4.08 us
    pallas_call x1, Pallas kernels, against_call(): pl.pallas_call(kernel, grid_spec=spec, out_shape=jax.ShapeDtypeStruct((nc...  3.66 us
    another operation x7, other arithmetic, gather_col(): have = jnp.stack([lo, hi], axis=0).reshape((-1,) + have.shape[1:])  3.13 us
    ppermute x2, starting transfers between devices, _swap(): return lax.ppermute(x, axis, perm)  1.77 us
    another operation x2, other arithmetic, gather_row(): have = jnp.stack([lo, hi], axis=0).reshape((-1,) + have.shape[1:])  1.51 us
    add x4, other arithmetic, scatter_sum_col(): keep + _swap_col(other, row_size, col_size, (order[0][t], order[1][t]))  1.44 us
  transfers between devices with their start and end apart: 10, of which 6 were waited for; matrix products, arithmetic and copies ran while one was open for 20% of the time, Pallas kernels for 12%

profile of v19, /device:TPU:0, one launch (start us, length us, event | category | flops | bytes accessed | tf_op | source)
XLA Modules:
  0.0 66.7 jit_solution(10446335880994777616)
XLA Ops:
  0.0 0.5 collective-permute-start
  0.5 3.7 %collective-permute-start.5 = (bf16[1,2,128,128]{2,3,1,0:T(8,128)(2,1)}, bf16[1,2,128,128]{2,3,1,0:T(8,128)(2,1)S(1)}, u32[]{:S(2)}, u32[]{:S(2)}) collective-permute-start(bf16[1,2,128,128]{2,3,1,0:T(8,128)(2,1)} %bitcast.103), channel_id=1, source_target_pairs={{0,8},{1,9},{2,10},{3,11},{4,12},{5,13},{6,14},{7,15},{8,0},{9,1},... | collective-permute-start | bytes 196616 | tf_op jit(solution)/shard_map/ppermute | solution.py:31
  4.1 1.2 %multiply_add_fusion.1 = (s32[128]{0:T(128)}, s32[128]{0:T(128)S(1)}) fusion(s32[]{:T(128)S(6)} %select_n.141, s32[]{:T(128)S(6)} %select_n.143, s32[]{:T(128)S(6)} %select_n.142, s32[1,1,128]{2,1,0:T(1,128)} %param.9), kind=kLoop, calls=%fused_computation.36 | loop fusion | flops 4736 | bytes 1548 | tf_op jit(solution)/shard_map/add | solution.py:223
  5.3 1.2 %clamp_bitcast_fusion.cols_ref = s32[128]{0:T(128)} fusion(s32[1,1,128]{2,1,0:T(1,128)} %param.10), kind=kLoop, calls=%fused_computation.35 | loop fusion | flops 128 | bytes 1024 | tf_op jit(solution)/shard_map/jit(clip)/min | solution.py:210
  7.2 1.2 %collective-permute-done.5 = bf16[1,2,128,128]{2,3,1,0:T(8,128)(2,1)S(1)} collective-permute-done((bf16[1,2,128,128]{2,3,1,0:T(8,128)(2,1)}, bf16[1,2,128,128]{2,3,1,0:T(8,128)(2,1)S(1)}, u32[]{:S(2)}, u32[]{:S(2)}) %collective-permute-start.5) | collective-permute-done | bytes 65568 | tf_op jit(solution)/shard_map/ppermute | solution.py:31
  8.4 0.9 %select_bitcast_fusion.7 = (bf16[1,1,2,128,128]{3,4,2,1,0:T(8,128)(2,1)S(1)}, bf16[1,1,2,128,128]{3,4,2,1,0:T(8,128)(2,1)S(1)}) fusion(bf16[1,2,128,128]{2,3,1,0:T(8,128)(2,1)} %bitcast.104, bf16[1,2,128,128]{2,3,1,0:T(8,128)(2,1)S(1)} %collective-permute-done.5, pred[]{:T(512)S(6)} %eq.23), kind=kLoop, calls=%fused_computation.23 | loop fusion | flops 65536 | bytes 262145 | tf_op jit(solution)/shard_map/stack | solution.py:90
  9.3 0.7 %maximum_bitcast_fusion = bf16[2,2,128,128]{2,3,1,0:T(8,128)(2,1)} fusion(bf16[1,1,2,128,128]{3,4,2,1,0:T(8,128)(2,1)S(1)} %get-tuple-element.18, bf16[1,1,2,128,128]{3,4,2,1,0:T(8,128)(2,1)S(1)} %get-tuple-element.17), kind=kLoop, calls=%fused_computation.16 | loop fusion | flops 65536 | bytes 262144 | tf_op jit(solution)/shard_map/reshape | solution.py:90
  9.9 1.5 %collective-permute-start.6 = (bf16[2,2,128,128]{2,3,1,0:T(8,128)(2,1)}, bf16[2,2,128,128]{2,3,1,0:T(8,128)(2,1)S(1)}, u32[]{:S(2)}, u32[]{:S(2)}) collective-permute-start(bf16[2,2,128,128]{2,3,1,0:T(8,128)(2,1)} %maximum_bitcast_fusion), channel_id=1, source_target_pairs={{0,1},{1,0},{2,3},{3,2},{4,5},{5,4},{6,7},{7,6},{8,9},{9,8},{10,11... | collective-permute-start | bytes 393224 | tf_op jit(solution)/shard_map/ppermute | solution.py:31
  11.5 0.9 %select_bitcast_fusion.9 = (bf16[1,1,256,128]{3,2,1,0:T(8,128)(2,1)S(1)}, bf16[1,1,256,128]{3,2,1,0:T(8,128)(2,1)S(1)}) fusion(bf16[1,256,128]{2,1,0:T(8,128)(2,1)S(1)} %collective-permute-done, pred[]{:T(512)S(6)} %eq.19, bf16[256,128]{1,0:T(8,128)(2,1)} %param.7), kind=kLoop, calls=%fused_computation.25 | loop fusion | flops 65536 | bytes 262145 | tf_op jit(solution)/shard_map/stack | solution.py:52
  12.3 0.7 pad_maximum_fusion.3
  13.0 4.1 %shard_map.73 = f32[32,128,128]{2,1,0:T(8,128)} custom-call(s32[128]{0:T(128)} %get-tuple-element.5.rows_ref, s32[128]{0:T(128)} %clamp_bitcast_fusion.cols_ref, s32[1]{0:T(128)} %bitcast.2.cnt_ref, bf16[128,128,128]{2,1,0:T(8,128)(2,1)} %bitcast.91, bf16[4,128,128]{2,1,0:T(8,128)(2,1)} %bitcast.100), custom_call_target="tpu_custom_call" | custom-call | tf_op jit(solution)/shard_map/pallas_call | solution.py:147
  17.1 1.3 %dynamic-slice_bitcast_fusion = f32[2,2,2,2,128,128]{5,4,3,2,1,0:T(8,128)S(1)} fusion(f32[2,2,2,2,2,128,128]{6,5,4,3,2,1,0:T(8,128)} %bitcast.93, s32[]{:T(128)S(6)} %select_n.149), kind=kLoop, calls=%fused_computation.4 | loop fusion | bytes 2097156 | tf_op jit(solution)/shard_map/jit(dynamic_index_in_dim)/squeeze | solution.py:103
  18.7 0.8 %copy.12 = bf16[4,2,128,128]{3,2,1,0:T(8,128)(2,1)} copy(bf16[4,2,128,128]{2,3,1,0:T(8,128)(2,1)S(1)} %bitcast.98) | data formatting | bytes 524288 | tf_op jit(solution)/shard_map/reshape | solution.py:90
  19.6 1.6 %collective-permute-start.7 = (bf16[4,2,128,128]{3,2,1,0:T(8,128)(2,1)}, bf16[4,2,128,128]{3,2,1,0:T(8,128)(2,1)S(1)}, u32[]{:S(2)}, u32[]{:S(2)}) collective-permute-start(bf16[4,2,128,128]{3,2,1,0:T(8,128)(2,1)} %copy.12), channel_id=1, source_target_pairs={{0,2},{1,3},{2,0},{3,1},{4,6},{5,7},{6,4},{7,5},{8,10},{9,11},{10,... | collective-permute-start | bytes 786440 | tf_op jit(solution)/shard_map/ppermute | solution.py:31
  21.1 5.0 %collective-permute-done.7 = bf16[4,2,128,128]{3,2,1,0:T(8,128)(2,1)S(1)} collective-permute-done((bf16[4,2,128,128]{3,2,1,0:T(8,128)(2,1)}, bf16[4,2,128,128]{3,2,1,0:T(8,128)(2,1)S(1)}, u32[]{:S(2)}, u32[]{:S(2)}) %collective-permute-start.7) | collective-permute-done | bytes 262176 | tf_op jit(solution)/shard_map/ppermute | solution.py:31
  26.2 1.0 %select_bitcast_fusion.3 = (bf16[1,4,2,128,128]{4,3,2,1,0:T(8,128)(2,1)S(1)}, bf16[1,4,2,128,128]{4,3,2,1,0:T(8,128)(2,1)S(1)}) fusion(bf16[4,2,128,128]{3,2,1,0:T(8,128)(2,1)} %copy.12, bf16[4,2,128,128]{3,2,1,0:T(8,128)(2,1)S(1)} %collective-permute-done.7, pred[]{:T(512)S(6)} %eq.21), kind=kLoop, calls=%fused_computation.13 | loop fusion | flops 262144 | bytes 1048577 | tf_op jit(solution)/shard_map/stack | solution.py:90
  27.2 4.3 %collective-permute-start.8 = (bf16[8,2,128,128]{3,2,1,0:T(8,128)(2,1)S(1)}, bf16[8,2,128,128]{3,2,1,0:T(8,128)(2,1)S(1)}, u32[]{:S(2)}, u32[]{:S(2)}) collective-permute-start(bf16[8,2,128,128]{3,2,1,0:T(8,128)(2,1)S(1)} %bitcast.96), channel_id=1, source_target_pairs={{0,4},{1,5},{2,6},{3,7},{4,0},{5,1},{6,2},{7,3},{8,12},{9,13},{10,... | collective-permute-start | bytes 1572872 | tf_op jit(solution)/shard_map/ppermute | solution.py:31
  31.5 0.5 multiply_add_fusion.rows_ref
  32.0 4.2 %collective-permute-done.1 = f32[2,2,2,2,128,128]{5,4,3,2,1,0:T(8,128)} collective-permute-done((f32[2,2,2,2,128,128]{5,4,3,2,1,0:T(8,128)S(1)}, f32[2,2,2,2,128,128]{5,4,3,2,1,0:T(8,128)}, u32[]{:S(2)}, u32[]{:S(2)}) %collective-permute-start.1) | collective-permute-done | bytes 1048608 | tf_op jit(solution)/shard_map/ppermute | solution.py:31
  36.2 1.3 %bitcast_add_fusion = f32[2,2,2,2,128,128]{5,4,3,2,1,0:T(8,128)S(1)} fusion(f32[2,2,2,2,128,128]{5,4,3,2,1,0:T(8,128)} %collective-permute-done.1, f32[2,2,2,2,2,128,128]{6,5,4,3,2,1,0:T(8,128)S(1)} %bitcast.94, s32[]{:T(128)S(6)} %select_n.148), kind=kLoop, calls=%fused_computation.3 | loop fusion | flops 262144 | bytes 3145732 | tf_op jit(solution)/shard_map/add | solution.py:104
  37.6 1.3 %collective-permute-start.2 = (f32[2,2,2,128,128]{4,3,2,1,0:T(8,128)S(1)}, f32[2,2,2,128,128]{4,3,2,1,0:T(8,128)S(1)}, u32[]{:S(2)}, u32[]{:S(2)}) collective-permute-start(f32[2,2,2,128,128]{4,3,2,1,0:T(8,128)S(1)} %dynamic-slice_bitcast_fusion.1), channel_id=1, source_target_pairs={{0,2},{1,3},{2,0},{3,1},{4,6},{5,7},{6,4},{7,5},{8,10},{9,11},{10,... | collective-permute-start | bytes 1572872 | tf_op jit(solution)/shard_map/ppermute | solution.py:31
  39.0 1.1 %pad_maximum_fusion = bf16[2,8,2,128,128]{4,3,2,1,0:T(8,128)(2,1)} fusion(bf16[1,8,2,128,128]{4,3,2,1,0:T(8,128)(2,1)S(1)} %get-tuple-element.8, bf16[1,8,2,128,128]{4,3,2,1,0:T(8,128)(2,1)S(1)} %get-tuple-element.7), kind=kLoop, calls=%fused_computation.2 | loop fusion | flops 524288 | bytes 2097152 | tf_op jit(solution)/shard_map/stack | solution.py:90
  40.1 3.7 %shard_map.74 = f32[4,128,128]{2,1,0:T(8,128)} custom-call(s32[128]{0:T(128)} %multiply_add_fusion.rows_ref, s32[128]{0:T(128)} %clamp_bitcast_fusion.cols_ref, s32[1]{0:T(128)} %bitcast.2.cnt_ref, bf16[128,128,128]{2,1,0:T(8,128)(2,1)} %bitcast.92, bf16[32,128,128]{2,1,0:T(8,128)(2,1)} %bitcast.95), custom_call_target="tpu_custom_call" | custom-call | tf_op jit(solution)/shard_map/pallas_call | solution.py:189
  43.7 1.0 %constant_dynamic-slice_fusion.1 = (f32[1,2,128,128]{3,2,1,0:T(8,128)S(1)}, f32[1,2,128,128]{3,2,1,0:T(8,128)S(1)}) fusion(f32[2,2,128,128]{3,2,1,0:T(8,128)} %bitcast.97, s32[]{:T(128)S(6)} %select_n.168, s32[]{:T(128)S(6)} %select_n.169), kind=kLoop, calls=%fused_computation.27 | loop fusion | bytes 524296 | tf_op jit(solution)/shard_map/jit(dynamic_index_in_dim)/dynamic_slice | solution.py:71
  44.8 1.3 %collective-permute-start.9 = (f32[2,128,128]{1,2,0:T(8,128)S(1)}, f32[2,128,128]{1,2,0:T(8,128)S(1)}, u32[]{:S(2)}, u32[]{:S(2)}) collective-permute-start(f32[2,128,128]{1,2,0:T(8,128)S(1)} %bitcast.105), channel_id=1, source_target_pairs={{0,16},{16,0},{1,17},{17,1},{2,18},{18,2},{3,19},{19,3},{4,20},{20... | collective-permute-start | bytes 393224 | tf_op jit(solution)/shard_map/ppermute | solution.py:36
  46.1 0.7 %collective-permute-done.2 = f32[2,2,2,128,128]{4,3,2,1,0:T(8,128)S(1)} collective-permute-done((f32[2,2,2,128,128]{4,3,2,1,0:T(8,128)S(1)}, f32[2,2,2,128,128]{4,3,2,1,0:T(8,128)S(1)}, u32[]{:S(2)}, u32[]{:S(2)}) %collective-permute-start.2) | collective-permute-done | bytes 524320 | tf_op jit(solution)/shard_map/ppermute | solution.py:31
  46.9 2.7 %collective-permute-start.3 = (f32[2,2,128,128]{3,2,1,0:T(8,128)S(1)}, f32[2,2,128,128]{3,2,1,0:T(8,128)S(1)}, u32[]{:S(2)}, u32[]{:S(2)}) collective-permute-start(f32[2,2,128,128]{3,2,1,0:T(8,128)S(1)} %dynamic-slice_bitcast_fusion.2), channel_id=1, source_target_pairs={{0,4},{1,5},{2,6},{3,7},{4,0},{5,1},{6,2},{7,3},{8,12},{9,13},{10,... | collective-permute-start | bytes 786440 | tf_op jit(solution)/shard_map/ppermute | solution.py:31
  49.7 4.2 %collective-permute-done.3 = f32[2,2,128,128]{3,2,1,0:T(8,128)S(1)} collective-permute-done((f32[2,2,128,128]{3,2,1,0:T(8,128)S(1)}, f32[2,2,128,128]{3,2,1,0:T(8,128)S(1)}, u32[]{:S(2)}, u32[]{:S(2)}) %collective-permute-start.3) | collective-permute-done | bytes 262176 | tf_op jit(solution)/shard_map/ppermute | solution.py:31
  54.0 6.0 %collective-permute-start.4 = (f32[2,128,128]{2,1,0:T(8,128)S(1)}, f32[2,128,128]{2,1,0:T(8,128)S(1)}, u32[]{:S(2)}, u32[]{:S(2)}) collective-permute-start(f32[2,128,128]{2,1,0:T(8,128)S(1)} %dynamic-slice_bitcast_fusion.3), channel_id=1, source_target_pairs={{0,8},{1,9},{2,10},{3,11},{4,12},{5,13},{6,14},{7,15},{8,0},{9,1},... | collective-permute-start | bytes 393224 | tf_op jit(solution)/shard_map/ppermute | solution.py:31
  60.0 0.2 fusion.1
  60.3 5.5 %collective-permute-done.4 = f32[2,128,128]{2,1,0:T(8,128)S(1)} collective-permute-done((f32[2,128,128]{2,1,0:T(8,128)S(1)}, f32[2,128,128]{2,1,0:T(8,128)S(1)}, u32[]{:S(2)}, u32[]{:S(2)}) %collective-permute-start.4) | collective-permute-done | bytes 131104 | tf_op jit(solution)/shard_map/ppermute | solution.py:31
  65.8 0.9 %fusion = bf16[256,256]{1,0:T(8,128)(2,1)} fusion(f32[256,256]{1,0:T(8,128)S(1)} %fusion.1, f32[256,128]{1,0:T(8,128)S(1)} %bitcast.101, bf16[128,256]{1,0:T(8,128)(2,1)S(1)} %copy-done.2), kind=kOutput, calls=%fused_computation.1 | convolution fusion | flops 100794368 | bytes 589824 | tf_op jit(solution)/shard_map/dot_general | solution.py:246
  (26 shorter events, 0.9 us)
Async XLA Ops:
  0.0 60.0 %copy-start = (bf16[128,256]{1,0:T(8,128)(2,1)S(1)}, bf16[128,256]{1,0:T(8,128)(2,1)}, u32[]{:S(2)}) copy-start(bf16[128,256]{1,0:T(8,128)(2,1)} %param.13) | copy-start | bytes 196612
  0.0 11.5 %collective-permute-start = (bf16[1,256,128]{2,1,0:T(8,128)(2,1)}, bf16[1,256,128]{2,1,0:T(8,128)(2,1)S(1)}, u32[]{:S(2)}, u32[]{:S(2)}) collective-permute-start(bf16[1,256,128]{2,1,0:T(8,128)(2,1)} %bitcast.102), channel_id=1, source_target_pairs={{0,16},{16,0},{1,17},{17,1},{2,18},{18,2},{3,19},{19,3},{4,20},{20... | collective-permute-start | bytes 196616 | tf_op jit(solution)/shard_map/ppermute | solution.py:36
  0.5 8.0 %collective-permute-start.5 = (bf16[1,2,128,128]{2,3,1,0:T(8,128)(2,1)}, bf16[1,2,128,128]{2,3,1,0:T(8,128)(2,1)S(1)}, u32[]{:S(2)}, u32[]{:S(2)}) collective-permute-start(bf16[1,2,128,128]{2,3,1,0:T(8,128)(2,1)} %bitcast.103), channel_id=1, source_target_pairs={{0,8},{1,9},{2,10},{3,11},{4,12},{5,13},{6,14},{7,15},{8,0},{9,1},... | collective-permute-start | bytes 196616 | tf_op jit(solution)/shard_map/ppermute | solution.py:31
  9.9 8.7 %collective-permute-start.6 = (bf16[2,2,128,128]{2,3,1,0:T(8,128)(2,1)}, bf16[2,2,128,128]{2,3,1,0:T(8,128)(2,1)S(1)}, u32[]{:S(2)}, u32[]{:S(2)}) collective-permute-start(bf16[2,2,128,128]{2,3,1,0:T(8,128)(2,1)} %maximum_bitcast_fusion), channel_id=1, source_target_pairs={{0,1},{1,0},{2,3},{3,2},{4,5},{5,4},{6,7},{7,6},{8,9},{9,8},{10,11... | collective-permute-start | bytes 393224 | tf_op jit(solution)/shard_map/ppermute | solution.py:31
  18.4 13.1 %copy-start.3 = (s32[1,1,128]{2,1,0:T(1,128)S(1)}, s32[1,1,128]{2,1,0:T(1,128)}, u32[]{:S(2)}) copy-start(s32[1,1,128]{2,1,0:T(1,128)} %param.9) | copy-start | bytes 1540
  18.4 17.8 %copy-start.1 = (f32[32,128,128]{2,1,0:T(8,128)S(1)}, f32[32,128,128]{2,1,0:T(8,128)}, u32[]{:S(2)}) copy-start(f32[32,128,128]{2,1,0:T(8,128)} %shard_map.73) | copy-start | bytes 6291460
  18.4 17.8 %collective-permute-start.1 = (f32[2,2,2,2,128,128]{5,4,3,2,1,0:T(8,128)S(1)}, f32[2,2,2,2,128,128]{5,4,3,2,1,0:T(8,128)}, u32[]{:S(2)}, u32[]{:S(2)}) collective-permute-start(f32[2,2,2,2,128,128]{5,4,3,2,1,0:T(8,128)S(1)} %dynamic-slice_bitcast_fusion), channel_id=1, source_target_pairs={{0,1},{1,0},{2,3},{3,2},{4,5},{5,4},{6,7},{7,6},{8,9},{9,8},{10,11... | collective-permute-start | bytes 3145736 | tf_op jit(solution)/shard_map/ppermute | solution.py:31
  19.6 6.6 %collective-permute-start.7 = (bf16[4,2,128,128]{3,2,1,0:T(8,128)(2,1)}, bf16[4,2,128,128]{3,2,1,0:T(8,128)(2,1)S(1)}, u32[]{:S(2)}, u32[]{:S(2)}) collective-permute-start(bf16[4,2,128,128]{3,2,1,0:T(8,128)(2,1)} %copy.12), channel_id=1, source_target_pairs={{0,2},{1,3},{2,0},{3,1},{4,6},{5,7},{6,4},{7,5},{8,10},{9,11},{10,... | collective-permute-start | bytes 786440 | tf_op jit(solution)/shard_map/ppermute | solution.py:31
  27.2 11.7 %collective-permute-start.8 = (bf16[8,2,128,128]{3,2,1,0:T(8,128)(2,1)S(1)}, bf16[8,2,128,128]{3,2,1,0:T(8,128)(2,1)S(1)}, u32[]{:S(2)}, u32[]{:S(2)}) collective-permute-start(bf16[8,2,128,128]{3,2,1,0:T(8,128)(2,1)S(1)} %bitcast.96), channel_id=1, source_target_pairs={{0,4},{1,5},{2,6},{3,7},{4,0},{5,1},{6,2},{7,3},{8,12},{9,13},{10,... | collective-permute-start | bytes 1572872 | tf_op jit(solution)/shard_map/ppermute | solution.py:31
  37.6 9.2 %collective-permute-start.2 = (f32[2,2,2,128,128]{4,3,2,1,0:T(8,128)S(1)}, f32[2,2,2,128,128]{4,3,2,1,0:T(8,128)S(1)}, u32[]{:S(2)}, u32[]{:S(2)}) collective-permute-start(f32[2,2,2,128,128]{4,3,2,1,0:T(8,128)S(1)} %dynamic-slice_bitcast_fusion.1), channel_id=1, source_target_pairs={{0,2},{1,3},{2,0},{3,1},{4,6},{5,7},{6,4},{7,5},{8,10},{9,11},{10,... | collective-permute-start | bytes 1572872 | tf_op jit(solution)/shard_map/ppermute | solution.py:31
  44.8 21.0 %copy-start.2 = (bf16[128,256]{1,0:T(8,128)(2,1)S(1)}, bf16[128,256]{1,0:T(8,128)(2,1)}, u32[]{:S(2)}) copy-start(bf16[128,256]{1,0:T(8,128)(2,1)} %param.12) | copy-start | bytes 196612
  44.8 4.9 %collective-permute-start.9 = (f32[2,128,128]{1,2,0:T(8,128)S(1)}, f32[2,128,128]{1,2,0:T(8,128)S(1)}, u32[]{:S(2)}, u32[]{:S(2)}) collective-permute-start(f32[2,128,128]{1,2,0:T(8,128)S(1)} %bitcast.105), channel_id=1, source_target_pairs={{0,16},{16,0},{1,17},{17,1},{2,18},{18,2},{3,19},{19,3},{4,20},{20... | collective-permute-start | bytes 393224 | tf_op jit(solution)/shard_map/ppermute | solution.py:36
  46.9 7.0 %collective-permute-start.3 = (f32[2,2,128,128]{3,2,1,0:T(8,128)S(1)}, f32[2,2,128,128]{3,2,1,0:T(8,128)S(1)}, u32[]{:S(2)}, u32[]{:S(2)}) collective-permute-start(f32[2,2,128,128]{3,2,1,0:T(8,128)S(1)} %dynamic-slice_bitcast_fusion.2), channel_id=1, source_target_pairs={{0,4},{1,5},{2,6},{3,7},{4,0},{5,1},{6,2},{7,3},{8,12},{9,13},{10,... | collective-permute-start | bytes 786440 | tf_op jit(solution)/shard_map/ppermute | solution.py:31
  54.0 11.8 %collective-permute-start.4 = (f32[2,128,128]{2,1,0:T(8,128)S(1)}, f32[2,128,128]{2,1,0:T(8,128)S(1)}, u32[]{:S(2)}, u32[]{:S(2)}) collective-permute-start(f32[2,128,128]{2,1,0:T(8,128)S(1)} %dynamic-slice_bitcast_fusion.3), channel_id=1, source_target_pairs={{0,8},{1,9},{2,10},{3,11},{4,12},{5,13},{6,14},{7,15},{8,0},{9,1},... | collective-permute-start | bytes 393224 | tf_op jit(solution)/shard_map/ppermute | solution.py:31
